TPU v7x, 32 devices: a whole 2x2x4 slice. The times are simulated.
32 devices in a mesh: dp: 4 (over z), ctx: 2 (over y), head: 4 (over x, core).
Axes of the slice: x: 2, y: 2, z: 4, core: 2. Of those that a mesh axis runs over, the one named last changes fastest.
Arguments:
- hidden_in: bfloat16 [3072, 4096], P(('dp', 'ctx')), may hold values from -6 to 6
- w_query: bfloat16 [4096, 4096], P(('dp', 'ctx'), 'head'), may hold values from -0.09375 to 0.09375
- w_key: bfloat16 [4096, 512], P(('dp', 'ctx'), 'head'), may hold values from -0.09375 to 0.09375
- w_value: bfloat16 [4096, 512], P(('dp', 'ctx'), 'head'), may hold values from -0.09375 to 0.09375
- lengths: int32 [4, 8], P('dp'), may hold values from 1 to 384, 768 in all within a row
- attn_grad: bfloat16 [3072, 4096], P(('dp', 'ctx'), 'head'), may hold values from -6 to 6
Outputs:
- attended: bfloat16 [3072, 4096], P(('dp', 'ctx'), 'head')
- grad_input: bfloat16 [3072, 4096], P(('dp', 'ctx'), 'head')
- grad_query_w: float32 [4096, 4096], P(('dp', 'ctx'), 'head')
- grad_key_w: float32 [4096, 512], P(('dp', 'ctx'), 'head')
- grad_value_w: float32 [4096, 512], P(('dp', 'ctx'), 'head')
Inputs may be any that keep to these rules, and one draw needn't show every extreme that they name: `lengths`: each row sums to 768; the longest document of every row has exactly 384 positions.
All inputs are finite; a program needn't handle non-finite values.
Results may differ from a plain program's by a relative error of at most 0.018.
Values may be sent and summed in bfloat16 or wider, within the bound.
No kernel may reach another device: no remote copies, remote signals or barrier semaphores. Data moves between devices by JAX's collectives and lax.ppermute only.
A program may use at most 128 MiB of HBM per device.

v0:
```python
import jax
import jax.numpy as jnp
from jax import lax
from jax.sharding import PartitionSpec as P

scale_factor = 128.0 ** (-0.5)
neg_large = -1e30


def rope_tables(positions):
    inverse = jnp.power(500000.0, -jnp.arange(64, dtype=jnp.float32) / 64.0)
    angles = positions.astype(jnp.float32)[:, None] * inverse[None, :]
    return (jnp.cos(angles)[:, None, :], jnp.sin(angles)[:, None, :])


def rotate(entries, cosine, sine_table):
    first_half = entries[..., :64]
    second_half = entries[..., 64:]
    return jnp.concatenate(
        [
            first_half * cosine - second_half * sine_table,
            second_half * cosine + first_half * sine_table,
        ],
        -1,
    )


def unrotate(entries, cosine, sine_table):
    first_half = entries[..., :64]
    second_half = entries[..., 64:]
    return jnp.concatenate(
        [
            first_half * cosine + second_half * sine_table,
            second_half * cosine - first_half * sine_table,
        ],
        -1,
    )


def segment_ids(length_row, positions):
    ends = jnp.cumsum(length_row)
    return jnp.sum((positions[:, None] >= ends[None, :]).astype(jnp.int32), 1)


def block_scores(query_blk, key_blk, query_pos, key_pos, query_seg, key_seg):
    scores = (
        jnp.einsum("rhd,kd->hrk", query_blk, key_blk, preferred_element_type=jnp.float32)
        * scale_factor
    )
    allowed = (key_pos[None, :] <= query_pos[:, None]) & (key_seg[None, :] == query_seg[:, None])
    return (scores, allowed[None])


def grad_block(
    query_blk,
    dout_blk,
    total_blk,
    delta_blk,
    key_blk,
    value_blk,
    query_pos,
    key_pos,
    query_seg,
    key_seg,
):
    scores, allowed = block_scores(query_blk, key_blk, query_pos, key_pos, query_seg, key_seg)
    prob_rows = jnp.where(
        allowed, jnp.exp(jnp.where(allowed, scores - total_blk[..., None], neg_large)), 0.0
    )
    prob_b = prob_rows.astype(jnp.bfloat16)
    d_prob = jnp.einsum("rhd,kd->hrk", dout_blk, value_blk, preferred_element_type=jnp.float32)
    d_score = (scale_factor * prob_rows * (d_prob - delta_blk[..., None])).astype(jnp.bfloat16)
    return (prob_b, d_score)


def local(hidden_in, w_query, w_key, w_value, lengths, attn_grad):
    num_rows = hidden_in.shape[0]
    head_count = w_query.shape[1] // 128
    query_cols = head_count * 128
    start_row = lax.axis_index("ctx") * num_rows
    seq_len = num_rows * lax.axis_size("ctx")
    kblock = 512 if seq_len % 512 == 0 else 128
    positions = start_row + jnp.arange(num_rows, dtype=jnp.int32)
    all_pos = jnp.arange(seq_len, dtype=jnp.int32)
    seg_all = segment_ids(lengths[0], all_pos)
    seg_own = lax.dynamic_slice_in_dim(seg_all, start_row, num_rows)
    cosine, sine_table = rope_tables(positions)
    local_w = jnp.concatenate([w_query, w_key, w_value], 1)
    full_w = lax.all_gather(local_w, ("dp", "ctx"), axis=0, tiled=True)
    projected = jnp.dot(hidden_in, full_w, preferred_element_type=jnp.float32)
    query_rows = rotate(
        projected[:, :query_cols].reshape(num_rows, head_count, 128), cosine, sine_table
    ).astype(jnp.bfloat16)
    key_rows = rotate(
        projected[:, query_cols : query_cols + 128].reshape(num_rows, 1, 128), cosine, sine_table
    )[:, 0, :].astype(jnp.bfloat16)
    value_rows = projected[:, query_cols + 128 :].astype(jnp.bfloat16)
    key_all, value_all = (
        lax.all_gather(key_rows, "ctx", axis=0, tiled=True),
        lax.all_gather(value_rows, "ctx", axis=0, tiled=True),
    )
    causal_limit = (start_row + num_rows + kblock - 1) // kblock
    key_first = jnp.int32(0)

    def take_block(block_index):
        first_row = block_index * kblock
        return (
            lax.dynamic_slice_in_dim(key_all, first_row, kblock, 0),
            lax.dynamic_slice_in_dim(value_all, first_row, kblock, 0),
            lax.dynamic_slice_in_dim(all_pos, first_row, kblock, 0),
            lax.dynamic_slice_in_dim(seg_all, first_row, kblock, 0),
        )

    def stats_step(block_index, carried):
        run_max, run_sum = carried
        key_blk, value_blk, key_pos, key_seg = take_block(block_index)
        scores, allowed = block_scores(query_rows, key_blk, positions, key_pos, seg_own, key_seg)
        masked = jnp.where(allowed, scores, neg_large)
        new_max = jnp.maximum(run_max, jnp.max(masked, -1))
        terms = jnp.where(allowed, jnp.exp(masked - new_max[..., None]), 0.0)
        return (new_max, run_sum * jnp.exp(run_max - new_max) + jnp.sum(terms, -1))

    start_stats = (
        jnp.full((head_count, num_rows), neg_large, jnp.float32),
        jnp.zeros((head_count, num_rows), jnp.float32),
    )
    run_max, run_sum = lax.fori_loop(key_first, causal_limit, stats_step, start_stats)
    log_total = run_max + jnp.log(run_sum)

    def output_step(block_index, carried):
        key_blk, value_blk, key_pos, key_seg = take_block(block_index)
        scores, allowed = block_scores(query_rows, key_blk, positions, key_pos, seg_own, key_seg)
        prob_b = jnp.where(
            allowed, jnp.exp(jnp.where(allowed, scores - log_total[..., None], neg_large)), 0.0
        ).astype(jnp.bfloat16)
        return carried + jnp.einsum(
            "hrk,kd->rhd", prob_b, value_blk, preferred_element_type=jnp.float32
        )

    out_sum = lax.fori_loop(
        key_first, causal_limit, output_step, jnp.zeros((num_rows, head_count, 128), jnp.float32)
    )
    out_rows = out_sum.astype(jnp.bfloat16)
    attended = out_rows.reshape(num_rows, query_cols)
    dout_rows = attn_grad.reshape(num_rows, head_count, 128)
    delta_rows = jnp.einsum("rhd,rhd->hr", dout_rows, out_rows, preferred_element_type=jnp.float32)

    def sums_step(block_index, carried):
        grad_q, part_k, part_v = carried
        first_row = block_index * kblock
        key_blk, value_blk, key_pos, key_seg = take_block(block_index)
        prob_b, d_score = grad_block(
            query_rows,
            dout_rows,
            log_total,
            delta_rows,
            key_blk,
            value_blk,
            positions,
            key_pos,
            seg_own,
            key_seg,
        )
        grad_q = grad_q + jnp.einsum(
            "hrk,kd->rhd", d_score, key_blk, preferred_element_type=jnp.float32
        )
        block_k = jnp.einsum("hrk,rhd->kd", d_score, query_rows, preferred_element_type=jnp.float32)
        block_v = jnp.einsum("hrk,rhd->kd", prob_b, dout_rows, preferred_element_type=jnp.float32)
        part_k = lax.dynamic_update_slice_in_dim(
            part_k, lax.dynamic_slice_in_dim(part_k, first_row, kblock, 0) + block_k, first_row, 0
        )
        part_v = lax.dynamic_update_slice_in_dim(
            part_v, lax.dynamic_slice_in_dim(part_v, first_row, kblock, 0) + block_v, first_row, 0
        )
        return (grad_q, part_k, part_v)

    start_sums = (
        jnp.zeros((num_rows, head_count, 128), jnp.float32),
        jnp.zeros((seq_len, 128), jnp.float32),
        jnp.zeros((seq_len, 128), jnp.float32),
    )
    grad_q, part_k, part_v = lax.fori_loop(key_first, causal_limit, sums_step, start_sums)
    grad_k, grad_v = (
        lax.psum_scatter(part_k, "ctx", scatter_dimension=0, tiled=True),
        lax.psum_scatter(part_v, "ctx", scatter_dimension=0, tiled=True),
    )
    d_query = (
        unrotate(grad_q, cosine, sine_table).astype(jnp.bfloat16).reshape(num_rows, query_cols)
    )
    d_key = unrotate(grad_k[:, None, :], cosine, sine_table)[:, 0, :].astype(jnp.bfloat16)
    d_value = grad_v.astype(jnp.bfloat16)
    d_proj = jnp.concatenate([d_query, d_key, d_value], 1)
    input_part = lax.dot_general(
        d_proj, full_w, (((1,), (1,)), ((), ())), preferred_element_type=jnp.float32
    )
    grad_input = lax.psum_scatter(input_part, "head", scatter_dimension=1, tiled=True).astype(
        jnp.bfloat16
    )
    weight_sum = lax.psum_scatter(
        lax.dot_general(
            hidden_in, d_proj, (((0,), (0,)), ((), ())), preferred_element_type=jnp.float32
        ),
        ("dp", "ctx"),
        scatter_dimension=0,
        tiled=True,
    )
    return (
        attended,
        grad_input,
        weight_sum[:, :query_cols],
        weight_sum[:, query_cols : query_cols + 128],
        weight_sum[:, query_cols + 128 :],
    )


def solution(mesh):
    placed = (
        P(("dp", "ctx"), None),
        P(("dp", "ctx"), "head"),
        P(("dp", "ctx"), "head"),
        P(("dp", "ctx"), "head"),
        P("dp", None),
        P(("dp", "ctx"), "head"),
    )
    return jax.shard_map(
        local,
        mesh=mesh,
        in_specs=placed,
        out_specs=(
            P(("dp", "ctx"), "head"),
            P(("dp", "ctx"), "head"),
            P(("dp", "ctx"), "head"),
            P(("dp", "ctx"), "head"),
            P(("dp", "ctx"), "head"),
        ),
        check_vma=False,
    )
```

profile of v0, /device:TPU:0, one launch (start us, length us, event | category | flops | bytes accessed | tf_op | source)
XLA Modules:
  0.0 768.0 jit_solution(3426994083123436264)
XLA Ops:
  7.2 2.7 pad_maximum_fusion
  10.2 2.3 copy.51
  12.5 2.3 copy.55
  15.4 149.0 %all-gather.3.cloned.1.call-done = bf16[4096,1280]{1,0:T(8,128)(2,1)} async-done(((bf16[512,1280]{1,0:T(8,128)(2,1)}), bf16[4096,1280]{1,0:T(8,128)(2,1)}) %all-gather.3.cloned.1.call-update) | async-done | bytes 10485776 | tf_op jit(solution)/shard_map/all_gather | solution.py:89
  164.4 8.3 %convolution_bitcast_fusion.3 = f32[384,1280]{0,1:T(8,128)S(1)} fusion(bf16[4096,1280]{1,0:T(8,128)(2,1)} %all-gather.3.cloned.1.call-done, bf16[384,4096]{1,0:T(8,128)(2,1)S(1)} %copy-done), kind=kOutput, calls=%fused_computation.60 | convolution fusion | flops 4026531840 | bytes 15597568 | tf_op jit(solution)/shard_map/dot_general | solution.py:90
  172.9 5.4 all_gather.10
  179.0 1.0 pad_maximum_fusion.2
  179.9 2.3 copy.49
  182.2 5.3 all-gather
  187.7 6.6 while.39
  188.0 1.5 fusion.101
  190.2 1.5 fusion.101
  192.4 1.5 fusion.101
  194.3 1.3 broadcast.221.clone
  195.6 11.9 %while.40 = (s32[]{:T(128)}, f32[384,8,128]{0,2,1:T(8,128)}, s32[]{:T(128)}, bf16[768,128]{0,1:T(8,128)(2,1)}, s32[768]{0:T(1024)S(1)}, /*index=5*/s32[768]{0:T(...) while((s32[]{:T(128)}, f32[384,8,128]{0,2,1:T(8,128)}, ...), condition=%wide.region_7.8_spmd.clone, body=%wide.region_6.7_spmd.clone.sunk | while | flops 203833728 | bytes 4117191 | solution.py:140
  195.9 3.7 bitcast_add_fusion.4
  199.8 3.7 bitcast_add_fusion.4
  203.8 3.7 bitcast_add_fusion.4
  208.0 2.7 fusion.47
  210.8 0.8 broadcast.222.clone
  211.6 0.8 broadcast.222
  212.3 1.3 broadcast.221
  213.6 36.0 %while.41 = (s32[]{:T(128)}, f32[384,8,128]{0,2,1:T(8,128)}, f32[768,128]{0,1:T(8,128)}, f32[768,128]{1,0:T(8,128)}, s32[]{:T(128)}, /*index=5*/bf16[768,128]{1,...) while((s32[]{:T(128)}, f32[384,8,128]{0,2,1:T(8,128)}, ...), condition=%wide.region_9.10_spmd.clone, body=%wide.region_8.9_spmd.clone.sunk | while | flops 507429248 | bytes 23945156 | solution.py:182
  213.6 0.8 dynamic_slice.111
  214.6 0.9 constant_dynamic-slice_fusion.2
  215.5 1.8 fusion.115
  217.3 1.8 fusion.118
  219.2 1.2 fusion.116
  220.4 0.9 copy-done.2
  221.7 0.6 constant_dynamic-update-slice_fusion.2
  222.4 3.2 bitcast_add_fusion.5
  225.6 0.8 dynamic_slice.111
  226.6 0.9 constant_dynamic-slice_fusion.2
  227.5 1.8 fusion.115
  229.3 1.8 fusion.118
  231.1 1.2 fusion.116
  232.4 0.9 copy-done.2
  233.7 0.6 constant_dynamic-update-slice_fusion.2
  234.4 3.2 bitcast_add_fusion.5
  237.6 0.8 dynamic_slice.111
  238.6 0.9 constant_dynamic-slice_fusion.2
  239.5 1.8 fusion.115
  241.3 1.8 fusion.118
  243.1 1.2 fusion.116
  244.4 0.9 copy-done.2
  246.4 3.2 bitcast_add_fusion.5
  249.7 0.7 reduce-scatter.5.cloned.1.call-update
  250.6 1.6 add_convert_fusion
  252.2 1.0 pad_maximum_fusion.3
  253.2 62.3 %reduce-scatter.7.cloned.1.call-done = f32[384,128]{1,0:T(8,128)} async-done(((f32[768,128]{1,0:T(8,128)}), f32[384,128]{1,0:T(8,128)}) %reduce-scatter.7.cloned.1.call-update) | async-done | bytes 196624 | tf_op jit(solution)/shard_map/reduce_scatter | solution.py:185
  315.5 0.9 convert_element_type.49
  316.5 15.0 %reduce-scatter.5.cloned.1.call-done = f32[384,128]{0,1:T(8,128)} async-done(((f32[768,128]{0,1:T(8,128)}), f32[384,128]{0,1:T(8,128)}) %reduce-scatter.5.cloned.1.call-update) | async-done | bytes 196624 | tf_op jit(solution)/shard_map/reduce_scatter | solution.py:184
  331.5 1.4 fusion.62
  332.9 11.2 %fusion.48 = f32[384,4096]{1,0:T(8,128)} fusion(bf16[4096,1280]{1,0:T(8,128)(2,1)} %all-gather.3.cloned.1.call-done, bf16[384,128]{0,1:T(8,128)(2,1)S(1)} %copy.57, bf16[384,128]{0,1:T(8,128)(2,1)S(1)} %maximum_bitcast_fusion, bf16[384,1024]{0,1:T(8,128)(2,1)} %bitcast.143), kind=kOutput, calls=%fused_computation.71 | convolution fusion | flops 4029480960 | bytes 17760256 | tf_op jit(solution)/shard_map/dot_general | solution.py:193
  344.2 13.8 %convolution_bitcast_fusion.2 = f32[4096,1280]{0,1:T(8,128)} fusion(bf16[384,4096]{1,0:T(8,128)(2,1)S(1)} %copy-done, bf16[384,128]{0,1:T(8,128)(2,1)S(1)} %copy.57, bf16[384,128]{0,1:T(8,128)(2,1)S(1)} %maximum_bitcast_fusion, bf16[384,1024]{0,1:T(8,128)(2,1)} %bitcast.144), kind=kOutput, calls=%fused_computation.59 | convolution fusion | flops 4029480960 | bytes 25100288 | tf_op jit(solution)/shard_map/dot_general | solution.py:200
  358.0 2.3 copy.70
  360.3 42.3 %reduce-scatter.9.cloned.1.call-done = f32[384,1024]{1,0:T(8,128)} async-done(((f32[384,4096]{1,0:T(8,128)}), f32[384,1024]{1,0:T(8,128)}) %reduce-scatter.9.cloned.1.call-update) | async-done | bytes 1572880 | tf_op jit(solution)/shard_map/reduce_scatter | solution.py:196
  402.6 2.4 convert_element_type.50
  405.1 346.1 %reduce-scatter.11.cloned.1.call-done = f32[512,1280]{0,1:T(8,128)} async-done(((f32[4096,1280]{0,1:T(8,128)}), f32[512,1280]{0,1:T(8,128)}) %reduce-scatter.11.cloned.1.call-update) | async-done | bytes 2621456 | tf_op jit(solution)/shard_map/reduce_scatter | solution.py:199
  751.1 3.1 slice.66
  754.2 2.9 copy.58
  757.1 1.8 fusion.68
  758.9 1.8 copy.60
  760.6 0.8 copy.59
  (142 shorter events, 8.4 us)
Async XLA Ops:
  7.2 157.2 %copy-start = (bf16[384,4096]{1,0:T(8,128)(2,1)S(1)}, bf16[384,4096]{1,0:T(8,128)(2,1)}, u32[]{:S(2)}) copy-start(bf16[384,4096]{1,0:T(8,128)(2,1)} %param.12) | copy-start | bytes 9437188
  7.2 2.8 copy-start.15
  7.2 157.2 %all-gather.3.cloned.1.call-start = ((), (), s32[]{:S(2)}) async-start(), calls=%async_computation.4 | async-start | bytes 11796480 | tf_op jit(solution)/shard_map/all_gather | solution.py:89
  9.9 305.5 %reduce-scatter.7.cloned.1.call-start = ((), (), s32[]{:S(2)}) async-start(), calls=%async_computation.6 | async-start | bytes 589824 | tf_op jit(solution)/shard_map/reduce_scatter | solution.py:185
  14.9 163.3 %copy-start.11 = (f32[64]{0:T(128)}, f32[64]{0:T(128)S(1)}, u32[]{:S(2)}) copy-start(f32[64]{0:T(128)S(1)} %multiply_power_fusion) | copy-start | bytes 772
  14.9 163.3 %copy-start.8 = (f32[384]{0:T(512)}, f32[384]{0:T(512)S(1)}, u32[]{:S(2)}) copy-start(f32[384]{0:T(512)S(1)} %add_convert_fusion.2) | copy-start | bytes 4612
  15.4 163.3 %copy-start.4 = (f32[384,64]{0,1:T(8,128)}, f32[384,64]{0,1:T(8,128)S(1)}, u32[]{:S(2)}) copy-start(f32[384,64]{0,1:T(8,128)S(1)} %get-tuple-element.496) | copy-start | bytes 294916
  15.4 163.3 %copy-start.5 = (f32[384,64]{0,1:T(8,128)}, f32[384,64]{0,1:T(8,128)S(1)}, u32[]{:S(2)}) copy-start(f32[384,64]{0,1:T(8,128)S(1)} %get-tuple-element.497) | copy-start | bytes 294916
  207.5 0.6 copy-start.10
  213.6 0.8 copy-start.13
  213.6 3.7 copy-start.6
  215.5 1.8 copy-start.3
  219.2 2.1 copy-start.1
  220.4 0.9 copy-start.2
  222.4 3.2 copy-start.7
  222.4 3.2 copy-start.14
  225.6 0.8 copy-start.13
  225.6 3.7 copy-start.6
  227.5 1.8 copy-start.3
  231.1 2.1 copy-start.1
  232.4 0.9 copy-start.2
  234.4 3.2 copy-start.7
  234.4 3.2 copy-start.14
  237.6 0.8 copy-start.13
  237.6 3.7 copy-start.6
  239.5 1.8 copy-start.3
  243.1 2.1 copy-start.1
  244.4 0.9 copy-start.2
  246.4 3.2 copy-start.7
  246.4 3.2 copy-start.14
  249.6 81.9 %reduce-scatter.5.cloned.1.call-start = ((), (), s32[]{:S(2)}) async-start(), calls=%async_computation.5 | async-start | bytes 589824 | tf_op jit(solution)/shard_map/reduce_scatter | solution.py:184
  250.3 152.3 %reduce-scatter.9.cloned.1.call-start = ((), (), s32[]{:S(2)}) async-start(), calls=%async_computation.7 | async-start | bytes 7864320 | tf_op jit(solution)/shard_map/reduce_scatter | solution.py:196
  252.2 79.3 %copy-start.9 = (f32[384]{0:T(512)S(1)}, f32[384]{0:T(512)}, u32[]{:S(2)}) copy-start(f32[384]{0:T(512)} %copy-done.8) | copy-start | bytes 4612
  252.2 79.3 %copy-start.12 = (f32[64]{0:T(128)S(1)}, f32[64]{0:T(128)}, u32[]{:S(2)}) copy-start(f32[64]{0:T(128)} %copy-done.11) | copy-start | bytes 772
  344.1 407.0 %reduce-scatter.11.cloned.1.call-start = ((), (), s32[]{:S(2)}) async-start(), calls=%async_computation.8 | async-start | bytes 23592960 | tf_op jit(solution)/shard_map/reduce_scatter | solution.py:199
Sparse Core Ops, SparseCore 0:
  10.8 153.5 all-gather.2
  249.7 65.6 reduce-scatter.6
  318.4 13.0 reduce-scatter.4
  344.3 58.3 reduce-scatter.8
  406.9 344.1 reduce-scatter.10
where the time goes:
time: 770 us; the launch traced here: 768 us
  waiting for transfers between devices  615 us (80%)
  matrix products  74.2 us (10%)
  local copies, waits for them, and re-layouts  35.8 us (5%)
  other arithmetic  17 us (2%)
  between operations  14 us (2%)
  blocking collectives  10.7 us (1%)
    reduce_scatter x1, waiting for transfers between devices, local(): lax.psum_scatter(lax.dot_general(hidden_in, d_proj, (((0,), (0,)), ((), (...  346 us
    all_gather x1, waiting for transfers between devices, local(): full_w = lax.all_gather(local_w, ('dp', 'ctx'), axis=0, tiled=True)  149 us
    reduce_scatter x1, waiting for transfers between devices, local(): lax.psum_scatter(part_v, 'ctx', scatter_dimension=0, tiled=True)  62.3 us
    reduce_scatter x1, waiting for transfers between devices, local(): lax.psum_scatter(input_part, 'head', scatter_dimension=1, tiled=True)  42.3 us
  transfers between devices with their start and end apart: 5, of which 5 were waited for; matrix products, arithmetic and copies ran while one was open for 4% of the time, Pallas kernels for 0%

commit v1 on v0

v1 whole, which is shorter than its diff:
```python
import jax
import jax.numpy as jnp
from jax import lax
from jax.sharding import PartitionSpec as P

scale_factor = 128.0 ** (-0.5)
neg_large = -1e30


def rope_tables(positions):
    inverse = jnp.power(500000.0, -jnp.arange(64, dtype=jnp.float32) / 64.0)
    angles = positions.astype(jnp.float32)[:, None] * inverse[None, :]
    return (jnp.cos(angles)[:, None, :], jnp.sin(angles)[:, None, :])


def rotate(entries, cosine, sine_table):
    first_half = entries[..., :64]
    second_half = entries[..., 64:]
    return jnp.concatenate(
        [
            first_half * cosine - second_half * sine_table,
            second_half * cosine + first_half * sine_table,
        ],
        -1,
    )


def unrotate(entries, cosine, sine_table):
    first_half = entries[..., :64]
    second_half = entries[..., 64:]
    return jnp.concatenate(
        [
            first_half * cosine + second_half * sine_table,
            second_half * cosine - first_half * sine_table,
        ],
        -1,
    )


def segment_ids(length_row, positions):
    ends = jnp.cumsum(length_row)
    return jnp.sum((positions[:, None] >= ends[None, :]).astype(jnp.int32), 1)


def block_scores(query_blk, key_blk, query_pos, key_pos, query_seg, key_seg):
    scores = (
        jnp.einsum("rhd,kd->hrk", query_blk, key_blk, preferred_element_type=jnp.float32)
        * scale_factor
    )
    allowed = (key_pos[None, :] <= query_pos[:, None]) & (key_seg[None, :] == query_seg[:, None])
    return (scores, allowed[None])


def grad_block(
    query_blk,
    dout_blk,
    total_blk,
    delta_blk,
    key_blk,
    value_blk,
    query_pos,
    key_pos,
    query_seg,
    key_seg,
):
    scores, allowed = block_scores(query_blk, key_blk, query_pos, key_pos, query_seg, key_seg)
    prob_rows = jnp.where(
        allowed, jnp.exp(jnp.where(allowed, scores - total_blk[..., None], neg_large)), 0.0
    )
    prob_b = prob_rows.astype(jnp.bfloat16)
    d_prob = jnp.einsum("rhd,kd->hrk", dout_blk, value_blk, preferred_element_type=jnp.float32)
    d_score = (scale_factor * prob_rows * (d_prob - delta_blk[..., None])).astype(jnp.bfloat16)
    return (prob_b, d_score)


def attend_whole(query_rows, key_all, value_all, dout_rows, positions, all_pos, seg_own, seg_all):
    scores, allowed = block_scores(query_rows, key_all, positions, all_pos, seg_own, seg_all)
    masked = jnp.where(allowed, scores, neg_large)
    top_score = jnp.max(masked, -1)
    total = jnp.sum(jnp.where(allowed, jnp.exp(masked - top_score[..., None]), 0.0), -1)
    log_total = top_score + jnp.log(total)
    prob_rows = jnp.where(
        allowed, jnp.exp(jnp.where(allowed, scores - log_total[..., None], neg_large)), 0.0
    )
    prob_b = prob_rows.astype(jnp.bfloat16)
    out_rows = jnp.einsum(
        "hrk,kd->rhd", prob_b, value_all, preferred_element_type=jnp.float32
    ).astype(jnp.bfloat16)
    delta_rows = jnp.einsum("rhd,rhd->hr", dout_rows, out_rows, preferred_element_type=jnp.float32)
    d_prob = jnp.einsum("rhd,kd->hrk", dout_rows, value_all, preferred_element_type=jnp.float32)
    d_score = (scale_factor * prob_rows * (d_prob - delta_rows[..., None])).astype(jnp.bfloat16)
    grad_q = jnp.einsum("hrk,kd->rhd", d_score, key_all, preferred_element_type=jnp.float32)
    part_k = jnp.einsum("hrk,rhd->kd", d_score, query_rows, preferred_element_type=jnp.float32)
    part_v = jnp.einsum("hrk,rhd->kd", prob_b, dout_rows, preferred_element_type=jnp.float32)
    return out_rows, grad_q, part_k, part_v


def attend_blocked(query_rows, key_all, value_all, dout_rows, positions, all_pos, seg_own, seg_all, kblock):
    num_rows, head_count = query_rows.shape[0], query_rows.shape[1]
    seq_len = key_all.shape[0]
    causal_limit = (positions[-1] + kblock) // kblock
    key_first = jnp.int32(0)

    def take_block(block_index):
        first_row = block_index * kblock
        return (
            lax.dynamic_slice_in_dim(key_all, first_row, kblock, 0),
            lax.dynamic_slice_in_dim(value_all, first_row, kblock, 0),
            lax.dynamic_slice_in_dim(all_pos, first_row, kblock, 0),
            lax.dynamic_slice_in_dim(seg_all, first_row, kblock, 0),
        )

    def stats_step(block_index, carried):
        run_max, run_sum = carried
        key_blk, value_blk, key_pos, key_seg = take_block(block_index)
        scores, allowed = block_scores(query_rows, key_blk, positions, key_pos, seg_own, key_seg)
        masked = jnp.where(allowed, scores, neg_large)
        new_max = jnp.maximum(run_max, jnp.max(masked, -1))
        terms = jnp.where(allowed, jnp.exp(masked - new_max[..., None]), 0.0)
        return (new_max, run_sum * jnp.exp(run_max - new_max) + jnp.sum(terms, -1))

    start_stats = (
        jnp.full((head_count, num_rows), neg_large, jnp.float32),
        jnp.zeros((head_count, num_rows), jnp.float32),
    )
    run_max, run_sum = lax.fori_loop(key_first, causal_limit, stats_step, start_stats)
    log_total = run_max + jnp.log(run_sum)

    def output_step(block_index, carried):
        key_blk, value_blk, key_pos, key_seg = take_block(block_index)
        scores, allowed = block_scores(query_rows, key_blk, positions, key_pos, seg_own, key_seg)
        prob_b = jnp.where(
            allowed, jnp.exp(jnp.where(allowed, scores - log_total[..., None], neg_large)), 0.0
        ).astype(jnp.bfloat16)
        return carried + jnp.einsum(
            "hrk,kd->rhd", prob_b, value_blk, preferred_element_type=jnp.float32
        )

    out_sum = lax.fori_loop(
        key_first, causal_limit, output_step, jnp.zeros((num_rows, head_count, 128), jnp.float32)
    )
    out_rows = out_sum.astype(jnp.bfloat16)
    delta_rows = jnp.einsum("rhd,rhd->hr", dout_rows, out_rows, preferred_element_type=jnp.float32)

    def sums_step(block_index, carried):
        grad_q, part_k, part_v = carried
        first_row = block_index * kblock
        key_blk, value_blk, key_pos, key_seg = take_block(block_index)
        prob_b, d_score = grad_block(
            query_rows, dout_rows, log_total, delta_rows, key_blk, value_blk,
            positions, key_pos, seg_own, key_seg,
        )
        grad_q = grad_q + jnp.einsum(
            "hrk,kd->rhd", d_score, key_blk, preferred_element_type=jnp.float32
        )
        block_k = jnp.einsum("hrk,rhd->kd", d_score, query_rows, preferred_element_type=jnp.float32)
        block_v = jnp.einsum("hrk,rhd->kd", prob_b, dout_rows, preferred_element_type=jnp.float32)
        part_k = lax.dynamic_update_slice_in_dim(
            part_k, lax.dynamic_slice_in_dim(part_k, first_row, kblock, 0) + block_k, first_row, 0
        )
        part_v = lax.dynamic_update_slice_in_dim(
            part_v, lax.dynamic_slice_in_dim(part_v, first_row, kblock, 0) + block_v, first_row, 0
        )
        return (grad_q, part_k, part_v)

    start_sums = (
        jnp.zeros((num_rows, head_count, 128), jnp.float32),
        jnp.zeros((seq_len, 128), jnp.float32),
        jnp.zeros((seq_len, 128), jnp.float32),
    )
    grad_q, part_k, part_v = lax.fori_loop(key_first, causal_limit, sums_step, start_sums)
    return out_rows, grad_q, part_k, part_v


def local(hidden_in, w_query, w_key, w_value, lengths, attn_grad):
    num_rows = hidden_in.shape[0]
    head_count = w_query.shape[1] // 128
    query_cols = head_count * 128
    start_row = lax.axis_index("ctx") * num_rows
    seq_len = num_rows * lax.axis_size("ctx")
    positions = start_row + jnp.arange(num_rows, dtype=jnp.int32)
    all_pos = jnp.arange(seq_len, dtype=jnp.int32)
    seg_all = segment_ids(lengths[0], all_pos)
    seg_own = lax.dynamic_slice_in_dim(seg_all, start_row, num_rows)
    cosine, sine_table = rope_tables(positions)
    rows_axes = ("dp", "ctx")
    hidden_cols = lax.all_to_all(hidden_in, rows_axes, 1, 0, tiled=True)
    local_w = jnp.concatenate([w_query, w_key, w_value], 1)
    full_w = lax.all_gather(local_w, rows_axes, axis=0, tiled=True)
    projected = jnp.dot(hidden_in, full_w, preferred_element_type=jnp.float32)
    query_rows = rotate(
        projected[:, :query_cols].reshape(num_rows, head_count, 128), cosine, sine_table
    ).astype(jnp.bfloat16)
    key_rows = rotate(
        projected[:, query_cols : query_cols + 128].reshape(num_rows, 1, 128), cosine, sine_table
    )[:, 0, :].astype(jnp.bfloat16)
    value_rows = projected[:, query_cols + 128 :].astype(jnp.bfloat16)
    key_all, value_all = (
        lax.all_gather(key_rows, "ctx", axis=0, tiled=True),
        lax.all_gather(value_rows, "ctx", axis=0, tiled=True),
    )
    dout_rows = attn_grad.reshape(num_rows, head_count, 128)
    operands = (query_rows, key_all, value_all, dout_rows, positions, all_pos, seg_own, seg_all)
    if head_count * num_rows * seq_len <= (1 << 22):
        out_rows, grad_q, part_k, part_v = attend_whole(*operands)
    else:
        kblock = seq_len
        while head_count * num_rows * kblock > (1 << 22) and kblock % 256 == 0:
            kblock //= 2
        out_rows, grad_q, part_k, part_v = attend_blocked(*operands, kblock)
    attended = out_rows.reshape(num_rows, query_cols)
    grad_k, grad_v = (
        lax.psum_scatter(part_k, "ctx", scatter_dimension=0, tiled=True),
        lax.psum_scatter(part_v, "ctx", scatter_dimension=0, tiled=True),
    )
    d_query = (
        unrotate(grad_q, cosine, sine_table).astype(jnp.bfloat16).reshape(num_rows, query_cols)
    )
    d_key = unrotate(grad_k[:, None, :], cosine, sine_table)[:, 0, :].astype(jnp.bfloat16)
    d_value = grad_v.astype(jnp.bfloat16)
    d_proj = jnp.concatenate([d_query, d_key, d_value], 1)
    input_part = lax.dot_general(
        d_proj, full_w, (((1,), (1,)), ((), ())), preferred_element_type=jnp.float32
    )
    grad_input = lax.psum_scatter(input_part, "head", scatter_dimension=1, tiled=True).astype(
        jnp.bfloat16
    )
    d_proj_all = lax.all_gather(d_proj, rows_axes, axis=0, tiled=True)
    weight_sum = lax.dot_general(
        hidden_cols, d_proj_all, (((0,), (0,)), ((), ())), preferred_element_type=jnp.float32
    )
    return (
        attended,
        grad_input,
        weight_sum[:, :query_cols],
        weight_sum[:, query_cols : query_cols + 128],
        weight_sum[:, query_cols + 128 :],
    )


def solution(mesh):
    placed = (
        P(("dp", "ctx"), None),
        P(("dp", "ctx"), "head"),
        P(("dp", "ctx"), "head"),
        P(("dp", "ctx"), "head"),
        P("dp", None),
        P(("dp", "ctx"), "head"),
    )
    return jax.shard_map(
        local,
        mesh=mesh,
        in_specs=placed,
        out_specs=(
            P(("dp", "ctx"), "head"),
            P(("dp", "ctx"), "head"),
            P(("dp", "ctx"), "head"),
            P(("dp", "ctx"), "head"),
            P(("dp", "ctx"), "head"),
        ),
        check_vma=False,
    )
```

time: 770 us -> 458 us (0.59)
  waiting for transfers between devices: 615 us -> 236 us
  blocking collectives: 10.7 us -> 105 us
  matrix products: 74.2 us -> 58.2 us
  local copies, waits for them, and re-layouts: 35.8 us -> 22.9 us
    reduce_scatter x1 -> x0, waiting for transfers between devices: 346 us -> none  [local(): lax.psum_scatter(lax.dot_general(hidden_in, d_proj, (((0,), (0,)), ((), (...]
    all_to_all x0 -> x1, blocking collectives: none -> 93.8 us  [local(): hidden_cols = lax.all_to_all(hidden_in, rows_axes, 1, 0, tiled=True)]
    all_gather x1 -> x2, waiting for transfers between devices: 149 us -> 232 us  [the longest x1 150 us: local(): full_w = lax.all_gather(local_w, rows_axes, axis=0, tiled=True)]
    reduce_scatter x1, waiting for transfers between devices: 62.3 us -> 0.02 us  [local(): lax.psum_scatter(part_v, 'ctx', scatter_dimension=0, tiled=True)]
    reduce_scatter x1, waiting for transfers between devices: 42.3 us -> 0.01 us  [local(): lax.psum_scatter(input_part, 'head', scatter_dimension=1, tiled=True)]
    dot_general x16 -> x6, matrix products: 44.7 us -> 31.7 us  [the longest x1 7.78 us: attend_whole(): jnp.einsum('hrk,kd->rhd', prob_b, value_all, preferred_element_type=jnp.f...]
    reduce_scatter x1, waiting for transfers between devices: 15 us -> 4.22 us  [local(): lax.psum_scatter(part_k, 'ctx', scatter_dimension=0, tiled=True)]
    dot_general x6 -> x1, matrix products: 9.93 us -> 2.15 us  [block_scores(): jnp.einsum('rhd,kd->hrk', query_blk, key_blk, preferred_element_type=jnp....]
  transfers between devices with their start and end apart: 5 -> 5, of which waited for: 5 -> 3; matrix products, arithmetic and copies ran while one was open for 4% -> 9% of each run, Pallas kernels for 0% -> 0%
where the time goes in v1:
time: 458 us; the launch traced here: 457 us
  waiting for transfers between devices  236 us (52%)
  blocking collectives  105 us (23%)
  matrix products  58.2 us (13%)
  local copies, waits for them, and re-layouts  22.9 us (5%)
  other arithmetic  21 us (5%)
  between operations  14.1 us (3%)
    all_gather x1, waiting for transfers between devices, local(): full_w = lax.all_gather(local_w, rows_axes, axis=0, tiled=True)  150 us
    all_to_all x1, blocking collectives, local(): hidden_cols = lax.all_to_all(hidden_in, rows_axes, 1, 0, tiled=True)  93.8 us
    all_gather x1, waiting for transfers between devices, local(): d_proj_all = lax.all_gather(d_proj, rows_axes, axis=0, tiled=True)  81.6 us
    unnamed x39, local copies, waits for them, and re-layouts  17.3 us
    dot_general x1, matrix products, local(): lax.dot_general(d_proj, full_w, (((1,), (1,)), ((), ())), preferred_eleme...  16.1 us
  transfers between devices with their start and end apart: 5, of which 3 were waited for; matrix products, arithmetic and copies ran while one was open for 9% of the time, Pallas kernels for 0%

profile of v1, /device:TPU:0, one launch (start us, length us, event | category | flops | bytes accessed | tf_op | source)
XLA Modules:
  0.0 457.1 jit_solution(15336066016034326902)
XLA Ops:
  7.2 0.0 copy-start.2
  7.2 0.0 all-gather.4.cloned.1.call-start
  7.2 2.7 pad_maximum_fusion
  9.9 0.0 all-gather.4.cloned.1.call-update
  9.9 0.0 reduce-scatter.6.cloned.1.call-start
  10.0 0.2 reduce-window.8
  10.2 2.2 copy.97
  12.4 0.1 convert_reduce_fusion
  12.4 0.1 dynamic_slice.3
  12.6 0.3 fusion.7
  12.9 1.5 multiply_cosine_fusion
  14.4 150.0 %all-gather.4.cloned.1.call-done = bf16[4096,1280]{1,0:T(8,128)(2,1)} async-done(((bf16[512,1280]{1,0:T(8,128)(2,1)}), bf16[4096,1280]{1,0:T(8,128)(2,1)}) %all-gather.4.cloned.1.call-update) | async-done | bytes 10485776 | tf_op jit(solution)/shard_map/all_gather | solution.py:189
  164.4 8.3 %convolution_bitcast_fusion.1 = f32[384,1280]{0,1:T(8,128)S(1)} fusion(bf16[4096,1280]{1,0:T(8,128)(2,1)} %all-gather.4.cloned.1.call-done, bf16[384,4096]{1,0:T(8,128)(2,1)S(1)} %copy-done.2), kind=kOutput, calls=%fused_computation.12 | convolution fusion | flops 4026531840 | bytes 15597568 | tf_op jit(solution)/shard_map/dot_general | solution.py:190
  172.7 0.1 slice.61
  172.8 0.7 slice_bitcast_fusion
  173.5 0.1 fusion.40
  173.7 0.5 copy.95
  174.1 1.6 copy.94
  175.8 1.4 fusion.26
  177.2 5.3 %all-gather = bf16[768,1,128]{0,2,1:T(8,128)(2,1)S(1)} all-gather(bf16[384,1,128]{0,2,1:T(8,128)(2,1)S(1)} %pad_maximum_fusion.6), channel_id=2, replica_groups=mesh['dp'=4,'ctx'=2,'head'=4] {'ctx'}, dimensions={0}, use_global_device_ids=true | all-gather | bytes 294912 | tf_op jit(solution)/shard_map/all_gather | solution.py:199
  182.5 2.0 subtract_convert_fusion.1
  184.5 2.1 fusion.5
  186.6 0.0 copy-start.10
  186.7 2.2 select_reduce_fusion
  188.9 5.5 %all_gather.13 = bf16[768,128]{0,1:T(8,128)(2,1)S(1)} all-gather(bf16[384,128]{0,1:T(8,128)(2,1)S(1)} %slice.85), channel_id=1, replica_groups=mesh['dp'=4,'ctx'=2,'head'=4] {'ctx'}, dimensions={0}, use_global_device_ids=true | all-gather | bytes 294912 | tf_op jit(solution)/shard_map/all_gather | solution.py:200
  194.4 3.0 convolution_bitcast_fusion.3
  197.4 7.8 %bitcast_convert_fusion = (f32[8,384,128]{1,2,0:T(8,128)}, bf16[128,8,384]{2,0,1:T(8,128)(2,1)}) fusion(f32[768,384,8]{1,0,2:T(8,128)} %copy-done, f32[8,384]{1,0:T(8,128)S(1)} %log_add_fusion, pred[384,768]{0,1:T(8,128)(4,1)S(1)} %fusion.7, bf16[768,128]{0,1:T(8,128)(2,1)S(1)} %all_gather.13), kind=kOutput, calls=%fused_computation.30 | convolution fusion | flops 616562688 | bytes 12300288 | tf_op jit(solution)/shard_map/hrk,kd->rhd/dot_general | solution.py:86
  205.2 0.0 reduce-scatter.6.cloned.1.call-update
  205.2 0.0 reduce-scatter.4.cloned.1.call-start
  205.2 2.0 copy.86
  207.2 2.3 multiply_reduce_fusion
  209.5 1.0 copy.87
  210.5 7.6 %fusion.1 = bf16[8,384,768]{1,2,0:T(8,128)(2,1)S(1)} fusion(f32[768,384,8]{1,0,2:T(8,128)} %copy-done, f32[8,384]{1,0:T(8,128)S(1)} %copy.87, f32[8,384]{1,0:T(8,128)S(1)} %log_add_fusion, pred[384,768]{0,1:T(8,128)(4,1)S(1)} %fusion.7, bf16[768,128]{0,1:T(8,128)(2,1)} %copy-done.11, bf16[384,1024]{1,0:T(8,128)(2,1)} %param.11), kind=kOutput, calls=%fused_computation.2 | convolution fusion | flops 622854144 | bytes 15458304 | tf_op jit(solution)/shard_map/rhd,kd->hrk/dot_general | solution.py:90
  218.2 2.2 copy-done.1
  220.4 2.5 convolution_bitcast_fusion.4
  222.9 0.0 reduce-scatter.4.cloned.1.call-update
  222.9 0.0 copy-start.6
  222.9 0.3 reduce-scatter.8.cloned.1.call-start
  223.2 4.3 convolution_bitcast_fusion.2
  227.5 0.6 add_convert_fusion
  228.1 0.4 pad_maximum_fusion.3
  228.6 0.4 copy.68
  229.0 0.0 copy-start.5
  229.0 0.0 reduce-scatter.6.cloned.1.call-done
  229.0 1.2 convert_element_type.52
  230.2 0.1 copy.71
  230.3 4.2 reduce-scatter.4.cloned.1.call-done
  234.5 1.4 fusion.30
  235.9 16.1 %fusion.36 = f32[384,4096]{1,0:T(8,128)} fusion(bf16[4096,1280]{1,0:T(8,128)(2,1)} %all-gather.4.cloned.1.call-done, bf16[384,128]{0,1:T(8,128)(2,1)S(1)} %copy.71, bf16[384,128]{0,1:T(8,128)(2,1)S(1)} %maximum_bitcast_fusion, bf16[384,1024]{0,1:T(8,128)(2,1)S(1)} %bitcast.101), kind=kOutput, calls=%fused_computation.70 | convolution fusion | flops 4029480960 | bytes 17760256 | tf_op jit(solution)/shard_map/dot_general | solution.py:222
  252.0 0.0 reduce-scatter.8.cloned.1.call-update
  252.0 0.0 all-gather.6.cloned.1.call-start
  252.1 2.3 pad_maximum_fusion.1
  254.4 0.0 all-gather.6.cloned.1.call-update
  254.4 2.8 copy.72
  257.3 93.8 %all_to_all.19 = bf16[384,8,512]{0,2,1:T(8,128)(2,1)S(1)} all-to-all(bf16[384,8,512]{0,2,1:T(8,128)(2,1)} %bitcast.97), channel_id=1, replica_groups=mesh['dp'=4,'ctx'=2,'head'=4] {'dp','ctx'}, dimensions={1} | all-to-all | bytes 6291456 | tf_op jit(solution)/shard_map/all_to_all | solution.py:187
  351.0 2.9 copy.73
  354.0 2.4 copy.74
  356.4 2.4 convert_element_type.53
  358.8 81.6 %all-gather.6.cloned.1.call-done = bf16[3072,1280]{0,1:T(8,128)(2,1)} async-done(((bf16[384,1280]{0,1:T(8,128)(2,1)}), bf16[3072,1280]{0,1:T(8,128)(2,1)}) %all-gather.6.cloned.1.call-update) | async-done | bytes 7864336 | tf_op jit(solution)/shard_map/all_gather | solution.py:228
  440.4 6.5 %convolution_bitcast_fusion = f32[512,1280]{0,1:T(8,128)S(1)} fusion(bf16[3072,1280]{0,1:T(8,128)(2,1)} %all-gather.6.cloned.1.call-done, bf16[3072,512]{1,0:T(8,128)(2,1)S(1)} %bitcast.99), kind=kOutput, calls=%fused_computation.11 | convolution fusion | flops 4026531840 | bytes 13631488 | tf_op jit(solution)/shard_map/dot_general | solution.py:229
  446.9 0.2 slice.68
  447.1 1.8 copy.75
  448.9 0.8 copy.76
  449.8 0.8 copy.77
  (34 shorter events, 0.2 us)
Async XLA Ops:
  7.2 2.8 copy-start.14
  7.2 157.2 %copy-start.2 = (bf16[384,4096]{1,0:T(8,128)(2,1)S(1)}, bf16[384,4096]{1,0:T(8,128)(2,1)}, u32[]{:S(2)}) copy-start(bf16[384,4096]{1,0:T(8,128)(2,1)} %param.6) | copy-start | bytes 9437188
  7.2 157.2 %all-gather.4.cloned.1.call-start = ((), (), s32[]{:S(2)}) async-start(), calls=%async_computation.4 | async-start | bytes 11796480 | tf_op jit(solution)/shard_map/all_gather | solution.py:189
  9.9 219.1 %reduce-scatter.6.cloned.1.call-start = ((), (), s32[]{:S(2)}) async-start(), calls=%async_computation.6 | async-start | bytes 589824 | tf_op jit(solution)/shard_map/reduce_scatter | solution.py:214
  12.5 163.2 %copy-start.12 = (f32[64]{0:T(128)}, f32[64]{0:T(128)S(1)}, u32[]{:S(2)}) copy-start(f32[64]{0:T(128)S(1)} %multiply_power_fusion) | copy-start | bytes 772
  182.5 4.2 copy-start.8
  186.6 7.8 %copy-start = (f32[768,384,8]{1,0,2:T(8,128)}, f32[768,384,8]{1,0,2:T(8,128)S(1)}, u32[]{:S(2)}) copy-start(f32[768,384,8]{1,0,2:T(8,128)S(1)} %get-tuple-element.40) | copy-start | bytes 28311556
  186.6 7.8 %copy-start.10 = (bf16[384,1024]{1,0:T(8,128)(2,1)S(1)}, bf16[384,1024]{1,0:T(8,128)(2,1)}, u32[]{:S(2)}) copy-start(bf16[384,1024]{1,0:T(8,128)(2,1)} %param.11) | copy-start | bytes 2359300
  194.4 3.0 copy-start.11
  205.2 29.3 %reduce-scatter.4.cloned.1.call-start = ((), (), s32[]{:S(2)}) async-start(), calls=%async_computation.5 | async-start | bytes 589824 | tf_op jit(solution)/shard_map/reduce_scatter | solution.py:213
  218.2 2.2 copy-start.1
  220.4 2.8 copy-start.9
  222.9 4.6 %copy-start.6 = (f32[384,64]{1,0:T(8,128)S(1)}, f32[384,64]{1,0:T(8,128)}, u32[]{:S(2)}) copy-start(f32[384,64]{1,0:T(8,128)} %get-tuple-element.37) | copy-start | bytes 294916
  222.9 4.6 %copy-start.7 = (f32[384,64]{1,0:T(8,128)S(1)}, f32[384,64]{1,0:T(8,128)}, u32[]{:S(2)}) copy-start(f32[384,64]{1,0:T(8,128)} %get-tuple-element.38) | copy-start | bytes 294916
  222.9 133.5 %reduce-scatter.8.cloned.1.call-start = ((), (), s32[]{:S(2)}) async-start(), calls=%async_computation.7 | async-start | bytes 7864320 | tf_op jit(solution)/shard_map/reduce_scatter | solution.py:225
  228.1 6.4 %copy-start.13 = (f32[64]{0:T(128)S(1)}, f32[64]{0:T(128)}, u32[]{:S(2)}) copy-start(f32[64]{0:T(128)} %copy-done.12) | copy-start | bytes 772
  229.0 23.0 %copy-start.5 = (bf16[384,8,128]{0,2,1:T(8,128)(2,1)}, bf16[384,8,128]{0,2,1:T(8,128)(2,1)S(1)}, u32[]{:S(2)}) copy-start(bf16[384,8,128]{0,2,1:T(8,128)(2,1)S(1)} %copy.68) | copy-start | bytes 2359300
  252.0 2.4 copy-start.3
  252.0 188.4 %all-gather.6.cloned.1.call-start = ((), (), s32[]{:S(2)}) async-start(), calls=%async_computation.8 | async-start | bytes 8847360 | tf_op jit(solution)/shard_map/all_gather | solution.py:228
  354.0 86.4 %copy-start.4 = (bf16[8,384,512]{2,1,0:T(8,128)(2,1)S(1)}, bf16[8,384,512]{2,1,0:T(8,128)(2,1)}, u32[]{:S(2)}) copy-start(bf16[8,384,512]{2,1,0:T(8,128)(2,1)} %copy.73) | copy-start | bytes 9437188
Sparse Core Ops, SparseCore 0:
  10.8 153.5 all-gather.3
  205.3 11.3 reduce-scatter.5
  223.0 11.4 reduce-scatter.3
  252.1 58.3 reduce-scatter.7
  313.2 127.1 all-gather.5

commit v2 on v1

--- a/solution.py
+++ b/solution.py
@@ -184,9 +184,26 @@
     seg_own = lax.dynamic_slice_in_dim(seg_all, start_row, num_rows)
     cosine, sine_table = rope_tables(positions)
     rows_axes = ("dp", "ctx")
-    hidden_cols = lax.all_to_all(hidden_in, rows_axes, 1, 0, tiled=True)
+    group_count = lax.axis_size(rows_axes)
+    head_groups = lax.axis_size("head")
+    if num_rows % head_groups == 0:
+        quarter = num_rows // head_groups
+        own_rows = lax.dynamic_slice_in_dim(hidden_in, lax.axis_index("head") * quarter, quarter, 0)
+        cols_part = lax.all_to_all(own_rows, rows_axes, 1, 0, tiled=True)
+    else:
+        cols_part = lax.all_to_all(hidden_in, rows_axes, 1, 0, tiled=True)
     local_w = jnp.concatenate([w_query, w_key, w_value], 1)
     full_w = lax.all_gather(local_w, rows_axes, axis=0, tiled=True)
+    cols_part, full_w = lax.optimization_barrier((cols_part, full_w))
+    if num_rows % head_groups == 0:
+        cols_all = lax.all_gather(cols_part, "head", axis=0, tiled=False)
+        hidden_cols = (
+            cols_all.reshape(head_groups, group_count, quarter, -1)
+            .transpose(1, 0, 2, 3)
+            .reshape(group_count * num_rows, -1)
+        )
+    else:
+        hidden_cols = cols_part
     projected = jnp.dot(hidden_in, full_w, preferred_element_type=jnp.float32)
     query_rows = rotate(
         projected[:, :query_cols].reshape(num_rows, head_count, 128), cosine, sine_table
@@ -199,6 +216,7 @@
         lax.all_gather(key_rows, "ctx", axis=0, tiled=True),
         lax.all_gather(value_rows, "ctx", axis=0, tiled=True),
     )
+    hidden_cols, attn_grad = lax.optimization_barrier((hidden_cols, attn_grad))
     dout_rows = attn_grad.reshape(num_rows, head_count, 128)
     operands = (query_rows, key_all, value_all, dout_rows, positions, all_pos, seg_own, seg_all)
     if head_count * num_rows * seq_len <= (1 << 22):

time: 458 us -> 472 us (1.031)
  waiting for transfers between devices: 236 us -> 337 us
  blocking collectives: 105 us -> 10.9 us
  starting transfers between devices: 0.43 us -> 8 us
    all_to_all x1 -> x0, blocking collectives: 93.8 us -> none  [local(): hidden_cols = lax.all_to_all(hidden_in, rows_axes, 1, 0, tiled=True)]
    reduce_scatter x1, waiting for transfers between devices: 0.01 us -> 56 us  [local(): lax.psum_scatter(input_part, 'head', scatter_dimension=1, tiled=True)]
    all_gather x1, waiting for transfers between devices: 81.6 us -> 119 us  [local(): d_proj_all = lax.all_gather(d_proj, rows_axes, axis=0, tiled=True)]
    all_to_all x0 -> x1, waiting for transfers between devices: none -> 36.5 us  [local(): cols_part = lax.all_to_all(own_rows, rows_axes, 1, 0, tiled=True)]
    all_gather x1, waiting for transfers between devices: 150 us -> 121 us  [local(): full_w = lax.all_gather(local_w, rows_axes, axis=0, tiled=True)]
    all_to_all x0 -> x1, starting transfers between devices: none -> 7.28 us  [local(): cols_part = lax.all_to_all(own_rows, rows_axes, 1, 0, tiled=True)]
    unnamed x39 -> x35, local copies, waits for them, and re-layouts: 17.3 us -> 11.2 us
  transfers between devices with their start and end apart: 5 -> 7, of which waited for: 3 -> 5; matrix products, arithmetic and copies ran while one was open for 9% -> 11% of each run, Pallas kernels for 0% -> 0%
where the time goes in v2:
time: 472 us; the launch traced here: 471 us
  waiting for transfers between devices  337 us (71%)
  matrix products  62.6 us (13%)
  local copies, waits for them, and re-layouts  21.7 us (5%)
  other arithmetic  16.4 us (3%)
  between operations  14.5 us (3%)
  blocking collectives  10.9 us (2%)
  starting transfers between devices  8 us (2%)
    all_gather x1, waiting for transfers between devices, local(): full_w = lax.all_gather(local_w, rows_axes, axis=0, tiled=True)  121 us
    all_gather x1, waiting for transfers between devices, local(): d_proj_all = lax.all_gather(d_proj, rows_axes, axis=0, tiled=True)  119 us
    reduce_scatter x1, waiting for transfers between devices, local(): lax.psum_scatter(input_part, 'head', scatter_dimension=1, tiled=True)  56 us
    all_to_all x1, waiting for transfers between devices, local(): cols_part = lax.all_to_all(own_rows, rows_axes, 1, 0, tiled=True)  36.5 us
    dot_general x1, matrix products, local(): lax.dot_general(d_proj, full_w, (((1,), (1,)), ((), ())), preferred_eleme...  16.1 us
    unnamed x35, local copies, waits for them, and re-layouts  11.2 us
  transfers between devices with their start and end apart: 7, of which 5 were waited for; matrix products, arithmetic and copies ran while one was open for 11% of the time, Pallas kernels for 0%

profile of v2, /device:TPU:0, one launch (start us, length us, event | category | flops | bytes accessed | tf_op | source)
XLA Modules:
  0.0 471.3 jit_solution(4731177936313566955)
XLA Ops:
  7.2 0.0 all-gather.6.cloned.1.call-start
  7.2 2.7 pad_maximum_fusion
  9.9 0.0 all-gather.6.cloned.1.call-update
  9.9 0.1 constant_dynamic-slice_fusion
  10.0 1.0 copy.111
  10.9 7.3 %all-to-all-start = ((bf16[96,8,512]{2,0,1:T(8,128)(2,1)}), bf16[96,8,512]{2,0,1:T(8,128)(2,1)}, u32[]{:S(2)}, u32[]{:S(2)}) async-start(bf16[96,8,512]{2,0,1:T(8,128)(2,1)} %bitcast.106), calls=%async_computation | async-start | bytes 1572864 | tf_op jit(solution)/shard_map/all_to_all | solution.py:192
  18.2 0.0 all-gather.10.cloned.1.call-start
  18.3 0.2 reduce-window.8
  18.5 0.1 convert_reduce_fusion
  18.6 0.1 dynamic_slice.7
  18.6 36.5 %all-to-all-done = bf16[96,8,512]{2,0,1:T(8,128)(2,1)} async-done(((bf16[96,8,512]{2,0,1:T(8,128)(2,1)}), bf16[96,8,512]{2,0,1:T(8,128)(2,1)}, u32[]{:S(2)}, u32[]{:S(2)}) %all-to-all-start) | async-done | bytes 786464 | tf_op jit(solution)/shard_map/all_to_all | solution.py:192
  55.1 120.8 %all-gather.6.cloned.1.call-done = bf16[4096,1280]{1,0:T(8,128)(2,1)} async-done(((bf16[512,1280]{1,0:T(8,128)(2,1)}), bf16[4096,1280]{1,0:T(8,128)(2,1)}) %all-gather.6.cloned.1.call-update) | async-done | bytes 10485776 | tf_op jit(solution)/shard_map/all_gather | solution.py:196
  176.0 0.0 all-gather.10.cloned.1.call-update
  176.0 0.0 reduce-scatter.6.cloned.1.call-start
  176.1 0.3 fusion.7
  176.4 1.5 multiply_cosine_fusion
  177.9 8.3 %convolution_bitcast_fusion = f32[384,1280]{0,1:T(8,128)S(1)} fusion(bf16[4096,1280]{1,0:T(8,128)(2,1)} %all-gather.6.cloned.1.call-done, bf16[384,4096]{1,0:T(8,128)(2,1)S(1)} %copy-done), kind=kOutput, calls=%fused_computation.11 | convolution fusion | flops 4026531840 | bytes 15597568 | tf_op jit(solution)/shard_map/dot_general | solution.py:207
  186.2 0.1 slice.61
  186.4 1.5 fusion.40
  187.8 0.2 copy-done.4
  188.0 1.6 copy.98
  189.6 2.7 copy.97
  192.4 0.9 slice_bitcast_fusion
  193.3 0.4 fusion.26
  193.8 5.3 %all-gather = bf16[768,1,128]{0,2,1:T(8,128)(2,1)S(1)} all-gather(bf16[384,1,128]{0,2,1:T(8,128)(2,1)S(1)} %pad_maximum_fusion.6), channel_id=2, replica_groups=mesh['dp'=4,'ctx'=2,'head'=4] {'ctx'}, dimensions={0}, use_global_device_ids=true | all-gather | bytes 294912 | tf_op jit(solution)/shard_map/all_gather | solution.py:216
  199.1 5.6 %all_gather.19 = bf16[768,128]{0,1:T(8,128)(2,1)} all-gather(bf16[384,128]{0,1:T(8,128)(2,1)S(1)} %slice.85), channel_id=1, replica_groups=mesh['dp'=4,'ctx'=2,'head'=4] {'ctx'}, dimensions={0}, use_global_device_ids=true | all-gather | bytes 294912 | tf_op jit(solution)/shard_map/all_gather | solution.py:217
  204.6 2.0 subtract_convert_fusion.1
  206.6 2.2 fusion.5
  208.8 2.2 select_reduce_fusion
  211.0 1.3 copy-done.2
  212.4 4.0 copy.72
  216.4 0.2 copy.101
  216.6 0.2 bitcast_convert_fusion
  216.8 1.7 copy.90
  218.5 6.9 %convolution_bitcast_fusion.2 = f32[768,128]{1,0:T(8,128)} fusion(f32[768,384,8]{1,0,2:T(8,128)} %copy-done.2, f32[8,384]{1,0:T(8,128)S(1)} %log_add_fusion, pred[384,768]{0,1:T(8,128)(4,1)S(1)} %fusion.7, bf16[384,1024]{1,0:T(8,128)(2,1)} %param.11), kind=kOutput, calls=%fused_computation.20 | convolution fusion | flops 615776256 | bytes 10924032 | tf_op jit(solution)/shard_map/hrk,rhd->kd/dot_general | solution.py:94
  225.4 0.0 reduce-scatter.6.cloned.1.call-update
  225.4 0.3 reduce-scatter.4.cloned.1.call-start
  225.7 7.5 %multiply_reduce_fusion = (f32[8,384]{1,0:T(8,128)S(1)}, bf16[128,8,384]{2,0,1:T(8,128)(2,1)}) fusion(f32[8,384,128]{1,2,0:T(8,128)S(1)} %copy-done.9, f32[768,384,8]{1,0,2:T(8,128)} %copy-done.2, f32[8,384]{1,0:T(8,128)S(1)} %log_add_fusion, pred[384,768]{0,1:T(8,128)(4,1)S(1)} %fusion.7, bf16[768,128]{0,1:T(8,128)(2,1)} %all_gather.19), kind=kOutput, calls=%fused_computation.12 | convolution fusion | flops 617346048 | bytes 12312576 | tf_op jit(solution)/shard_map/hrk,kd->rhd/dot_general | solution.py:86
  233.2 6.2 %fusion.1 = bf16[8,384,768]{1,2,0:T(8,128)(2,1)S(1)} fusion(f32[768,384,8]{1,0,2:T(8,128)} %copy-done.2, f32[8,384]{1,0:T(8,128)S(1)} %get-tuple-element.54, f32[8,384]{1,0:T(8,128)S(1)} %log_add_fusion, pred[384,768]{0,1:T(8,128)(4,1)S(1)} %fusion.7, bf16[768,128]{0,1:T(8,128)(2,1)S(1)} %copy-done.13, bf16[384,1024]{1,0:T(8,128)(2,1)S(1)} %copy-done.11), kind=kOutput, calls=%fused_computation.2 | convolution fusion | flops 622854144 | bytes 15458304 | tf_op jit(solution)/shard_map/rhd,kd->hrk/dot_general | solution.py:90
  239.4 2.2 copy-done.3
  241.6 2.5 convolution_bitcast_fusion.3
  244.1 0.0 reduce-scatter.4.cloned.1.call-update
  244.2 0.0 reduce-scatter.8.cloned.1.call-start
  244.2 4.4 convolution_bitcast_fusion.1
  248.6 0.6 add_convert_fusion
  249.3 0.4 pad_maximum_fusion.3
  249.7 0.4 copy.77
  250.1 0.0 reduce-scatter.6.cloned.1.call-done
  250.1 0.9 convert_element_type.52
  251.0 0.1 copy.80
  251.2 4.5 reduce-scatter.4.cloned.1.call-done
  255.6 1.4 fusion.30
  257.0 16.1 %fusion.36 = f32[384,4096]{1,0:T(8,128)} fusion(bf16[4096,1280]{1,0:T(8,128)(2,1)} %all-gather.6.cloned.1.call-done, bf16[384,128]{0,1:T(8,128)(2,1)S(1)} %copy.80, bf16[384,128]{0,1:T(8,128)(2,1)S(1)} %maximum_bitcast_fusion, bf16[384,1024]{0,1:T(8,128)(2,1)S(1)} %bitcast.108), kind=kOutput, calls=%fused_computation.71 | convolution fusion | flops 4029480960 | bytes 17760256 | tf_op jit(solution)/shard_map/dot_general | solution.py:240
  273.1 0.0 reduce-scatter.8.cloned.1.call-update
  273.1 0.3 all-gather.8.cloned.1.call-start
  273.4 1.0 pad_maximum_fusion.1
  274.5 0.0 all-gather.8.cloned.1.call-update
  274.5 1.2 copy.81
  275.7 56.0 %reduce-scatter.8.cloned.1.call-done = f32[384,1024]{1,0:T(8,128)} async-done(((f32[384,4096]{1,0:T(8,128)}), f32[384,1024]{1,0:T(8,128)}) %reduce-scatter.8.cloned.1.call-update) | async-done | bytes 1572880 | tf_op jit(solution)/shard_map/reduce_scatter | solution.py:243
  331.6 2.4 convert_element_type.53
  334.0 119.3 %all-gather.8.cloned.1.call-done = bf16[3072,1280]{0,1:T(8,128)(2,1)} async-done(((bf16[384,1280]{0,1:T(8,128)(2,1)}), bf16[3072,1280]{0,1:T(8,128)(2,1)}) %all-gather.8.cloned.1.call-update) | async-done | bytes 7864336 | tf_op jit(solution)/shard_map/all_gather | solution.py:246
  453.4 8.6 %fusion.41 = f32[512,1280]{1,0:T(8,128)S(1)} fusion(bf16[3072,512]{1,0:T(8,128)(2,1)} %bitcast.104, bf16[3072,1280]{0,1:T(8,128)(2,1)} %all-gather.8.cloned.1.call-done), kind=kOutput, calls=%fused_computation.74 | convolution fusion | flops 4026531840 | bytes 13631488 | tf_op jit(solution)/shard_map/dot_general | solution.py:247
  462.0 1.6 slice.68
  463.6 0.8 fusion.39
  (35 shorter events, 0.1 us)
Async XLA Ops:
  7.2 2.8 copy-start
  7.2 168.8 %all-gather.6.cloned.1.call-start = ((), (), s32[]{:S(2)}) async-start(), calls=%async_computation.4 | async-start | bytes 11796480 | tf_op jit(solution)/shard_map/all_gather | solution.py:196
  9.9 8.4 %copy-start.14 = (s32[1,8]{1,0:T(1,128)S(1)}, s32[1,8]{1,0:T(1,128)}, u32[]{:S(2)}) copy-start(s32[1,8]{1,0:T(1,128)} %param.10) | copy-start | bytes 100
  10.9 44.2 %all-to-all-start = ((bf16[96,8,512]{2,0,1:T(8,128)(2,1)}), bf16[96,8,512]{2,0,1:T(8,128)(2,1)}, u32[]{:S(2)}, u32[]{:S(2)}) async-start(bf16[96,8,512]{2,0,1:T(8,128)(2,1)} %bitcast.106), calls=%async_computation | async-start | bytes 1572864 | tf_op jit(solution)/shard_map/all_to_all | solution.py:192
  18.2 194.2 %all-gather.10.cloned.1.call-start = ((), (), s32[]{:S(2)}) async-start(), calls=%async_computation.9 | async-start | bytes 3932160 | tf_op jit(solution)/shard_map/all_gather | solution.py:199
  176.0 74.1 %reduce-scatter.6.cloned.1.call-start = ((), (), s32[]{:S(2)}) async-start(), calls=%async_computation.6 | async-start | bytes 589824 | tf_op jit(solution)/shard_map/reduce_scatter | solution.py:232
  186.2 1.8 copy-start.4
  199.1 9.7 %copy-start.7 = (bf16[768,1,128]{0,2,1:T(8,128)(2,1)}, bf16[768,1,128]{0,2,1:T(8,128)(2,1)S(1)}, u32[]{:S(2)}) copy-start(bf16[768,1,128]{0,2,1:T(8,128)(2,1)S(1)} %all-gather) | copy-start | bytes 589828
  208.8 3.6 copy-start.2
  212.4 4.0 copy-start.10
  218.5 7.2 %copy-start.9 = (f32[8,384,128]{1,2,0:T(8,128)S(1)}, f32[8,384,128]{1,2,0:T(8,128)}, u32[]{:S(2)}) copy-start(f32[8,384,128]{1,2,0:T(8,128)} %copy.90) | copy-start | bytes 4718596
  225.4 30.2 %reduce-scatter.4.cloned.1.call-start = ((), (), s32[]{:S(2)}) async-start(), calls=%async_computation.5 | async-start | bytes 589824 | tf_op jit(solution)/shard_map/reduce_scatter | solution.py:231
  225.7 7.5 %copy-start.11 = (bf16[384,1024]{1,0:T(8,128)(2,1)S(1)}, bf16[384,1024]{1,0:T(8,128)(2,1)}, u32[]{:S(2)}) copy-start(bf16[384,1024]{1,0:T(8,128)(2,1)} %param.11) | copy-start | bytes 2359300
  225.7 7.5 %copy-start.13 = (bf16[768,128]{0,1:T(8,128)(2,1)S(1)}, bf16[768,128]{0,1:T(8,128)(2,1)}, u32[]{:S(2)}) copy-start(bf16[768,128]{0,1:T(8,128)(2,1)} %all_gather.19) | copy-start | bytes 589828
  239.4 2.2 copy-start.3
  241.6 2.6 copy-start.8
  244.1 4.5 copy-start.5
  244.2 4.5 copy-start.6
  244.2 87.5 %reduce-scatter.8.cloned.1.call-start = ((), (), s32[]{:S(2)}) async-start(), calls=%async_computation.7 | async-start | bytes 7864320 | tf_op jit(solution)/shard_map/reduce_scatter | solution.py:243
  273.1 1.4 copy-start.12
  273.1 180.2 %all-gather.8.cloned.1.call-start = ((), (), s32[]{:S(2)}) async-start(), calls=%async_computation.8 | async-start | bytes 8847360 | tf_op jit(solution)/shard_map/all_gather | solution.py:246
  453.4 11.1 %copy-start.1 = (bf16[384,4096]{1,0:T(8,128)(2,1)S(1)}, bf16[384,4096]{1,0:T(8,128)(2,1)}, u32[]{:S(2)}) copy-start(bf16[384,4096]{1,0:T(8,128)(2,1)} %param.6) | copy-start | bytes 9437188
Sparse Core Ops, SparseCore 0:
  10.8 165.1 all-gather.5
  177.5 26.7 all-gather.9
  225.5 11.3 reduce-scatter.5
  244.3 11.3 reduce-scatter.3
  273.2 58.3 reduce-scatter.7
  334.3 118.9 all-gather.7

commit v3 on v2

--- a/solution.py
+++ b/solution.py
@@ -240,9 +240,11 @@
     input_part = lax.dot_general(
         d_proj, full_w, (((1,), (1,)), ((), ())), preferred_element_type=jnp.float32
     )
-    grad_input = lax.psum_scatter(input_part, "head", scatter_dimension=1, tiled=True).astype(
-        jnp.bfloat16
-    )
+    input_cols = input_part.shape[1] // head_groups
+    input_split = lax.all_to_all(
+        input_part.reshape(num_rows, head_groups, input_cols), "head", 1, 1, tiled=False
+    )
+    grad_input = jnp.sum(input_split, axis=1).astype(jnp.bfloat16)
     d_proj_all = lax.all_gather(d_proj, rows_axes, axis=0, tiled=True)
     weight_sum = lax.dot_general(
         hidden_cols, d_proj_all, (((0,), (0,)), ((), ())), preferred_element_type=jnp.float32

time: 472 us -> 395 us (0.84)
  waiting for transfers between devices: 337 us -> 259 us
  matrix products: 62.6 us -> 53.5 us
  starting transfers between devices: 8 us -> 13.7 us
    all_gather x1, waiting for transfers between devices: 119 us -> 28.3 us  [local(): d_proj_all = lax.all_gather(d_proj, rows_axes, axis=0, tiled=True)]
    all_to_all x0 -> x1, waiting for transfers between devices: none -> 69.2 us  [local(): lax.all_to_all(input_part.reshape(num_rows, head_groups, input_cols), 'he...]
    reduce_scatter x1 -> x0, waiting for transfers between devices: 56 us -> none  [local(): lax.psum_scatter(input_part, 'head', scatter_dimension=1, tiled=True)]
    dot_general x1, matrix products: 16.1 us -> 7.02 us  [local(): lax.dot_general(d_proj, full_w, (((1,), (1,)), ((), ())), preferred_eleme...]
    all_to_all x0 -> x1, starting transfers between devices: none -> 5.7 us  [local(): lax.all_to_all(input_part.reshape(num_rows, head_groups, input_cols), 'he...]
  transfers between devices with their start and end apart: 7 -> 7, of which waited for: 5 -> 5; matrix products, arithmetic and copies ran while one was open for 11% -> 16% of each run, Pallas kernels for 0% -> 0%
where the time goes in v3:
time: 395 us
  waiting for transfers between devices  259 us (66%)
  matrix products  53.5 us (14%)
  local copies, waits for them, and re-layouts  24.9 us (6%)
  other arithmetic  18.6 us (5%)
  between operations  14.1 us (4%)
  starting transfers between devices  13.7 us (3%)
  blocking collectives  10.9 us (3%)
    all_gather x1, waiting for transfers between devices, local(): full_w = lax.all_gather(local_w, rows_axes, axis=0, tiled=True)  121 us
    all_to_all x1, waiting for transfers between devices, local(): lax.all_to_all(input_part.reshape(num_rows, head_groups, input_cols), 'he...  69.2 us
    all_to_all x1, waiting for transfers between devices, local(): cols_part = lax.all_to_all(own_rows, rows_axes, 1, 0, tiled=True)  36.5 us
    all_gather x1, waiting for transfers between devices, local(): d_proj_all = lax.all_gather(d_proj, rows_axes, axis=0, tiled=True)  28.3 us
    unnamed x35, local copies, waits for them, and re-layouts  11.1 us
    dot_general x1, matrix products, local(): lax.dot_general(hidden_cols, d_proj_all, (((0,), (0,)), ((), ())), prefer...  8.61 us
    dot_general x1, matrix products, local(): projected = jnp.dot(hidden_in, full_w, preferred_element_type=jnp.float32)  8.32 us
  transfers between devices with their start and end apart: 7, of which 5 were waited for; matrix products, arithmetic and copies ran while one was open for 16% of the time, Pallas kernels for 0%

profile of v3, /device:TPU:0, one launch (start us, length us, event | category | flops | bytes accessed | tf_op | source)
XLA Modules:
  0.0 394.9 jit_solution(10567672449674154778)
XLA Ops:
  7.2 0.0 all-gather.6.cloned.1.call-start
  7.2 2.7 pad_maximum_fusion
  9.9 0.0 all-gather.6.cloned.1.call-update
  9.9 0.1 constant_dynamic-slice_fusion
  10.0 1.0 copy.116
  10.9 7.3 %all-to-all-start = ((bf16[96,8,512]{2,0,1:T(8,128)(2,1)}), bf16[96,8,512]{2,0,1:T(8,128)(2,1)}, u32[]{:S(2)}, u32[]{:S(2)}) async-start(bf16[96,8,512]{2,0,1:T(8,128)(2,1)} %bitcast.112), calls=%async_computation | async-start | bytes 1572864 | tf_op jit(solution)/shard_map/all_to_all | solution.py:192
  18.2 0.0 all-gather.10.cloned.1.call-start
  18.3 0.2 reduce-window.8
  18.5 0.1 convert_reduce_fusion
  18.6 0.1 dynamic_slice.7
  18.6 36.5 %all-to-all-done = bf16[96,8,512]{2,0,1:T(8,128)(2,1)} async-done(((bf16[96,8,512]{2,0,1:T(8,128)(2,1)}), bf16[96,8,512]{2,0,1:T(8,128)(2,1)}, u32[]{:S(2)}, u32[]{:S(2)}) %all-to-all-start) | async-done | bytes 786464 | tf_op jit(solution)/shard_map/all_to_all | solution.py:192
  55.1 120.8 %all-gather.6.cloned.1.call-done = bf16[4096,1280]{1,0:T(8,128)(2,1)} async-done(((bf16[512,1280]{1,0:T(8,128)(2,1)}), bf16[4096,1280]{1,0:T(8,128)(2,1)}) %all-gather.6.cloned.1.call-update) | async-done | bytes 10485776 | tf_op jit(solution)/shard_map/all_gather | solution.py:196
  176.0 0.0 all-gather.10.cloned.1.call-update
  176.0 0.0 reduce-scatter.5.cloned.1.call-start
  176.1 0.3 fusion.7
  176.4 1.5 multiply_cosine_fusion
  177.9 8.3 %convolution_bitcast_fusion = f32[384,1280]{0,1:T(8,128)S(1)} fusion(bf16[4096,1280]{1,0:T(8,128)(2,1)} %all-gather.6.cloned.1.call-done, bf16[384,4096]{1,0:T(8,128)(2,1)S(1)} %copy-done), kind=kOutput, calls=%fused_computation.12 | convolution fusion | flops 4026531840 | bytes 15597568 | tf_op jit(solution)/shard_map/dot_general | solution.py:207
  186.2 0.1 slice.61
  186.4 1.5 fusion.40
  187.9 0.2 copy-done.4
  188.0 1.6 copy.100
  189.6 2.7 copy.99
  192.4 0.9 slice_bitcast_fusion
  193.3 0.4 fusion.26
  193.8 5.3 %all-gather = bf16[768,1,128]{0,2,1:T(8,128)(2,1)S(1)} all-gather(bf16[384,1,128]{0,2,1:T(8,128)(2,1)S(1)} %pad_maximum_fusion.6), channel_id=2, replica_groups=mesh['dp'=4,'ctx'=2,'head'=4] {'ctx'}, dimensions={0}, use_global_device_ids=true | all-gather | bytes 294912 | tf_op jit(solution)/shard_map/all_gather | solution.py:216
  199.1 5.6 %all_gather.19 = bf16[768,128]{0,1:T(8,128)(2,1)} all-gather(bf16[384,128]{0,1:T(8,128)(2,1)S(1)} %slice.85), channel_id=1, replica_groups=mesh['dp'=4,'ctx'=2,'head'=4] {'ctx'}, dimensions={0}, use_global_device_ids=true | all-gather | bytes 294912 | tf_op jit(solution)/shard_map/all_gather | solution.py:217
  204.6 2.0 subtract_convert_fusion.1
  206.6 2.2 fusion.5
  208.8 2.2 select_reduce_fusion
  211.0 1.3 copy-done.2
  212.4 4.0 %copy.73 = bf16[4,8,96,512]{3,2,0,1:T(8,128)(2,1)} copy(bf16[4,8,96,512]{3,2,1,0:T(8,128)(2,1)} %bitcast.111) | data formatting | bytes 6291456 | tf_op jit(solution)/shard_map/reshape | solution.py:201
  216.5 0.2 copy.104
  216.6 0.2 bitcast_convert_fusion
  216.8 1.7 copy.92
  218.5 6.9 %convolution_bitcast_fusion.2 = f32[768,128]{1,0:T(8,128)} fusion(f32[768,384,8]{1,0,2:T(8,128)} %copy-done.2, f32[8,384]{1,0:T(8,128)S(1)} %log_add_fusion, pred[384,768]{0,1:T(8,128)(4,1)S(1)} %fusion.7, bf16[384,1024]{1,0:T(8,128)(2,1)} %param.11), kind=kOutput, calls=%fused_computation.21 | convolution fusion | flops 615776256 | bytes 10924032 | tf_op jit(solution)/shard_map/hrk,rhd->kd/dot_general | solution.py:94
  225.4 0.0 reduce-scatter.5.cloned.1.call-update
  225.4 0.3 reduce-scatter.3.cloned.1.call-start
  225.7 7.5 %multiply_reduce_fusion = (f32[8,384]{1,0:T(8,128)S(1)}, bf16[128,8,384]{2,0,1:T(8,128)(2,1)}) fusion(f32[8,384,128]{1,2,0:T(8,128)S(1)} %copy-done.9, f32[768,384,8]{1,0,2:T(8,128)} %copy-done.2, f32[8,384]{1,0:T(8,128)S(1)} %log_add_fusion, pred[384,768]{0,1:T(8,128)(4,1)S(1)} %fusion.7, bf16[768,128]{0,1:T(8,128)(2,1)} %all_gather.19), kind=kOutput, calls=%fused_computation.13 | convolution fusion | flops 617346048 | bytes 12312576 | tf_op jit(solution)/shard_map/hrk,kd->rhd/dot_general | solution.py:86
  233.2 6.2 %fusion.1 = bf16[8,384,768]{1,2,0:T(8,128)(2,1)S(1)} fusion(f32[768,384,8]{1,0,2:T(8,128)} %copy-done.2, f32[8,384]{1,0:T(8,128)S(1)} %get-tuple-element.54, f32[8,384]{1,0:T(8,128)S(1)} %log_add_fusion, pred[384,768]{0,1:T(8,128)(4,1)S(1)} %fusion.7, bf16[768,128]{0,1:T(8,128)(2,1)S(1)} %copy-done.13, bf16[384,1024]{1,0:T(8,128)(2,1)S(1)} %copy-done.11), kind=kOutput, calls=%fused_computation.2 | convolution fusion | flops 622854144 | bytes 15458304 | tf_op jit(solution)/shard_map/rhd,kd->hrk/dot_general | solution.py:90
  239.4 2.2 copy-done.3
  241.6 2.5 convolution_bitcast_fusion.3
  244.2 0.0 reduce-scatter.3.cloned.1.call-update
  244.2 0.3 all-gather.8.cloned.1.call-start
  244.5 4.3 %convolution_bitcast_fusion.1 = f32[384,8,128]{2,0,1:T(8,128)S(1)} fusion(bf16[8,384,768]{1,2,0:T(8,128)(2,1)} %copy-done.3, bf16[768,1,128]{0,2,1:T(8,128)(2,1)S(1)} %copy-done.8), kind=kOutput, calls=%fused_computation.18 | convolution fusion | flops 603979776 | bytes 6488064 | tf_op jit(solution)/shard_map/hrk,kd->rhd/dot_general | solution.py:92
  248.8 0.6 add_convert_fusion
  249.4 0.4 pad_maximum_fusion.3
  249.9 0.4 copy.78
  250.2 0.0 reduce-scatter.5.cloned.1.call-done
  250.3 0.9 convert_element_type.52
  251.2 0.1 copy.81
  251.3 4.3 %reduce-scatter.3.cloned.1.call-done = f32[384,128]{0,1:T(8,128)} async-done(((f32[768,128]{0,1:T(8,128)}), f32[384,128]{0,1:T(8,128)}) %reduce-scatter.3.cloned.1.call-update) | async-done | bytes 196624 | tf_op jit(solution)/shard_map/reduce_scatter | solution.py:231
  255.7 1.4 fusion.30
  257.1 1.0 pad_maximum_fusion.1
  258.1 0.0 all-gather.8.cloned.1.call-update
  258.1 7.0 %fusion.36 = f32[384,4096]{1,0:T(8,128)S(1)} fusion(bf16[4096,1280]{1,0:T(8,128)(2,1)} %all-gather.6.cloned.1.call-done, bf16[384,128]{0,1:T(8,128)(2,1)S(1)} %copy.81, bf16[384,128]{0,1:T(8,128)(2,1)S(1)} %maximum_bitcast_fusion, bf16[384,1024]{0,1:T(8,128)(2,1)S(1)} %bitcast.115), kind=kOutput, calls=%fused_computation.72 | convolution fusion | flops 4029480960 | bytes 17760256 | tf_op jit(solution)/shard_map/dot_general | solution.py:240
  265.2 3.2 copy.115
  268.3 5.7 %all-to-all-start.1 = ((f32[384,4,1024]{2,0,1:T(8,128)}), f32[384,4,1024]{2,0,1:T(8,128)}, u32[]{:S(2)}, u32[]{:S(2)}) async-start(f32[384,4,1024]{2,0,1:T(8,128)} %bitcast.107), calls=%async_computation.3 | async-start | bytes 12582912 | tf_op jit(solution)/shard_map/all_to_all | solution.py:244
  274.0 1.2 copy.83
  275.2 69.2 %all-to-all-done.1 = f32[384,4,1024]{2,0,1:T(8,128)} async-done(((f32[384,4,1024]{2,0,1:T(8,128)}), f32[384,4,1024]{2,0,1:T(8,128)}, u32[]{:S(2)}, u32[]{:S(2)}) %all-to-all-start.1) | async-done | bytes 6291488 | tf_op jit(solution)/shard_map/all_to_all | solution.py:244
  344.4 4.6 %reduce_sum.29 = bf16[384,1024]{1,0:T(8,128)(2,1)} reduce(f32[384,4,1024]{2,0,1:T(8,128)} %all-to-all-done.1, f32[]{:T(128)} %constant.32.clone.1), dimensions={1}, to_apply=%region_6.7 | reduce | flops 1179648 | bytes 7077892 | tf_op jit(solution)/shard_map/reduce_sum | solution.py:247
  349.0 28.3 %all-gather.8.cloned.1.call-done = bf16[3072,1280]{0,1:T(8,128)(2,1)} async-done(((bf16[384,1280]{0,1:T(8,128)(2,1)}), bf16[3072,1280]{0,1:T(8,128)(2,1)}) %all-gather.8.cloned.1.call-update) | async-done | bytes 7864336 | tf_op jit(solution)/shard_map/all_gather | solution.py:248
  377.3 8.6 %fusion.41 = f32[512,1280]{1,0:T(8,128)S(1)} fusion(bf16[3072,512]{1,0:T(8,128)(2,1)} %bitcast.110, bf16[3072,1280]{0,1:T(8,128)(2,1)} %all-gather.8.cloned.1.call-done), kind=kOutput, calls=%fused_computation.75 | convolution fusion | flops 4026531840 | bytes 13631488 | tf_op jit(solution)/shard_map/dot_general | solution.py:249
  385.9 1.6 slice.68
  387.6 0.8 fusion.39
  (35 shorter events, 0.1 us)
Async XLA Ops:
  7.2 2.8 copy-start
  7.2 168.8 %all-gather.6.cloned.1.call-start = ((), (), s32[]{:S(2)}) async-start(), calls=%async_computation.4 | async-start | bytes 11796480 | tf_op jit(solution)/shard_map/all_gather | solution.py:196
  9.9 8.4 %copy-start.14 = (s32[1,8]{1,0:T(1,128)S(1)}, s32[1,8]{1,0:T(1,128)}, u32[]{:S(2)}) copy-start(s32[1,8]{1,0:T(1,128)} %param.10) | copy-start | bytes 100
  10.9 44.2 %all-to-all-start = ((bf16[96,8,512]{2,0,1:T(8,128)(2,1)}), bf16[96,8,512]{2,0,1:T(8,128)(2,1)}, u32[]{:S(2)}, u32[]{:S(2)}) async-start(bf16[96,8,512]{2,0,1:T(8,128)(2,1)} %bitcast.112), calls=%async_computation | async-start | bytes 1572864 | tf_op jit(solution)/shard_map/all_to_all | solution.py:192
  18.2 194.2 %all-gather.10.cloned.1.call-start = ((), (), s32[]{:S(2)}) async-start(), calls=%async_computation.8 | async-start | bytes 3932160 | tf_op jit(solution)/shard_map/all_gather | solution.py:199
  176.0 74.3 %reduce-scatter.5.cloned.1.call-start = ((), (), s32[]{:S(2)}) async-start(), calls=%async_computation.6 | async-start | bytes 589824 | tf_op jit(solution)/shard_map/reduce_scatter | solution.py:232
  186.2 1.8 copy-start.4
  199.1 9.7 %copy-start.7 = (bf16[768,1,128]{0,2,1:T(8,128)(2,1)}, bf16[768,1,128]{0,2,1:T(8,128)(2,1)S(1)}, u32[]{:S(2)}) copy-start(bf16[768,1,128]{0,2,1:T(8,128)(2,1)S(1)} %all-gather) | copy-start | bytes 589828
  208.8 3.6 copy-start.2
  212.4 4.1 %copy-start.10 = (bf16[384,1024]{1,0:T(8,128)(2,1)S(1)}, bf16[384,1024]{1,0:T(8,128)(2,1)}, u32[]{:S(2)}) copy-start(bf16[384,1024]{1,0:T(8,128)(2,1)} %param.11) | copy-start | bytes 2359300
  218.5 7.2 %copy-start.9 = (f32[8,384,128]{1,2,0:T(8,128)S(1)}, f32[8,384,128]{1,2,0:T(8,128)}, u32[]{:S(2)}) copy-start(f32[8,384,128]{1,2,0:T(8,128)} %copy.92) | copy-start | bytes 4718596
  225.4 30.2 %reduce-scatter.3.cloned.1.call-start = ((), (), s32[]{:S(2)}) async-start(), calls=%async_computation.5 | async-start | bytes 589824 | tf_op jit(solution)/shard_map/reduce_scatter | solution.py:231
  225.7 7.5 %copy-start.11 = (bf16[384,1024]{1,0:T(8,128)(2,1)S(1)}, bf16[384,1024]{1,0:T(8,128)(2,1)}, u32[]{:S(2)}) copy-start(bf16[384,1024]{1,0:T(8,128)(2,1)} %param.11) | copy-start | bytes 2359300
  225.7 7.5 %copy-start.13 = (bf16[768,128]{0,1:T(8,128)(2,1)S(1)}, bf16[768,128]{0,1:T(8,128)(2,1)}, u32[]{:S(2)}) copy-start(bf16[768,128]{0,1:T(8,128)(2,1)} %all_gather.19) | copy-start | bytes 589828
  239.4 2.2 copy-start.3
  241.6 2.9 copy-start.8
  244.2 4.6 %copy-start.5 = (f32[384,64]{1,0:T(8,128)S(1)}, f32[384,64]{1,0:T(8,128)}, u32[]{:S(2)}) copy-start(f32[384,64]{1,0:T(8,128)} %get-tuple-element.50) | copy-start | bytes 294916
  244.2 4.6 %copy-start.6 = (f32[384,64]{1,0:T(8,128)S(1)}, f32[384,64]{1,0:T(8,128)}, u32[]{:S(2)}) copy-start(f32[384,64]{1,0:T(8,128)} %get-tuple-element.51) | copy-start | bytes 294916
  244.2 133.1 %all-gather.8.cloned.1.call-start = ((), (), s32[]{:S(2)}) async-start(), calls=%async_computation.7 | async-start | bytes 8847360 | tf_op jit(solution)/shard_map/all_gather | solution.py:248
  268.3 5.7 %copy-start.12 = (bf16[128,8,384]{2,0,1:T(8,128)(2,1)S(1)}, bf16[128,8,384]{2,0,1:T(8,128)(2,1)}, u32[]{:S(2)}) copy-start(bf16[128,8,384]{2,0,1:T(8,128)(2,1)} %get-tuple-element.55) | copy-start | bytes 2359300
  268.3 76.1 %all-to-all-start.1 = ((f32[384,4,1024]{2,0,1:T(8,128)}), f32[384,4,1024]{2,0,1:T(8,128)}, u32[]{:S(2)}, u32[]{:S(2)}) async-start(f32[384,4,1024]{2,0,1:T(8,128)} %bitcast.107), calls=%async_computation.3 | async-start | bytes 12582912 | tf_op jit(solution)/shard_map/all_to_all | solution.py:244
  377.3 11.1 %copy-start.1 = (bf16[384,4096]{1,0:T(8,128)(2,1)S(1)}, bf16[384,4096]{1,0:T(8,128)(2,1)}, u32[]{:S(2)}) copy-start(bf16[384,4096]{1,0:T(8,128)(2,1)} %param.6) | copy-start | bytes 9437188
Sparse Core Ops, SparseCore 0:
  10.8 165.1 all-gather.5
  177.5 26.7 all-gather.9
  225.6 11.3 reduce-scatter.4
  244.3 11.3 reduce-scatter.2
  258.3 119.0 all-gather.7

commit v4 on v3

--- a/solution.py
+++ b/solution.py
@@ -172,9 +172,22 @@
     return out_rows, grad_q, part_k, part_v
 
 
+def attend(query_rows, key_all, value_all, dout_rows, positions, all_pos, seg_own, seg_all):
+    head_count, num_rows, seq_len = query_rows.shape[1], query_rows.shape[0], key_all.shape[0]
+    operands = (query_rows, key_all, value_all, dout_rows, positions, all_pos, seg_own, seg_all)
+    if head_count * num_rows * seq_len <= (1 << 22):
+        return attend_whole(*operands)
+    kblock = seq_len
+    while head_count * num_rows * kblock > (1 << 21) and kblock % 256 == 0:
+        kblock //= 2
+    return attend_blocked(*operands, kblock)
+
+
 def local(hidden_in, w_query, w_key, w_value, lengths, attn_grad):
     num_rows = hidden_in.shape[0]
     head_count = w_query.shape[1] // 128
+    first_heads = head_count // 2 if head_count % 2 == 0 else head_count
+    first_cols = first_heads * 128
     query_cols = head_count * 128
     start_row = lax.axis_index("ctx") * num_rows
     seq_len = num_rows * lax.axis_size("ctx")
@@ -192,9 +205,9 @@
         cols_part = lax.all_to_all(own_rows, rows_axes, 1, 0, tiled=True)
     else:
         cols_part = lax.all_to_all(hidden_in, rows_axes, 1, 0, tiled=True)
-    local_w = jnp.concatenate([w_query, w_key, w_value], 1)
-    full_w = lax.all_gather(local_w, rows_axes, axis=0, tiled=True)
-    cols_part, full_w = lax.optimization_barrier((cols_part, full_w))
+    local_a = jnp.concatenate([w_query[:, :first_cols], w_key, w_value], 1)
+    full_a = lax.all_gather(local_a, rows_axes, axis=0, tiled=True)
+    cols_part, full_a, w_query = lax.optimization_barrier((cols_part, full_a, w_query))
     if num_rows % head_groups == 0:
         cols_all = lax.all_gather(cols_part, "head", axis=0, tiled=False)
         hidden_cols = (
@@ -204,58 +217,80 @@
         )
     else:
         hidden_cols = cols_part
-    projected = jnp.dot(hidden_in, full_w, preferred_element_type=jnp.float32)
-    query_rows = rotate(
-        projected[:, :query_cols].reshape(num_rows, head_count, 128), cosine, sine_table
+    proj_a = jnp.dot(hidden_in, full_a, preferred_element_type=jnp.float32)
+    query_a = rotate(
+        proj_a[:, :first_cols].reshape(num_rows, first_heads, 128), cosine, sine_table
     ).astype(jnp.bfloat16)
     key_rows = rotate(
-        projected[:, query_cols : query_cols + 128].reshape(num_rows, 1, 128), cosine, sine_table
+        proj_a[:, first_cols : first_cols + 128].reshape(num_rows, 1, 128), cosine, sine_table
     )[:, 0, :].astype(jnp.bfloat16)
-    value_rows = projected[:, query_cols + 128 :].astype(jnp.bfloat16)
+    value_rows = proj_a[:, first_cols + 128 :].astype(jnp.bfloat16)
     key_all, value_all = (
         lax.all_gather(key_rows, "ctx", axis=0, tiled=True),
         lax.all_gather(value_rows, "ctx", axis=0, tiled=True),
     )
-    hidden_cols, attn_grad = lax.optimization_barrier((hidden_cols, attn_grad))
     dout_rows = attn_grad.reshape(num_rows, head_count, 128)
-    operands = (query_rows, key_all, value_all, dout_rows, positions, all_pos, seg_own, seg_all)
-    if head_count * num_rows * seq_len <= (1 << 22):
-        out_rows, grad_q, part_k, part_v = attend_whole(*operands)
-    else:
-        kblock = seq_len
-        while head_count * num_rows * kblock > (1 << 22) and kblock % 256 == 0:
-            kblock //= 2
-        out_rows, grad_q, part_k, part_v = attend_blocked(*operands, kblock)
-    attended = out_rows.reshape(num_rows, query_cols)
+    shared = (key_all, value_all)
+    masks = (positions, all_pos, seg_own, seg_all)
+    out_a, grad_qa, part_k, part_v = attend(query_a, *shared, dout_rows[:, :first_heads], *masks)
+    d_query_a = unrotate(grad_qa, cosine, sine_table).astype(jnp.bfloat16).reshape(num_rows, -1)
+    out_parts, d_query_parts = [out_a], [d_query_a]
+    if first_heads < head_count:
+        w_rest = w_query[:, first_cols:]
+        full_b = lax.all_gather(w_rest, rows_axes, axis=0, tiled=True)
+        d_query_a, full_b = lax.optimization_barrier((d_query_a, full_b))
+        early_all = lax.all_gather(d_query_a, rows_axes, axis=0, tiled=True)
+        proj_b = jnp.dot(hidden_in, full_b, preferred_element_type=jnp.float32)
+        query_b = rotate(
+            proj_b.reshape(num_rows, head_count - first_heads, 128), cosine, sine_table
+        ).astype(jnp.bfloat16)
+        out_b, grad_qb, part_kb, part_vb = attend(
+            query_b, *shared, dout_rows[:, first_heads:], *masks
+        )
+        early_all, hidden_cols, part_kb, part_vb = lax.optimization_barrier(
+            (early_all, hidden_cols, part_kb, part_vb)
+        )
+        part_k, part_v = part_k + part_kb, part_v + part_vb
+        out_parts.append(out_b)
+        d_query_b = unrotate(grad_qb, cosine, sine_table).astype(jnp.bfloat16).reshape(num_rows, -1)
+        d_query_parts.append(d_query_b)
+    attended = jnp.concatenate(out_parts, 1).reshape(num_rows, query_cols)
     grad_k, grad_v = (
         lax.psum_scatter(part_k, "ctx", scatter_dimension=0, tiled=True),
         lax.psum_scatter(part_v, "ctx", scatter_dimension=0, tiled=True),
     )
-    d_query = (
-        unrotate(grad_q, cosine, sine_table).astype(jnp.bfloat16).reshape(num_rows, query_cols)
-    )
     d_key = unrotate(grad_k[:, None, :], cosine, sine_table)[:, 0, :].astype(jnp.bfloat16)
     d_value = grad_v.astype(jnp.bfloat16)
-    d_proj = jnp.concatenate([d_query, d_key, d_value], 1)
+    d_proj_a = jnp.concatenate([d_query_a, d_key, d_value], 1)
     input_part = lax.dot_general(
-        d_proj, full_w, (((1,), (1,)), ((), ())), preferred_element_type=jnp.float32
-    )
+        d_proj_a, full_a, (((1,), (1,)), ((), ())), preferred_element_type=jnp.float32
+    )
+    if first_heads < head_count:
+        input_part = input_part + lax.dot_general(
+            d_query_b, full_b, (((1,), (1,)), ((), ())), preferred_element_type=jnp.float32
+        )
+        late_proj = jnp.concatenate([d_query_b, d_key, d_value], 1)
+        early_sum = lax.dot_general(
+            hidden_cols, early_all, (((0,), (0,)), ((), ())), preferred_element_type=jnp.float32
+        )
+    else:
+        late_proj = jnp.concatenate([d_key, d_value], 1)
+        early_all = lax.all_gather(d_query_a, rows_axes, axis=0, tiled=True)
+        early_sum = lax.dot_general(
+            hidden_cols, early_all, (((0,), (0,)), ((), ())), preferred_element_type=jnp.float32
+        )
     input_cols = input_part.shape[1] // head_groups
     input_split = lax.all_to_all(
         input_part.reshape(num_rows, head_groups, input_cols), "head", 1, 1, tiled=False
     )
     grad_input = jnp.sum(input_split, axis=1).astype(jnp.bfloat16)
-    d_proj_all = lax.all_gather(d_proj, rows_axes, axis=0, tiled=True)
-    weight_sum = lax.dot_general(
-        hidden_cols, d_proj_all, (((0,), (0,)), ((), ())), preferred_element_type=jnp.float32
-    )
-    return (
-        attended,
-        grad_input,
-        weight_sum[:, :query_cols],
-        weight_sum[:, query_cols : query_cols + 128],
-        weight_sum[:, query_cols + 128 :],
-    )
+    late_all = lax.all_gather(late_proj, rows_axes, axis=0, tiled=True)
+    late_sum = lax.dot_general(
+        hidden_cols, late_all, (((0,), (0,)), ((), ())), preferred_element_type=jnp.float32
+    )
+    query_w = jnp.concatenate([early_sum, late_sum[:, : query_cols - first_cols]], 1)
+    rest = late_sum[:, query_cols - first_cols :]
+    return (attended, grad_input, query_w, rest[:, :128], rest[:, 128:])
 
 
 def solution(mesh):

time: 395 us -> 446 us (1.13); the launches traced: 395 us -> 441 us
  blocking collectives: 10.9 us -> 56 us
  waiting for transfers between devices: 259 us -> 237 us
  local copies, waits for them, and re-layouts: 24.9 us -> 43.2 us
  other arithmetic: 18.6 us -> 27.7 us
  starting transfers between devices: 13.7 us -> 6.24 us
    all_to_all x0 -> x1, blocking collectives: none -> 44.9 us  [local(): cols_part = lax.all_to_all(own_rows, rows_axes, 1, 0, tiled=True)]
    all_to_all x1 -> x0, waiting for transfers between devices: 36.5 us -> none  [local(): cols_part = lax.all_to_all(own_rows, rows_axes, 1, 0, tiled=True)]
    all_gather x1, waiting for transfers between devices: 0.01 us -> 26.2 us  [local(): cols_all = lax.all_gather(cols_part, 'head', axis=0, tiled=False)]
    all_gather x2 -> x4, waiting for transfers between devices: 149 us -> 131 us  [the longest x1 69.1 us: local(): full_a = lax.all_gather(local_a, rows_axes, axis=0, tiled=True)]
    reduce_scatter x1, waiting for transfers between devices: 0.02 us -> 14.5 us  [local(): lax.psum_scatter(part_v, 'ctx', scatter_dimension=0, tiled=True)]
    unnamed x35 -> x67, local copies, waits for them, and re-layouts: 11.1 us -> 24.1 us
    all_to_all x1, waiting for transfers between devices: 69.2 us -> 61.7 us  [local(): lax.all_to_all(input_part.reshape(num_rows, head_groups, input_cols), 'he...]
    all_to_all x1 -> x0, starting transfers between devices: 7.28 us -> none  [local(): cols_part = lax.all_to_all(own_rows, rows_axes, 1, 0, tiled=True)]
  transfers between devices with their start and end apart: 7 -> 8, of which waited for: 5 -> 7; matrix products, arithmetic and copies ran while one was open for 16% -> 22% of each run, Pallas kernels for 0% -> 0%
where the time goes in v4:
time: 446 us; the launch traced here: 441 us
  waiting for transfers between devices  237 us (53%)
  blocking collectives  56 us (13%)
  matrix products  55.9 us (13%)
  local copies, waits for them, and re-layouts  43.2 us (10%)
  other arithmetic  27.7 us (6%)
  between operations  15 us (3%)
  starting transfers between devices  6.24 us (1%)
    all_gather x1, waiting for transfers between devices, local(): full_a = lax.all_gather(local_a, rows_axes, axis=0, tiled=True)  69.1 us
    all_to_all x1, waiting for transfers between devices, local(): lax.all_to_all(input_part.reshape(num_rows, head_groups, input_cols), 'he...  61.7 us
    all_to_all x1, blocking collectives, local(): cols_part = lax.all_to_all(own_rows, rows_axes, 1, 0, tiled=True)  44.9 us
    all_gather x1, waiting for transfers between devices, local(): early_all = lax.all_gather(d_query_a, rows_axes, axis=0, tiled=True)  43.1 us
    all_gather x1, waiting for transfers between devices, local(): cols_all = lax.all_gather(cols_part, 'head', axis=0, tiled=False)  26.2 us
    unnamed x67, local copies, waits for them, and re-layouts  24.1 us
    all_gather x1, waiting for transfers between devices, local(): full_b = lax.all_gather(w_rest, rows_axes, axis=0, tiled=True)  19.3 us
    reduce_scatter x1, waiting for transfers between devices, local(): lax.psum_scatter(part_v, 'ctx', scatter_dimension=0, tiled=True)  14.5 us
  transfers between devices with their start and end apart: 8, of which 7 were waited for; matrix products, arithmetic and copies ran while one was open for 22% of the time, Pallas kernels for 0%

profile of v4, /device:TPU:0, one launch (start us, length us, event | category | flops | bytes accessed | tf_op | source)
XLA Modules:
  0.0 440.8 jit_solution(5144511457910652141)
XLA Ops:
  7.2 1.2 slice.70
  8.5 1.9 pad_maximum_fusion.1
  10.6 44.9 %all_to_all.24 = bf16[96,8,512]{2,0,1:T(8,128)(2,1)} all-to-all(bf16[96,8,512]{2,0,1:T(8,128)(2,1)S(1)} %bitcast.179), channel_id=1, replica_groups=mesh['dp'=4,'ctx'=2,'head'=4] {'dp','ctx'}, dimensions={1} | all-to-all | bytes 1572864 | tf_op jit(solution)/shard_map/all_to_all | solution.py:205
  55.5 69.1 %all-gather.8.cloned.1.call-done = bf16[4096,768]{1,0:T(8,128)(2,1)} async-done(((bf16[512,768]{1,0:T(8,128)(2,1)}), bf16[4096,768]{1,0:T(8,128)(2,1)}) %all-gather.8.cloned.1.call-update) | async-done | bytes 6291472 | tf_op jit(solution)/shard_map/all_gather | solution.py:209
  124.6 1.9 slice.81
  126.7 2.3 copy.119
  129.0 2.0 fusion.60
  131.0 0.9 copy.173
  132.4 1.5 multiply_cosine_fusion
  134.0 5.6 %convolution_bitcast_fusion = f32[384,768]{0,1:T(8,128)S(1)} fusion(bf16[4096,768]{1,0:T(8,128)(2,1)} %all-gather.8.cloned.1.call-done, bf16[384,4096]{1,0:T(8,128)(2,1)S(1)} %copy-done), kind=kOutput, calls=%fused_computation.25 | convolution fusion | flops 2415919104 | bytes 10616832 | tf_op jit(solution)/shard_map/dot_general | solution.py:220
  139.7 1.1 fusion.62
  140.9 2.2 copy.171
  143.0 2.1 copy.172
  145.2 0.9 slice_bitcast_fusion
  146.6 5.3 %all-gather = bf16[768,1,128]{0,2,1:T(8,128)(2,1)S(1)} all-gather(bf16[384,1,128]{0,2,1:T(8,128)(2,1)S(1)} %pad_maximum_fusion.12), channel_id=2, replica_groups=mesh['dp'=4,'ctx'=2,'head'=4] {'ctx'}, dimensions={0}, use_global_device_ids=true | all-gather | bytes 294912 | tf_op jit(solution)/shard_map/all_gather | solution.py:229
  151.9 5.8 %all_gather.25 = bf16[768,128]{0,1:T(8,128)(2,1)S(1)} all-gather(bf16[384,128]{0,1:T(8,128)(2,1)S(1)} %slice.138), channel_id=1, replica_groups=mesh['dp'=4,'ctx'=2,'head'=4] {'ctx'}, dimensions={0}, use_global_device_ids=true | all-gather | bytes 294912 | tf_op jit(solution)/shard_map/all_gather | solution.py:230
  157.7 2.1 subtract_convert_fusion.3
  159.9 1.2 fusion.10
  161.1 1.2 select_reduce_fusion.1
  162.3 2.4 bitcast_convert_fusion.1
  164.8 2.3 copy.151
  167.0 1.5 multiply_reduce_fusion.1
  168.6 4.5 %fusion.6 = bf16[4,384,768]{1,2,0:T(8,128)(2,1)S(1)} fusion(f32[768,384,4]{1,0,2:T(8,128)} %copy-done.2, f32[4,384]{1,0:T(4,128)S(1)} %multiply_reduce_fusion.1, f32[4,384]{1,0:T(4,128)S(1)} %log_add_fusion.1, pred[384,768]{0,1:T(8,128)(4,1)S(1)} %fusion.16, bf16[768,128]{0,1:T(8,128)(2,1)} %copy-done.22, bf16[384,8,128]{0,2,1:T(8,128)(2,1)} %bitcast.171), kind=kOutput, calls=%fused_computation.12 | convolution fusion | flops 311427072 | bytes 7974912 | tf_op jit(solution)/shard_map/rhd,kd->hrk/dot_general | solution.py:90
  173.1 1.5 copy-done.4
  174.7 1.1 convolution_bitcast_fusion.2
  176.1 1.0 pad_maximum_fusion.9
  177.1 1.9 copy.124
  179.0 19.3 %all-gather.10.cloned.1.call-done = bf16[4096,512]{1,0:T(8,128)(2,1)} async-done(((bf16[512,512]{1,0:T(8,128)(2,1)}), bf16[4096,512]{1,0:T(8,128)(2,1)}) %all-gather.10.cloned.1.call-update) | async-done | bytes 4194320 | tf_op jit(solution)/shard_map/all_gather | solution.py:240
  198.6 1.9 copy.176
  200.5 26.2 %all-gather.16.cloned.1.call-done = bf16[3072,512]{1,0:T(8,128)(2,1)} async-done(((bf16[768,512]{1,0:T(8,128)(2,1)}), bf16[3072,512]{1,0:T(8,128)(2,1)}) %all-gather.16.cloned.1.call-update) | async-done | bytes 3145744 | tf_op jit(solution)/shard_map/all_gather | solution.py:212
  226.7 4.1 copy.129
  230.8 2.4 fusion.63
  233.8 1.2 subtract_convert_fusion.1
  235.1 1.2 fusion.11
  236.3 1.2 select_reduce_fusion
  237.5 2.1 bitcast_convert_fusion
  240.2 4.6 %fusion.1 = bf16[4,384,768]{1,2,0:T(8,128)(2,1)S(1)} fusion(f32[768,384,4]{1,0,2:T(8,128)} %copy-done.3, f32[4,384]{1,0:T(4,128)S(1)} %multiply_reduce_fusion, f32[4,384]{1,0:T(4,128)S(1)} %log_add_fusion, pred[384,768]{0,1:T(8,128)(4,1)S(1)} %fusion.16, bf16[768,128]{0,1:T(8,128)(2,1)} %copy-done.22, bf16[384,8,128]{0,2,1:T(8,128)(2,1)} %bitcast.172), kind=kOutput, calls=%fused_computation.4 | convolution fusion | flops 311427072 | bytes 7974912 | tf_op jit(solution)/shard_map/rhd,kd->hrk/dot_general | solution.py:90
  244.8 1.6 convolution_bitcast_fusion.5
  246.5 2.1 convolution_bitcast_fusion.4
  248.6 43.1 %all-gather.12.cloned.1.call-done = bf16[3072,512]{0,1:T(8,128)(2,1)} async-done(((bf16[384,512]{0,1:T(8,128)(2,1)}), bf16[3072,512]{0,1:T(8,128)(2,1)}) %all-gather.12.cloned.1.call-update) | async-done | bytes 3145744 | tf_op jit(solution)/shard_map/all_gather | solution.py:242
  291.7 1.9 copy.133
  293.6 3.6 fusion.14
  297.3 4.7 %fusion.15 = f32[768,128]{1,0:T(8,128)} fusion(f32[768,128]{1,0:T(8,128)} %convolution_bitcast_fusion.4, bf16[384,8,128]{0,2,1:T(8,128)(2,1)} %bitcast.173, f32[768,384,4]{1,0,2:T(8,128)} %copy-done.2, f32[4,384]{1,0:T(4,128)S(1)} %log_add_fusion.1, pred[384,768]{0,1:T(8,128)(4,1)S(1)} %fusion.16), kind=kOutput, calls=%fused_computation.35 | convolution fusion | flops 307986432 | bytes 6199296 | tf_op jit(solution)/shard_map/hrk,rhd->kd/dot_general | solution.py:94
  302.2 2.0 convolution_bitcast_fusion.1
  304.2 1.3 add_convert_fusion
  306.0 2.8 reduce-scatter.3.cloned.1.call-done
  308.7 1.4 fusion.42
  310.1 14.5 %reduce-scatter.5.cloned.1.call-done = f32[384,128]{1,0:T(8,128)} async-done(((f32[768,128]{1,0:T(8,128)}), f32[384,128]{1,0:T(8,128)}) %reduce-scatter.5.cloned.1.call-update) | async-done | bytes 196624 | tf_op jit(solution)/shard_map/reduce_scatter | solution.py:260
  324.7 0.9 convert_element_type.74
  325.7 0.9 pad_maximum_fusion.3
  326.7 5.0 %fusion.17 = f32[384,4096]{1,0:T(8,128)S(1)} fusion(bf16[4096,768]{1,0:T(8,128)(2,1)} %all-gather.8.cloned.1.call-done, bf16[384,128]{0,1:T(8,128)(2,1)S(1)} %copy.134, bf16[384,128]{0,1:T(8,128)(2,1)S(1)} %maximum_bitcast_fusion, bf16[384,512]{0,1:T(8,128)(2,1)S(1)} %bitcast.181), kind=kOutput, calls=%fused_computation.55 | convolution fusion | flops 2417688576 | bytes 13172736 | tf_op jit(solution)/shard_map/dot_general | solution.py:265
  331.6 2.0 convolution_add_fusion
  333.6 3.4 copy.182
  337.0 5.8 %all-to-all-start.1 = ((f32[384,4,1024]{2,0,1:T(8,128)}), f32[384,4,1024]{2,0,1:T(8,128)}, u32[]{:S(2)}, u32[]{:S(2)}) async-start(f32[384,4,1024]{2,0,1:T(8,128)} %bitcast.162), calls=%async_computation.3 | async-start | bytes 12582912 | tf_op jit(solution)/shard_map/all_to_all | solution.py:283
  342.8 2.0 pad_maximum_fusion.2
  344.8 2.3 copy.141
  347.1 4.7 %fusion.65 = f32[512,512]{0,1:T(8,128)} fusion(bf16[3072,512]{0,1:T(8,128)(2,1)} %all-gather.12.cloned.1.call-done, bf16[3072,512]{1,0:T(8,128)(2,1)S(1)} %bitcast.167), kind=kOutput, calls=%fused_computation.120 | convolution fusion | flops 1610612736 | bytes 7340032 | tf_op jit(solution)/shard_map/dot_general | solution.py:273
  351.8 61.7 %all-to-all-done.1 = f32[384,4,1024]{2,0,1:T(8,128)} async-done(((f32[384,4,1024]{2,0,1:T(8,128)}), f32[384,4,1024]{2,0,1:T(8,128)}, u32[]{:S(2)}, u32[]{:S(2)}) %all-to-all-start.1) | async-done | bytes 6291488 | tf_op jit(solution)/shard_map/all_to_all | solution.py:283
  413.5 4.6 %reduce_sum.39 = bf16[384,1024]{1,0:T(8,128)(2,1)} reduce(f32[384,4,1024]{2,0,1:T(8,128)} %all-to-all-done.1, f32[]{:T(128)} %constant.32.clone.1), dimensions={1}, to_apply=%region_8.9 | reduce | flops 1179648 | bytes 7077892 | tf_op jit(solution)/shard_map/reduce_sum | solution.py:286
  418.1 5.0 %fusion.64 = f32[512,768]{1,0:T(8,128)S(1)} fusion(bf16[3072,512]{1,0:T(8,128)(2,1)S(1)} %bitcast.168, bf16[3072,768]{0,1:T(8,128)(2,1)} %all-gather.14.cloned.1.call-done), kind=kOutput, calls=%fused_computation.119 | convolution fusion | flops 2415919104 | bytes 9437184 | tf_op jit(solution)/shard_map/dot_general | solution.py:288
  423.1 1.1 slice.109
  425.0 2.7 copy.177
  427.7 3.1 pad_maximum_fusion
  430.8 2.9 copy.142
  (95 shorter events, 5.0 us)
Async XLA Ops:
  7.2 3.3 copy-start
  7.2 119.4 %copy-start.24 = (s32[1,8]{1,0:T(1,128)S(1)}, s32[1,8]{1,0:T(1,128)}, u32[]{:S(2)}) copy-start(s32[1,8]{1,0:T(1,128)} %param.10) | copy-start | bytes 100
  7.2 117.4 %all-gather.8.cloned.1.call-start = ((), (), s32[]{:S(2)}) async-start(), calls=%async_computation.4 | async-start | bytes 7077888 | tf_op jit(solution)/shard_map/all_gather | solution.py:209
  10.4 187.9 %all-gather.10.cloned.1.call-start = ((), (), s32[]{:S(2)}) async-start(), calls=%async_computation.5 | async-start | bytes 4718592 | tf_op jit(solution)/shard_map/all_gather | solution.py:240
  126.5 100.2 %all-gather.16.cloned.1.call-start = ((), (), s32[]{:S(2)}) async-start(), calls=%async_computation.10 | async-start | bytes 3932160 | tf_op jit(solution)/shard_map/all_gather | solution.py:212
  134.0 157.8 %all-gather.12.cloned.1.call-start = ((), (), s32[]{:S(2)}) async-start(), calls=%async_computation.6 | async-start | bytes 3538944 | tf_op jit(solution)/shard_map/all_gather | solution.py:242
  139.6 1.3 copy-start.20
  151.9 8.0 %copy-start.5 = (bf16[768,1,128]{0,2,1:T(8,128)(2,1)}, bf16[768,1,128]{0,2,1:T(8,128)(2,1)S(1)}, u32[]{:S(2)}) copy-start(bf16[768,1,128]{0,2,1:T(8,128)(2,1)S(1)} %all-gather) | copy-start | bytes 589828
  157.7 4.6 %copy-start.22 = (bf16[768,128]{0,1:T(8,128)(2,1)}, bf16[768,128]{0,1:T(8,128)(2,1)S(1)}, u32[]{:S(2)}) copy-start(bf16[768,128]{0,1:T(8,128)(2,1)S(1)} %all_gather.25) | copy-start | bytes 589828
  159.8 1.3 copy-start.12
  159.8 1.3 copy-start.14
  161.1 3.7 copy-start.2
  168.6 6.1 %copy-start.6 = (bf16[768,1,128]{0,2,1:T(8,128)(2,1)S(1)}, bf16[768,1,128]{0,2,1:T(8,128)(2,1)}, u32[]{:S(2)}) copy-start(bf16[768,1,128]{0,2,1:T(8,128)(2,1)} %copy-done.5) | copy-start | bytes 589828
  168.6 7.2 %copy-start.8 = (f32[384,64]{1,0:T(8,128)S(1)}, f32[384,64]{1,0:T(8,128)}, u32[]{:S(2)}) copy-start(f32[384,64]{1,0:T(8,128)} %get-tuple-element.68) | copy-start | bytes 294916
  168.6 7.2 %copy-start.9 = (f32[384,64]{1,0:T(8,128)S(1)}, f32[384,64]{1,0:T(8,128)}, u32[]{:S(2)}) copy-start(f32[384,64]{1,0:T(8,128)} %get-tuple-element.69) | copy-start | bytes 294916
  173.1 1.5 copy-start.4
  198.3 110.4 %reduce-scatter.3.cloned.1.call-start = ((), (), s32[]{:S(2)}) async-start(), calls=%async_computation.7 | async-start | bytes 589824 | tf_op jit(solution)/shard_map/reduce_scatter | solution.py:259
  226.7 4.1 copy-start.10
  233.2 1.9 copy-start.7
  235.1 2.4 copy-start.23
  236.3 3.4 copy-start.3
  237.5 2.4 copy-start.19
  239.9 6.5 %slice-start = ((s8[4718592]{0:T(1024)(128)(4,1)}), s8[4194304]{0:T(1024)(128)(4,1)S(1)}, s32[]{:S(2)}) async-start(s8[4718592]{0:T(1024)(128)(4,1)} %bitcast.163), calls=%async_computation.11 | async-start | bytes 8388608
  240.2 6.2 %slice-start.1 = ((s8[4718592]{0:T(1024)(128)(4,1)}), s8[524288]{0:T(1024)(128)(4,1)S(1)}, s32[]{:S(2)}) async-start(s8[4718592]{0:T(1024)(128)(4,1)} %bitcast.163), calls=%async_computation.12 | async-start | bytes 1048576
  244.8 1.6 copy-start.17
  246.5 47.2 %copy-start.13 = (bf16[384,4,64]{2,0,1:T(8,128)(2,1)S(1)}, bf16[384,4,64]{2,0,1:T(8,128)(2,1)}, u32[]{:S(2)}) copy-start(bf16[384,4,64]{2,0,1:T(8,128)(2,1)} %copy-done.12) | copy-start | bytes 589828
  246.5 47.2 %copy-start.15 = (bf16[384,4,64]{2,0,1:T(8,128)(2,1)S(1)}, bf16[384,4,64]{2,0,1:T(8,128)(2,1)}, u32[]{:S(2)}) copy-start(bf16[384,4,64]{2,0,1:T(8,128)(2,1)} %copy-done.14) | copy-start | bytes 589828
  297.3 27.4 %reduce-scatter.5.cloned.1.call-start = ((), (), s32[]{:S(2)}) async-start(), calls=%async_computation.8 | async-start | bytes 589824 | tf_op jit(solution)/shard_map/reduce_scatter | solution.py:260
  302.1 24.5 %copy-start.18 = (bf16[384,4,128]{0,2,1:T(8,128)(2,1)S(1)}, bf16[384,4,128]{0,2,1:T(8,128)(2,1)}, u32[]{:S(2)}) copy-start(bf16[384,4,128]{0,2,1:T(8,128)(2,1)} %copy.124) | copy-start | bytes 1179652
  302.1 116.0 %all-gather.14.cloned.1.call-start = ((), (), s32[]{:S(2)}) async-start(), calls=%async_computation.9 | async-start | bytes 5308416 | tf_op jit(solution)/shard_map/all_gather | solution.py:287
  326.7 5.0 %copy-start.11 = (bf16[4096,512]{1,0:T(8,128)(2,1)S(1)}, bf16[4096,512]{1,0:T(8,128)(2,1)}, u32[]{:S(2)}) copy-start(bf16[4096,512]{1,0:T(8,128)(2,1)} %all-gather.10.cloned.1.call-done) | copy-start | bytes 12582916
  337.0 5.8 %copy-start.21 = (bf16[128,4,384]{2,0,1:T(8,128)(2,1)S(1)}, bf16[128,4,384]{2,0,1:T(8,128)(2,1)}, u32[]{:S(2)}) copy-start(bf16[128,4,384]{2,0,1:T(8,128)(2,1)} %get-tuple-element.73) | copy-start | bytes 1179652
  337.0 10.1 %copy-start.16 = (bf16[4,8,96,512]{3,2,0,1:T(8,128)(2,1)S(1)}, bf16[4,8,96,512]{3,2,0,1:T(8,128)(2,1)}, u32[]{:S(2)}) copy-start(bf16[4,8,96,512]{3,2,0,1:T(8,128)(2,1)} %copy.129) | copy-start | bytes 9437188
  337.0 76.5 %all-to-all-start.1 = ((f32[384,4,1024]{2,0,1:T(8,128)}), f32[384,4,1024]{2,0,1:T(8,128)}, u32[]{:S(2)}, u32[]{:S(2)}) async-start(f32[384,4,1024]{2,0,1:T(8,128)} %bitcast.162), calls=%async_computation.3 | async-start | bytes 12582912 | tf_op jit(solution)/shard_map/all_to_all | solution.py:283
  425.0 8.7 %copy-start.1 = (bf16[384,4096]{1,0:T(8,128)(2,1)S(1)}, bf16[384,4096]{1,0:T(8,128)(2,1)}, u32[]{:S(2)}) copy-start(bf16[384,4096]{1,0:T(8,128)(2,1)} %param.6) | copy-start | bytes 9437188
Sparse Core Ops, SparseCore 0:
  10.8 113.7 all-gather.7
  126.7 71.5 all-gather.9
  199.9 26.7 all-gather.15
  228.6 63.0 all-gather.11
  297.4 11.2 reduce-scatter.2
  311.5 13.1 reduce-scatter.4
  327.3 80.9 all-gather.13

commit v5 on v4

--- a/solution.py
+++ b/solution.py
@@ -199,24 +199,16 @@
     rows_axes = ("dp", "ctx")
     group_count = lax.axis_size(rows_axes)
     head_groups = lax.axis_size("head")
-    if num_rows % head_groups == 0:
+    local_a = jnp.concatenate([w_query[:, :first_cols], w_key, w_value], 1)
+    full_a = lax.all_gather(local_a, rows_axes, axis=0, tiled=True)
+    full_a, w_query, hidden_in = lax.optimization_barrier((full_a, w_query, hidden_in))
+    split_rows = num_rows % head_groups == 0
+    if split_rows:
         quarter = num_rows // head_groups
         own_rows = lax.dynamic_slice_in_dim(hidden_in, lax.axis_index("head") * quarter, quarter, 0)
         cols_part = lax.all_to_all(own_rows, rows_axes, 1, 0, tiled=True)
     else:
         cols_part = lax.all_to_all(hidden_in, rows_axes, 1, 0, tiled=True)
-    local_a = jnp.concatenate([w_query[:, :first_cols], w_key, w_value], 1)
-    full_a = lax.all_gather(local_a, rows_axes, axis=0, tiled=True)
-    cols_part, full_a, w_query = lax.optimization_barrier((cols_part, full_a, w_query))
-    if num_rows % head_groups == 0:
-        cols_all = lax.all_gather(cols_part, "head", axis=0, tiled=False)
-        hidden_cols = (
-            cols_all.reshape(head_groups, group_count, quarter, -1)
-            .transpose(1, 0, 2, 3)
-            .reshape(group_count * num_rows, -1)
-        )
-    else:
-        hidden_cols = cols_part
     proj_a = jnp.dot(hidden_in, full_a, preferred_element_type=jnp.float32)
     query_a = rotate(
         proj_a[:, :first_cols].reshape(num_rows, first_heads, 128), cosine, sine_table
@@ -238,7 +230,7 @@
     if first_heads < head_count:
         w_rest = w_query[:, first_cols:]
         full_b = lax.all_gather(w_rest, rows_axes, axis=0, tiled=True)
-        d_query_a, full_b = lax.optimization_barrier((d_query_a, full_b))
+        d_query_a, full_b, cols_part = lax.optimization_barrier((d_query_a, full_b, cols_part))
         early_all = lax.all_gather(d_query_a, rows_axes, axis=0, tiled=True)
         proj_b = jnp.dot(hidden_in, full_b, preferred_element_type=jnp.float32)
         query_b = rotate(
@@ -247,6 +239,16 @@
         out_b, grad_qb, part_kb, part_vb = attend(
             query_b, *shared, dout_rows[:, first_heads:], *masks
         )
+        if split_rows:
+            spread = jnp.broadcast_to(cols_part[None], (head_groups,) + cols_part.shape)
+            cols_all = lax.all_to_all(spread, "head", 0, 0, tiled=False)
+            hidden_cols = (
+                cols_all.reshape(head_groups, group_count, quarter, -1)
+                .transpose(1, 0, 2, 3)
+                .reshape(group_count * num_rows, -1)
+            )
+        else:
+            hidden_cols = cols_part
         early_all, hidden_cols, part_kb, part_vb = lax.optimization_barrier(
             (early_all, hidden_cols, part_kb, part_vb)
         )
@@ -274,6 +276,14 @@
             hidden_cols, early_all, (((0,), (0,)), ((), ())), preferred_element_type=jnp.float32
         )
     else:
+        hidden_cols = cols_part
+        if split_rows:
+            cols_all = lax.all_gather(cols_part, "head", axis=0, tiled=False)
+            hidden_cols = (
+                cols_all.reshape(head_groups, group_count, quarter, -1)
+                .transpose(1, 0, 2, 3)
+                .reshape(group_count * num_rows, -1)
+            )
         late_proj = jnp.concatenate([d_key, d_value], 1)
         early_all = lax.all_gather(d_query_a, rows_axes, axis=0, tiled=True)
         early_sum = lax.dot_general(

time: 446 us -> 422 us (0.946)
  blocking collectives: 56 us -> 10.6 us
  starting transfers between devices: 6.24 us -> 15.9 us
  local copies, waits for them, and re-layouts: 43.2 us -> 48 us
    all_to_all x0 -> x2, waiting for transfers between devices: none -> 49.7 us  [the longest x1 26.7 us: local(): cols_part = lax.all_to_all(own_rows, rows_axes, 1, 0, tiled=True)]
    all_to_all x1 -> x0, blocking collectives: 44.9 us -> none  [local(): cols_part = lax.all_to_all(own_rows, rows_axes, 1, 0, tiled=True)]
    all_gather x1, waiting for transfers between devices: 43.1 us -> 8.1 us  [local(): early_all = lax.all_gather(d_query_a, rows_axes, axis=0, tiled=True)]
    all_gather x1, waiting for transfers between devices: 69.1 us -> 102 us  [local(): full_a = lax.all_gather(local_a, rows_axes, axis=0, tiled=True)]
    all_gather x1 -> x0, waiting for transfers between devices: 26.2 us -> none  [local(): cols_all = lax.all_gather(cols_part, 'head', axis=0, tiled=False)]
    all_gather x1, waiting for transfers between devices: 19.3 us -> 1.14 us  [local(): full_b = lax.all_gather(w_rest, rows_axes, axis=0, tiled=True)]
    all_to_all x0 -> x2, starting transfers between devices: none -> 8.98 us  [the longest x1 4.77 us: local(): cols_all = lax.all_to_all(spread, 'head', 0, 0, tiled=False)]
    unnamed x67 -> x66, local copies, waits for them, and re-layouts: 24.1 us -> 21.2 us
  transfers between devices with their start and end apart: 8 -> 9, of which waited for: 7 -> 8; matrix products, arithmetic and copies ran while one was open for 22% -> 25% of each run, Pallas kernels for 0% -> 0%
where the time goes in v5:
time: 422 us; the launch traced here: 414 us
  waiting for transfers between devices  240 us (57%)
  matrix products  57.5 us (14%)
  local copies, waits for them, and re-layouts  48 us (11%)
  other arithmetic  26.8 us (6%)
  starting transfers between devices  15.9 us (4%)
  between operations  14.9 us (4%)
  blocking collectives  10.6 us (3%)
    all_gather x1, waiting for transfers between devices, local(): full_a = lax.all_gather(local_a, rows_axes, axis=0, tiled=True)  102 us
    all_to_all x1, waiting for transfers between devices, local(): lax.all_to_all(input_part.reshape(num_rows, head_groups, input_cols), 'he...  61.7 us
    all_to_all x1, waiting for transfers between devices, local(): cols_part = lax.all_to_all(own_rows, rows_axes, 1, 0, tiled=True)  26.7 us
    all_to_all x1, waiting for transfers between devices, local(): cols_all = lax.all_to_all(spread, 'head', 0, 0, tiled=False)  23 us
    unnamed x66, local copies, waits for them, and re-layouts  21.2 us
    reduce_scatter x1, waiting for transfers between devices, local(): lax.psum_scatter(part_v, 'ctx', scatter_dimension=0, tiled=True)  14.5 us
    dot_general x2, matrix products, attend_whole(): jnp.einsum('rhd,kd->hrk', dout_rows, value_all, preferred_element_type=jn...  9.09 us
  transfers between devices with their start and end apart: 9, of which 8 were waited for; matrix products, arithmetic and copies ran while one was open for 25% of the time, Pallas kernels for 0%

profile of v5, /device:TPU:0, one launch (start us, length us, event | category | flops | bytes accessed | tf_op | source)
XLA Modules:
  0.0 413.7 jit_solution(15113371067236720433)
XLA Ops:
  7.2 1.2 slice.70
  8.5 1.9 pad_maximum_fusion.1
  10.5 102.1 %all-gather.6.cloned.1.call-done = bf16[4096,768]{1,0:T(8,128)(2,1)} async-done(((bf16[512,768]{1,0:T(8,128)(2,1)}), bf16[4096,768]{1,0:T(8,128)(2,1)}) %all-gather.6.cloned.1.call-update) | async-done | bytes 6291472 | tf_op jit(solution)/shard_map/all_gather | solution.py:203
  112.5 1.9 slice.81
  114.6 2.3 copy.148
  116.9 1.9 fusion.60
  120.3 1.5 multiply_cosine_fusion
  121.8 5.4 %fusion.63 = f32[384,768]{1,0:T(8,128)S(1)} fusion(bf16[384,4096]{1,0:T(8,128)(2,1)S(1)} %copy-done, bf16[4096,768]{1,0:T(8,128)(2,1)} %all-gather.6.cloned.1.call-done), kind=kOutput, calls=%fused_computation.116 | convolution fusion | flops 2415919104 | bytes 10616832 | tf_op jit(solution)/shard_map/dot_general | solution.py:212
  127.2 1.0 slice.96
  128.9 2.3 reshape.242
  131.1 1.7 copy.202
  132.9 1.4 fusion.38
  134.3 5.3 %all-gather = bf16[768,1,128]{0,2,1:T(8,128)(2,1)S(1)} all-gather(bf16[384,1,128]{0,2,1:T(8,128)(2,1)S(1)} %pad_maximum_fusion.12), channel_id=2, replica_groups=mesh['dp'=4,'ctx'=2,'head'=4] {'ctx'}, dimensions={0}, use_global_device_ids=true | all-gather | bytes 294912 | tf_op jit(solution)/shard_map/all_gather | solution.py:221
  139.6 5.3 %all_gather.19 = bf16[768,128]{1,0:T(8,128)(2,1)S(1)} all-gather(bf16[384,128]{1,0:T(8,128)(2,1)S(1)} %slice.137), channel_id=1, replica_groups=mesh['dp'=4,'ctx'=2,'head'=4] {'ctx'}, dimensions={0}, use_global_device_ids=true | all-gather | bytes 294912 | tf_op jit(solution)/shard_map/all_gather | solution.py:222
  144.9 1.9 fusion.62
  146.8 1.3 subtract_convert_fusion.3
  148.1 1.2 fusion.10
  149.4 1.2 select_reduce_fusion.1
  150.6 2.4 bitcast_convert_fusion.1
  153.0 2.3 copy.181
  156.3 4.2 %all-to-all-start = ((bf16[96,8,512]{2,0,1:T(8,128)(2,1)}), bf16[96,8,512]{2,0,1:T(8,128)(2,1)}, u32[]{:S(2)}, u32[]{:S(2)}) async-start(bf16[96,8,512]{2,0,1:T(8,128)(2,1)} %bitcast.168), calls=%async_computation | async-start | bytes 1572864 | tf_op jit(solution)/shard_map/all_to_all | solution.py:209
  161.1 1.5 multiply_reduce_fusion.1
  162.6 4.5 %fusion.6 = bf16[4,384,768]{1,2,0:T(8,128)(2,1)S(1)} fusion(f32[768,384,4]{1,0,2:T(8,128)} %copy-done.2, f32[4,384]{1,0:T(4,128)S(1)} %multiply_reduce_fusion.1, f32[4,384]{1,0:T(4,128)S(1)} %log_add_fusion.1, pred[384,768]{0,1:T(8,128)(4,1)S(1)} %fusion.16, bf16[768,128]{1,0:T(8,128)(2,1)} %copy-done.22, bf16[384,8,128]{0,2,1:T(8,128)(2,1)} %bitcast.164), kind=kOutput, calls=%fused_computation.12 | convolution fusion | flops 311427072 | bytes 7974912 | tf_op jit(solution)/shard_map/rhd,kd->hrk/dot_general | solution.py:90
  167.1 1.4 copy-done.4
  168.5 1.1 convolution_bitcast_fusion.1
  170.0 1.0 pad_maximum_fusion.9
  171.0 1.9 copy.152
  172.9 26.7 %all-to-all-done = bf16[96,8,512]{2,0,1:T(8,128)(2,1)} async-done(((bf16[96,8,512]{2,0,1:T(8,128)(2,1)}), bf16[96,8,512]{2,0,1:T(8,128)(2,1)}, u32[]{:S(2)}, u32[]{:S(2)}) %all-to-all-start) | async-done | bytes 786464 | tf_op jit(solution)/shard_map/all_to_all | solution.py:209
  199.5 1.1 all-gather.8.cloned.1.call-done
  200.7 1.9 copy.208
  202.6 4.6 %fusion.64 = f32[384,512]{0,1:T(8,128)S(1)} fusion(bf16[384,4096]{1,0:T(8,128)(2,1)S(1)} %copy-done, bf16[4096,512]{1,0:T(8,128)(2,1)} %all-gather.8.cloned.1.call-done), kind=kOutput, calls=%fused_computation.117 | convolution fusion | flops 1610612736 | bytes 8126464 | tf_op jit(solution)/shard_map/dot_general | solution.py:235
  207.8 3.2 broadcast_in_dim.76
  211.0 4.8 %all-to-all-start.1 = ((bf16[4,768,512]{2,1,0:T(8,128)(2,1)}), bf16[4,768,512]{2,1,0:T(8,128)(2,1)}, u32[]{:S(2)}, u32[]{:S(2)}) async-start(bf16[4,768,512]{2,1,0:T(8,128)(2,1)} %broadcast_in_dim.76), calls=%async_computation.1 | async-start | bytes 6291456 | tf_op jit(solution)/shard_map/all_to_all | solution.py:244
  216.3 1.2 fusion.11
  217.5 1.2 select_reduce_fusion
  218.7 2.1 bitcast_convert_fusion
  221.4 4.6 %fusion.1 = bf16[4,384,768]{1,2,0:T(8,128)(2,1)S(1)} fusion(f32[768,384,4]{1,0,2:T(8,128)} %copy-done.3, f32[4,384]{1,0:T(4,128)S(1)} %multiply_reduce_fusion, f32[4,384]{1,0:T(4,128)S(1)} %log_add_fusion, pred[384,768]{0,1:T(8,128)(4,1)S(1)} %fusion.16, bf16[768,128]{1,0:T(8,128)(2,1)} %copy-done.22, bf16[384,8,128]{0,2,1:T(8,128)(2,1)} %bitcast.165), kind=kOutput, calls=%fused_computation.4 | convolution fusion | flops 311427072 | bytes 7974912 | tf_op jit(solution)/shard_map/rhd,kd->hrk/dot_general | solution.py:90
  226.0 1.6 convolution_bitcast_fusion.4
  227.6 2.1 convolution_bitcast_fusion.3
  229.8 23.0 %all-to-all-done.1 = bf16[4,768,512]{2,1,0:T(8,128)(2,1)} async-done(((bf16[4,768,512]{2,1,0:T(8,128)(2,1)}), bf16[4,768,512]{2,1,0:T(8,128)(2,1)}, u32[]{:S(2)}, u32[]{:S(2)}) %all-to-all-start.1) | async-done | bytes 3145760 | tf_op jit(solution)/shard_map/all_to_all | solution.py:244
  252.8 4.0 copy.160
  256.8 8.1 %all-gather.10.cloned.1.call-done = bf16[3072,512]{0,1:T(8,128)(2,1)} async-done(((bf16[384,512]{0,1:T(8,128)(2,1)}), bf16[3072,512]{0,1:T(8,128)(2,1)}) %all-gather.10.cloned.1.call-update) | async-done | bytes 3145744 | tf_op jit(solution)/shard_map/all_gather | solution.py:234
  264.9 1.9 copy.163
  266.8 3.4 fusion.14
  270.3 4.7 %fusion.15 = f32[768,128]{1,0:T(8,128)} fusion(f32[768,128]{1,0:T(8,128)} %convolution_bitcast_fusion.3, bf16[384,8,128]{0,2,1:T(8,128)(2,1)} %bitcast.166, f32[768,384,4]{1,0,2:T(8,128)} %copy-done.2, f32[4,384]{1,0:T(4,128)S(1)} %log_add_fusion.1, pred[384,768]{0,1:T(8,128)(4,1)S(1)} %fusion.16), kind=kOutput, calls=%fused_computation.34 | convolution fusion | flops 307986432 | bytes 6199296 | tf_op jit(solution)/shard_map/hrk,rhd->kd/dot_general | solution.py:94
  275.3 2.0 convolution_bitcast_fusion
  277.3 1.3 add_convert_fusion
  279.1 2.6 reduce-scatter.3.cloned.1.call-done
  281.7 1.4 fusion.42
  283.1 14.5 %reduce-scatter.5.cloned.1.call-done = f32[384,128]{1,0:T(8,128)} async-done(((f32[768,128]{1,0:T(8,128)}), f32[384,128]{1,0:T(8,128)}) %reduce-scatter.5.cloned.1.call-update) | async-done | bytes 196624 | tf_op jit(solution)/shard_map/reduce_scatter | solution.py:262
  299.6 5.0 %fusion.17 = f32[384,4096]{1,0:T(8,128)S(1)} fusion(bf16[4096,768]{1,0:T(8,128)(2,1)} %all-gather.6.cloned.1.call-done, bf16[384,128]{0,1:T(8,128)(2,1)S(1)} %copy.164, bf16[384,128]{0,1:T(8,128)(2,1)S(1)} %maximum_bitcast_fusion, bf16[384,512]{0,1:T(8,128)(2,1)S(1)} %bitcast.172), kind=kOutput, calls=%fused_computation.54 | convolution fusion | flops 2417688576 | bytes 13172736 | tf_op jit(solution)/shard_map/dot_general | solution.py:267
  304.6 2.0 convolution_add_fusion
  306.5 3.4 copy.218
  309.9 5.8 %all-to-all-start.2 = ((f32[384,4,1024]{2,0,1:T(8,128)}), f32[384,4,1024]{2,0,1:T(8,128)}, u32[]{:S(2)}, u32[]{:S(2)}) async-start(f32[384,4,1024]{2,0,1:T(8,128)} %bitcast.156), calls=%async_computation.4 | async-start | bytes 12582912 | tf_op jit(solution)/shard_map/all_to_all | solution.py:293
  315.7 2.0 pad_maximum_fusion.2
  317.7 2.3 copy.171
  320.0 4.7 %fusion.66 = f32[512,512]{0,1:T(8,128)} fusion(bf16[3072,512]{0,1:T(8,128)(2,1)} %all-gather.10.cloned.1.call-done, bf16[3072,512]{1,0:T(8,128)(2,1)S(1)} %bitcast.161), kind=kOutput, calls=%fused_computation.119 | convolution fusion | flops 1610612736 | bytes 7340032 | tf_op jit(solution)/shard_map/dot_general | solution.py:275
  324.7 61.7 %all-to-all-done.2 = f32[384,4,1024]{2,0,1:T(8,128)} async-done(((f32[384,4,1024]{2,0,1:T(8,128)}), f32[384,4,1024]{2,0,1:T(8,128)}, u32[]{:S(2)}, u32[]{:S(2)}) %all-to-all-start.2) | async-done | bytes 6291488 | tf_op jit(solution)/shard_map/all_to_all | solution.py:293
  386.4 4.6 %reduce_sum.39 = bf16[384,1024]{1,0:T(8,128)(2,1)} reduce(f32[384,4,1024]{2,0,1:T(8,128)} %all-to-all-done.2, f32[]{:T(128)} %constant.30.clone.1), dimensions={1}, to_apply=%region_8.9 | reduce | flops 1179648 | bytes 7077892 | tf_op jit(solution)/shard_map/reduce_sum | solution.py:296
  391.0 5.0 %fusion.65 = f32[512,768]{1,0:T(8,128)S(1)} fusion(bf16[3072,512]{1,0:T(8,128)(2,1)S(1)} %bitcast.162, bf16[3072,768]{0,1:T(8,128)(2,1)} %all-gather.12.cloned.1.call-done), kind=kOutput, calls=%fused_computation.118 | convolution fusion | flops 2415919104 | bytes 9437184 | tf_op jit(solution)/shard_map/dot_general | solution.py:298
  396.0 1.1 slice.109
  397.9 2.7 copy.209
  400.6 3.1 pad_maximum_fusion
  403.7 2.9 copy.172
  (96 shorter events, 9.6 us)
Async XLA Ops:
  7.2 114.6 %copy-start = (bf16[384,4096]{1,0:T(8,128)(2,1)S(1)}, bf16[384,4096]{1,0:T(8,128)(2,1)}, u32[]{:S(2)}) copy-start(bf16[384,4096]{1,0:T(8,128)(2,1)} %param.6) | copy-start | bytes 9437188
  7.2 107.3 %copy-start.24 = (s32[1,8]{1,0:T(1,128)S(1)}, s32[1,8]{1,0:T(1,128)}, u32[]{:S(2)}) copy-start(s32[1,8]{1,0:T(1,128)} %param.10) | copy-start | bytes 100
  7.2 105.3 %all-gather.6.cloned.1.call-start = ((), (), s32[]{:S(2)}) async-start(), calls=%async_computation.5 | async-start | bytes 7077888 | tf_op jit(solution)/shard_map/all_gather | solution.py:203
  10.4 190.3 %all-gather.8.cloned.1.call-start = ((), (), s32[]{:S(2)}) async-start(), calls=%async_computation.6 | async-start | bytes 4718592 | tf_op jit(solution)/shard_map/all_gather | solution.py:232
  139.6 9.8 %copy-start.5 = (bf16[768,1,128]{0,2,1:T(8,128)(2,1)}, bf16[768,1,128]{0,2,1:T(8,128)(2,1)S(1)}, u32[]{:S(2)}) copy-start(bf16[768,1,128]{0,2,1:T(8,128)(2,1)S(1)} %all-gather) | copy-start | bytes 589828
  144.9 5.7 %copy-start.22 = (bf16[768,128]{1,0:T(8,128)(2,1)}, bf16[768,128]{1,0:T(8,128)(2,1)S(1)}, u32[]{:S(2)}) copy-start(bf16[768,128]{1,0:T(8,128)(2,1)S(1)} %all_gather.19) | copy-start | bytes 589828
  148.1 1.3 copy-start.13
  148.1 1.3 copy-start.15
  149.3 3.6 copy-start.2
  156.3 43.3 %all-to-all-start = ((bf16[96,8,512]{2,0,1:T(8,128)(2,1)}), bf16[96,8,512]{2,0,1:T(8,128)(2,1)}, u32[]{:S(2)}, u32[]{:S(2)}) async-start(bf16[96,8,512]{2,0,1:T(8,128)(2,1)} %bitcast.168), calls=%async_computation | async-start | bytes 1572864 | tf_op jit(solution)/shard_map/all_to_all | solution.py:209
  160.5 104.4 %all-gather.10.cloned.1.call-start = ((), (), s32[]{:S(2)}) async-start(), calls=%async_computation.7 | async-start | bytes 3538944 | tf_op jit(solution)/shard_map/all_gather | solution.py:234
  162.6 5.9 %copy-start.6 = (bf16[768,1,128]{0,2,1:T(8,128)(2,1)S(1)}, bf16[768,1,128]{0,2,1:T(8,128)(2,1)}, u32[]{:S(2)}) copy-start(bf16[768,1,128]{0,2,1:T(8,128)(2,1)} %copy-done.5) | copy-start | bytes 589828
  162.6 7.0 %copy-start.8 = (f32[384,64]{1,0:T(8,128)S(1)}, f32[384,64]{1,0:T(8,128)}, u32[]{:S(2)}) copy-start(f32[384,64]{1,0:T(8,128)} %get-tuple-element.75) | copy-start | bytes 294916
  162.6 7.0 %copy-start.10 = (f32[384,64]{1,0:T(8,128)S(1)}, f32[384,64]{1,0:T(8,128)}, u32[]{:S(2)}) copy-start(f32[384,64]{1,0:T(8,128)} %get-tuple-element.76) | copy-start | bytes 294916
  167.1 1.4 copy-start.4
  207.8 8.2 %copy-start.9 = (f32[384,64]{1,0:T(8,128)S(1)}, f32[384,64]{1,0:T(8,128)}, u32[]{:S(2)}) copy-start(f32[384,64]{1,0:T(8,128)} %get-tuple-element.75) | copy-start | bytes 294916
  207.8 8.2 %copy-start.11 = (f32[384,64]{1,0:T(8,128)S(1)}, f32[384,64]{1,0:T(8,128)}, u32[]{:S(2)}) copy-start(f32[384,64]{1,0:T(8,128)} %get-tuple-element.76) | copy-start | bytes 294916
  211.0 5.2 %copy-start.7 = (bf16[768,1,128]{0,2,1:T(8,128)(2,1)S(1)}, bf16[768,1,128]{0,2,1:T(8,128)(2,1)}, u32[]{:S(2)}) copy-start(bf16[768,1,128]{0,2,1:T(8,128)(2,1)} %copy-done.5) | copy-start | bytes 589828
  211.0 41.8 %all-to-all-start.1 = ((bf16[4,768,512]{2,1,0:T(8,128)(2,1)}), bf16[4,768,512]{2,1,0:T(8,128)(2,1)}, u32[]{:S(2)}, u32[]{:S(2)}) async-start(bf16[4,768,512]{2,1,0:T(8,128)(2,1)} %broadcast_in_dim.76), calls=%async_computation.1 | async-start | bytes 6291456 | tf_op jit(solution)/shard_map/all_to_all | solution.py:244
  215.8 65.9 %reduce-scatter.3.cloned.1.call-start = ((), (), s32[]{:S(2)}) async-start(), calls=%async_computation.8 | async-start | bytes 589824 | tf_op jit(solution)/shard_map/reduce_scatter | solution.py:261
  216.3 2.4 copy-start.23
  217.5 3.3 copy-start.3
  218.7 2.4 copy-start.20
  221.1 6.5 %slice-start = ((s8[4718592]{0:T(1024)(128)(4,1)}), s8[4194304]{0:T(1024)(128)(4,1)S(1)}, s32[]{:S(2)}) async-start(s8[4718592]{0:T(1024)(128)(4,1)} %bitcast.157), calls=%async_computation.11 | async-start | bytes 8388608
  221.4 6.2 %slice-start.1 = ((s8[4718592]{0:T(1024)(128)(4,1)}), s8[524288]{0:T(1024)(128)(4,1)S(1)}, s32[]{:S(2)}) async-start(s8[4718592]{0:T(1024)(128)(4,1)} %bitcast.157), calls=%async_computation.12 | async-start | bytes 1048576
  226.0 1.6 copy-start.18
  229.8 37.0 %copy-start.14 = (bf16[384,4,64]{2,0,1:T(8,128)(2,1)S(1)}, bf16[384,4,64]{2,0,1:T(8,128)(2,1)}, u32[]{:S(2)}) copy-start(bf16[384,4,64]{2,0,1:T(8,128)(2,1)} %copy-done.13) | copy-start | bytes 589828
  229.8 37.0 %copy-start.16 = (bf16[384,4,64]{2,0,1:T(8,128)(2,1)S(1)}, bf16[384,4,64]{2,0,1:T(8,128)(2,1)}, u32[]{:S(2)}) copy-start(bf16[384,4,64]{2,0,1:T(8,128)(2,1)} %copy-done.15) | copy-start | bytes 589828
  270.2 27.4 %reduce-scatter.5.cloned.1.call-start = ((), (), s32[]{:S(2)}) async-start(), calls=%async_computation.9 | async-start | bytes 589824 | tf_op jit(solution)/shard_map/reduce_scatter | solution.py:262
  275.0 24.5 %copy-start.19 = (bf16[384,4,128]{0,2,1:T(8,128)(2,1)S(1)}, bf16[384,4,128]{0,2,1:T(8,128)(2,1)}, u32[]{:S(2)}) copy-start(bf16[384,4,128]{0,2,1:T(8,128)(2,1)} %copy.152) | copy-start | bytes 1179652
  275.0 116.0 %all-gather.12.cloned.1.call-start = ((), (), s32[]{:S(2)}) async-start(), calls=%async_computation.10 | async-start | bytes 5308416 | tf_op jit(solution)/shard_map/all_gather | solution.py:297
  299.6 5.0 %copy-start.12 = (bf16[4096,512]{1,0:T(8,128)(2,1)S(1)}, bf16[4096,512]{1,0:T(8,128)(2,1)}, u32[]{:S(2)}) copy-start(bf16[4096,512]{1,0:T(8,128)(2,1)} %all-gather.8.cloned.1.call-done) | copy-start | bytes 12582916
  309.9 5.8 %copy-start.21 = (bf16[128,4,384]{2,0,1:T(8,128)(2,1)S(1)}, bf16[128,4,384]{2,0,1:T(8,128)(2,1)}, u32[]{:S(2)}) copy-start(bf16[128,4,384]{2,0,1:T(8,128)(2,1)} %get-tuple-element.80) | copy-start | bytes 1179652
  309.9 10.1 %copy-start.17 = (bf16[8,4,96,512]{3,2,1,0:T(8,128)(2,1)S(1)}, bf16[8,4,96,512]{3,2,1,0:T(8,128)(2,1)}, u32[]{:S(2)}) copy-start(bf16[8,4,96,512]{3,2,1,0:T(8,128)(2,1)} %copy.160) | copy-start | bytes 9437188
  309.9 76.5 %all-to-all-start.2 = ((f32[384,4,1024]{2,0,1:T(8,128)}), f32[384,4,1024]{2,0,1:T(8,128)}, u32[]{:S(2)}, u32[]{:S(2)}) async-start(f32[384,4,1024]{2,0,1:T(8,128)} %bitcast.156), calls=%async_computation.4 | async-start | bytes 12582912 | tf_op jit(solution)/shard_map/all_to_all | solution.py:293
  397.9 8.6 %copy-start.1 = (bf16[384,4096]{1,0:T(8,128)(2,1)S(1)}, bf16[384,4096]{1,0:T(8,128)(2,1)}, u32[]{:S(2)}) copy-start(bf16[384,4096]{1,0:T(8,128)(2,1)} %param.6) | copy-start | bytes 9437188
Sparse Core Ops, SparseCore 0:
  10.8 101.7 all-gather.5
  114.7 85.9 all-gather.7
  202.7 62.0 all-gather.9
  270.3 11.2 reduce-scatter.2
  284.4 13.1 reduce-scatter.4
  300.1 80.9 all-gather.11

commit v6 on v5

--- a/solution.py
+++ b/solution.py
@@ -230,7 +230,7 @@
     if first_heads < head_count:
         w_rest = w_query[:, first_cols:]
         full_b = lax.all_gather(w_rest, rows_axes, axis=0, tiled=True)
-        d_query_a, full_b, cols_part = lax.optimization_barrier((d_query_a, full_b, cols_part))
+        d_query_a, full_b = lax.optimization_barrier((d_query_a, full_b))
         early_all = lax.all_gather(d_query_a, rows_axes, axis=0, tiled=True)
         proj_b = jnp.dot(hidden_in, full_b, preferred_element_type=jnp.float32)
         query_b = rotate(
@@ -239,6 +239,10 @@
         out_b, grad_qb, part_kb, part_vb = attend(
             query_b, *shared, dout_rows[:, first_heads:], *masks
         )
+        early_all, cols_part, part_kb, part_vb = lax.optimization_barrier(
+            (early_all, cols_part, part_kb, part_vb)
+        )
+        hidden_cols = cols_part
         if split_rows:
             spread = jnp.broadcast_to(cols_part[None], (head_groups,) + cols_part.shape)
             cols_all = lax.all_to_all(spread, "head", 0, 0, tiled=False)
@@ -247,11 +251,6 @@
                 .transpose(1, 0, 2, 3)
                 .reshape(group_count * num_rows, -1)
             )
-        else:
-            hidden_cols = cols_part
-        early_all, hidden_cols, part_kb, part_vb = lax.optimization_barrier(
-            (early_all, hidden_cols, part_kb, part_vb)
-        )
         part_k, part_v = part_k + part_kb, part_v + part_vb
         out_parts.append(out_b)
         d_query_b = unrotate(grad_qb, cosine, sine_table).astype(jnp.bfloat16).reshape(num_rows, -1)
@@ -291,9 +290,10 @@
         )
     input_cols = input_part.shape[1] // head_groups
     input_split = lax.all_to_all(
-        input_part.reshape(num_rows, head_groups, input_cols), "head", 1, 1, tiled=False
-    )
-    grad_input = jnp.sum(input_split, axis=1).astype(jnp.bfloat16)
+        input_part.astype(jnp.bfloat16).reshape(num_rows, head_groups, input_cols),
+        "head", 1, 1, tiled=False,
+    )
+    grad_input = jnp.sum(input_split.astype(jnp.float32), axis=1).astype(jnp.bfloat16)
     late_all = lax.all_gather(late_proj, rows_axes, axis=0, tiled=True)
     late_sum = lax.dot_general(
         hidden_cols, late_all, (((0,), (0,)), ((), ())), preferred_element_type=jnp.float32

time: 422 us -> 412 us (0.976)
    all_to_all x1, waiting for transfers between devices: 61.7 us -> 25.7 us  [local(): lax.all_to_all(input_part.astype(jnp.bfloat16).reshape(num_rows, head_gro...]
    all_gather x1, waiting for transfers between devices: 8.1 us -> 35.6 us  [local(): early_all = lax.all_gather(d_query_a, rows_axes, axis=0, tiled=True)]
    all_gather x1, waiting for transfers between devices: 1.14 us -> 18.4 us  [local(): full_b = lax.all_gather(w_rest, rows_axes, axis=0, tiled=True)]
    all_to_all x1, waiting for transfers between devices: 26.7 us -> 11.6 us  [local(): cols_part = lax.all_to_all(own_rows, rows_axes, 1, 0, tiled=True)]
    reduce_scatter x1, waiting for transfers between devices: 2.61 us -> 14.8 us  [local(): lax.psum_scatter(part_k, 'ctx', scatter_dimension=0, tiled=True)]
    reduce_scatter x1, waiting for transfers between devices: 14.5 us -> 3.11 us  [local(): lax.psum_scatter(part_v, 'ctx', scatter_dimension=0, tiled=True)]
    all_to_all x1, waiting for transfers between devices: 23 us -> 28 us  [local(): cols_all = lax.all_to_all(spread, 'head', 0, 0, tiled=False)]
    unnamed x66 -> x68, local copies, waits for them, and re-layouts: 21.2 us -> 23.1 us
  transfers between devices with their start and end apart: 9 -> 9, of which waited for: 8 -> 8; matrix products, arithmetic and copies ran while one was open for 25% -> 24% of each run, Pallas kernels for 0% -> 0%
where the time goes in v6:
time: 412 us; the launch traced here: 407 us
  waiting for transfers between devices  239 us (58%)
  matrix products  56.1 us (14%)
  local copies, waits for them, and re-layouts  47.2 us (11%)
  other arithmetic  24.8 us (6%)
  between operations  14.9 us (4%)
  starting transfers between devices  13.2 us (3%)
  blocking collectives  11.1 us (3%)
    all_gather x1, waiting for transfers between devices, local(): full_a = lax.all_gather(local_a, rows_axes, axis=0, tiled=True)  102 us
    all_gather x1, waiting for transfers between devices, local(): early_all = lax.all_gather(d_query_a, rows_axes, axis=0, tiled=True)  35.6 us
    all_to_all x1, waiting for transfers between devices, local(): cols_all = lax.all_to_all(spread, 'head', 0, 0, tiled=False)  28 us
    all_to_all x1, waiting for transfers between devices, local(): lax.all_to_all(input_part.astype(jnp.bfloat16).reshape(num_rows, head_gro...  25.7 us
    unnamed x68, local copies, waits for them, and re-layouts  23.1 us
    all_gather x1, waiting for transfers between devices, local(): full_b = lax.all_gather(w_rest, rows_axes, axis=0, tiled=True)  18.4 us
    reduce_scatter x1, waiting for transfers between devices, local(): lax.psum_scatter(part_k, 'ctx', scatter_dimension=0, tiled=True)  14.8 us
    all_to_all x1, waiting for transfers between devices, local(): cols_part = lax.all_to_all(own_rows, rows_axes, 1, 0, tiled=True)  11.6 us
  transfers between devices with their start and end apart: 9, of which 8 were waited for; matrix products, arithmetic and copies ran while one was open for 24% of the time, Pallas kernels for 0%

profile of v6, /device:TPU:0, one launch (start us, length us, event | category | flops | bytes accessed | tf_op | source)
XLA Modules:
  0.0 406.7 jit_solution(399087149256440462)
XLA Ops:
  7.2 1.2 slice.70
  8.5 1.9 pad_maximum_fusion.1
  10.5 102.1 %all-gather.6.cloned.1.call-done = bf16[4096,768]{1,0:T(8,128)(2,1)} async-done(((bf16[512,768]{1,0:T(8,128)(2,1)}), bf16[4096,768]{1,0:T(8,128)(2,1)}) %all-gather.6.cloned.1.call-update) | async-done | bytes 6291472 | tf_op jit(solution)/shard_map/all_gather | solution.py:203
  112.5 1.9 slice.81
  114.7 2.3 copy.148
  117.0 1.9 fusion.60
  120.4 1.5 multiply_cosine_fusion
  121.9 5.4 %fusion.63 = f32[384,768]{1,0:T(8,128)S(1)} fusion(bf16[384,4096]{1,0:T(8,128)(2,1)S(1)} %copy-done, bf16[4096,768]{1,0:T(8,128)(2,1)} %all-gather.6.cloned.1.call-done), kind=kOutput, calls=%fused_computation.116 | convolution fusion | flops 2415919104 | bytes 10616832 | tf_op jit(solution)/shard_map/dot_general | solution.py:212
  128.9 2.3 reshape.242
  131.2 1.7 copy.202
  132.9 1.4 fusion.38
  134.4 5.3 %all-gather = bf16[768,1,128]{0,2,1:T(8,128)(2,1)S(1)} all-gather(bf16[384,1,128]{0,2,1:T(8,128)(2,1)S(1)} %pad_maximum_fusion.12), channel_id=2, replica_groups=mesh['dp'=4,'ctx'=2,'head'=4] {'ctx'}, dimensions={0}, use_global_device_ids=true | all-gather | bytes 294912 | tf_op jit(solution)/shard_map/all_gather | solution.py:221
  139.6 5.8 %all_gather.19 = bf16[768,128]{1,0:T(8,128)(2,1)S(1)} all-gather(bf16[384,128]{1,0:T(8,128)(2,1)S(1)} %slice.137), channel_id=1, replica_groups=mesh['dp'=4,'ctx'=2,'head'=4] {'ctx'}, dimensions={0}, use_global_device_ids=true | all-gather | bytes 294912 | tf_op jit(solution)/shard_map/all_gather | solution.py:222
  145.5 2.1 fusion.62
  147.6 1.2 subtract_convert_fusion.3
  148.8 1.2 fusion.10
  150.1 1.2 select_reduce_fusion.1
  151.3 2.4 bitcast_convert_fusion.1
  153.7 2.3 copy.181
  156.0 1.5 multiply_reduce_fusion.1
  157.6 4.5 %fusion.6 = bf16[4,384,768]{1,2,0:T(8,128)(2,1)S(1)} fusion(f32[768,384,4]{1,0,2:T(8,128)} %copy-done.2, f32[4,384]{1,0:T(4,128)S(1)} %multiply_reduce_fusion.1, f32[4,384]{1,0:T(4,128)S(1)} %log_add_fusion.1, pred[384,768]{0,1:T(8,128)(4,1)S(1)} %fusion.16, bf16[768,128]{1,0:T(8,128)(2,1)} %copy-done.22, bf16[384,8,128]{0,2,1:T(8,128)(2,1)} %bitcast.164), kind=kOutput, calls=%fused_computation.11 | convolution fusion | flops 311427072 | bytes 7974912 | tf_op jit(solution)/shard_map/rhd,kd->hrk/dot_general | solution.py:90
  162.1 1.5 copy-done.4
  163.5 1.1 convolution_bitcast_fusion.1
  166.0 1.9 copy.152
  167.9 18.4 %all-gather.8.cloned.1.call-done = bf16[4096,512]{1,0:T(8,128)(2,1)} async-done(((bf16[512,512]{1,0:T(8,128)(2,1)}), bf16[4096,512]{1,0:T(8,128)(2,1)}) %all-gather.8.cloned.1.call-update) | async-done | bytes 4194320 | tf_op jit(solution)/shard_map/all_gather | solution.py:232
  186.3 1.9 copy.208
  189.2 4.2 %all-to-all-start = ((bf16[96,8,512]{2,0,1:T(8,128)(2,1)}), bf16[96,8,512]{2,0,1:T(8,128)(2,1)}, u32[]{:S(2)}, u32[]{:S(2)}) async-start(bf16[96,8,512]{2,0,1:T(8,128)(2,1)} %bitcast.168), calls=%async_computation | async-start | bytes 1572864 | tf_op jit(solution)/shard_map/all_to_all | solution.py:209
  193.7 4.7 %fusion.64 = f32[384,512]{0,1:T(8,128)S(1)} fusion(bf16[384,4096]{1,0:T(8,128)(2,1)S(1)} %copy-done, bf16[4096,512]{1,0:T(8,128)(2,1)} %all-gather.8.cloned.1.call-done), kind=kOutput, calls=%fused_computation.117 | convolution fusion | flops 1610612736 | bytes 8126464 | tf_op jit(solution)/shard_map/dot_general | solution.py:235
  199.0 1.2 subtract_convert_fusion.1
  200.3 1.2 fusion.11
  201.5 1.2 select_reduce_fusion
  202.7 2.1 bitcast_convert_fusion
  205.4 4.6 %fusion.1 = bf16[4,384,768]{1,2,0:T(8,128)(2,1)S(1)} fusion(f32[768,384,4]{1,0,2:T(8,128)} %copy-done.3, f32[4,384]{1,0:T(4,128)S(1)} %multiply_reduce_fusion, f32[4,384]{1,0:T(4,128)S(1)} %log_add_fusion, pred[384,768]{0,1:T(8,128)(4,1)S(1)} %fusion.16, bf16[768,128]{1,0:T(8,128)(2,1)} %copy-done.22, bf16[384,8,128]{0,2,1:T(8,128)(2,1)} %bitcast.165), kind=kOutput, calls=%fused_computation.3 | convolution fusion | flops 311427072 | bytes 7974912 | tf_op jit(solution)/shard_map/rhd,kd->hrk/dot_general | solution.py:90
  210.0 1.6 convolution_bitcast_fusion.4
  211.6 2.2 convolution_bitcast_fusion.3
  213.8 11.6 %all-to-all-done = bf16[96,8,512]{2,0,1:T(8,128)(2,1)} async-done(((bf16[96,8,512]{2,0,1:T(8,128)(2,1)}), bf16[96,8,512]{2,0,1:T(8,128)(2,1)}, u32[]{:S(2)}, u32[]{:S(2)}) %all-to-all-start) | async-done | bytes 786464 | tf_op jit(solution)/shard_map/all_to_all | solution.py:209
  225.4 35.6 %all-gather.10.cloned.1.call-done = bf16[3072,512]{0,1:T(8,128)(2,1)} async-done(((bf16[384,512]{0,1:T(8,128)(2,1)}), bf16[3072,512]{0,1:T(8,128)(2,1)}) %all-gather.10.cloned.1.call-update) | async-done | bytes 3145744 | tf_op jit(solution)/shard_map/all_gather | solution.py:234
  261.0 5.0 %fusion.15 = f32[768,128]{1,0:T(8,128)} fusion(f32[768,128]{1,0:T(8,128)} %convolution_bitcast_fusion.3, bf16[384,8,128]{0,2,1:T(8,128)(2,1)} %bitcast.166, f32[768,384,4]{1,0,2:T(8,128)} %copy-done.2, f32[4,384]{1,0:T(4,128)S(1)} %log_add_fusion.1, pred[384,768]{0,1:T(8,128)(4,1)S(1)} %fusion.16), kind=kOutput, calls=%fused_computation.34 | convolution fusion | flops 307986432 | bytes 6199296 | tf_op jit(solution)/shard_map/hrk,rhd->kd/dot_general | solution.py:94
  266.1 2.0 copy.162
  268.1 3.4 fusion.14
  271.6 1.0 convolution_bitcast_fusion
  272.7 1.3 add_convert_fusion.1
  274.4 3.1 reduce-scatter.5.cloned.1.call-done
  278.6 14.8 %reduce-scatter.3.cloned.1.call-done = f32[384,128]{0,1:T(8,128)} async-done(((f32[768,128]{0,1:T(8,128)}), f32[384,128]{0,1:T(8,128)}) %reduce-scatter.3.cloned.1.call-update) | async-done | bytes 196624 | tf_op jit(solution)/shard_map/reduce_scatter | solution.py:260
  293.4 1.4 fusion.42
  295.7 3.1 broadcast_in_dim.77
  298.9 4.6 %all-to-all-start.2 = ((bf16[4,768,512]{2,1,0:T(8,128)(2,1)}), bf16[4,768,512]{2,1,0:T(8,128)(2,1)}, u32[]{:S(2)}, u32[]{:S(2)}) async-start(bf16[4,768,512]{2,1,0:T(8,128)(2,1)} %broadcast_in_dim.77), calls=%async_computation.4 | async-start | bytes 6291456 | tf_op jit(solution)/shard_map/all_to_all | solution.py:248
  303.5 5.1 %fusion.17 = f32[384,4096]{1,0:T(8,128)S(1)} fusion(bf16[4096,768]{1,0:T(8,128)(2,1)} %all-gather.6.cloned.1.call-done, bf16[384,128]{0,1:T(8,128)(2,1)S(1)} %copy.163, bf16[384,128]{0,1:T(8,128)(2,1)S(1)} %maximum_bitcast_fusion, bf16[384,512]{0,1:T(8,128)(2,1)S(1)} %bitcast.172), kind=kOutput, calls=%fused_computation.54 | convolution fusion | flops 2417688576 | bytes 13172736 | tf_op jit(solution)/shard_map/dot_general | solution.py:266
  308.6 1.8 add_convert_fusion
  310.5 2.0 copy.218
  312.5 28.0 %all-to-all-done.2 = bf16[4,768,512]{2,1,0:T(8,128)(2,1)} async-done(((bf16[4,768,512]{2,1,0:T(8,128)(2,1)}), bf16[4,768,512]{2,1,0:T(8,128)(2,1)}, u32[]{:S(2)}, u32[]{:S(2)}) %all-to-all-start.2) | async-done | bytes 3145760 | tf_op jit(solution)/shard_map/all_to_all | solution.py:248
  340.5 4.0 all-to-all-start.1
  344.5 2.0 pad_maximum_fusion.2
  346.5 2.3 copy.171
  348.8 2.4 copy.168
  351.1 1.7 copy-done.17
  352.9 2.8 fusion.66
  355.7 25.7 %all-to-all-done.1 = bf16[384,4,1024]{2,0,1:T(8,128)(2,1)S(1)} async-done(((bf16[384,4,1024]{2,0,1:T(8,128)(2,1)}), bf16[384,4,1024]{2,0,1:T(8,128)(2,1)S(1)}, u32[]{:S(2)}, u32[]{:S(2)}) %all-to-all-start.1) | async-done | bytes 3145760 | tf_op jit(solution)/shard_map/all_to_all | solution.py:292
  381.4 1.7 reduce_sum.42
  383.1 5.9 %fusion.65 = f32[512,768]{1,0:T(8,128)S(1)} fusion(bf16[3072,512]{1,0:T(8,128)(2,1)} %bitcast.162, bf16[3072,768]{0,1:T(8,128)(2,1)} %all-gather.12.cloned.1.call-done), kind=kOutput, calls=%fused_computation.118 | convolution fusion | flops 2415919104 | bytes 9437184 | tf_op jit(solution)/shard_map/dot_general | solution.py:298
  389.0 1.1 slice.109
  391.0 2.7 copy.209
  393.7 3.1 pad_maximum_fusion
  396.7 2.9 copy.172
  (98 shorter events, 10.6 us)
Async XLA Ops:
  7.2 114.7 %copy-start = (bf16[384,4096]{1,0:T(8,128)(2,1)S(1)}, bf16[384,4096]{1,0:T(8,128)(2,1)}, u32[]{:S(2)}) copy-start(bf16[384,4096]{1,0:T(8,128)(2,1)} %param.6) | copy-start | bytes 9437188
  7.2 107.3 %copy-start.25 = (s32[1,8]{1,0:T(1,128)S(1)}, s32[1,8]{1,0:T(1,128)}, u32[]{:S(2)}) copy-start(s32[1,8]{1,0:T(1,128)} %param.10) | copy-start | bytes 100
  7.2 105.3 %all-gather.6.cloned.1.call-start = ((), (), s32[]{:S(2)}) async-start(), calls=%async_computation.5 | async-start | bytes 7077888 | tf_op jit(solution)/shard_map/all_gather | solution.py:203
  10.4 175.9 %all-gather.8.cloned.1.call-start = ((), (), s32[]{:S(2)}) async-start(), calls=%async_computation.6 | async-start | bytes 4718592 | tf_op jit(solution)/shard_map/all_gather | solution.py:232
  114.4 146.6 %all-gather.10.cloned.1.call-start = ((), (), s32[]{:S(2)}) async-start(), calls=%async_computation.7 | async-start | bytes 3538944 | tf_op jit(solution)/shard_map/all_gather | solution.py:234
  139.6 10.4 %copy-start.5 = (bf16[768,1,128]{0,2,1:T(8,128)(2,1)}, bf16[768,1,128]{0,2,1:T(8,128)(2,1)S(1)}, u32[]{:S(2)}) copy-start(bf16[768,1,128]{0,2,1:T(8,128)(2,1)S(1)} %all-gather) | copy-start | bytes 589828
  145.5 5.8 %copy-start.22 = (bf16[768,128]{1,0:T(8,128)(2,1)}, bf16[768,128]{1,0:T(8,128)(2,1)S(1)}, u32[]{:S(2)}) copy-start(bf16[768,128]{1,0:T(8,128)(2,1)S(1)} %all_gather.19) | copy-start | bytes 589828
  148.8 1.3 copy-start.13
  148.8 1.3 copy-start.15
  150.1 3.6 copy-start.2
  157.5 6.0 %copy-start.6 = (bf16[768,1,128]{0,2,1:T(8,128)(2,1)S(1)}, bf16[768,1,128]{0,2,1:T(8,128)(2,1)}, u32[]{:S(2)}) copy-start(bf16[768,1,128]{0,2,1:T(8,128)(2,1)} %copy-done.5) | copy-start | bytes 589828
  157.5 7.1 %copy-start.9 = (f32[384,64]{1,0:T(8,128)S(1)}, f32[384,64]{1,0:T(8,128)}, u32[]{:S(2)}) copy-start(f32[384,64]{1,0:T(8,128)} %get-tuple-element.73) | copy-start | bytes 294916
  157.5 7.1 %copy-start.11 = (f32[384,64]{1,0:T(8,128)S(1)}, f32[384,64]{1,0:T(8,128)}, u32[]{:S(2)}) copy-start(f32[384,64]{1,0:T(8,128)} %get-tuple-element.74) | copy-start | bytes 294916
  162.1 1.5 copy-start.4
  189.2 36.2 %all-to-all-start = ((bf16[96,8,512]{2,0,1:T(8,128)(2,1)}), bf16[96,8,512]{2,0,1:T(8,128)(2,1)}, u32[]{:S(2)}, u32[]{:S(2)}) async-start(bf16[96,8,512]{2,0,1:T(8,128)(2,1)} %bitcast.168), calls=%async_computation | async-start | bytes 1572864 | tf_op jit(solution)/shard_map/all_to_all | solution.py:209
  193.5 84.1 %reduce-scatter.5.cloned.1.call-start = ((), (), s32[]{:S(2)}) async-start(), calls=%async_computation.9 | async-start | bytes 589824 | tf_op jit(solution)/shard_map/reduce_scatter | solution.py:261
  198.4 1.9 copy-start.7
  200.3 2.4 copy-start.23
  201.5 3.3 copy-start.3
  202.7 2.4 copy-start.20
  205.1 6.5 %slice-start = ((s8[4718592]{0:T(1024)(128)(4,1)}), s8[4194304]{0:T(1024)(128)(4,1)S(1)}, s32[]{:S(2)}) async-start(s8[4718592]{0:T(1024)(128)(4,1)} %bitcast.155), calls=%async_computation.11 | async-start | bytes 8388608
  205.4 6.2 %slice-start.1 = ((s8[4718592]{0:T(1024)(128)(4,1)}), s8[524288]{0:T(1024)(128)(4,1)S(1)}, s32[]{:S(2)}) async-start(s8[4718592]{0:T(1024)(128)(4,1)} %bitcast.155), calls=%async_computation.12 | async-start | bytes 1048576
  210.0 1.6 copy-start.18
  261.0 7.1 %copy-start.14 = (bf16[384,4,64]{2,0,1:T(8,128)(2,1)S(1)}, bf16[384,4,64]{2,0,1:T(8,128)(2,1)}, u32[]{:S(2)}) copy-start(bf16[384,4,64]{2,0,1:T(8,128)(2,1)} %copy-done.13) | copy-start | bytes 589828
  261.0 7.1 %copy-start.16 = (bf16[384,4,64]{2,0,1:T(8,128)(2,1)S(1)}, bf16[384,4,64]{2,0,1:T(8,128)(2,1)}, u32[]{:S(2)}) copy-start(bf16[384,4,64]{2,0,1:T(8,128)(2,1)} %copy-done.15) | copy-start | bytes 589828
  266.0 5.6 %copy-start.8 = (bf16[768,1,128]{0,2,1:T(8,128)(2,1)S(1)}, bf16[768,1,128]{0,2,1:T(8,128)(2,1)}, u32[]{:S(2)}) copy-start(bf16[768,1,128]{0,2,1:T(8,128)(2,1)} %copy-done.5) | copy-start | bytes 589828
  266.0 6.6 %copy-start.10 = (f32[384,64]{1,0:T(8,128)S(1)}, f32[384,64]{1,0:T(8,128)}, u32[]{:S(2)}) copy-start(f32[384,64]{1,0:T(8,128)} %get-tuple-element.73) | copy-start | bytes 294916
  266.1 27.4 %reduce-scatter.3.cloned.1.call-start = ((), (), s32[]{:S(2)}) async-start(), calls=%async_computation.8 | async-start | bytes 589824 | tf_op jit(solution)/shard_map/reduce_scatter | solution.py:260
  271.6 111.5 %all-gather.12.cloned.1.call-start = ((), (), s32[]{:S(2)}) async-start(), calls=%async_computation.10 | async-start | bytes 5308416 | tf_op jit(solution)/shard_map/all_gather | solution.py:297
  295.7 7.8 %copy-start.19 = (bf16[384,4,128]{0,2,1:T(8,128)(2,1)S(1)}, bf16[384,4,128]{0,2,1:T(8,128)(2,1)}, u32[]{:S(2)}) copy-start(bf16[384,4,128]{0,2,1:T(8,128)(2,1)} %copy.152) | copy-start | bytes 1179652
  298.9 41.6 %all-to-all-start.2 = ((bf16[4,768,512]{2,1,0:T(8,128)(2,1)}), bf16[4,768,512]{2,1,0:T(8,128)(2,1)}, u32[]{:S(2)}, u32[]{:S(2)}) async-start(bf16[4,768,512]{2,1,0:T(8,128)(2,1)} %broadcast_in_dim.77), calls=%async_computation.4 | async-start | bytes 6291456 | tf_op jit(solution)/shard_map/all_to_all | solution.py:248
  303.5 5.1 %copy-start.12 = (bf16[4096,512]{1,0:T(8,128)(2,1)S(1)}, bf16[4096,512]{1,0:T(8,128)(2,1)}, u32[]{:S(2)}) copy-start(bf16[4096,512]{1,0:T(8,128)(2,1)} %all-gather.8.cloned.1.call-done) | copy-start | bytes 12582916
  312.5 32.0 %copy-start.21 = (bf16[128,4,384]{2,0,1:T(8,128)(2,1)S(1)}, bf16[128,4,384]{2,0,1:T(8,128)(2,1)}, u32[]{:S(2)}) copy-start(bf16[128,4,384]{2,0,1:T(8,128)(2,1)} %get-tuple-element.78) | copy-start | bytes 1179652
  340.5 40.8 %all-to-all-start.1 = ((bf16[384,4,1024]{2,0,1:T(8,128)(2,1)}), bf16[384,4,1024]{2,0,1:T(8,128)(2,1)S(1)}, u32[]{:S(2)}, u32[]{:S(2)}) async-start(bf16[384,4,1024]{2,0,1:T(8,128)(2,1)} %bitcast.158), calls=%async_computation.3 | async-start | bytes 6291456 | tf_op jit(solution)/shard_map/all_to_all | solution.py:292
  348.8 4.1 %copy-start.24 = (bf16[3072,512]{0,1:T(8,128)(2,1)S(1)}, bf16[3072,512]{0,1:T(8,128)(2,1)}, u32[]{:S(2)}) copy-start(bf16[3072,512]{0,1:T(8,128)(2,1)} %all-gather.10.cloned.1.call-done) | copy-start | bytes 9437188
  351.1 1.7 copy-start.17
  391.0 8.6 %copy-start.1 = (bf16[384,4096]{1,0:T(8,128)(2,1)S(1)}, bf16[384,4096]{1,0:T(8,128)(2,1)}, u32[]{:S(2)}) copy-start(bf16[384,4096]{1,0:T(8,128)(2,1)} %param.6) | copy-start | bytes 9437188
Sparse Core Ops, SparseCore 0:
  10.8 101.7 all-gather.5
  114.7 71.5 all-gather.7
  188.4 72.5 all-gather.9
  266.2 11.2 reduce-scatter.4
  280.3 13.1 reduce-scatter.2
  295.9 80.9 all-gather.11

commit v7 on v4

--- a/solution.py
+++ b/solution.py
@@ -199,24 +199,23 @@
     rows_axes = ("dp", "ctx")
     group_count = lax.axis_size(rows_axes)
     head_groups = lax.axis_size("head")
-    if num_rows % head_groups == 0:
+    local_a = jnp.concatenate([w_query[:, :first_cols], w_key, w_value], 1)
+    full_a = lax.all_gather(local_a, rows_axes, axis=0, tiled=True)
+    split_rows = num_rows % head_groups == 0
+    if split_rows:
         quarter = num_rows // head_groups
         own_rows = lax.dynamic_slice_in_dim(hidden_in, lax.axis_index("head") * quarter, quarter, 0)
         cols_part = lax.all_to_all(own_rows, rows_axes, 1, 0, tiled=True)
-    else:
-        cols_part = lax.all_to_all(hidden_in, rows_axes, 1, 0, tiled=True)
-    local_a = jnp.concatenate([w_query[:, :first_cols], w_key, w_value], 1)
-    full_a = lax.all_gather(local_a, rows_axes, axis=0, tiled=True)
-    cols_part, full_a, w_query = lax.optimization_barrier((cols_part, full_a, w_query))
-    if num_rows % head_groups == 0:
-        cols_all = lax.all_gather(cols_part, "head", axis=0, tiled=False)
+        spread = jnp.broadcast_to(cols_part[None], (head_groups,) + cols_part.shape)
+        cols_all = lax.all_to_all(spread, "head", 0, 0, tiled=False)
         hidden_cols = (
             cols_all.reshape(head_groups, group_count, quarter, -1)
             .transpose(1, 0, 2, 3)
             .reshape(group_count * num_rows, -1)
         )
     else:
-        hidden_cols = cols_part
+        hidden_cols = lax.all_to_all(hidden_in, rows_axes, 1, 0, tiled=True)
+    full_a, w_query, hidden_cols = lax.optimization_barrier((full_a, w_query, hidden_cols))
     proj_a = jnp.dot(hidden_in, full_a, preferred_element_type=jnp.float32)
     query_a = rotate(
         proj_a[:, :first_cols].reshape(num_rows, first_heads, 128), cosine, sine_table
@@ -247,9 +246,7 @@
         out_b, grad_qb, part_kb, part_vb = attend(
             query_b, *shared, dout_rows[:, first_heads:], *masks
         )
-        early_all, hidden_cols, part_kb, part_vb = lax.optimization_barrier(
-            (early_all, hidden_cols, part_kb, part_vb)
-        )
+        early_all, part_kb, part_vb = lax.optimization_barrier((early_all, part_kb, part_vb))
         part_k, part_v = part_k + part_kb, part_v + part_vb
         out_parts.append(out_b)
         d_query_b = unrotate(grad_qb, cosine, sine_table).astype(jnp.bfloat16).reshape(num_rows, -1)
@@ -281,9 +278,10 @@
         )
     input_cols = input_part.shape[1] // head_groups
     input_split = lax.all_to_all(
-        input_part.reshape(num_rows, head_groups, input_cols), "head", 1, 1, tiled=False
-    )
-    grad_input = jnp.sum(input_split, axis=1).astype(jnp.bfloat16)
+        input_part.astype(jnp.bfloat16).reshape(num_rows, head_groups, input_cols),
+        "head", 1, 1, tiled=False,
+    )
+    grad_input = jnp.sum(input_split.astype(jnp.float32), axis=1).astype(jnp.bfloat16)
     late_all = lax.all_gather(late_proj, rows_axes, axis=0, tiled=True)
     late_sum = lax.dot_general(
         hidden_cols, late_all, (((0,), (0,)), ((), ())), preferred_element_type=jnp.float32

time: 446 us -> 407 us (0.913)
  waiting for transfers between devices: 237 us -> 162 us
  blocking collectives: 56 us -> 95.4 us
    all_gather x1, waiting for transfers between devices: 69.1 us -> 27.4 us  [local(): full_a = lax.all_gather(local_a, rows_axes, axis=0, tiled=True)]
    all_to_all x0 -> x1, blocking collectives: none -> 39.5 us  [local(): cols_all = lax.all_to_all(spread, 'head', 0, 0, tiled=False)]
    all_to_all x1, waiting for transfers between devices: 61.7 us -> 27 us  [local(): lax.all_to_all(input_part.astype(jnp.bfloat16).reshape(num_rows, head_gro...]
    all_gather x1, waiting for transfers between devices: 0.01 us -> 29.9 us  [local(): late_all = lax.all_gather(late_proj, rows_axes, axis=0, tiled=True)]
    all_gather x1 -> x0, waiting for transfers between devices: 26.2 us -> none  [local(): cols_all = lax.all_gather(cols_part, 'head', axis=0, tiled=False)]
    reshape x2 -> x1, local copies, waits for them, and re-layouts: 7.52 us -> 2.05 us  [local(): input_part.astype(jnp.bfloat16).reshape(num_rows, head_groups, input_cols)]
    unnamed x67 -> x61, local copies, waits for them, and re-layouts: 24.1 us -> 23.9 us
  transfers between devices with their start and end apart: 8 -> 7, of which waited for: 7 -> 7; matrix products, arithmetic and copies ran while one was open for 22% -> 23% of each run, Pallas kernels for 0% -> 0%
where the time goes in v7:
time: 407 us; the launch traced here: 402 us
  waiting for transfers between devices  162 us (40%)
  blocking collectives  95.4 us (23%)
  matrix products  59.7 us (15%)
  local copies, waits for them, and re-layouts  39.8 us (10%)
  other arithmetic  24.8 us (6%)
  between operations  14.9 us (4%)
  starting transfers between devices  4.71 us (1%)
    all_to_all x1, blocking collectives, local(): cols_part = lax.all_to_all(own_rows, rows_axes, 1, 0, tiled=True)  44.8 us
    all_gather x1, waiting for transfers between devices, local(): early_all = lax.all_gather(d_query_a, rows_axes, axis=0, tiled=True)  41.2 us
    all_to_all x1, blocking collectives, local(): cols_all = lax.all_to_all(spread, 'head', 0, 0, tiled=False)  39.5 us
    all_gather x1, waiting for transfers between devices, local(): late_all = lax.all_gather(late_proj, rows_axes, axis=0, tiled=True)  29.9 us
    all_gather x1, waiting for transfers between devices, local(): full_a = lax.all_gather(local_a, rows_axes, axis=0, tiled=True)  27.4 us
    all_to_all x1, waiting for transfers between devices, local(): lax.all_to_all(input_part.astype(jnp.bfloat16).reshape(num_rows, head_gro...  27 us
    unnamed x61, local copies, waits for them, and re-layouts  23.9 us
    all_gather x1, waiting for transfers between devices, local(): full_b = lax.all_gather(w_rest, rows_axes, axis=0, tiled=True)  19.5 us
  transfers between devices with their start and end apart: 7, of which 7 were waited for; matrix products, arithmetic and copies ran while one was open for 23% of the time, Pallas kernels for 0%

profile of v7, /device:TPU:0, one launch (start us, length us, event | category | flops | bytes accessed | tf_op | source)
XLA Modules:
  0.0 401.6 jit_solution(7636800604412377836)
XLA Ops:
  7.2 1.2 slice.70
  8.5 1.9 pad_maximum_fusion.1
  10.6 44.8 %all_to_all.26 = bf16[96,8,512]{2,0,1:T(8,128)(2,1)S(1)} all-to-all(bf16[96,8,512]{2,0,1:T(8,128)(2,1)S(1)} %bitcast.178), channel_id=1, replica_groups=mesh['dp'=4,'ctx'=2,'head'=4] {'dp','ctx'}, dimensions={1} | all-to-all | bytes 1572864 | tf_op jit(solution)/shard_map/all_to_all | solution.py:208
  55.6 39.5 %all_to_all.27 = bf16[4,768,512]{2,1,0:T(8,128)(2,1)S(1)} all-to-all(bf16[4,768,512]{2,1,0:T(8,128)(2,1)S(1)} %broadcast_in_dim.76), channel_id=1, replica_groups=mesh['dp'=4,'ctx'=2,'head'=4] {'head'}, dimensions={0} | all-to-all | bytes 6291456 | tf_op jit(solution)/shard_map/all_to_all | solution.py:210
  95.1 2.0 copy.114
  97.1 27.4 %all-gather.6.cloned.1.call-done = bf16[4096,768]{1,0:T(8,128)(2,1)} async-done(((bf16[512,768]{1,0:T(8,128)(2,1)}), bf16[4096,768]{1,0:T(8,128)(2,1)}) %all-gather.6.cloned.1.call-update) | async-done | bytes 6291472 | tf_op jit(solution)/shard_map/all_gather | solution.py:203
  124.6 1.9 slice.81
  126.7 2.3 copy.119
  129.0 2.0 fusion.60
  131.0 0.9 copy.172
  132.4 1.5 multiply_cosine_fusion
  133.9 5.6 %convolution_bitcast_fusion = f32[384,768]{0,1:T(8,128)S(1)} fusion(bf16[4096,768]{1,0:T(8,128)(2,1)} %all-gather.6.cloned.1.call-done, bf16[384,4096]{1,0:T(8,128)(2,1)S(1)} %copy-done), kind=kOutput, calls=%fused_computation.25 | convolution fusion | flops 2415919104 | bytes 10616832 | tf_op jit(solution)/shard_map/dot_general | solution.py:219
  139.6 1.1 fusion.62
  140.8 2.2 copy.170
  142.9 2.1 copy.171
  145.1 0.9 slice_bitcast_fusion
  146.5 5.3 %all-gather = bf16[768,1,128]{0,2,1:T(8,128)(2,1)S(1)} all-gather(bf16[384,1,128]{0,2,1:T(8,128)(2,1)S(1)} %pad_maximum_fusion.12), channel_id=2, replica_groups=mesh['dp'=4,'ctx'=2,'head'=4] {'ctx'}, dimensions={0}, use_global_device_ids=true | all-gather | bytes 294912 | tf_op jit(solution)/shard_map/all_gather | solution.py:228
  151.8 5.8 %all_gather.19 = bf16[768,128]{0,1:T(8,128)(2,1)S(1)} all-gather(bf16[384,128]{0,1:T(8,128)(2,1)S(1)} %slice.138), channel_id=1, replica_groups=mesh['dp'=4,'ctx'=2,'head'=4] {'ctx'}, dimensions={0}, use_global_device_ids=true | all-gather | bytes 294912 | tf_op jit(solution)/shard_map/all_gather | solution.py:229
  157.6 2.1 subtract_convert_fusion.3
  159.8 1.2 fusion.10
  161.0 1.2 select_reduce_fusion.1
  162.2 2.5 bitcast_convert_fusion.1
  164.7 2.3 copy.150
  167.0 1.5 multiply_reduce_fusion.1
  168.5 4.5 %fusion.6 = bf16[4,384,768]{1,2,0:T(8,128)(2,1)S(1)} fusion(f32[768,384,4]{1,0,2:T(8,128)} %copy-done.2, f32[4,384]{1,0:T(4,128)S(1)} %multiply_reduce_fusion.1, f32[4,384]{1,0:T(4,128)S(1)} %log_add_fusion.1, pred[384,768]{0,1:T(8,128)(4,1)S(1)} %fusion.16, bf16[768,128]{0,1:T(8,128)(2,1)} %copy-done.19, bf16[384,8,128]{0,2,1:T(8,128)(2,1)} %bitcast.171), kind=kOutput, calls=%fused_computation.11 | convolution fusion | flops 311427072 | bytes 7974912 | tf_op jit(solution)/shard_map/rhd,kd->hrk/dot_general | solution.py:90
  173.0 1.4 copy-done.4
  174.4 1.1 convolution_bitcast_fusion.2
  175.9 1.0 pad_maximum_fusion.9
  176.9 1.9 copy.124
  178.8 19.5 %all-gather.8.cloned.1.call-done = bf16[4096,512]{1,0:T(8,128)(2,1)} async-done(((bf16[512,512]{1,0:T(8,128)(2,1)}), bf16[4096,512]{1,0:T(8,128)(2,1)}) %all-gather.8.cloned.1.call-update) | async-done | bytes 4194320 | tf_op jit(solution)/shard_map/all_gather | solution.py:239
  198.5 1.9 copy.175
  200.5 4.6 %fusion.63 = f32[512,384]{1,0:T(8,128)S(1)} fusion(bf16[4096,512]{1,0:T(8,128)(2,1)} %all-gather.8.cloned.1.call-done, bf16[384,4096]{1,0:T(8,128)(2,1)S(1)} %copy-done), kind=kOutput, calls=%fused_computation.118 | convolution fusion | flops 1610612736 | bytes 8126464 | tf_op jit(solution)/shard_map/dot_general | solution.py:242
  205.6 1.3 subtract_convert_fusion.1
  206.9 1.2 fusion.11
  208.2 1.2 select_reduce_fusion
  209.4 2.1 bitcast_convert_fusion
  212.1 4.6 %fusion.1 = bf16[4,384,768]{1,2,0:T(8,128)(2,1)S(1)} fusion(f32[768,384,4]{1,0,2:T(8,128)} %copy-done.3, f32[4,384]{1,0:T(4,128)S(1)} %multiply_reduce_fusion, f32[4,384]{1,0:T(4,128)S(1)} %log_add_fusion, pred[384,768]{0,1:T(8,128)(4,1)S(1)} %fusion.16, bf16[768,128]{0,1:T(8,128)(2,1)} %copy-done.19, bf16[384,8,128]{0,2,1:T(8,128)(2,1)} %bitcast.172), kind=kOutput, calls=%fused_computation.3 | convolution fusion | flops 311427072 | bytes 7974912 | tf_op jit(solution)/shard_map/rhd,kd->hrk/dot_general | solution.py:90
  216.7 1.6 convolution_bitcast_fusion.5
  218.3 2.1 convolution_bitcast_fusion.4
  220.5 41.2 %all-gather.10.cloned.1.call-done = bf16[3072,512]{0,1:T(8,128)(2,1)} async-done(((bf16[384,512]{0,1:T(8,128)(2,1)}), bf16[3072,512]{0,1:T(8,128)(2,1)}) %all-gather.10.cloned.1.call-update) | async-done | bytes 3145744 | tf_op jit(solution)/shard_map/all_gather | solution.py:241
  261.7 1.9 copy.132
  263.6 3.4 fusion.14
  267.4 4.7 %fusion.15 = f32[768,128]{1,0:T(8,128)} fusion(f32[768,128]{1,0:T(8,128)} %convolution_bitcast_fusion.4, bf16[384,8,128]{0,2,1:T(8,128)(2,1)} %bitcast.173, f32[768,384,4]{1,0,2:T(8,128)} %copy-done.2, f32[4,384]{1,0:T(4,128)S(1)} %log_add_fusion.1, pred[384,768]{0,1:T(8,128)(4,1)S(1)} %fusion.16), kind=kOutput, calls=%fused_computation.35 | convolution fusion | flops 307986432 | bytes 6199296 | tf_op jit(solution)/shard_map/hrk,rhd->kd/dot_general | solution.py:94
  272.2 2.0 convolution_bitcast_fusion.1
  274.1 1.3 add_convert_fusion.1
  275.9 2.6 reduce-scatter.3.cloned.1.call-done
  278.6 1.4 fusion.42
  279.9 14.5 %reduce-scatter.5.cloned.1.call-done = f32[384,128]{1,0:T(8,128)} async-done(((f32[768,128]{1,0:T(8,128)}), f32[384,128]{1,0:T(8,128)}) %reduce-scatter.5.cloned.1.call-update) | async-done | bytes 196624 | tf_op jit(solution)/shard_map/reduce_scatter | solution.py:257
  294.5 0.9 convert_element_type.76
  296.5 5.0 %fusion.17 = f32[384,4096]{1,0:T(8,128)S(1)} fusion(bf16[4096,768]{1,0:T(8,128)(2,1)} %all-gather.6.cloned.1.call-done, bf16[384,128]{0,1:T(8,128)(2,1)S(1)} %copy.133, bf16[384,128]{0,1:T(8,128)(2,1)S(1)} %maximum_bitcast_fusion, bf16[384,512]{0,1:T(8,128)(2,1)} %bitcast.181), kind=kOutput, calls=%fused_computation.55 | convolution fusion | flops 2417688576 | bytes 13172736 | tf_op jit(solution)/shard_map/dot_general | solution.py:262
  301.5 1.9 add_convert_fusion
  303.3 2.0 copy.181
  305.4 4.1 %all-to-all-start.2 = ((bf16[384,4,1024]{2,0,1:T(8,128)(2,1)}), bf16[384,4,1024]{2,0,1:T(8,128)(2,1)S(1)}, u32[]{:S(2)}, u32[]{:S(2)}) async-start(bf16[384,4,1024]{2,0,1:T(8,128)(2,1)} %bitcast.164), calls=%async_computation.4 | async-start | bytes 6291456 | tf_op jit(solution)/shard_map/all_to_all | solution.py:280
  309.5 2.0 pad_maximum_fusion.2
  311.5 2.3 copy.140
  313.8 5.6 %fusion.65 = f32[512,512]{0,1:T(8,128)} fusion(bf16[3072,512]{0,1:T(8,128)(2,1)} %all-gather.10.cloned.1.call-done, bf16[3072,512]{1,0:T(8,128)(2,1)} %bitcast.168), kind=kOutput, calls=%fused_computation.120 | convolution fusion | flops 1610612736 | bytes 7340032 | tf_op jit(solution)/shard_map/dot_general | solution.py:270
  319.4 27.0 %all-to-all-done.2 = bf16[384,4,1024]{2,0,1:T(8,128)(2,1)S(1)} async-done(((bf16[384,4,1024]{2,0,1:T(8,128)(2,1)}), bf16[384,4,1024]{2,0,1:T(8,128)(2,1)S(1)}, u32[]{:S(2)}, u32[]{:S(2)}) %all-to-all-start.2) | async-done | bytes 3145760 | tf_op jit(solution)/shard_map/all_to_all | solution.py:280
  346.4 1.7 reduce_sum.42
  348.1 29.9 %all-gather.12.cloned.1.call-done = bf16[3072,768]{0,1:T(8,128)(2,1)} async-done(((bf16[384,768]{0,1:T(8,128)(2,1)}), bf16[3072,768]{0,1:T(8,128)(2,1)}) %all-gather.12.cloned.1.call-update) | async-done | bytes 4718608 | tf_op jit(solution)/shard_map/all_gather | solution.py:285
  378.0 5.9 %fusion.64 = f32[512,768]{1,0:T(8,128)S(1)} fusion(bf16[3072,512]{1,0:T(8,128)(2,1)} %bitcast.169, bf16[3072,768]{0,1:T(8,128)(2,1)} %all-gather.12.cloned.1.call-done), kind=kOutput, calls=%fused_computation.119 | convolution fusion | flops 2415919104 | bytes 9437184 | tf_op jit(solution)/shard_map/dot_general | solution.py:286
  383.9 1.1 slice.109
  385.9 2.7 copy.176
  388.6 3.1 pad_maximum_fusion
  391.6 2.9 copy.141
  (88 shorter events, 6.2 us)
Async XLA Ops:
  7.2 3.3 copy-start
  7.2 117.4 %all-gather.6.cloned.1.call-start = ((), (), s32[]{:S(2)}) async-start(), calls=%async_computation.5 | async-start | bytes 7077888 | tf_op jit(solution)/shard_map/all_gather | solution.py:203
  10.4 187.9 %all-gather.8.cloned.1.call-start = ((), (), s32[]{:S(2)}) async-start(), calls=%async_computation.6 | async-start | bytes 4718592 | tf_op jit(solution)/shard_map/all_gather | solution.py:239
  95.1 31.4 %copy-start.21 = (s32[1,8]{1,0:T(1,128)S(1)}, s32[1,8]{1,0:T(1,128)}, u32[]{:S(2)}) copy-start(s32[1,8]{1,0:T(1,128)} %param.10) | copy-start | bytes 100
  126.5 135.2 %all-gather.10.cloned.1.call-start = ((), (), s32[]{:S(2)}) async-start(), calls=%async_computation.7 | async-start | bytes 3538944 | tf_op jit(solution)/shard_map/all_gather | solution.py:241
  139.5 1.3 copy-start.17
  151.8 8.0 %copy-start.5 = (bf16[768,1,128]{0,2,1:T(8,128)(2,1)}, bf16[768,1,128]{0,2,1:T(8,128)(2,1)S(1)}, u32[]{:S(2)}) copy-start(bf16[768,1,128]{0,2,1:T(8,128)(2,1)S(1)} %all-gather) | copy-start | bytes 589828
  157.6 4.6 %copy-start.19 = (bf16[768,128]{0,1:T(8,128)(2,1)}, bf16[768,128]{0,1:T(8,128)(2,1)S(1)}, u32[]{:S(2)}) copy-start(bf16[768,128]{0,1:T(8,128)(2,1)S(1)} %all_gather.19) | copy-start | bytes 589828
  159.7 1.3 copy-start.11
  159.7 1.3 copy-start.13
  161.0 3.7 copy-start.2
  168.5 5.9 %copy-start.6 = (bf16[768,1,128]{0,2,1:T(8,128)(2,1)S(1)}, bf16[768,1,128]{0,2,1:T(8,128)(2,1)}, u32[]{:S(2)}) copy-start(bf16[768,1,128]{0,2,1:T(8,128)(2,1)} %copy-done.5) | copy-start | bytes 589828
  168.5 7.0 %copy-start.8 = (f32[384,64]{1,0:T(8,128)S(1)}, f32[384,64]{1,0:T(8,128)}, u32[]{:S(2)}) copy-start(f32[384,64]{1,0:T(8,128)} %get-tuple-element.66) | copy-start | bytes 294916
  168.5 7.0 %copy-start.9 = (f32[384,64]{1,0:T(8,128)S(1)}, f32[384,64]{1,0:T(8,128)}, u32[]{:S(2)}) copy-start(f32[384,64]{1,0:T(8,128)} %get-tuple-element.67) | copy-start | bytes 294916
  173.0 1.4 copy-start.4
  198.3 80.2 %reduce-scatter.3.cloned.1.call-start = ((), (), s32[]{:S(2)}) async-start(), calls=%async_computation.8 | async-start | bytes 589824 | tf_op jit(solution)/shard_map/reduce_scatter | solution.py:256
  205.0 1.9 copy-start.7
  206.9 2.4 copy-start.20
  208.2 3.4 copy-start.3
  209.4 2.4 copy-start.16
  211.8 6.5 %slice-start = ((s8[4718592]{0:T(1024)(128)(4,1)}), s8[4194304]{0:T(1024)(128)(4,1)S(1)}, s32[]{:S(2)}) async-start(s8[4718592]{0:T(1024)(128)(4,1)} %bitcast.161), calls=%async_computation.11 | async-start | bytes 8388608
  212.1 6.2 %slice-start.1 = ((s8[4718592]{0:T(1024)(128)(4,1)}), s8[524288]{0:T(1024)(128)(4,1)S(1)}, s32[]{:S(2)}) async-start(s8[4718592]{0:T(1024)(128)(4,1)} %bitcast.161), calls=%async_computation.12 | async-start | bytes 1048576
  216.7 1.6 copy-start.15
  218.3 45.3 %copy-start.12 = (bf16[384,4,64]{2,0,1:T(8,128)(2,1)S(1)}, bf16[384,4,64]{2,0,1:T(8,128)(2,1)}, u32[]{:S(2)}) copy-start(bf16[384,4,64]{2,0,1:T(8,128)(2,1)} %copy-done.11) | copy-start | bytes 589828
  218.3 45.3 %copy-start.14 = (bf16[384,4,64]{2,0,1:T(8,128)(2,1)S(1)}, bf16[384,4,64]{2,0,1:T(8,128)(2,1)}, u32[]{:S(2)}) copy-start(bf16[384,4,64]{2,0,1:T(8,128)(2,1)} %copy-done.13) | copy-start | bytes 589828
  267.1 27.4 %reduce-scatter.5.cloned.1.call-start = ((), (), s32[]{:S(2)}) async-start(), calls=%async_computation.9 | async-start | bytes 589824 | tf_op jit(solution)/shard_map/reduce_scatter | solution.py:257
  272.1 105.9 %all-gather.12.cloned.1.call-start = ((), (), s32[]{:S(2)}) async-start(), calls=%async_computation.10 | async-start | bytes 5308416 | tf_op jit(solution)/shard_map/all_gather | solution.py:285
  296.4 5.0 %copy-start.10 = (bf16[4096,512]{1,0:T(8,128)(2,1)S(1)}, bf16[4096,512]{1,0:T(8,128)(2,1)}, u32[]{:S(2)}) copy-start(bf16[4096,512]{1,0:T(8,128)(2,1)} %all-gather.8.cloned.1.call-done) | copy-start | bytes 12582916
  305.4 4.1 %copy-start.18 = (bf16[128,4,384]{2,0,1:T(8,128)(2,1)S(1)}, bf16[128,4,384]{2,0,1:T(8,128)(2,1)}, u32[]{:S(2)}) copy-start(bf16[128,4,384]{2,0,1:T(8,128)(2,1)} %get-tuple-element.71) | copy-start | bytes 1179652
  305.4 41.0 %all-to-all-start.2 = ((bf16[384,4,1024]{2,0,1:T(8,128)(2,1)}), bf16[384,4,1024]{2,0,1:T(8,128)(2,1)S(1)}, u32[]{:S(2)}, u32[]{:S(2)}) async-start(bf16[384,4,1024]{2,0,1:T(8,128)(2,1)} %bitcast.164), calls=%async_computation.4 | async-start | bytes 6291456 | tf_op jit(solution)/shard_map/all_to_all | solution.py:280
  385.9 8.6 %copy-start.1 = (bf16[384,4096]{1,0:T(8,128)(2,1)S(1)}, bf16[384,4096]{1,0:T(8,128)(2,1)}, u32[]{:S(2)}) copy-start(bf16[384,4096]{1,0:T(8,128)(2,1)} %param.6) | copy-start | bytes 9437188
Sparse Core Ops, SparseCore 0:
  10.8 113.7 all-gather.5
  126.7 71.5 all-gather.7
  200.4 61.3 all-gather.9
  267.2 11.2 reduce-scatter.2
  281.3 13.1 reduce-scatter.4
  296.9 80.9 all-gather.11

commit v8 on v7

--- a/solution.py
+++ b/solution.py
@@ -224,10 +224,18 @@
         proj_a[:, first_cols : first_cols + 128].reshape(num_rows, 1, 128), cosine, sine_table
     )[:, 0, :].astype(jnp.bfloat16)
     value_rows = proj_a[:, first_cols + 128 :].astype(jnp.bfloat16)
-    key_all, value_all = (
-        lax.all_gather(key_rows, "ctx", axis=0, tiled=True),
-        lax.all_gather(value_rows, "ctx", axis=0, tiled=True),
-    )
+    ctx_index, ctx_count = lax.axis_index("ctx"), lax.axis_size("ctx")
+    kv_rows = jnp.concatenate([key_rows, value_rows], 1)
+    if ctx_count == 2:
+        kv_other = lax.ppermute(kv_rows, "ctx", [(0, 1), (1, 0)])
+        kv_all = jnp.where(
+            ctx_index == 0,
+            jnp.concatenate([kv_rows, kv_other], 0),
+            jnp.concatenate([kv_other, kv_rows], 0),
+        )
+    else:
+        kv_all = lax.all_gather(kv_rows, "ctx", axis=0, tiled=True)
+    key_all, value_all = kv_all[:, :128], kv_all[:, 128:]
     dout_rows = attn_grad.reshape(num_rows, head_count, 128)
     shared = (key_all, value_all)
     masks = (positions, all_pos, seg_own, seg_all)
@@ -252,10 +260,14 @@
         d_query_b = unrotate(grad_qb, cosine, sine_table).astype(jnp.bfloat16).reshape(num_rows, -1)
         d_query_parts.append(d_query_b)
     attended = jnp.concatenate(out_parts, 1).reshape(num_rows, query_cols)
-    grad_k, grad_v = (
-        lax.psum_scatter(part_k, "ctx", scatter_dimension=0, tiled=True),
-        lax.psum_scatter(part_v, "ctx", scatter_dimension=0, tiled=True),
-    )
+    parts_kv = jnp.concatenate([part_k, part_v], 1)
+    if ctx_count == 2:
+        own_part = lax.dynamic_slice_in_dim(parts_kv, ctx_index * num_rows, num_rows, 0)
+        away_part = lax.dynamic_slice_in_dim(parts_kv, (1 - ctx_index) * num_rows, num_rows, 0)
+        grad_kv = own_part + lax.ppermute(away_part, "ctx", [(0, 1), (1, 0)])
+    else:
+        grad_kv = lax.psum_scatter(parts_kv, "ctx", scatter_dimension=0, tiled=True)
+    grad_k, grad_v = grad_kv[:, :128], grad_kv[:, 128:]
     d_key = unrotate(grad_k[:, None, :], cosine, sine_table)[:, 0, :].astype(jnp.bfloat16)
     d_value = grad_v.astype(jnp.bfloat16)
     d_proj_a = jnp.concatenate([d_query_a, d_key, d_value], 1)

time: 407 us -> 394 us (0.968)
  blocking collectives: 95.4 us -> 84.3 us
    reduce_scatter x2 -> x0, waiting for transfers between devices: 17.1 us -> none  [the longest x1 14.5 us: local(): lax.psum_scatter(part_v, 'ctx', scatter_dimension=0, tiled=True)]
    all_gather x2 -> x0, blocking collectives: 11.1 us -> none  [the longest x1 5.81 us: local(): lax.all_gather(value_rows, 'ctx', axis=0, tiled=True)]
    ppermute x0 -> x2, waiting for transfers between devices: none -> 8.72 us  [the longest x1 8.72 us: local(): grad_kv = own_part + lax.ppermute(away_part, 'ctx', [(0, 1), (1, 0)])]
    all_gather x1, waiting for transfers between devices: 19.5 us -> 28.1 us  [local(): full_b = lax.all_gather(w_rest, rows_axes, axis=0, tiled=True)]
    unnamed x61 -> x71, local copies, waits for them, and re-layouts: 23.9 us -> 24.4 us
  transfers between devices with their start and end apart: 7 -> 7, of which waited for: 7 -> 6; matrix products, arithmetic and copies ran while one was open for 23% -> 22% of each run, Pallas kernels for 0% -> 0%
where the time goes in v8:
time: 394 us; the launch traced here: 390 us
  waiting for transfers between devices  160 us (41%)
  blocking collectives  84.3 us (21%)
  matrix products  57.4 us (15%)
  local copies, waits for them, and re-layouts  40.3 us (10%)
  other arithmetic  26.7 us (7%)
  between operations  14.7 us (4%)
  starting transfers between devices  6.59 us (2%)
    all_to_all x1, blocking collectives, local(): cols_part = lax.all_to_all(own_rows, rows_axes, 1, 0, tiled=True)  44.8 us
    all_gather x1, waiting for transfers between devices, local(): early_all = lax.all_gather(d_query_a, rows_axes, axis=0, tiled=True)  41 us
    all_to_all x1, blocking collectives, local(): cols_all = lax.all_to_all(spread, 'head', 0, 0, tiled=False)  39.5 us
    all_gather x1, waiting for transfers between devices, local(): full_b = lax.all_gather(w_rest, rows_axes, axis=0, tiled=True)  28.1 us
    all_gather x1, waiting for transfers between devices, local(): late_all = lax.all_gather(late_proj, rows_axes, axis=0, tiled=True)  28 us
    all_gather x1, waiting for transfers between devices, local(): full_a = lax.all_gather(local_a, rows_axes, axis=0, tiled=True)  27.4 us
    all_to_all x1, waiting for transfers between devices, local(): lax.all_to_all(input_part.astype(jnp.bfloat16).reshape(num_rows, head_gro...  27 us
    unnamed x71, local copies, waits for them, and re-layouts  24.4 us
  transfers between devices with their start and end apart: 7, of which 6 were waited for; matrix products, arithmetic and copies ran while one was open for 22% of the time, Pallas kernels for 0%

profile of v8, /device:TPU:0, one launch (start us, length us, event | category | flops | bytes accessed | tf_op | source)
XLA Modules:
  0.0 390.2 jit_solution(7988635082533047727)
XLA Ops:
  7.2 1.2 slice.83
  8.5 1.9 pad_maximum_fusion.1
  10.6 44.8 %all_to_all.26 = bf16[96,8,512]{2,0,1:T(8,128)(2,1)S(1)} all-to-all(bf16[96,8,512]{2,0,1:T(8,128)(2,1)S(1)} %bitcast.173), channel_id=1, replica_groups=mesh['dp'=4,'ctx'=2,'head'=4] {'dp','ctx'}, dimensions={1} | all-to-all | bytes 1572864 | tf_op jit(solution)/shard_map/all_to_all | solution.py:208
  55.6 39.5 %all_to_all.27 = bf16[4,768,512]{2,1,0:T(8,128)(2,1)S(1)} all-to-all(bf16[4,768,512]{2,1,0:T(8,128)(2,1)S(1)} %broadcast_in_dim.76), channel_id=1, replica_groups=mesh['dp'=4,'ctx'=2,'head'=4] {'head'}, dimensions={0} | all-to-all | bytes 6291456 | tf_op jit(solution)/shard_map/all_to_all | solution.py:210
  95.1 2.0 copy.126
  97.1 27.4 %all-gather.5.cloned.1.call-done = bf16[4096,768]{1,0:T(8,128)(2,1)} async-done(((bf16[512,768]{1,0:T(8,128)(2,1)}), bf16[4096,768]{1,0:T(8,128)(2,1)}) %all-gather.5.cloned.1.call-update) | async-done | bytes 6291472 | tf_op jit(solution)/shard_map/all_gather | solution.py:203
  124.6 1.9 slice.96
  126.7 2.3 copy.131
  129.0 2.0 fusion.55
  131.0 0.9 copy.188
  132.4 1.5 multiply_cosine_fusion
  133.9 6.1 %convolution_bitcast_fusion = f32[384,768]{0,1:T(8,128)S(1)} fusion(bf16[4096,768]{1,0:T(8,128)(2,1)} %all-gather.5.cloned.1.call-done, bf16[384,4096]{1,0:T(8,128)(2,1)S(1)} %copy-done), kind=kOutput, calls=%fused_computation.25 | convolution fusion | flops 2415919104 | bytes 10616832 | tf_op jit(solution)/shard_map/dot_general | solution.py:219
  142.6 0.9 fusion.57
  143.5 2.2 copy.186
  145.7 2.1 copy.187
  147.8 1.7 subtract_convert_fusion.3
  149.5 1.5 maximum_select_fusion
  151.1 1.2 fusion.10
  152.3 1.2 select_reduce_fusion.1
  153.5 2.4 bitcast_convert_fusion.1
  155.9 2.3 copy.164
  158.2 1.7 multiply_reduce_fusion.1
  160.0 4.5 %fusion.6 = bf16[4,384,768]{1,2,0:T(8,128)(2,1)S(1)} fusion(f32[768,384,4]{1,0,2:T(8,128)} %copy-done.2, f32[4,384]{1,0:T(4,128)S(1)} %multiply_reduce_fusion.1, f32[4,384]{1,0:T(4,128)S(1)} %log_add_fusion.1, pred[384,768]{0,1:T(8,128)(4,1)S(1)} %fusion.16, bf16[768,256]{0,1:T(8,128)(2,1)} %copy-done.11, bf16[384,8,128]{0,2,1:T(8,128)(2,1)} %bitcast.166), kind=kOutput, calls=%fused_computation.11 | convolution fusion | flops 311427072 | bytes 7974912 | tf_op jit(solution)/shard_map/rhd,kd->hrk/dot_general | solution.py:90
  164.5 1.4 copy-done.4
  165.9 1.1 convolution_bitcast_fusion.2
  167.3 1.0 pad_maximum_fusion.9
  168.3 1.9 copy.136
  170.2 28.1 %all-gather.7.cloned.1.call-done = bf16[4096,512]{1,0:T(8,128)(2,1)} async-done(((bf16[512,512]{1,0:T(8,128)(2,1)}), bf16[4096,512]{1,0:T(8,128)(2,1)}) %all-gather.7.cloned.1.call-update) | async-done | bytes 4194320 | tf_op jit(solution)/shard_map/all_gather | solution.py:247
  198.5 1.9 copy.191
  200.5 4.5 %fusion.58 = f32[512,384]{1,0:T(8,128)S(1)} fusion(bf16[4096,512]{1,0:T(8,128)(2,1)} %all-gather.7.cloned.1.call-done, bf16[384,4096]{1,0:T(8,128)(2,1)S(1)} %copy-done), kind=kOutput, calls=%fused_computation.123 | convolution fusion | flops 1610612736 | bytes 8126464 | tf_op jit(solution)/shard_map/dot_general | solution.py:250
  205.6 1.3 subtract_convert_fusion.1
  206.9 1.2 fusion.11
  208.2 1.2 select_reduce_fusion
  209.4 2.1 bitcast_convert_fusion
  212.1 4.5 %fusion.1 = bf16[4,384,768]{1,2,0:T(8,128)(2,1)S(1)} fusion(f32[768,384,4]{1,0,2:T(8,128)} %copy-done.3, f32[4,384]{1,0:T(4,128)S(1)} %multiply_reduce_fusion, f32[4,384]{1,0:T(4,128)S(1)} %log_add_fusion, pred[384,768]{0,1:T(8,128)(4,1)S(1)} %fusion.16, bf16[768,256]{0,1:T(8,128)(2,1)S(1)} %copy-done.13, bf16[384,8,128]{0,2,1:T(8,128)(2,1)} %bitcast.167), kind=kOutput, calls=%fused_computation.3 | convolution fusion | flops 311427072 | bytes 7974912 | tf_op jit(solution)/shard_map/rhd,kd->hrk/dot_general | solution.py:90
  216.7 1.6 convolution_bitcast_fusion.5
  218.3 1.0 convolution_bitcast_fusion.1
  219.3 1.4 convolution_bitcast_fusion.4
  220.8 41.0 %all-gather.9.cloned.1.call-done = bf16[3072,512]{0,1:T(8,128)(2,1)} async-done(((bf16[384,512]{0,1:T(8,128)(2,1)}), bf16[3072,512]{0,1:T(8,128)(2,1)}) %all-gather.9.cloned.1.call-update) | async-done | bytes 3145744 | tf_op jit(solution)/shard_map/all_gather | solution.py:249
  261.7 1.1 copy.148
  262.9 5.0 %fusion.15 = f32[768,128]{0,1:T(8,128)} fusion(f32[768,128]{0,1:T(8,128)} %copy.148, bf16[384,8,128]{0,2,1:T(8,128)(2,1)} %bitcast.168, f32[768,384,4]{1,0,2:T(8,128)} %copy-done.2, f32[4,384]{1,0:T(4,128)S(1)} %log_add_fusion.1, pred[384,768]{0,1:T(8,128)(4,1)S(1)} %fusion.16), kind=kOutput, calls=%fused_computation.35 | convolution fusion | flops 307986432 | bytes 6199296 | tf_op jit(solution)/shard_map/hrk,rhd->kd/dot_general | solution.py:94
  267.9 2.0 copy.145
  269.8 2.2 fusion.14
  272.1 1.9 fusion.19
  273.9 1.5 collective-permute-start.1
  276.2 8.7 %collective-permute-done.1 = f32[384,256]{0,1:T(8,128)S(1)} collective-permute-done((f32[384,256]{0,1:T(8,128)}, f32[384,256]{0,1:T(8,128)S(1)}, u32[]{:S(2)}, u32[]{:S(2)}) %collective-permute-start.1) | collective-permute-done | bytes 393248 | tf_op jit(solution)/shard_map/ppermute | solution.py:267
  284.9 1.0 fusion.21
  286.4 0.9 pad_maximum_fusion.3
  287.3 5.0 %fusion.17 = f32[384,4096]{1,0:T(8,128)S(1)} fusion(bf16[4096,768]{1,0:T(8,128)(2,1)} %all-gather.5.cloned.1.call-done, bf16[384,128]{0,1:T(8,128)(2,1)S(1)} %slice.171, bf16[384,128]{0,1:T(8,128)(2,1)S(1)} %maximum_bitcast_fusion.1, bf16[384,512]{0,1:T(8,128)(2,1)S(1)} %bitcast.176), kind=kOutput, calls=%fused_computation.59 | convolution fusion | flops 2417688576 | bytes 13172736 | tf_op jit(solution)/shard_map/dot_general | solution.py:274
  292.3 1.8 add_convert_fusion
  294.2 2.0 copy.197
  296.2 4.1 %all-to-all-start.2 = ((bf16[384,4,1024]{2,0,1:T(8,128)(2,1)}), bf16[384,4,1024]{2,0,1:T(8,128)(2,1)S(1)}, u32[]{:S(2)}, u32[]{:S(2)}) async-start(bf16[384,4,1024]{2,0,1:T(8,128)(2,1)} %bitcast.159), calls=%async_computation.2 | async-start | bytes 6291456 | tf_op jit(solution)/shard_map/all_to_all | solution.py:292
  300.3 2.0 pad_maximum_fusion.2
  302.3 2.3 copy.154
  304.6 5.7 %fusion.60 = f32[512,512]{0,1:T(8,128)} fusion(bf16[3072,512]{0,1:T(8,128)(2,1)} %all-gather.9.cloned.1.call-done, bf16[3072,512]{1,0:T(8,128)(2,1)} %bitcast.163), kind=kOutput, calls=%fused_computation.125 | convolution fusion | flops 1610612736 | bytes 7340032 | tf_op jit(solution)/shard_map/dot_general | solution.py:282
  310.2 27.0 %all-to-all-done.2 = bf16[384,4,1024]{2,0,1:T(8,128)(2,1)S(1)} async-done(((bf16[384,4,1024]{2,0,1:T(8,128)(2,1)}), bf16[384,4,1024]{2,0,1:T(8,128)(2,1)S(1)}, u32[]{:S(2)}, u32[]{:S(2)}) %all-to-all-start.2) | async-done | bytes 3145760 | tf_op jit(solution)/shard_map/all_to_all | solution.py:292
  337.2 1.7 reduce_sum.42
  338.9 28.0 %all-gather.11.cloned.1.call-done = bf16[3072,768]{0,1:T(8,128)(2,1)} async-done(((bf16[384,768]{0,1:T(8,128)(2,1)}), bf16[3072,768]{0,1:T(8,128)(2,1)}) %all-gather.11.cloned.1.call-update) | async-done | bytes 4718608 | tf_op jit(solution)/shard_map/all_gather | solution.py:297
  366.9 5.9 %fusion.59 = f32[512,768]{1,0:T(8,128)S(1)} fusion(bf16[3072,512]{1,0:T(8,128)(2,1)} %bitcast.164, bf16[3072,768]{0,1:T(8,128)(2,1)} %all-gather.11.cloned.1.call-done), kind=kOutput, calls=%fused_computation.124 | convolution fusion | flops 2415919104 | bytes 9437184 | tf_op jit(solution)/shard_map/dot_general | solution.py:298
  372.9 1.1 slice.130
  374.0 0.8 fusion.54
  374.8 2.7 copy.192
  377.5 3.1 pad_maximum_fusion
  380.6 2.9 copy.155
  (99 shorter events, 6.9 us)
Async XLA Ops:
  7.2 3.3 copy-start
  7.2 117.4 %all-gather.5.cloned.1.call-start = ((), (), s32[]{:S(2)}) async-start(), calls=%async_computation.3 | async-start | bytes 7077888 | tf_op jit(solution)/shard_map/all_gather | solution.py:203
  10.4 187.9 %all-gather.7.cloned.1.call-start = ((), (), s32[]{:S(2)}) async-start(), calls=%async_computation.4 | async-start | bytes 4718592 | tf_op jit(solution)/shard_map/all_gather | solution.py:247
  95.1 31.4 %copy-start.26 = (s32[1,8]{1,0:T(1,128)S(1)}, s32[1,8]{1,0:T(1,128)}, u32[]{:S(2)}) copy-start(s32[1,8]{1,0:T(1,128)} %param.10) | copy-start | bytes 100
  126.5 135.3 %all-gather.9.cloned.1.call-start = ((), (), s32[]{:S(2)}) async-start(), calls=%async_computation.5 | async-start | bytes 3538944 | tf_op jit(solution)/shard_map/all_gather | solution.py:249
  140.5 0.6 copy-start.24
  141.9 7.6 %collective-permute-start = (bf16[384,256]{0,1:T(8,128)(2,1)}, bf16[384,256]{0,1:T(8,128)(2,1)}, u32[]{:S(2)}, u32[]{:S(2)}) collective-permute-start(bf16[384,256]{0,1:T(8,128)(2,1)} %pad_maximum_fusion.12), channel_id=1, source_target_pairs={{0,4},{4,0},{1,5},{5,1},{2,6},{6,2},{3,7},{7,3},{8,12},{12,8},{9,1... | collective-permute-start | bytes 589832 | tf_op jit(solution)/shard_map/ppermute | solution.py:230
  149.5 1.5 copy-start.17
  149.5 2.8 copy-start.18
  151.0 2.5 copy-start.11
  152.3 3.6 copy-start.2
  159.9 5.9 %copy-start.12 = (bf16[768,256]{0,1:T(8,128)(2,1)S(1)}, bf16[768,256]{0,1:T(8,128)(2,1)}, u32[]{:S(2)}) copy-start(bf16[768,256]{0,1:T(8,128)(2,1)} %copy-done.11) | copy-start | bytes 1179652
  159.9 7.0 %copy-start.6 = (f32[384,64]{1,0:T(8,128)S(1)}, f32[384,64]{1,0:T(8,128)}, u32[]{:S(2)}) copy-start(f32[384,64]{1,0:T(8,128)} %get-tuple-element.66) | copy-start | bytes 294916
  160.0 7.0 %copy-start.8 = (f32[384,64]{1,0:T(8,128)S(1)}, f32[384,64]{1,0:T(8,128)}, u32[]{:S(2)}) copy-start(f32[384,64]{1,0:T(8,128)} %get-tuple-element.67) | copy-start | bytes 294916
  164.5 1.4 copy-start.4
  198.3 168.6 %all-gather.11.cloned.1.call-start = ((), (), s32[]{:S(2)}) async-start(), calls=%async_computation.6 | async-start | bytes 5308416 | tf_op jit(solution)/shard_map/all_gather | solution.py:297
  205.0 1.9 copy-start.13
  206.9 2.4 copy-start.15
  208.2 3.4 copy-start.3
  209.4 2.4 copy-start.22
  211.8 7.5 %slice-start = ((s8[4718592]{0:T(1024)(128)(4,1)}), s8[4194304]{0:T(1024)(128)(4,1)S(1)}, s32[]{:S(2)}) async-start(s8[4718592]{0:T(1024)(128)(4,1)} %bitcast.156), calls=%async_computation.7 | async-start | bytes 8388608
  212.1 4.5 %copy-start.16 = (bf16[384,4,64]{2,0,1:T(8,128)(2,1)S(1)}, bf16[384,4,64]{2,0,1:T(8,128)(2,1)}, u32[]{:S(2)}) copy-start(bf16[384,4,64]{2,0,1:T(8,128)(2,1)} %copy-done.15) | copy-start | bytes 589828
  212.1 7.2 %slice-start.1 = ((s8[4718592]{0:T(1024)(128)(4,1)}), s8[524288]{0:T(1024)(128)(4,1)S(1)}, s32[]{:S(2)}) async-start(s8[4718592]{0:T(1024)(128)(4,1)} %bitcast.156), calls=%async_computation.8 | async-start | bytes 1048576
  216.6 1.6 copy-start.14
  216.6 2.7 copy-start.20
  262.9 7.0 %copy-start.5 = (bf16[4,384,768]{1,2,0:T(8,128)(2,1)S(1)}, bf16[4,384,768]{1,2,0:T(8,128)(2,1)}, u32[]{:S(2)}) copy-start(bf16[4,384,768]{1,2,0:T(8,128)(2,1)} %copy-done.4) | copy-start | bytes 7077892
  267.9 7.5 %copy-start.7 = (f32[384,64]{1,0:T(8,128)S(1)}, f32[384,64]{1,0:T(8,128)}, u32[]{:S(2)}) copy-start(f32[384,64]{1,0:T(8,128)} %get-tuple-element.66) | copy-start | bytes 294916
  267.9 7.5 %copy-start.9 = (f32[384,64]{1,0:T(8,128)S(1)}, f32[384,64]{1,0:T(8,128)}, u32[]{:S(2)}) copy-start(f32[384,64]{1,0:T(8,128)} %get-tuple-element.67) | copy-start | bytes 294916
  272.0 3.7 copy-start.19
  272.1 12.9 %copy-start.23 = (f32[768,128]{0,1:T(8,128)S(1)}, f32[768,128]{0,1:T(8,128)}, u32[]{:S(2)}) copy-start(f32[768,128]{0,1:T(8,128)} %fusion.15) | copy-start | bytes 1179652
  273.9 13.4 %copy-start.21 = (bf16[384,4,128]{0,2,1:T(8,128)(2,1)S(1)}, bf16[384,4,128]{0,2,1:T(8,128)(2,1)}, u32[]{:S(2)}) copy-start(bf16[384,4,128]{0,2,1:T(8,128)(2,1)} %copy.136) | copy-start | bytes 1179652
  273.9 11.0 %collective-permute-start.1 = (f32[384,256]{0,1:T(8,128)}, f32[384,256]{0,1:T(8,128)S(1)}, u32[]{:S(2)}, u32[]{:S(2)}) collective-permute-start(f32[384,256]{0,1:T(8,128)} %fusion.19), channel_id=1, source_target_pairs={{0,4},{4,0},{1,5},{5,1},{2,6},{6,2},{3,7},{7,3},{8,12},{12,8},{9,1... | collective-permute-start | bytes 1179656 | tf_op jit(solution)/shard_map/ppermute | solution.py:267
  287.3 5.0 %copy-start.10 = (bf16[4096,512]{1,0:T(8,128)(2,1)S(1)}, bf16[4096,512]{1,0:T(8,128)(2,1)}, u32[]{:S(2)}) copy-start(bf16[4096,512]{1,0:T(8,128)(2,1)} %all-gather.7.cloned.1.call-done) | copy-start | bytes 12582916
  296.2 4.1 %copy-start.25 = (bf16[128,4,384]{2,0,1:T(8,128)(2,1)S(1)}, bf16[128,4,384]{2,0,1:T(8,128)(2,1)}, u32[]{:S(2)}) copy-start(bf16[128,4,384]{2,0,1:T(8,128)(2,1)} %get-tuple-element.71) | copy-start | bytes 1179652
  296.2 41.0 %all-to-all-start.2 = ((bf16[384,4,1024]{2,0,1:T(8,128)(2,1)}), bf16[384,4,1024]{2,0,1:T(8,128)(2,1)S(1)}, u32[]{:S(2)}, u32[]{:S(2)}) async-start(bf16[384,4,1024]{2,0,1:T(8,128)(2,1)} %bitcast.159), calls=%async_computation.2 | async-start | bytes 6291456 | tf_op jit(solution)/shard_map/all_to_all | solution.py:292
  374.8 8.6 %copy-start.1 = (bf16[384,4096]{1,0:T(8,128)(2,1)S(1)}, bf16[384,4096]{1,0:T(8,128)(2,1)}, u32[]{:S(2)}) copy-start(bf16[384,4096]{1,0:T(8,128)(2,1)} %param.6) | copy-start | bytes 9437188
Sparse Core Ops, SparseCore 0:
  10.8 113.7 all-gather.4
  126.7 71.5 all-gather.6
  200.4 61.3 all-gather.8
  287.4 79.4 all-gather.10

commit v9 on v8

--- a/solution.py
+++ b/solution.py
@@ -206,6 +206,11 @@
         quarter = num_rows // head_groups
         own_rows = lax.dynamic_slice_in_dim(hidden_in, lax.axis_index("head") * quarter, quarter, 0)
         cols_part = lax.all_to_all(own_rows, rows_axes, 1, 0, tiled=True)
+    else:
+        cols_part = lax.all_to_all(hidden_in, rows_axes, 1, 0, tiled=True)
+    full_a, w_query, cols_part = lax.optimization_barrier((full_a, w_query, cols_part))
+    hidden_cols = cols_part
+    if split_rows:
         spread = jnp.broadcast_to(cols_part[None], (head_groups,) + cols_part.shape)
         cols_all = lax.all_to_all(spread, "head", 0, 0, tiled=False)
         hidden_cols = (
@@ -213,9 +218,6 @@
             .transpose(1, 0, 2, 3)
             .reshape(group_count * num_rows, -1)
         )
-    else:
-        hidden_cols = lax.all_to_all(hidden_in, rows_axes, 1, 0, tiled=True)
-    full_a, w_query, hidden_cols = lax.optimization_barrier((full_a, w_query, hidden_cols))
     proj_a = jnp.dot(hidden_in, full_a, preferred_element_type=jnp.float32)
     query_a = rotate(
         proj_a[:, :first_cols].reshape(num_rows, first_heads, 128), cosine, sine_table
@@ -245,7 +247,7 @@
     if first_heads < head_count:
         w_rest = w_query[:, first_cols:]
         full_b = lax.all_gather(w_rest, rows_axes, axis=0, tiled=True)
-        d_query_a, full_b = lax.optimization_barrier((d_query_a, full_b))
+        d_query_a, full_b, hidden_cols = lax.optimization_barrier((d_query_a, full_b, hidden_cols))
         early_all = lax.all_gather(d_query_a, rows_axes, axis=0, tiled=True)
         proj_b = jnp.dot(hidden_in, full_b, preferred_element_type=jnp.float32)
         query_b = rotate(
@@ -254,11 +256,11 @@
         out_b, grad_qb, part_kb, part_vb = attend(
             query_b, *shared, dout_rows[:, first_heads:], *masks
         )
-        early_all, part_kb, part_vb = lax.optimization_barrier((early_all, part_kb, part_vb))
+        d_query_b = unrotate(grad_qb, cosine, sine_table).astype(jnp.bfloat16).reshape(num_rows, -1)
+        early_all, d_query_b = lax.optimization_barrier((early_all, d_query_b))
+        mid_all = lax.all_gather(d_query_b, rows_axes, axis=0, tiled=True)
         part_k, part_v = part_k + part_kb, part_v + part_vb
         out_parts.append(out_b)
-        d_query_b = unrotate(grad_qb, cosine, sine_table).astype(jnp.bfloat16).reshape(num_rows, -1)
-        d_query_parts.append(d_query_b)
     attended = jnp.concatenate(out_parts, 1).reshape(num_rows, query_cols)
     parts_kv = jnp.concatenate([part_k, part_v], 1)
     if ctx_count == 2:
@@ -278,9 +280,12 @@
         input_part = input_part + lax.dot_general(
             d_query_b, full_b, (((1,), (1,)), ((), ())), preferred_element_type=jnp.float32
         )
-        late_proj = jnp.concatenate([d_query_b, d_key, d_value], 1)
+        late_proj = jnp.concatenate([d_key, d_value], 1)
         early_sum = lax.dot_general(
-            hidden_cols, early_all, (((0,), (0,)), ((), ())), preferred_element_type=jnp.float32
+            hidden_cols,
+            jnp.concatenate([early_all, mid_all], 1),
+            (((0,), (0,)), ((), ())),
+            preferred_element_type=jnp.float32,
         )
     else:
         late_proj = jnp.concatenate([d_key, d_value], 1)
@@ -294,12 +299,15 @@
         "head", 1, 1, tiled=False,
     )
     grad_input = jnp.sum(input_split.astype(jnp.float32), axis=1).astype(jnp.bfloat16)
-    late_all = lax.all_gather(late_proj, rows_axes, axis=0, tiled=True)
+    late_spread = jnp.broadcast_to(late_proj[None], (group_count,) + late_proj.shape)
+    late_all = lax.all_to_all(late_spread, rows_axes, 0, 0, tiled=False).reshape(
+        group_count * num_rows, -1
+    )
     late_sum = lax.dot_general(
         hidden_cols, late_all, (((0,), (0,)), ((), ())), preferred_element_type=jnp.float32
     )
-    query_w = jnp.concatenate([early_sum, late_sum[:, : query_cols - first_cols]], 1)
-    rest = late_sum[:, query_cols - first_cols :]
+    query_w = early_sum
+    rest = late_sum
     return (attended, grad_input, query_w, rest[:, :128], rest[:, 128:])
 
 

time: 394 us -> 388 us (0.985)
  blocking collectives: 84.3 us -> 44.9 us
  waiting for transfers between devices: 160 us -> 193 us
  starting transfers between devices: 6.59 us -> 15.8 us
  matrix products: 57.4 us -> 52.5 us
    all_to_all x0 -> x2, waiting for transfers between devices: none -> 54.9 us  [the longest x1 40.4 us: local(): lax.all_to_all(late_spread, rows_axes, 0, 0, tiled=False)]
    all_gather x1, waiting for transfers between devices: 27.4 us -> 69.1 us  [local(): full_a = lax.all_gather(local_a, rows_axes, axis=0, tiled=True)]
    all_to_all x1 -> x0, blocking collectives: 39.5 us -> none  [local(): cols_all = lax.all_to_all(spread, 'head', 0, 0, tiled=False)]
    all_gather x1, waiting for transfers between devices: 28 us -> 0.01 us  [local(): mid_all = lax.all_gather(d_query_b, rows_axes, axis=0, tiled=True)]
    all_gather x1, waiting for transfers between devices: 28.1 us -> 0.66 us  [local(): full_b = lax.all_gather(w_rest, rows_axes, axis=0, tiled=True)]
    all_gather x1, waiting for transfers between devices: 41 us -> 31.8 us  [local(): early_all = lax.all_gather(d_query_a, rows_axes, axis=0, tiled=True)]
    all_to_all x0 -> x2, starting transfers between devices: none -> 8.95 us  [the longest x1 4.64 us: local(): cols_all = lax.all_to_all(spread, 'head', 0, 0, tiled=False)]
    unnamed x71 -> x75, local copies, waits for them, and re-layouts: 24.4 us -> 19 us
  transfers between devices with their start and end apart: 7 -> 9, of which waited for: 6 -> 7; matrix products, arithmetic and copies ran while one was open for 22% -> 24% of each run, Pallas kernels for 0% -> 0%
where the time goes in v9:
time: 388 us; the launch traced here: 382 us
  waiting for transfers between devices  193 us (50%)
  matrix products  52.5 us (14%)
  blocking collectives  44.9 us (12%)
  local copies, waits for them, and re-layouts  38.7 us (10%)
  other arithmetic  22.8 us (6%)
  starting transfers between devices  15.8 us (4%)
  between operations  15 us (4%)
    all_gather x1, waiting for transfers between devices, local(): full_a = lax.all_gather(local_a, rows_axes, axis=0, tiled=True)  69.1 us
    all_to_all x1, blocking collectives, local(): cols_part = lax.all_to_all(own_rows, rows_axes, 1, 0, tiled=True)  44.9 us
    all_to_all x1, waiting for transfers between devices, local(): lax.all_to_all(late_spread, rows_axes, 0, 0, tiled=False)  40.4 us
    all_gather x1, waiting for transfers between devices, local(): early_all = lax.all_gather(d_query_a, rows_axes, axis=0, tiled=True)  31.8 us
    all_to_all x1, waiting for transfers between devices, local(): lax.all_to_all(input_part.astype(jnp.bfloat16).reshape(num_rows, head_gro...  29.5 us
    unnamed x75, local copies, waits for them, and re-layouts  19 us
    all_to_all x1, waiting for transfers between devices, local(): cols_all = lax.all_to_all(spread, 'head', 0, 0, tiled=False)  14.5 us
    dot_general x2, matrix products, attend_whole(): jnp.einsum('rhd,kd->hrk', dout_rows, value_all, preferred_element_type=jn...  9.03 us
  transfers between devices with their start and end apart: 9, of which 7 were waited for; matrix products, arithmetic and copies ran while one was open for 24% of the time, Pallas kernels for 0%

profile of v9, /device:TPU:0, one launch (start us, length us, event | category | flops | bytes accessed | tf_op | source)
XLA Modules:
  0.0 382.3 jit_solution(12080339259532846178)
XLA Ops:
  7.2 1.2 slice.77
  8.5 1.9 pad_maximum_fusion
  10.6 44.9 %all_to_all.34 = bf16[96,8,512]{2,0,1:T(8,128)(2,1)} all-to-all(bf16[96,8,512]{2,0,1:T(8,128)(2,1)S(1)} %bitcast.174), channel_id=1, replica_groups=mesh['dp'=4,'ctx'=2,'head'=4] {'dp','ctx'}, dimensions={1} | all-to-all | bytes 1572864 | tf_op jit(solution)/shard_map/all_to_all | solution.py:208
  55.5 69.1 %all-gather.5.cloned.1.call-done = bf16[4096,768]{1,0:T(8,128)(2,1)} async-done(((bf16[512,768]{1,0:T(8,128)(2,1)}), bf16[4096,768]{1,0:T(8,128)(2,1)}) %all-gather.5.cloned.1.call-update) | async-done | bytes 6291472 | tf_op jit(solution)/shard_map/all_gather | solution.py:203
  124.6 1.9 slice.90
  126.7 2.3 copy.132
  128.9 1.9 fusion.63
  130.9 1.9 copy.195
  132.8 1.0 copy.198
  134.3 1.5 multiply_cosine_fusion
  135.8 5.6 %convolution_bitcast_fusion = f32[384,768]{0,1:T(8,128)S(1)} fusion(bf16[4096,768]{1,0:T(8,128)(2,1)} %all-gather.5.cloned.1.call-done, bf16[384,4096]{1,0:T(8,128)(2,1)S(1)} %copy-done), kind=kOutput, calls=%fused_computation.28 | convolution fusion | flops 2415919104 | bytes 10616832 | tf_op jit(solution)/shard_map/dot_general | solution.py:221
  142.0 0.6 copy-done.25
  142.6 0.7 pad_maximum_fusion.6
  143.8 0.9 fusion.65
  144.8 2.2 copy.193
  146.9 2.1 copy.194
  149.1 3.1 broadcast_in_dim.82
  152.2 4.6 %all-to-all-start.1 = ((bf16[4,768,512]{2,1,0:T(8,128)(2,1)}), bf16[4,768,512]{2,1,0:T(8,128)(2,1)}, u32[]{:S(2)}, u32[]{:S(2)}) async-start(bf16[4,768,512]{2,1,0:T(8,128)(2,1)} %broadcast_in_dim.82), calls=%async_computation.1 | async-start | bytes 6291456 | tf_op jit(solution)/shard_map/all_to_all | solution.py:215
  157.0 1.7 subtract_convert_fusion.3
  158.7 1.5 maximum_select_fusion
  160.3 1.2 fusion.14
  161.6 1.2 select_reduce_fusion.1
  162.7 2.4 bitcast_convert_fusion.1
  165.2 2.3 copy.167
  167.5 1.5 multiply_reduce_fusion.1
  169.0 4.5 %fusion.10 = bf16[4,384,768]{1,2,0:T(8,128)(2,1)S(1)} fusion(f32[768,384,4]{1,0,2:T(8,128)} %copy-done.2, f32[4,384]{1,0:T(4,128)S(1)} %multiply_reduce_fusion.1, f32[4,384]{1,0:T(4,128)S(1)} %log_add_fusion.1, pred[384,768]{0,1:T(8,128)(4,1)S(1)} %fusion.20, bf16[768,256]{0,1:T(8,128)(2,1)} %copy-done.13, bf16[384,8,128]{0,2,1:T(8,128)(2,1)} %bitcast.167), kind=kOutput, calls=%fused_computation.15 | convolution fusion | flops 311427072 | bytes 7974912 | tf_op jit(solution)/shard_map/rhd,kd->hrk/dot_general | solution.py:90
  173.6 1.4 copy-done.5
  174.9 1.1 convolution_bitcast_fusion.2
  176.4 1.0 pad_maximum_fusion.3
  177.4 1.9 copy.137
  179.3 14.5 %all-to-all-done.1 = bf16[4,768,512]{2,1,0:T(8,128)(2,1)} async-done(((bf16[4,768,512]{2,1,0:T(8,128)(2,1)}), bf16[4,768,512]{2,1,0:T(8,128)(2,1)}, u32[]{:S(2)}, u32[]{:S(2)}) %all-to-all-start.1) | async-done | bytes 3145760 | tf_op jit(solution)/shard_map/all_to_all | solution.py:215
  193.8 3.9 %copy.138 = bf16[8,4,96,512]{3,2,1,0:T(8,128)(2,1)} copy(bf16[8,4,96,512]{3,2,0,1:T(8,128)(2,1)} %bitcast.25) | data formatting | bytes 6291456 | tf_op jit(solution)/shard_map/transpose | solution.py:218
  197.7 0.7 all-gather.7.cloned.1.call-done
  198.4 5.4 %fusion.67 = f32[512,384]{1,0:T(8,128)} fusion(bf16[4096,512]{1,0:T(8,128)(2,1)} %all-gather.7.cloned.1.call-done, bf16[384,4096]{1,0:T(8,128)(2,1)S(1)} %copy-done), kind=kOutput, calls=%fused_computation.128 | convolution fusion | flops 1610612736 | bytes 8126464 | tf_op jit(solution)/shard_map/dot_general | solution.py:252
  204.1 1.2 fusion.64
  205.8 1.2 subtract_convert_fusion.1
  207.1 1.2 fusion.15
  208.3 1.2 select_reduce_fusion
  209.5 2.1 bitcast_convert_fusion
  212.3 4.5 %fusion.5 = bf16[4,384,768]{1,2,0:T(8,128)(2,1)S(1)} fusion(f32[768,384,4]{1,0,2:T(8,128)} %copy-done.3, f32[4,384]{1,0:T(4,128)S(1)} %multiply_reduce_fusion, f32[4,384]{1,0:T(4,128)S(1)} %log_add_fusion, pred[384,768]{0,1:T(8,128)(4,1)S(1)} %fusion.20, bf16[768,256]{0,1:T(8,128)(2,1)S(1)} %copy-done.15, bf16[384,8,128]{0,2,1:T(8,128)(2,1)} %bitcast.168), kind=kOutput, calls=%fused_computation.7 | convolution fusion | flops 311427072 | bytes 7974912 | tf_op jit(solution)/shard_map/rhd,kd->hrk/dot_general | solution.py:90
  216.8 1.0 convolution_bitcast_fusion.5
  217.9 1.0 fusion.18
  218.9 1.6 convolution_bitcast_fusion.3
  220.6 1.7 fusion.19
  222.3 0.8 fusion.27
  223.1 0.9 collective-permute-start.1
  223.9 1.1 convolution_bitcast_fusion.1
  225.9 0.9 copy.155
  226.8 6.6 %collective-permute-done.1 = f32[384,256]{0,1:T(8,128)S(1)} collective-permute-done((f32[384,256]{0,1:T(8,128)}, f32[384,256]{0,1:T(8,128)S(1)}, u32[]{:S(2)}, u32[]{:S(2)}) %collective-permute-start.1) | collective-permute-done | bytes 393248 | tf_op jit(solution)/shard_map/ppermute | solution.py:269
  233.5 31.8 %all-gather.9.cloned.1.call-done = bf16[3072,512]{0,1:T(8,128)(2,1)} async-done(((bf16[384,512]{0,1:T(8,128)(2,1)}), bf16[3072,512]{0,1:T(8,128)(2,1)}) %all-gather.9.cloned.1.call-update) | async-done | bytes 3145744 | tf_op jit(solution)/shard_map/all_gather | solution.py:251
  266.0 1.2 broadcast_in_dim.84
  267.2 4.3 %all-to-all-start.3 = ((bf16[8,384,256]{2,1,0:T(8,128)(2,1)}), bf16[8,384,256]{2,1,0:T(8,128)(2,1)}, u32[]{:S(2)}, u32[]{:S(2)}) async-start(bf16[8,384,256]{2,1,0:T(8,128)(2,1)} %broadcast_in_dim.84), calls=%async_computation.3 | async-start | bytes 3145728 | tf_op jit(solution)/shard_map/all_to_all | solution.py:303
  271.6 5.1 %fusion.21 = f32[384,4096]{1,0:T(8,128)S(1)} fusion(bf16[4096,768]{1,0:T(8,128)(2,1)} %all-gather.5.cloned.1.call-done, bf16[384,128]{0,1:T(8,128)(2,1)S(1)} %slice.163, bf16[384,128]{0,1:T(8,128)(2,1)S(1)} %maximum_bitcast_fusion.1, bf16[384,512]{0,1:T(8,128)(2,1)S(1)} %bitcast.177), kind=kOutput, calls=%fused_computation.58 | convolution fusion | flops 2417688576 | bytes 13172736 | tf_op jit(solution)/shard_map/dot_general | solution.py:276
  276.7 1.9 add_convert_fusion
  278.6 2.1 copy.203
  280.7 40.4 %all-to-all-done.3 = bf16[8,384,256]{2,1,0:T(8,128)(2,1)} async-done(((bf16[8,384,256]{2,1,0:T(8,128)(2,1)}), bf16[8,384,256]{2,1,0:T(8,128)(2,1)}, u32[]{:S(2)}, u32[]{:S(2)}) %all-to-all-start.3) | async-done | bytes 1572896 | tf_op jit(solution)/shard_map/all_to_all | solution.py:303
  321.1 4.9 %all-to-all-start.2 = ((bf16[384,4,1024]{2,0,1:T(8,128)(2,1)}), bf16[384,4,1024]{2,0,1:T(8,128)(2,1)}, u32[]{:S(2)}, u32[]{:S(2)}) async-start(bf16[384,4,1024]{2,0,1:T(8,128)(2,1)} %bitcast.163), calls=%async_computation.2 | async-start | bytes 6291456 | tf_op jit(solution)/shard_map/all_to_all | solution.py:297
  326.0 2.0 pad_maximum_fusion.1
  328.0 2.3 copy.158
  330.3 2.4 fusion.68
  332.7 0.8 fusion.66
  333.5 29.5 %all-to-all-done.2 = bf16[384,4,1024]{2,0,1:T(8,128)(2,1)} async-done(((bf16[384,4,1024]{2,0,1:T(8,128)(2,1)}), bf16[384,4,1024]{2,0,1:T(8,128)(2,1)}, u32[]{:S(2)}, u32[]{:S(2)}) %all-to-all-start.2) | async-done | bytes 3145760 | tf_op jit(solution)/shard_map/all_to_all | solution.py:297
  363.0 3.6 reduce_sum.42
  366.6 8.7 %fusion = f32[512,1024]{1,0:T(8,128)} fusion(bf16[3072,512]{1,0:T(8,128)(2,1)} %bitcast.161, bf16[3072,512]{0,1:T(8,128)(2,1)} %all-gather.11.cloned.1.call-done, bf16[3072,512]{0,1:T(8,128)(2,1)} %all-gather.9.cloned.1.call-done), kind=kOutput, calls=%fused_computation | convolution fusion | flops 3233808384 | bytes 11534336 | tf_op jit(solution)/shard_map/dot_general | solution.py:284
  (105 shorter events, 5.6 us)
Async XLA Ops:
  7.2 3.3 copy-start
  7.2 119.3 %copy-start.27 = (s32[1,8]{1,0:T(1,128)S(1)}, s32[1,8]{1,0:T(1,128)}, u32[]{:S(2)}) copy-start(s32[1,8]{1,0:T(1,128)} %param.10) | copy-start | bytes 100
  7.2 117.4 %all-gather.5.cloned.1.call-start = ((), (), s32[]{:S(2)}) async-start(), calls=%async_computation.4 | async-start | bytes 7077888 | tf_op jit(solution)/shard_map/all_gather | solution.py:203
  10.4 188.0 %all-gather.7.cloned.1.call-start = ((), (), s32[]{:S(2)}) async-start(), calls=%async_computation.5 | async-start | bytes 4718592 | tf_op jit(solution)/shard_map/all_gather | solution.py:249
  141.9 0.6 copy-start.25
  143.3 15.4 %collective-permute-start = (bf16[384,256]{0,1:T(8,128)(2,1)}, bf16[384,256]{0,1:T(8,128)(2,1)}, u32[]{:S(2)}, u32[]{:S(2)}) collective-permute-start(bf16[384,256]{0,1:T(8,128)(2,1)} %pad_maximum_fusion.6), channel_id=1, source_target_pairs={{0,4},{4,0},{1,5},{5,1},{2,6},{6,2},{3,7},{7,3},{8,12},{12,8},{9,1... | collective-permute-start | bytes 589832 | tf_op jit(solution)/shard_map/ppermute | solution.py:232
  152.2 41.6 %all-to-all-start.1 = ((bf16[4,768,512]{2,1,0:T(8,128)(2,1)}), bf16[4,768,512]{2,1,0:T(8,128)(2,1)}, u32[]{:S(2)}, u32[]{:S(2)}) async-start(bf16[4,768,512]{2,1,0:T(8,128)(2,1)} %broadcast_in_dim.82), calls=%async_computation.1 | async-start | bytes 6291456 | tf_op jit(solution)/shard_map/all_to_all | solution.py:215
  156.8 108.5 %all-gather.9.cloned.1.call-start = ((), (), s32[]{:S(2)}) async-start(), calls=%async_computation.6 | async-start | bytes 3538944 | tf_op jit(solution)/shard_map/all_gather | solution.py:251
  158.7 1.6 copy-start.18
  158.7 2.8 copy-start.20
  160.3 2.5 copy-start.13
  161.5 3.6 copy-start.2
  169.0 5.9 %copy-start.14 = (bf16[768,256]{0,1:T(8,128)(2,1)S(1)}, bf16[768,256]{0,1:T(8,128)(2,1)}, u32[]{:S(2)}) copy-start(bf16[768,256]{0,1:T(8,128)(2,1)} %copy-done.13) | copy-start | bytes 1179652
  169.0 7.0 %copy-start.7 = (f32[384,64]{1,0:T(8,128)S(1)}, f32[384,64]{1,0:T(8,128)}, u32[]{:S(2)}) copy-start(f32[384,64]{1,0:T(8,128)} %get-tuple-element.66) | copy-start | bytes 294916
  169.0 7.0 %copy-start.9 = (f32[384,64]{1,0:T(8,128)S(1)}, f32[384,64]{1,0:T(8,128)}, u32[]{:S(2)}) copy-start(f32[384,64]{1,0:T(8,128)} %get-tuple-element.67) | copy-start | bytes 294916
  173.6 1.4 copy-start.5
  203.8 3.3 copy-start.15
  203.8 162.8 %all-gather.11.cloned.1.call-start = ((), (), s32[]{:S(2)}) async-start(), calls=%async_computation.7 | async-start | bytes 3538944 | tf_op jit(solution)/shard_map/all_gather | solution.py:261
  207.1 2.4 copy-start.16
  208.3 3.4 copy-start.3
  209.5 2.4 copy-start.24
  211.9 6.9 %slice-start.2 = ((s8[4718592]{0:T(1024)(128)(4,1)}), s8[4194304]{0:T(1024)(128)(4,1)S(1)}, s32[]{:S(2)}) async-start(s8[4718592]{0:T(1024)(128)(4,1)} %bitcast.158), calls=%async_computation.10 | async-start | bytes 8388608
  212.2 4.6 %copy-start.17 = (bf16[384,4,64]{2,0,1:T(8,128)(2,1)S(1)}, bf16[384,4,64]{2,0,1:T(8,128)(2,1)}, u32[]{:S(2)}) copy-start(bf16[384,4,64]{2,0,1:T(8,128)(2,1)} %copy-done.16) | copy-start | bytes 589828
  212.2 5.6 %copy-start.6 = (bf16[4,384,768]{1,2,0:T(8,128)(2,1)S(1)}, bf16[4,384,768]{1,2,0:T(8,128)(2,1)}, u32[]{:S(2)}) copy-start(bf16[4,384,768]{1,2,0:T(8,128)(2,1)} %copy-done.5) | copy-start | bytes 7077892
  212.3 5.6 %copy-start.19 = (bf16[384,4,64]{2,0,1:T(8,128)(2,1)S(1)}, bf16[384,4,64]{2,0,1:T(8,128)(2,1)}, u32[]{:S(2)}) copy-start(bf16[384,4,64]{2,0,1:T(8,128)(2,1)} %copy-done.18) | copy-start | bytes 589828
  212.3 5.6 %copy-start.21 = (bf16[384,4,64]{2,0,1:T(8,128)(2,1)S(1)}, bf16[384,4,64]{2,0,1:T(8,128)(2,1)}, u32[]{:S(2)}) copy-start(bf16[384,4,64]{2,0,1:T(8,128)(2,1)} %copy-done.20) | copy-start | bytes 589828
  212.3 6.6 %slice-start.3 = ((s8[4718592]{0:T(1024)(128)(4,1)}), s8[524288]{0:T(1024)(128)(4,1)S(1)}, s32[]{:S(2)}) async-start(s8[4718592]{0:T(1024)(128)(4,1)} %bitcast.158), calls=%async_computation.11 | async-start | bytes 1048576
  216.8 2.0 copy-start.22
  217.8 2.7 slice-start
  218.9 1.7 slice-start.1
  220.6 4.4 %copy-start.8 = (f32[384,64]{1,0:T(8,128)S(1)}, f32[384,64]{1,0:T(8,128)}, u32[]{:S(2)}) copy-start(f32[384,64]{1,0:T(8,128)} %get-tuple-element.66) | copy-start | bytes 294916
  220.6 4.4 %copy-start.10 = (f32[384,64]{1,0:T(8,128)S(1)}, f32[384,64]{1,0:T(8,128)}, u32[]{:S(2)}) copy-start(f32[384,64]{1,0:T(8,128)} %get-tuple-element.67) | copy-start | bytes 294916
  223.1 10.3 %collective-permute-start.1 = (f32[384,256]{0,1:T(8,128)}, f32[384,256]{0,1:T(8,128)S(1)}, u32[]{:S(2)}, u32[]{:S(2)}) collective-permute-start(f32[384,256]{0,1:T(8,128)} %fusion.27), channel_id=1, source_target_pairs={{0,4},{4,0},{1,5},{5,1},{2,6},{6,2},{3,7},{7,3},{8,12},{12,8},{9,1... | collective-permute-start | bytes 1179656 | tf_op jit(solution)/shard_map/ppermute | solution.py:269
  225.9 45.7 %copy-start.23 = (bf16[384,4,128]{0,2,1:T(8,128)(2,1)S(1)}, bf16[384,4,128]{0,2,1:T(8,128)(2,1)}, u32[]{:S(2)}) copy-start(bf16[384,4,128]{0,2,1:T(8,128)(2,1)} %copy.137) | copy-start | bytes 1179652
  267.2 53.8 %all-to-all-start.3 = ((bf16[8,384,256]{2,1,0:T(8,128)(2,1)}), bf16[8,384,256]{2,1,0:T(8,128)(2,1)}, u32[]{:S(2)}, u32[]{:S(2)}) async-start(bf16[8,384,256]{2,1,0:T(8,128)(2,1)} %broadcast_in_dim.84), calls=%async_computation.3 | async-start | bytes 3145728 | tf_op jit(solution)/shard_map/all_to_all | solution.py:303
  271.6 5.2 %copy-start.11 = (bf16[384,4,128]{0,2,1:T(8,128)(2,1)S(1)}, bf16[384,4,128]{0,2,1:T(8,128)(2,1)}, u32[]{:S(2)}) copy-start(bf16[384,4,128]{0,2,1:T(8,128)(2,1)} %copy.155) | copy-start | bytes 1179652
  271.6 5.2 %copy-start.12 = (bf16[4096,512]{1,0:T(8,128)(2,1)S(1)}, bf16[4096,512]{1,0:T(8,128)(2,1)}, u32[]{:S(2)}) copy-start(bf16[4096,512]{1,0:T(8,128)(2,1)} %all-gather.7.cloned.1.call-done) | copy-start | bytes 12582916
  280.7 45.3 %copy-start.26 = (bf16[128,4,384]{2,0,1:T(8,128)(2,1)S(1)}, bf16[128,4,384]{2,0,1:T(8,128)(2,1)}, u32[]{:S(2)}) copy-start(bf16[128,4,384]{2,0,1:T(8,128)(2,1)} %get-tuple-element.71) | copy-start | bytes 1179652
  321.1 9.2 %copy-start.4 = (bf16[8,4,96,512]{3,2,1,0:T(8,128)(2,1)S(1)}, bf16[8,4,96,512]{3,2,1,0:T(8,128)(2,1)}, u32[]{:S(2)}) copy-start(bf16[8,4,96,512]{3,2,1,0:T(8,128)(2,1)} %copy.138) | copy-start | bytes 9437188
  321.1 41.9 %all-to-all-start.2 = ((bf16[384,4,1024]{2,0,1:T(8,128)(2,1)}), bf16[384,4,1024]{2,0,1:T(8,128)(2,1)}, u32[]{:S(2)}, u32[]{:S(2)}) async-start(bf16[384,4,1024]{2,0,1:T(8,128)(2,1)} %bitcast.163), calls=%async_computation.2 | async-start | bytes 6291456 | tf_op jit(solution)/shard_map/all_to_all | solution.py:297
  366.6 8.7 %copy-start.1 = (bf16[384,4096]{1,0:T(8,128)(2,1)S(1)}, bf16[384,4096]{1,0:T(8,128)(2,1)}, u32[]{:S(2)}) copy-start(bf16[384,4096]{1,0:T(8,128)(2,1)} %param.6) | copy-start | bytes 9437188
Sparse Core Ops, SparseCore 0:
  10.8 113.7 all-gather.4
  126.7 71.6 all-gather.6
  203.9 61.3 all-gather.8
  267.2 83.3 all-gather.10

commit v10 on v9

--- a/solution.py
+++ b/solution.py
@@ -298,6 +298,7 @@
         input_part.astype(jnp.bfloat16).reshape(num_rows, head_groups, input_cols),
         "head", 1, 1, tiled=False,
     )
+    input_split, late_proj = lax.optimization_barrier((input_split, late_proj))
     grad_input = jnp.sum(input_split.astype(jnp.float32), axis=1).astype(jnp.bfloat16)
     late_spread = jnp.broadcast_to(late_proj[None], (group_count,) + late_proj.shape)
     late_all = lax.all_to_all(late_spread, rows_axes, 0, 0, tiled=False).reshape(

time: 388 us -> 397 us (1.023)
  matrix products: 52.5 us -> 59.6 us
    all_gather x1, waiting for transfers between devices: 31.8 us -> 24.1 us  [local(): early_all = lax.all_gather(d_query_a, rows_axes, axis=0, tiled=True)]
    all_to_all x1, waiting for transfers between devices: 29.5 us -> 36.3 us  [local(): lax.all_to_all(input_part.astype(jnp.bfloat16).reshape(num_rows, head_gro...]
    dot_general x1, matrix products: 1.85 us -> 5.91 us  [local(): lax.dot_general(d_query_b, full_b, (((1,), (1,)), ((), ())), preferred_el...]
    unnamed x75 -> x81, local copies, waits for them, and re-layouts: 19 us -> 20.5 us
  transfers between devices with their start and end apart: 9 -> 9, of which waited for: 7 -> 7; matrix products, arithmetic and copies ran while one was open for 24% -> 23% of each run, Pallas kernels for 0% -> 0%
where the time goes in v10:
time: 397 us; the launch traced here: 392 us
  waiting for transfers between devices  196 us (49%)
  matrix products  59.6 us (15%)
  blocking collectives  44.9 us (11%)
  local copies, waits for them, and re-layouts  38.3 us (10%)
  other arithmetic  23.7 us (6%)
  between operations  15 us (4%)
  starting transfers between devices  14.9 us (4%)
    all_gather x1, waiting for transfers between devices, local(): full_a = lax.all_gather(local_a, rows_axes, axis=0, tiled=True)  69.1 us
    all_to_all x1, blocking collectives, local(): cols_part = lax.all_to_all(own_rows, rows_axes, 1, 0, tiled=True)  44.9 us
    all_to_all x1, waiting for transfers between devices, local(): lax.all_to_all(late_spread, rows_axes, 0, 0, tiled=False)  42.9 us
    all_to_all x1, waiting for transfers between devices, local(): lax.all_to_all(input_part.astype(jnp.bfloat16).reshape(num_rows, head_gro...  36.3 us
    all_gather x1, waiting for transfers between devices, local(): early_all = lax.all_gather(d_query_a, rows_axes, axis=0, tiled=True)  24.1 us
    unnamed x81, local copies, waits for them, and re-layouts  20.5 us
    all_to_all x1, waiting for transfers between devices, local(): cols_all = lax.all_to_all(spread, 'head', 0, 0, tiled=False)  14.5 us
    dot_general x2, matrix products, attend_whole(): jnp.einsum('rhd,kd->hrk', dout_rows, value_all, preferred_element_type=jn...  9.16 us
  transfers between devices with their start and end apart: 9, of which 7 were waited for; matrix products, arithmetic and copies ran while one was open for 23% of the time, Pallas kernels for 0%

profile of v10, /device:TPU:0, one launch (start us, length us, event | category | flops | bytes accessed | tf_op | source)
XLA Modules:
  0.0 392.0 jit_solution(13445292392469701661)
XLA Ops:
  7.2 1.2 slice.77
  8.5 1.9 pad_maximum_fusion
  10.6 44.9 %all_to_all.34 = bf16[96,8,512]{2,0,1:T(8,128)(2,1)} all-to-all(bf16[96,8,512]{2,0,1:T(8,128)(2,1)S(1)} %bitcast.174), channel_id=1, replica_groups=mesh['dp'=4,'ctx'=2,'head'=4] {'dp','ctx'}, dimensions={1} | all-to-all | bytes 1572864 | tf_op jit(solution)/shard_map/all_to_all | solution.py:208
  55.5 69.1 %all-gather.5.cloned.1.call-done = bf16[4096,768]{1,0:T(8,128)(2,1)} async-done(((bf16[512,768]{1,0:T(8,128)(2,1)}), bf16[4096,768]{1,0:T(8,128)(2,1)}) %all-gather.5.cloned.1.call-update) | async-done | bytes 6291472 | tf_op jit(solution)/shard_map/all_gather | solution.py:203
  124.6 1.9 slice.90
  126.7 2.3 copy.132
  128.9 1.9 fusion.63
  130.9 1.9 copy.195
  132.8 1.0 copy.198
  134.3 1.5 multiply_cosine_fusion
  135.8 5.6 %convolution_bitcast_fusion = f32[384,768]{0,1:T(8,128)S(1)} fusion(bf16[4096,768]{1,0:T(8,128)(2,1)} %all-gather.5.cloned.1.call-done, bf16[384,4096]{1,0:T(8,128)(2,1)S(1)} %copy-done), kind=kOutput, calls=%fused_computation.28 | convolution fusion | flops 2415919104 | bytes 10616832 | tf_op jit(solution)/shard_map/dot_general | solution.py:221
  142.0 0.6 copy-done.25
  142.6 0.7 pad_maximum_fusion.6
  143.8 0.9 fusion.65
  144.7 2.2 copy.193
  146.9 2.1 copy.194
  149.0 3.1 broadcast_in_dim.82
  152.1 4.6 %all-to-all-start.1 = ((bf16[4,768,512]{2,1,0:T(8,128)(2,1)}), bf16[4,768,512]{2,1,0:T(8,128)(2,1)}, u32[]{:S(2)}, u32[]{:S(2)}) async-start(bf16[4,768,512]{2,1,0:T(8,128)(2,1)} %broadcast_in_dim.82), calls=%async_computation.1 | async-start | bytes 6291456 | tf_op jit(solution)/shard_map/all_to_all | solution.py:215
  157.0 1.7 subtract_convert_fusion.3
  158.7 1.6 maximum_select_fusion
  160.3 1.2 fusion.14
  161.5 1.2 select_reduce_fusion.1
  162.7 2.4 bitcast_convert_fusion.1
  165.2 2.3 copy.167
  167.4 1.5 multiply_reduce_fusion.1
  169.0 4.5 %fusion.10 = bf16[4,384,768]{1,2,0:T(8,128)(2,1)S(1)} fusion(f32[768,384,4]{1,0,2:T(8,128)} %copy-done.2, f32[4,384]{1,0:T(4,128)S(1)} %multiply_reduce_fusion.1, f32[4,384]{1,0:T(4,128)S(1)} %log_add_fusion.1, pred[384,768]{0,1:T(8,128)(4,1)S(1)} %fusion.20, bf16[768,256]{0,1:T(8,128)(2,1)} %copy-done.13, bf16[384,8,128]{0,2,1:T(8,128)(2,1)} %bitcast.167), kind=kOutput, calls=%fused_computation.15 | convolution fusion | flops 311427072 | bytes 7974912 | tf_op jit(solution)/shard_map/rhd,kd->hrk/dot_general | solution.py:90
  173.5 1.4 copy-done.6
  174.9 1.1 convolution_bitcast_fusion.2
  176.4 1.0 pad_maximum_fusion.3
  177.3 1.9 copy.137
  179.3 14.5 %all-to-all-done.1 = bf16[4,768,512]{2,1,0:T(8,128)(2,1)} async-done(((bf16[4,768,512]{2,1,0:T(8,128)(2,1)}), bf16[4,768,512]{2,1,0:T(8,128)(2,1)}, u32[]{:S(2)}, u32[]{:S(2)}) %all-to-all-start.1) | async-done | bytes 3145760 | tf_op jit(solution)/shard_map/all_to_all | solution.py:215
  193.8 3.9 copy.138
  197.7 0.7 all-gather.7.cloned.1.call-done
  198.4 4.6 %fusion.67 = f32[512,384]{1,0:T(8,128)S(1)} fusion(bf16[4096,512]{1,0:T(8,128)(2,1)} %all-gather.7.cloned.1.call-done, bf16[384,4096]{1,0:T(8,128)(2,1)S(1)} %copy-done), kind=kOutput, calls=%fused_computation.128 | convolution fusion | flops 1610612736 | bytes 8126464 | tf_op jit(solution)/shard_map/dot_general | solution.py:252
  203.6 1.2 subtract_convert_fusion.1
  204.8 1.5 fusion.15
  206.3 1.2 select_reduce_fusion
  207.5 2.1 bitcast_convert_fusion
  210.3 4.6 %fusion.5 = bf16[4,384,768]{1,2,0:T(8,128)(2,1)S(1)} fusion(f32[768,384,4]{1,0,2:T(8,128)} %copy-done.3, f32[4,384]{1,0:T(4,128)S(1)} %multiply_reduce_fusion, f32[4,384]{1,0:T(4,128)S(1)} %log_add_fusion, pred[384,768]{0,1:T(8,128)(4,1)S(1)} %fusion.20, bf16[768,256]{0,1:T(8,128)(2,1)S(1)} %copy-done.15, bf16[384,8,128]{0,2,1:T(8,128)(2,1)} %bitcast.168), kind=kOutput, calls=%fused_computation.7 | convolution fusion | flops 311427072 | bytes 7974912 | tf_op jit(solution)/shard_map/rhd,kd->hrk/dot_general | solution.py:90
  214.9 1.0 convolution_bitcast_fusion.5
  216.0 1.0 fusion.18
  217.0 1.6 convolution_bitcast_fusion.3
  218.7 1.7 fusion.19
  220.4 0.8 fusion.27
  221.2 1.0 collective-permute-start.1
  222.1 1.1 convolution_bitcast_fusion.1
  224.0 7.6 %collective-permute-done.1 = f32[384,256]{0,1:T(8,128)} collective-permute-done((f32[384,256]{0,1:T(8,128)}, f32[384,256]{0,1:T(8,128)}, u32[]{:S(2)}, u32[]{:S(2)}) %collective-permute-start.1) | collective-permute-done | bytes 393248 | tf_op jit(solution)/shard_map/ppermute | solution.py:269
  231.6 1.0 fusion.29
  233.2 8.7 %fusion.21 = f32[384,4096]{1,0:T(8,128)} fusion(bf16[4096,768]{1,0:T(8,128)(2,1)} %all-gather.5.cloned.1.call-done, bf16[384,128]{0,1:T(8,128)(2,1)S(1)} %slice.163, bf16[384,128]{0,1:T(8,128)(2,1)S(1)} %maximum_bitcast_fusion.1, bf16[384,512]{0,1:T(8,128)(2,1)S(1)} %bitcast.177), kind=kOutput, calls=%fused_computation.58 | convolution fusion | flops 2417688576 | bytes 13172736 | tf_op jit(solution)/shard_map/dot_general | solution.py:276
  241.9 24.1 %all-gather.9.cloned.1.call-done = bf16[3072,512]{0,1:T(8,128)(2,1)} async-done(((bf16[384,512]{0,1:T(8,128)(2,1)}), bf16[3072,512]{0,1:T(8,128)(2,1)}) %all-gather.9.cloned.1.call-update) | async-done | bytes 3145744 | tf_op jit(solution)/shard_map/all_gather | solution.py:251
  266.0 5.9 %add_convert_fusion = bf16[384,4096]{1,0:T(8,128)(2,1)S(1)} fusion(f32[384,4096]{1,0:T(8,128)} %fusion.21, bf16[384,512]{0,1:T(8,128)(2,1)S(1)} %bitcast.164, bf16[4096,512]{1,0:T(8,128)(2,1)} %all-gather.7.cloned.1.call-done), kind=kOutput, calls=%fused_computation.4 | convolution fusion | flops 1613758464 | bytes 14024704 | tf_op jit(solution)/shard_map/dot_general | solution.py:280
  271.9 2.1 copy.203
  274.0 3.8 all-to-all-start.2
  278.5 36.3 %all-to-all-done.2 = bf16[384,4,1024]{2,0,1:T(8,128)(2,1)S(1)} async-done(((bf16[384,4,1024]{2,0,1:T(8,128)(2,1)}), bf16[384,4,1024]{2,0,1:T(8,128)(2,1)S(1)}, u32[]{:S(2)}, u32[]{:S(2)}) %all-to-all-start.2) | async-done | bytes 3145760 | tf_op jit(solution)/shard_map/all_to_all | solution.py:297
  314.9 1.5 copy-done.5
  316.4 1.2 broadcast_in_dim.84
  317.7 4.6 %all-to-all-start.3 = ((bf16[8,384,256]{2,1,0:T(8,128)(2,1)}), bf16[8,384,256]{2,1,0:T(8,128)(2,1)}, u32[]{:S(2)}, u32[]{:S(2)}) async-start(bf16[8,384,256]{2,1,0:T(8,128)(2,1)} %broadcast_in_dim.84), calls=%async_computation.3 | async-start | bytes 3145728 | tf_op jit(solution)/shard_map/all_to_all | solution.py:304
  322.2 2.1 pad_maximum_fusion.1
  324.3 2.3 copy.158
  326.6 3.6 reduce_sum.42
  330.2 42.9 %all-to-all-done.3 = bf16[8,384,256]{2,1,0:T(8,128)(2,1)} async-done(((bf16[8,384,256]{2,1,0:T(8,128)(2,1)}), bf16[8,384,256]{2,1,0:T(8,128)(2,1)}, u32[]{:S(2)}, u32[]{:S(2)}) %all-to-all-start.3) | async-done | bytes 1572896 | tf_op jit(solution)/shard_map/all_to_all | solution.py:304
  373.1 2.4 fusion.68
  375.5 0.8 fusion.66
  376.4 8.7 %fusion = f32[512,1024]{1,0:T(8,128)} fusion(bf16[3072,512]{1,0:T(8,128)(2,1)} %bitcast.161, bf16[3072,512]{0,1:T(8,128)(2,1)} %all-gather.11.cloned.1.call-done, bf16[3072,512]{0,1:T(8,128)(2,1)} %all-gather.9.cloned.1.call-done), kind=kOutput, calls=%fused_computation | convolution fusion | flops 3233808384 | bytes 11534336 | tf_op jit(solution)/shard_map/dot_general | solution.py:284
  (111 shorter events, 5.9 us)
Async XLA Ops:
  7.2 3.3 copy-start
  7.2 119.3 %copy-start.30 = (s32[1,8]{1,0:T(1,128)S(1)}, s32[1,8]{1,0:T(1,128)}, u32[]{:S(2)}) copy-start(s32[1,8]{1,0:T(1,128)} %param.10) | copy-start | bytes 100
  7.2 117.4 %all-gather.5.cloned.1.call-start = ((), (), s32[]{:S(2)}) async-start(), calls=%async_computation.4 | async-start | bytes 7077888 | tf_op jit(solution)/shard_map/all_gather | solution.py:203
  10.4 188.0 %all-gather.7.cloned.1.call-start = ((), (), s32[]{:S(2)}) async-start(), calls=%async_computation.5 | async-start | bytes 4718592 | tf_op jit(solution)/shard_map/all_gather | solution.py:249
  141.9 0.6 copy-start.25
  143.3 15.4 %collective-permute-start = (bf16[384,256]{0,1:T(8,128)(2,1)}, bf16[384,256]{0,1:T(8,128)(2,1)}, u32[]{:S(2)}, u32[]{:S(2)}) collective-permute-start(bf16[384,256]{0,1:T(8,128)(2,1)} %pad_maximum_fusion.6), channel_id=1, source_target_pairs={{0,4},{4,0},{1,5},{5,1},{2,6},{6,2},{3,7},{7,3},{8,12},{12,8},{9,1... | collective-permute-start | bytes 589832 | tf_op jit(solution)/shard_map/ppermute | solution.py:232
  152.1 41.6 %all-to-all-start.1 = ((bf16[4,768,512]{2,1,0:T(8,128)(2,1)}), bf16[4,768,512]{2,1,0:T(8,128)(2,1)}, u32[]{:S(2)}, u32[]{:S(2)}) async-start(bf16[4,768,512]{2,1,0:T(8,128)(2,1)} %broadcast_in_dim.82), calls=%async_computation.1 | async-start | bytes 6291456 | tf_op jit(solution)/shard_map/all_to_all | solution.py:215
  156.8 109.2 %all-gather.9.cloned.1.call-start = ((), (), s32[]{:S(2)}) async-start(), calls=%async_computation.6 | async-start | bytes 3538944 | tf_op jit(solution)/shard_map/all_gather | solution.py:251
  158.7 1.6 copy-start.18
  158.7 2.8 copy-start.20
  160.2 2.5 copy-start.13
  161.5 3.6 copy-start.2
  169.0 5.9 %copy-start.14 = (bf16[768,256]{0,1:T(8,128)(2,1)S(1)}, bf16[768,256]{0,1:T(8,128)(2,1)}, u32[]{:S(2)}) copy-start(bf16[768,256]{0,1:T(8,128)(2,1)} %copy-done.13) | copy-start | bytes 1179652
  169.0 7.0 %copy-start.8 = (f32[384,64]{1,0:T(8,128)S(1)}, f32[384,64]{1,0:T(8,128)}, u32[]{:S(2)}) copy-start(f32[384,64]{1,0:T(8,128)} %get-tuple-element.70) | copy-start | bytes 294916
  169.0 7.0 %copy-start.10 = (f32[384,64]{1,0:T(8,128)S(1)}, f32[384,64]{1,0:T(8,128)}, u32[]{:S(2)}) copy-start(f32[384,64]{1,0:T(8,128)} %get-tuple-element.71) | copy-start | bytes 294916
  173.5 1.4 copy-start.6
  202.9 1.9 copy-start.15
  204.8 2.7 copy-start.16
  206.3 3.4 copy-start.3
  207.5 2.4 copy-start.24
  209.9 7.0 %slice-start.2 = ((s8[4718592]{0:T(1024)(128)(4,1)}), s8[4194304]{0:T(1024)(128)(4,1)S(1)}, s32[]{:S(2)}) async-start(s8[4718592]{0:T(1024)(128)(4,1)} %bitcast.158), calls=%async_computation.10 | async-start | bytes 8388608
  210.2 4.7 %copy-start.17 = (bf16[384,4,64]{2,0,1:T(8,128)(2,1)S(1)}, bf16[384,4,64]{2,0,1:T(8,128)(2,1)}, u32[]{:S(2)}) copy-start(bf16[384,4,64]{2,0,1:T(8,128)(2,1)} %copy-done.16) | copy-start | bytes 589828
  210.2 5.7 %copy-start.7 = (bf16[4,384,768]{1,2,0:T(8,128)(2,1)S(1)}, bf16[4,384,768]{1,2,0:T(8,128)(2,1)}, u32[]{:S(2)}) copy-start(bf16[4,384,768]{1,2,0:T(8,128)(2,1)} %copy-done.6) | copy-start | bytes 7077892
  210.2 5.7 %copy-start.19 = (bf16[384,4,64]{2,0,1:T(8,128)(2,1)S(1)}, bf16[384,4,64]{2,0,1:T(8,128)(2,1)}, u32[]{:S(2)}) copy-start(bf16[384,4,64]{2,0,1:T(8,128)(2,1)} %copy-done.18) | copy-start | bytes 589828
  210.2 5.7 %copy-start.21 = (bf16[384,4,64]{2,0,1:T(8,128)(2,1)S(1)}, bf16[384,4,64]{2,0,1:T(8,128)(2,1)}, u32[]{:S(2)}) copy-start(bf16[384,4,64]{2,0,1:T(8,128)(2,1)} %copy-done.20) | copy-start | bytes 589828
  210.3 6.7 %slice-start.3 = ((s8[4718592]{0:T(1024)(128)(4,1)}), s8[524288]{0:T(1024)(128)(4,1)S(1)}, s32[]{:S(2)}) async-start(s8[4718592]{0:T(1024)(128)(4,1)} %bitcast.158), calls=%async_computation.11 | async-start | bytes 1048576
  214.9 2.0 copy-start.22
  216.0 2.7 slice-start
  217.0 1.7 slice-start.1
  218.7 4.5 %copy-start.9 = (f32[384,64]{1,0:T(8,128)S(1)}, f32[384,64]{1,0:T(8,128)}, u32[]{:S(2)}) copy-start(f32[384,64]{1,0:T(8,128)} %get-tuple-element.70) | copy-start | bytes 294916
  218.7 4.5 %copy-start.11 = (f32[384,64]{1,0:T(8,128)S(1)}, f32[384,64]{1,0:T(8,128)}, u32[]{:S(2)}) copy-start(f32[384,64]{1,0:T(8,128)} %get-tuple-element.71) | copy-start | bytes 294916
  221.2 12.0 %copy-start.23 = (bf16[384,4,128]{0,2,1:T(8,128)(2,1)S(1)}, bf16[384,4,128]{0,2,1:T(8,128)(2,1)}, u32[]{:S(2)}) copy-start(bf16[384,4,128]{0,2,1:T(8,128)(2,1)} %copy.137) | copy-start | bytes 1179652
  221.2 10.5 %collective-permute-start.1 = (f32[384,256]{0,1:T(8,128)}, f32[384,256]{0,1:T(8,128)}, u32[]{:S(2)}, u32[]{:S(2)}) collective-permute-start(f32[384,256]{0,1:T(8,128)} %fusion.27), channel_id=1, source_target_pairs={{0,4},{4,0},{1,5},{5,1},{2,6},{6,2},{3,7},{7,3},{8,12},{12,8},{9,1... | collective-permute-start | bytes 1179656 | tf_op jit(solution)/shard_map/ppermute | solution.py:269
  224.0 42.0 %copy-start.12 = (bf16[384,4,128]{0,2,1:T(8,128)(2,1)}, bf16[384,4,128]{0,2,1:T(8,128)(2,1)S(1)}, u32[]{:S(2)}) copy-start(bf16[384,4,128]{0,2,1:T(8,128)(2,1)S(1)} %copy.155) | copy-start | bytes 1179652
  232.7 9.2 %copy-start.26 = (bf16[384,128]{0,1:T(8,128)(2,1)}, bf16[384,128]{0,1:T(8,128)(2,1)S(1)}, u32[]{:S(2)}) copy-start(bf16[384,128]{0,1:T(8,128)(2,1)S(1)} %slice.163) | copy-start | bytes 294916
  233.2 8.7 %copy-start.28 = (bf16[384,128]{0,1:T(8,128)(2,1)}, bf16[384,128]{0,1:T(8,128)(2,1)S(1)}, u32[]{:S(2)}) copy-start(bf16[384,128]{0,1:T(8,128)(2,1)S(1)} %maximum_bitcast_fusion.1) | copy-start | bytes 294916
  274.0 4.4 %copy-start.27 = (bf16[384,128]{0,1:T(8,128)(2,1)S(1)}, bf16[384,128]{0,1:T(8,128)(2,1)}, u32[]{:S(2)}) copy-start(bf16[384,128]{0,1:T(8,128)(2,1)} %copy-done.26) | copy-start | bytes 294916
  274.0 4.4 %copy-start.29 = (bf16[384,128]{0,1:T(8,128)(2,1)S(1)}, bf16[384,128]{0,1:T(8,128)(2,1)}, u32[]{:S(2)}) copy-start(bf16[384,128]{0,1:T(8,128)(2,1)} %copy-done.28) | copy-start | bytes 294916
  274.0 40.7 %all-to-all-start.2 = ((bf16[384,4,1024]{2,0,1:T(8,128)(2,1)}), bf16[384,4,1024]{2,0,1:T(8,128)(2,1)S(1)}, u32[]{:S(2)}, u32[]{:S(2)}) async-start(bf16[384,4,1024]{2,0,1:T(8,128)(2,1)} %bitcast.163), calls=%async_computation.2 | async-start | bytes 6291456 | tf_op jit(solution)/shard_map/all_to_all | solution.py:297
  277.8 98.5 %all-gather.11.cloned.1.call-start = ((), (), s32[]{:S(2)}) async-start(), calls=%async_computation.7 | async-start | bytes 3538944 | tf_op jit(solution)/shard_map/all_gather | solution.py:261
  314.7 1.7 copy-start.5
  317.7 55.4 %copy-start.4 = (bf16[8,4,96,512]{3,2,1,0:T(8,128)(2,1)S(1)}, bf16[8,4,96,512]{3,2,1,0:T(8,128)(2,1)}, u32[]{:S(2)}) copy-start(bf16[8,4,96,512]{3,2,1,0:T(8,128)(2,1)} %copy.138) | copy-start | bytes 9437188
  317.7 55.4 %all-to-all-start.3 = ((bf16[8,384,256]{2,1,0:T(8,128)(2,1)}), bf16[8,384,256]{2,1,0:T(8,128)(2,1)}, u32[]{:S(2)}, u32[]{:S(2)}) async-start(bf16[8,384,256]{2,1,0:T(8,128)(2,1)} %broadcast_in_dim.84), calls=%async_computation.3 | async-start | bytes 3145728 | tf_op jit(solution)/shard_map/all_to_all | solution.py:304
  376.4 8.7 %copy-start.1 = (bf16[384,4096]{1,0:T(8,128)(2,1)S(1)}, bf16[384,4096]{1,0:T(8,128)(2,1)}, u32[]{:S(2)}) copy-start(bf16[384,4096]{1,0:T(8,128)(2,1)} %param.6) | copy-start | bytes 9437188
Sparse Core Ops, SparseCore 0:
  10.8 113.7 all-gather.4
  126.7 71.6 all-gather.6
  203.7 62.2 all-gather.8
  280.4 85.5 all-gather.10

commit v11 on v8

--- a/solution.py
+++ b/solution.py
@@ -206,6 +206,11 @@
         quarter = num_rows // head_groups
         own_rows = lax.dynamic_slice_in_dim(hidden_in, lax.axis_index("head") * quarter, quarter, 0)
         cols_part = lax.all_to_all(own_rows, rows_axes, 1, 0, tiled=True)
+    else:
+        cols_part = lax.all_to_all(hidden_in, rows_axes, 1, 0, tiled=True)
+    full_a, w_query, cols_part = lax.optimization_barrier((full_a, w_query, cols_part))
+    hidden_cols = cols_part
+    if split_rows:
         spread = jnp.broadcast_to(cols_part[None], (head_groups,) + cols_part.shape)
         cols_all = lax.all_to_all(spread, "head", 0, 0, tiled=False)
         hidden_cols = (
@@ -213,9 +218,6 @@
             .transpose(1, 0, 2, 3)
             .reshape(group_count * num_rows, -1)
         )
-    else:
-        hidden_cols = lax.all_to_all(hidden_in, rows_axes, 1, 0, tiled=True)
-    full_a, w_query, hidden_cols = lax.optimization_barrier((full_a, w_query, hidden_cols))
     proj_a = jnp.dot(hidden_in, full_a, preferred_element_type=jnp.float32)
     query_a = rotate(
         proj_a[:, :first_cols].reshape(num_rows, first_heads, 128), cosine, sine_table
@@ -245,7 +247,7 @@
     if first_heads < head_count:
         w_rest = w_query[:, first_cols:]
         full_b = lax.all_gather(w_rest, rows_axes, axis=0, tiled=True)
-        d_query_a, full_b = lax.optimization_barrier((d_query_a, full_b))
+        d_query_a, full_b, hidden_cols = lax.optimization_barrier((d_query_a, full_b, hidden_cols))
         early_all = lax.all_gather(d_query_a, rows_axes, axis=0, tiled=True)
         proj_b = jnp.dot(hidden_in, full_b, preferred_element_type=jnp.float32)
         query_b = rotate(
@@ -254,11 +256,9 @@
         out_b, grad_qb, part_kb, part_vb = attend(
             query_b, *shared, dout_rows[:, first_heads:], *masks
         )
-        early_all, part_kb, part_vb = lax.optimization_barrier((early_all, part_kb, part_vb))
+        d_query_b = unrotate(grad_qb, cosine, sine_table).astype(jnp.bfloat16).reshape(num_rows, -1)
         part_k, part_v = part_k + part_kb, part_v + part_vb
         out_parts.append(out_b)
-        d_query_b = unrotate(grad_qb, cosine, sine_table).astype(jnp.bfloat16).reshape(num_rows, -1)
-        d_query_parts.append(d_query_b)
     attended = jnp.concatenate(out_parts, 1).reshape(num_rows, query_cols)
     parts_kv = jnp.concatenate([part_k, part_v], 1)
     if ctx_count == 2:

time: 394 us -> 371 us (0.942)
  blocking collectives: 84.3 us -> 44.9 us
  waiting for transfers between devices: 160 us -> 176 us
  matrix products: 57.4 us -> 51.4 us
  starting transfers between devices: 6.59 us -> 10.9 us
    all_gather x1, waiting for transfers between devices: 27.4 us -> 69.1 us  [local(): full_a = lax.all_gather(local_a, rows_axes, axis=0, tiled=True)]
    all_gather x1, waiting for transfers between devices: 41 us -> 0.01 us  [local(): early_all = lax.all_gather(d_query_a, rows_axes, axis=0, tiled=True)]
    all_to_all x1 -> x0, blocking collectives: 39.5 us -> none  [local(): cols_all = lax.all_to_all(spread, 'head', 0, 0, tiled=False)]
    all_gather x1, waiting for transfers between devices: 28.1 us -> 0.67 us  [local(): full_b = lax.all_gather(w_rest, rows_axes, axis=0, tiled=True)]
    all_gather x1, waiting for transfers between devices: 28 us -> 52.1 us  [local(): late_all = lax.all_gather(late_proj, rows_axes, axis=0, tiled=True)]
    all_to_all x0 -> x1, waiting for transfers between devices: none -> 14.1 us  [local(): cols_all = lax.all_to_all(spread, 'head', 0, 0, tiled=False)]
    all_to_all x1, waiting for transfers between devices: 27 us -> 32.6 us  [local(): lax.all_to_all(input_part.astype(jnp.bfloat16).reshape(num_rows, head_gro...]
    all_to_all x0 -> x1, starting transfers between devices: none -> 4.64 us  [local(): cols_all = lax.all_to_all(spread, 'head', 0, 0, tiled=False)]
  transfers between devices with their start and end apart: 7 -> 8, of which waited for: 6 -> 6; matrix products, arithmetic and copies ran while one was open for 22% -> 26% of each run, Pallas kernels for 0% -> 0%
where the time goes in v11:
time: 371 us; the launch traced here: 366 us
  waiting for transfers between devices  176 us (47%)
  matrix products  51.4 us (14%)
  blocking collectives  44.9 us (12%)
  local copies, waits for them, and re-layouts  42 us (11%)
  other arithmetic  25.6 us (7%)
  between operations  14.8 us (4%)
  starting transfers between devices  10.9 us (3%)
    all_gather x1, waiting for transfers between devices, local(): full_a = lax.all_gather(local_a, rows_axes, axis=0, tiled=True)  69.1 us
    all_gather x1, waiting for transfers between devices, local(): late_all = lax.all_gather(late_proj, rows_axes, axis=0, tiled=True)  52.1 us
    all_to_all x1, blocking collectives, local(): cols_part = lax.all_to_all(own_rows, rows_axes, 1, 0, tiled=True)  44.9 us
    all_to_all x1, waiting for transfers between devices, local(): lax.all_to_all(input_part.astype(jnp.bfloat16).reshape(num_rows, head_gro...  32.6 us
    unnamed x75, local copies, waits for them, and re-layouts  24.5 us
    all_to_all x1, waiting for transfers between devices, local(): cols_all = lax.all_to_all(spread, 'head', 0, 0, tiled=False)  14.1 us
    dot_general x2, matrix products, attend_whole(): jnp.einsum('rhd,kd->hrk', dout_rows, value_all, preferred_element_type=jn...  9.04 us
    ppermute x1, waiting for transfers between devices, local(): grad_kv = own_part + lax.ppermute(away_part, 'ctx', [(0, 1), (1, 0)])  7.58 us
  transfers between devices with their start and end apart: 8, of which 6 were waited for; matrix products, arithmetic and copies ran while one was open for 26% of the time, Pallas kernels for 0%

profile of v11, /device:TPU:0, one launch (start us, length us, event | category | flops | bytes accessed | tf_op | source)
XLA Modules:
  0.0 365.9 jit_solution(17147263962423661276)
XLA Ops:
  7.2 1.2 slice.83
  8.5 1.9 pad_maximum_fusion.1
  10.6 44.9 %all_to_all.29 = bf16[96,8,512]{2,0,1:T(8,128)(2,1)} all-to-all(bf16[96,8,512]{2,0,1:T(8,128)(2,1)S(1)} %bitcast.174), channel_id=1, replica_groups=mesh['dp'=4,'ctx'=2,'head'=4] {'dp','ctx'}, dimensions={1} | all-to-all | bytes 1572864 | tf_op jit(solution)/shard_map/all_to_all | solution.py:208
  55.5 69.1 %all-gather.5.cloned.1.call-done = bf16[4096,768]{1,0:T(8,128)(2,1)} async-done(((bf16[512,768]{1,0:T(8,128)(2,1)}), bf16[4096,768]{1,0:T(8,128)(2,1)}) %all-gather.5.cloned.1.call-update) | async-done | bytes 6291472 | tf_op jit(solution)/shard_map/all_gather | solution.py:203
  124.6 1.9 slice.96
  126.7 2.3 copy.138
  129.0 1.9 fusion.55
  130.9 1.9 copy.205
  132.9 0.9 copy.202
  134.3 1.5 multiply_cosine_fusion
  135.8 5.6 %convolution_bitcast_fusion = f32[384,768]{0,1:T(8,128)S(1)} fusion(bf16[4096,768]{1,0:T(8,128)(2,1)} %all-gather.5.cloned.1.call-done, bf16[384,4096]{1,0:T(8,128)(2,1)S(1)} %copy-done), kind=kOutput, calls=%fused_computation.25 | convolution fusion | flops 2415919104 | bytes 10616832 | tf_op jit(solution)/shard_map/dot_general | solution.py:221
  142.6 0.7 pad_maximum_fusion.12
  143.8 1.0 fusion.57
  144.8 2.2 copy.201
  146.9 2.1 copy.200
  149.1 3.1 broadcast_in_dim.76
  152.1 4.6 %all-to-all-start.1 = ((bf16[4,768,512]{2,1,0:T(8,128)(2,1)}), bf16[4,768,512]{2,1,0:T(8,128)(2,1)}, u32[]{:S(2)}, u32[]{:S(2)}) async-start(bf16[4,768,512]{2,1,0:T(8,128)(2,1)} %broadcast_in_dim.76), calls=%async_computation.1 | async-start | bytes 6291456 | tf_op jit(solution)/shard_map/all_to_all | solution.py:215
  157.4 1.8 subtract_convert_fusion.3
  159.2 1.5 maximum_select_fusion
  160.7 1.2 fusion.10
  161.9 1.2 select_reduce_fusion.1
  163.1 2.4 bitcast_convert_fusion.1
  165.6 2.3 copy.174
  167.9 1.5 multiply_reduce_fusion.1
  169.4 4.5 %fusion.6 = bf16[4,384,768]{1,2,0:T(8,128)(2,1)S(1)} fusion(f32[768,384,4]{1,0,2:T(8,128)} %copy-done.2, f32[4,384]{1,0:T(4,128)S(1)} %multiply_reduce_fusion.1, f32[4,384]{1,0:T(4,128)S(1)} %log_add_fusion.1, pred[384,768]{0,1:T(8,128)(4,1)S(1)} %fusion.16, bf16[768,256]{0,1:T(8,128)(2,1)} %copy-done.11, bf16[384,8,128]{0,2,1:T(8,128)(2,1)} %bitcast.167), kind=kOutput, calls=%fused_computation.11 | convolution fusion | flops 311427072 | bytes 7974912 | tf_op jit(solution)/shard_map/rhd,kd->hrk/dot_general | solution.py:90
  174.0 1.4 copy-done.4
  175.3 1.1 convolution_bitcast_fusion.2
  176.8 1.0 pad_maximum_fusion.9
  177.8 1.9 copy.143
  179.7 14.1 %all-to-all-done.1 = bf16[4,768,512]{2,1,0:T(8,128)(2,1)} async-done(((bf16[4,768,512]{2,1,0:T(8,128)(2,1)}), bf16[4,768,512]{2,1,0:T(8,128)(2,1)}, u32[]{:S(2)}, u32[]{:S(2)}) %all-to-all-start.1) | async-done | bytes 3145760 | tf_op jit(solution)/shard_map/all_to_all | solution.py:215
  193.8 3.9 %copy.144 = bf16[8,4,96,512]{3,2,1,0:T(8,128)(2,1)} copy(bf16[8,4,96,512]{3,2,0,1:T(8,128)(2,1)} %bitcast.25) | data formatting | bytes 6291456 | tf_op jit(solution)/shard_map/transpose | solution.py:218
  197.7 0.7 all-gather.7.cloned.1.call-done
  198.6 4.6 %fusion.58 = f32[512,384]{1,0:T(8,128)S(1)} fusion(bf16[4096,512]{1,0:T(8,128)(2,1)} %all-gather.7.cloned.1.call-done, bf16[384,4096]{1,0:T(8,128)(2,1)S(1)} %copy-done), kind=kOutput, calls=%fused_computation.123 | convolution fusion | flops 1610612736 | bytes 8126464 | tf_op jit(solution)/shard_map/dot_general | solution.py:252
  203.8 1.2 subtract_convert_fusion.1
  205.0 1.2 fusion.11
  206.3 1.2 select_reduce_fusion
  207.5 2.1 bitcast_convert_fusion
  210.2 4.5 %fusion.1 = bf16[4,384,768]{1,2,0:T(8,128)(2,1)S(1)} fusion(f32[768,384,4]{1,0,2:T(8,128)} %copy-done.3, f32[4,384]{1,0:T(4,128)S(1)} %multiply_reduce_fusion, f32[4,384]{1,0:T(4,128)S(1)} %log_add_fusion, pred[384,768]{0,1:T(8,128)(4,1)S(1)} %fusion.16, bf16[768,256]{0,1:T(8,128)(2,1)S(1)} %copy-done.13, bf16[384,8,128]{0,2,1:T(8,128)(2,1)} %bitcast.168), kind=kOutput, calls=%fused_computation.3 | convolution fusion | flops 311427072 | bytes 7974912 | tf_op jit(solution)/shard_map/rhd,kd->hrk/dot_general | solution.py:90
  214.8 1.0 convolution_bitcast_fusion.5
  215.8 1.0 fusion.14
  216.9 1.6 convolution_bitcast_fusion.3
  218.6 1.9 fusion.15
  220.4 0.8 fusion.19
  221.2 0.8 collective-permute-start.1
  222.0 1.1 convolution_bitcast_fusion.1
  223.9 7.6 %collective-permute-done.1 = f32[384,256]{0,1:T(8,128)} collective-permute-done((f32[384,256]{0,1:T(8,128)}, f32[384,256]{0,1:T(8,128)}, u32[]{:S(2)}, u32[]{:S(2)}) %collective-permute-start.1) | collective-permute-done | bytes 393248 | tf_op jit(solution)/shard_map/ppermute | solution.py:267
  231.5 1.1 fusion.21
  233.1 0.9 pad_maximum_fusion.3
  234.0 5.0 %fusion.17 = f32[384,4096]{1,0:T(8,128)S(1)} fusion(bf16[4096,768]{1,0:T(8,128)(2,1)} %all-gather.5.cloned.1.call-done, bf16[384,128]{0,1:T(8,128)(2,1)S(1)} %slice.171, bf16[384,128]{0,1:T(8,128)(2,1)S(1)} %maximum_bitcast_fusion.1, bf16[384,512]{0,1:T(8,128)(2,1)S(1)} %bitcast.177), kind=kOutput, calls=%fused_computation.59 | convolution fusion | flops 2417688576 | bytes 13172736 | tf_op jit(solution)/shard_map/dot_general | solution.py:274
  239.0 1.8 add_convert_fusion
  240.8 2.0 copy.211
  242.9 4.1 %all-to-all-start.2 = ((bf16[384,4,1024]{2,0,1:T(8,128)(2,1)}), bf16[384,4,1024]{2,0,1:T(8,128)(2,1)S(1)}, u32[]{:S(2)}, u32[]{:S(2)}) async-start(bf16[384,4,1024]{2,0,1:T(8,128)(2,1)} %bitcast.161), calls=%async_computation.2 | async-start | bytes 6291456 | tf_op jit(solution)/shard_map/all_to_all | solution.py:292
  247.0 2.0 pad_maximum_fusion.2
  249.0 2.3 copy.164
  251.2 32.6 %all-to-all-done.2 = bf16[384,4,1024]{2,0,1:T(8,128)(2,1)S(1)} async-done(((bf16[384,4,1024]{2,0,1:T(8,128)(2,1)}), bf16[384,4,1024]{2,0,1:T(8,128)(2,1)S(1)}, u32[]{:S(2)}, u32[]{:S(2)}) %all-to-all-start.2) | async-done | bytes 3145760 | tf_op jit(solution)/shard_map/all_to_all | solution.py:292
  283.9 1.7 reduce_sum.42
  285.6 5.8 %fusion.60 = f32[512,512]{0,1:T(8,128)} fusion(bf16[3072,512]{0,1:T(8,128)(2,1)} %all-gather.9.cloned.1.call-done, bf16[3072,512]{1,0:T(8,128)(2,1)} %bitcast.164), kind=kOutput, calls=%fused_computation.125 | convolution fusion | flops 1610612736 | bytes 7340032 | tf_op jit(solution)/shard_map/dot_general | solution.py:282
  291.4 52.1 %all-gather.11.cloned.1.call-done = bf16[3072,768]{0,1:T(8,128)(2,1)} async-done(((bf16[384,768]{0,1:T(8,128)(2,1)}), bf16[3072,768]{0,1:T(8,128)(2,1)}) %all-gather.11.cloned.1.call-update) | async-done | bytes 4718608 | tf_op jit(solution)/shard_map/all_gather | solution.py:297
  343.5 5.0 %fusion.59 = f32[512,768]{1,0:T(8,128)S(1)} fusion(bf16[3072,512]{1,0:T(8,128)(2,1)S(1)} %bitcast.165, bf16[3072,768]{0,1:T(8,128)(2,1)} %all-gather.11.cloned.1.call-done), kind=kOutput, calls=%fused_computation.124 | convolution fusion | flops 2415919104 | bytes 9437184 | tf_op jit(solution)/shard_map/dot_general | solution.py:298
  348.5 0.8 fusion.54
  349.3 1.1 slice.130
  350.4 2.7 copy.206
  353.1 3.1 pad_maximum_fusion
  356.2 2.9 copy.165
  (103 shorter events, 6.3 us)
Async XLA Ops:
  7.2 3.3 copy-start
  7.2 119.3 %copy-start.26 = (s32[1,8]{1,0:T(1,128)S(1)}, s32[1,8]{1,0:T(1,128)}, u32[]{:S(2)}) copy-start(s32[1,8]{1,0:T(1,128)} %param.10) | copy-start | bytes 100
  7.2 117.4 %all-gather.5.cloned.1.call-start = ((), (), s32[]{:S(2)}) async-start(), calls=%async_computation.3 | async-start | bytes 7077888 | tf_op jit(solution)/shard_map/all_gather | solution.py:203
  10.4 188.0 %all-gather.7.cloned.1.call-start = ((), (), s32[]{:S(2)}) async-start(), calls=%async_computation.4 | async-start | bytes 4718592 | tf_op jit(solution)/shard_map/all_gather | solution.py:249
  141.9 0.6 copy-start.24
  143.3 15.9 %collective-permute-start = (bf16[384,256]{0,1:T(8,128)(2,1)}, bf16[384,256]{0,1:T(8,128)(2,1)}, u32[]{:S(2)}, u32[]{:S(2)}) collective-permute-start(bf16[384,256]{0,1:T(8,128)(2,1)} %pad_maximum_fusion.12), channel_id=1, source_target_pairs={{0,4},{4,0},{1,5},{5,1},{2,6},{6,2},{3,7},{7,3},{8,12},{12,8},{9,1... | collective-permute-start | bytes 589832 | tf_op jit(solution)/shard_map/ppermute | solution.py:232
  152.1 41.6 %all-to-all-start.1 = ((bf16[4,768,512]{2,1,0:T(8,128)(2,1)}), bf16[4,768,512]{2,1,0:T(8,128)(2,1)}, u32[]{:S(2)}, u32[]{:S(2)}) async-start(bf16[4,768,512]{2,1,0:T(8,128)(2,1)} %broadcast_in_dim.76), calls=%async_computation.1 | async-start | bytes 6291456 | tf_op jit(solution)/shard_map/all_to_all | solution.py:215
  156.8 128.8 %all-gather.9.cloned.1.call-start = ((), (), s32[]{:S(2)}) async-start(), calls=%async_computation.5 | async-start | bytes 3538944 | tf_op jit(solution)/shard_map/all_gather | solution.py:251
  159.1 1.5 copy-start.16
  159.1 2.8 copy-start.18
  160.7 2.5 copy-start.11
  161.9 3.6 copy-start.2
  169.4 5.9 %copy-start.12 = (bf16[768,256]{0,1:T(8,128)(2,1)S(1)}, bf16[768,256]{0,1:T(8,128)(2,1)}, u32[]{:S(2)}) copy-start(bf16[768,256]{0,1:T(8,128)(2,1)} %copy-done.11) | copy-start | bytes 1179652
  169.4 7.0 %copy-start.6 = (f32[384,64]{1,0:T(8,128)S(1)}, f32[384,64]{1,0:T(8,128)}, u32[]{:S(2)}) copy-start(f32[384,64]{1,0:T(8,128)} %get-tuple-element.62) | copy-start | bytes 294916
  169.4 7.0 %copy-start.8 = (f32[384,64]{1,0:T(8,128)S(1)}, f32[384,64]{1,0:T(8,128)}, u32[]{:S(2)}) copy-start(f32[384,64]{1,0:T(8,128)} %get-tuple-element.63) | copy-start | bytes 294916
  174.0 1.4 copy-start.4
  198.4 145.1 %all-gather.11.cloned.1.call-start = ((), (), s32[]{:S(2)}) async-start(), calls=%async_computation.6 | async-start | bytes 5308416 | tf_op jit(solution)/shard_map/all_gather | solution.py:297
  203.2 1.9 copy-start.13
  205.0 2.4 copy-start.14
  206.3 3.4 copy-start.3
  207.5 2.4 copy-start.23
  209.9 6.9 %slice-start.2 = ((s8[4718592]{0:T(1024)(128)(4,1)}), s8[4194304]{0:T(1024)(128)(4,1)S(1)}, s32[]{:S(2)}) async-start(s8[4718592]{0:T(1024)(128)(4,1)} %bitcast.158), calls=%async_computation.9 | async-start | bytes 8388608
  210.2 4.6 %copy-start.15 = (bf16[384,4,64]{2,0,1:T(8,128)(2,1)S(1)}, bf16[384,4,64]{2,0,1:T(8,128)(2,1)}, u32[]{:S(2)}) copy-start(bf16[384,4,64]{2,0,1:T(8,128)(2,1)} %copy-done.14) | copy-start | bytes 589828
  210.2 5.6 %copy-start.5 = (bf16[4,384,768]{1,2,0:T(8,128)(2,1)S(1)}, bf16[4,384,768]{1,2,0:T(8,128)(2,1)}, u32[]{:S(2)}) copy-start(bf16[4,384,768]{1,2,0:T(8,128)(2,1)} %copy-done.4) | copy-start | bytes 7077892
  210.2 5.6 %copy-start.17 = (bf16[384,4,64]{2,0,1:T(8,128)(2,1)S(1)}, bf16[384,4,64]{2,0,1:T(8,128)(2,1)}, u32[]{:S(2)}) copy-start(bf16[384,4,64]{2,0,1:T(8,128)(2,1)} %copy-done.16) | copy-start | bytes 589828
  210.2 5.6 %copy-start.19 = (bf16[384,4,64]{2,0,1:T(8,128)(2,1)S(1)}, bf16[384,4,64]{2,0,1:T(8,128)(2,1)}, u32[]{:S(2)}) copy-start(bf16[384,4,64]{2,0,1:T(8,128)(2,1)} %copy-done.18) | copy-start | bytes 589828
  210.2 6.6 %slice-start.3 = ((s8[4718592]{0:T(1024)(128)(4,1)}), s8[524288]{0:T(1024)(128)(4,1)S(1)}, s32[]{:S(2)}) async-start(s8[4718592]{0:T(1024)(128)(4,1)} %bitcast.158), calls=%async_computation.10 | async-start | bytes 1048576
  214.8 2.0 copy-start.21
  215.8 2.7 slice-start
  216.8 1.7 slice-start.1
  218.5 4.6 %copy-start.7 = (f32[384,64]{1,0:T(8,128)S(1)}, f32[384,64]{1,0:T(8,128)}, u32[]{:S(2)}) copy-start(f32[384,64]{1,0:T(8,128)} %get-tuple-element.62) | copy-start | bytes 294916
  218.6 4.6 %copy-start.9 = (f32[384,64]{1,0:T(8,128)S(1)}, f32[384,64]{1,0:T(8,128)}, u32[]{:S(2)}) copy-start(f32[384,64]{1,0:T(8,128)} %get-tuple-element.63) | copy-start | bytes 294916
  221.2 10.3 %collective-permute-start.1 = (f32[384,256]{0,1:T(8,128)}, f32[384,256]{0,1:T(8,128)}, u32[]{:S(2)}, u32[]{:S(2)}) collective-permute-start(f32[384,256]{0,1:T(8,128)} %fusion.19), channel_id=1, source_target_pairs={{0,4},{4,0},{1,5},{5,1},{2,6},{6,2},{3,7},{7,3},{8,12},{12,8},{9,1... | collective-permute-start | bytes 1179656 | tf_op jit(solution)/shard_map/ppermute | solution.py:267
  223.1 10.9 %copy-start.22 = (bf16[384,4,128]{0,2,1:T(8,128)(2,1)S(1)}, bf16[384,4,128]{0,2,1:T(8,128)(2,1)}, u32[]{:S(2)}) copy-start(bf16[384,4,128]{0,2,1:T(8,128)(2,1)} %copy.143) | copy-start | bytes 1179652
  234.0 5.0 %copy-start.10 = (bf16[4096,512]{1,0:T(8,128)(2,1)S(1)}, bf16[4096,512]{1,0:T(8,128)(2,1)}, u32[]{:S(2)}) copy-start(bf16[4096,512]{1,0:T(8,128)(2,1)} %all-gather.7.cloned.1.call-done) | copy-start | bytes 12582916
  242.9 4.1 %copy-start.25 = (bf16[128,4,384]{2,0,1:T(8,128)(2,1)S(1)}, bf16[128,4,384]{2,0,1:T(8,128)(2,1)}, u32[]{:S(2)}) copy-start(bf16[128,4,384]{2,0,1:T(8,128)(2,1)} %get-tuple-element.67) | copy-start | bytes 1179652
  242.9 41.0 %all-to-all-start.2 = ((bf16[384,4,1024]{2,0,1:T(8,128)(2,1)}), bf16[384,4,1024]{2,0,1:T(8,128)(2,1)S(1)}, u32[]{:S(2)}, u32[]{:S(2)}) async-start(bf16[384,4,1024]{2,0,1:T(8,128)(2,1)} %bitcast.161), calls=%async_computation.2 | async-start | bytes 6291456 | tf_op jit(solution)/shard_map/all_to_all | solution.py:292
  285.6 57.9 %copy-start.20 = (bf16[8,4,96,512]{3,2,1,0:T(8,128)(2,1)S(1)}, bf16[8,4,96,512]{3,2,1,0:T(8,128)(2,1)}, u32[]{:S(2)}) copy-start(bf16[8,4,96,512]{3,2,1,0:T(8,128)(2,1)} %copy.144) | copy-start | bytes 9437188
  350.4 8.7 %copy-start.1 = (bf16[384,4096]{1,0:T(8,128)(2,1)S(1)}, bf16[384,4096]{1,0:T(8,128)(2,1)}, u32[]{:S(2)}) copy-start(bf16[384,4096]{1,0:T(8,128)(2,1)} %param.6) | copy-start | bytes 9437188
Sparse Core Ops, SparseCore 0:
  10.8 113.7 all-gather.4
  126.7 71.6 all-gather.6
  200.4 61.3 all-gather.8
  264.3 79.1 all-gather.10

commit v12 on v11

--- a/solution.py
+++ b/solution.py
@@ -202,22 +202,39 @@
     local_a = jnp.concatenate([w_query[:, :first_cols], w_key, w_value], 1)
     full_a = lax.all_gather(local_a, rows_axes, axis=0, tiled=True)
     split_rows = num_rows % head_groups == 0
+    dp_count, ctx_count = lax.axis_size("dp"), lax.axis_size("ctx")
+    ctx_index = lax.axis_index("ctx")
     if split_rows:
         quarter = num_rows // head_groups
         own_rows = lax.dynamic_slice_in_dim(hidden_in, lax.axis_index("head") * quarter, quarter, 0)
-        cols_part = lax.all_to_all(own_rows, rows_axes, 1, 0, tiled=True)
+        cols_part = lax.all_to_all(own_rows, "dp", 1, 0, tiled=True)
     else:
-        cols_part = lax.all_to_all(hidden_in, rows_axes, 1, 0, tiled=True)
+        cols_part = lax.all_to_all(hidden_in, "dp", 1, 0, tiled=True)
     full_a, w_query, cols_part = lax.optimization_barrier((full_a, w_query, cols_part))
     hidden_cols = cols_part
     if split_rows:
         spread = jnp.broadcast_to(cols_part[None], (head_groups,) + cols_part.shape)
         cols_all = lax.all_to_all(spread, "head", 0, 0, tiled=False)
         hidden_cols = (
-            cols_all.reshape(head_groups, group_count, quarter, -1)
+            cols_all.reshape(head_groups, dp_count, quarter, -1)
             .transpose(1, 0, 2, 3)
-            .reshape(group_count * num_rows, -1)
-        )
+            .reshape(dp_count * num_rows, -1)
+        )
+    weight_rows = w_query.shape[0]
+
+    def weight_grad(d_rows):
+        gathered = lax.all_gather(d_rows, "dp", axis=0, tiled=True)
+        partial = lax.dot_general(
+            hidden_cols, gathered, (((0,), (0,)), ((), ())), preferred_element_type=jnp.float32
+        )
+        if ctx_count == 2:
+            own_part = lax.dynamic_slice_in_dim(partial, ctx_index * weight_rows, weight_rows, 0)
+            away_part = lax.dynamic_slice_in_dim(
+                partial, (1 - ctx_index) * weight_rows, weight_rows, 0
+            )
+            return own_part + lax.ppermute(away_part, "ctx", [(0, 1), (1, 0)])
+        return lax.psum_scatter(partial, "ctx", scatter_dimension=0, tiled=True)
+
     proj_a = jnp.dot(hidden_in, full_a, preferred_element_type=jnp.float32)
     query_a = rotate(
         proj_a[:, :first_cols].reshape(num_rows, first_heads, 128), cosine, sine_table
@@ -226,7 +243,6 @@
         proj_a[:, first_cols : first_cols + 128].reshape(num_rows, 1, 128), cosine, sine_table
     )[:, 0, :].astype(jnp.bfloat16)
     value_rows = proj_a[:, first_cols + 128 :].astype(jnp.bfloat16)
-    ctx_index, ctx_count = lax.axis_index("ctx"), lax.axis_size("ctx")
     kv_rows = jnp.concatenate([key_rows, value_rows], 1)
     if ctx_count == 2:
         kv_other = lax.ppermute(kv_rows, "ctx", [(0, 1), (1, 0)])
@@ -248,7 +264,7 @@
         w_rest = w_query[:, first_cols:]
         full_b = lax.all_gather(w_rest, rows_axes, axis=0, tiled=True)
         d_query_a, full_b, hidden_cols = lax.optimization_barrier((d_query_a, full_b, hidden_cols))
-        early_all = lax.all_gather(d_query_a, rows_axes, axis=0, tiled=True)
+        early_sum = weight_grad(d_query_a)
         proj_b = jnp.dot(hidden_in, full_b, preferred_element_type=jnp.float32)
         query_b = rotate(
             proj_b.reshape(num_rows, head_count - first_heads, 128), cosine, sine_table
@@ -279,25 +295,16 @@
             d_query_b, full_b, (((1,), (1,)), ((), ())), preferred_element_type=jnp.float32
         )
         late_proj = jnp.concatenate([d_query_b, d_key, d_value], 1)
-        early_sum = lax.dot_general(
-            hidden_cols, early_all, (((0,), (0,)), ((), ())), preferred_element_type=jnp.float32
-        )
     else:
         late_proj = jnp.concatenate([d_key, d_value], 1)
-        early_all = lax.all_gather(d_query_a, rows_axes, axis=0, tiled=True)
-        early_sum = lax.dot_general(
-            hidden_cols, early_all, (((0,), (0,)), ((), ())), preferred_element_type=jnp.float32
-        )
+        early_sum = weight_grad(d_query_a)
     input_cols = input_part.shape[1] // head_groups
     input_split = lax.all_to_all(
         input_part.astype(jnp.bfloat16).reshape(num_rows, head_groups, input_cols),
         "head", 1, 1, tiled=False,
     )
     grad_input = jnp.sum(input_split.astype(jnp.float32), axis=1).astype(jnp.bfloat16)
-    late_all = lax.all_gather(late_proj, rows_axes, axis=0, tiled=True)
-    late_sum = lax.dot_general(
-        hidden_cols, late_all, (((0,), (0,)), ((), ())), preferred_element_type=jnp.float32
-    )
+    late_sum = weight_grad(late_proj)
     query_w = jnp.concatenate([early_sum, late_sum[:, : query_cols - first_cols]], 1)
     rest = late_sum[:, query_cols - first_cols :]
     return (attended, grad_input, query_w, rest[:, :128], rest[:, 128:])

time: 371 us -> 376 us (1.013)
  local copies, waits for them, and re-layouts: 42 us -> 46.7 us
    all_to_all x1, waiting for transfers between devices: 32.6 us -> 0.01 us  [local(): lax.all_to_all(input_part.astype(jnp.bfloat16).reshape(num_rows, head_gro...]
    ppermute x0 -> x2, waiting for transfers between devices: none -> 17.3 us  [weight_grad(): return own_part + lax.ppermute(away_part, 'ctx', [(0, 1), (1, 0)])]
    all_gather x2, waiting for transfers between devices: 52.1 us -> 63.9 us  [weight_grad(): gathered = lax.all_gather(d_rows, 'dp', axis=0, tiled=True)]
    add x0 -> x2, other arithmetic: none -> 3.98 us  [weight_grad(): return own_part + lax.ppermute(away_part, 'ctx', [(0, 1), (1, 0)])]
    unnamed x75 -> x84, local copies, waits for them, and re-layouts: 24.5 us -> 27.6 us
  transfers between devices with their start and end apart: 8 -> 10, of which waited for: 6 -> 7; matrix products, arithmetic and copies ran while one was open for 26% -> 21% of each run, Pallas kernels for 0% -> 0%
where the time goes in v12:
time: 376 us; the launch traced here: 371 us
  waiting for transfers between devices  175 us (47%)
  matrix products  50.5 us (13%)
  local copies, waits for them, and re-layouts  46.7 us (12%)
  blocking collectives  42.6 us (11%)
  other arithmetic  27.5 us (7%)
  between operations  15 us (4%)
  starting transfers between devices  13.3 us (4%)
    all_gather x1, waiting for transfers between devices, local(): full_a = lax.all_gather(local_a, rows_axes, axis=0, tiled=True)  70.5 us
    all_gather x2, waiting for transfers between devices, weight_grad(): gathered = lax.all_gather(d_rows, 'dp', axis=0, tiled=True)  63.9 us
    all_to_all x1, blocking collectives, local(): cols_part = lax.all_to_all(own_rows, 'dp', 1, 0, tiled=True)  42.6 us
    unnamed x84, local copies, waits for them, and re-layouts  27.6 us
    ppermute x2, waiting for transfers between devices, weight_grad(): return own_part + lax.ppermute(away_part, 'ctx', [(0, 1), (1, 0)])  17.3 us
    all_to_all x1, waiting for transfers between devices, local(): cols_all = lax.all_to_all(spread, 'head', 0, 0, tiled=False)  14.5 us
    dot_general x2, matrix products, weight_grad(): lax.dot_general(hidden_cols, gathered, (((0,), (0,)), ((), ())), preferre...  9.35 us
    dot_general x2, matrix products, attend_whole(): jnp.einsum('rhd,kd->hrk', dout_rows, value_all, preferred_element_type=jn...  9.03 us
  transfers between devices with their start and end apart: 10, of which 7 were waited for; matrix products, arithmetic and copies ran while one was open for 21% of the time, Pallas kernels for 0%

profile of v12, /device:TPU:0, one launch (start us, length us, event | category | flops | bytes accessed | tf_op | source)
XLA Modules:
  0.0 371.1 jit_solution(3205117347566148021)
XLA Ops:
  7.2 1.2 slice.83
  8.5 1.9 pad_maximum_fusion.1
  10.6 42.6 %all_to_all.29 = bf16[96,4,1024]{2,0,1:T(8,128)(2,1)} all-to-all(bf16[96,4,1024]{2,0,1:T(8,128)(2,1)S(1)} %bitcast.172), channel_id=1, replica_groups=mesh['dp'=4,'ctx'=2,'head'=4] {'dp'}, dimensions={1} | all-to-all | bytes 1572864 | tf_op jit(solution)/shard_map/all_to_all | solution.py:210
  53.2 70.5 %all-gather.5.cloned.1.call-done = bf16[4096,768]{1,0:T(8,128)(2,1)} async-done(((bf16[512,768]{1,0:T(8,128)(2,1)}), bf16[4096,768]{1,0:T(8,128)(2,1)}) %all-gather.5.cloned.1.call-update) | async-done | bytes 6291472 | tf_op jit(solution)/shard_map/all_gather | solution.py:203
  123.7 1.9 slice.96
  125.8 2.3 copy.142
  128.1 1.9 fusion.55
  130.0 2.0 copy.210
  133.4 1.5 multiply_cosine_fusion
  134.9 5.6 %convolution_bitcast_fusion = f32[384,768]{0,1:T(8,128)S(1)} fusion(bf16[4096,768]{1,0:T(8,128)(2,1)} %all-gather.5.cloned.1.call-done, bf16[384,4096]{1,0:T(8,128)(2,1)S(1)} %copy-done), kind=kOutput, calls=%fused_computation.26 | convolution fusion | flops 2415919104 | bytes 10616832 | tf_op jit(solution)/shard_map/dot_general | solution.py:238
  143.9 2.2 copy.206
  146.0 2.1 copy.205
  148.2 3.2 broadcast_in_dim.76
  151.4 4.7 %all-to-all-start.1 = ((bf16[4,384,1024]{2,1,0:T(8,128)(2,1)}), bf16[4,384,1024]{2,1,0:T(8,128)(2,1)}, u32[]{:S(2)}, u32[]{:S(2)}) async-start(bf16[4,384,1024]{2,1,0:T(8,128)(2,1)} %broadcast_in_dim.76), calls=%async_computation.1 | async-start | bytes 6291456 | tf_op jit(solution)/shard_map/all_to_all | solution.py:217
  156.3 1.7 subtract_convert_fusion.3
  158.0 1.5 maximum_select_fusion
  159.5 1.2 fusion.10
  160.8 1.2 select_reduce_fusion.1
  162.0 2.4 bitcast_convert_fusion.1
  164.4 2.3 copy.179
  166.7 1.5 multiply_reduce_fusion.1
  168.2 4.5 %fusion.6 = bf16[4,384,768]{1,2,0:T(8,128)(2,1)S(1)} fusion(f32[768,384,4]{1,0,2:T(8,128)} %copy-done.2, f32[4,384]{1,0:T(4,128)S(1)} %multiply_reduce_fusion.1, f32[4,384]{1,0:T(4,128)S(1)} %log_add_fusion.1, pred[384,768]{0,1:T(8,128)(4,1)S(1)} %fusion.16, bf16[768,256]{0,1:T(8,128)(2,1)} %copy-done.11, bf16[384,8,128]{0,2,1:T(8,128)(2,1)} %bitcast.165), kind=kOutput, calls=%fused_computation.11 | convolution fusion | flops 311427072 | bytes 7974912 | tf_op jit(solution)/shard_map/rhd,kd->hrk/dot_general | solution.py:90
  172.8 1.4 copy-done.4
  174.2 1.1 convolution_bitcast_fusion.2
  176.7 1.9 copy.147
  178.6 14.5 %all-to-all-done.1 = bf16[4,384,1024]{2,1,0:T(8,128)(2,1)} async-done(((bf16[4,384,1024]{2,1,0:T(8,128)(2,1)}), bf16[4,384,1024]{2,1,0:T(8,128)(2,1)}, u32[]{:S(2)}, u32[]{:S(2)}) %all-to-all-start.1) | async-done | bytes 3145760 | tf_op jit(solution)/shard_map/all_to_all | solution.py:217
  193.1 4.0 %copy.148 = bf16[4,4,96,1024]{3,2,1,0:T(8,128)(2,1)} copy(bf16[4,4,96,1024]{3,2,0,1:T(8,128)(2,1)} %bitcast.25) | data formatting | bytes 6291456 | tf_op jit(solution)/shard_map/transpose | solution.py:220
  197.5 4.6 %fusion.58 = f32[512,384]{1,0:T(8,128)S(1)} fusion(bf16[4096,512]{1,0:T(8,128)(2,1)} %all-gather.7.cloned.1.call-done, bf16[384,4096]{1,0:T(8,128)(2,1)S(1)} %copy-done), kind=kOutput, calls=%fused_computation.127 | convolution fusion | flops 1610612736 | bytes 8126464 | tf_op jit(solution)/shard_map/dot_general | solution.py:268
  202.6 1.2 subtract_convert_fusion.1
  203.9 1.4 fusion.11
  205.3 1.2 select_reduce_fusion
  206.5 2.3 convolution_bitcast_fusion.3
  208.9 2.1 bitcast_convert_fusion
  211.6 4.5 %fusion.1 = bf16[4,384,768]{1,2,0:T(8,128)(2,1)S(1)} fusion(f32[768,384,4]{1,0,2:T(8,128)} %copy-done.3, f32[4,384]{1,0:T(4,128)S(1)} %multiply_reduce_fusion, f32[4,384]{1,0:T(4,128)S(1)} %log_add_fusion, pred[384,768]{0,1:T(8,128)(4,1)S(1)} %fusion.16, bf16[768,256]{0,1:T(8,128)(2,1)S(1)} %copy-done.13, bf16[384,8,128]{0,2,1:T(8,128)(2,1)} %bitcast.166), kind=kOutput, calls=%fused_computation.3 | convolution fusion | flops 311427072 | bytes 7974912 | tf_op jit(solution)/shard_map/rhd,kd->hrk/dot_general | solution.py:90
  217.1 1.0 convolution_bitcast_fusion.1
  218.3 1.7 fusion.15
  220.1 1.0 fusion.14
  221.1 1.1 collective-permute-start.1
  223.1 8.3 %collective-permute-done.1 = f32[384,256]{0,1:T(8,128)S(1)} collective-permute-done((f32[384,256]{0,1:T(8,128)S(1)}, f32[384,256]{0,1:T(8,128)S(1)}, u32[]{:S(2)}, u32[]{:S(2)}) %collective-permute-start.1) | collective-permute-done | bytes 393248 | tf_op jit(solution)/shard_map/ppermute | solution.py:283
  231.4 1.1 fusion.21
  233.0 1.1 pad_maximum_fusion.3
  234.7 5.0 %fusion.17 = f32[384,4096]{1,0:T(8,128)S(1)} fusion(bf16[4096,768]{1,0:T(8,128)(2,1)} %all-gather.5.cloned.1.call-done, bf16[384,128]{0,1:T(8,128)(2,1)S(1)} %slice.171, bf16[384,128]{0,1:T(8,128)(2,1)S(1)} %maximum_bitcast_fusion.1, bf16[384,512]{0,1:T(8,128)(2,1)S(1)} %bitcast.175), kind=kOutput, calls=%fused_computation.61 | convolution fusion | flops 2417688576 | bytes 13172736 | tf_op jit(solution)/shard_map/dot_general | solution.py:290
  239.7 1.8 add_convert_fusion
  241.6 2.1 copy.215
  243.7 3.7 all-to-all-start.2
  247.4 36.2 %all-gather.11.cloned.1.call-done = bf16[1536,768]{0,1:T(8,128)(2,1)} async-done(((bf16[384,768]{0,1:T(8,128)(2,1)}), bf16[1536,768]{0,1:T(8,128)(2,1)}) %all-gather.11.cloned.1.call-update) | async-done | bytes 2359312 | tf_op jit(solution)/shard_map/all_gather | solution.py:226
  283.6 5.2 %fusion.60 = f32[1024,768]{0,1:T(8,128)S(1)} fusion(bf16[1536,768]{0,1:T(8,128)(2,1)} %all-gather.11.cloned.1.call-done, bf16[1536,1024]{1,0:T(8,128)(2,1)} %bitcast.162), kind=kOutput, calls=%fused_computation.129 | convolution fusion | flops 2415919104 | bytes 8650752 | tf_op jit(solution)/shard_map/dot_general | solution.py:227
  288.8 1.6 copy-done.22
  290.5 1.3 constant_dynamic-slice_fusion
  291.8 1.5 collective-permute-start.3
  293.3 27.6 %all-gather.9.cloned.1.call-done = bf16[1536,512]{0,1:T(8,128)(2,1)} async-done(((bf16[384,512]{0,1:T(8,128)(2,1)}), bf16[1536,512]{0,1:T(8,128)(2,1)}) %all-gather.9.cloned.1.call-update) | async-done | bytes 1572880 | tf_op jit(solution)/shard_map/all_gather | solution.py:226
  320.9 4.2 %fusion.59 = f32[1024,512]{0,1:T(8,128)S(1)} fusion(bf16[1536,512]{0,1:T(8,128)(2,1)} %all-gather.9.cloned.1.call-done, bf16[1536,1024]{1,0:T(8,128)(2,1)} %bitcast.163), kind=kOutput, calls=%fused_computation.128 | convolution fusion | flops 1610612736 | bytes 6815744 | tf_op jit(solution)/shard_map/dot_general | solution.py:227
  325.1 1.3 copy-done.25
  326.4 1.1 constant_dynamic-slice_fusion.1
  327.4 1.5 collective-permute-start.2
  328.9 2.0 pad_maximum_fusion.2
  330.9 2.3 copy.167
  333.2 1.7 reduce_sum.42
  334.9 17.3 %collective-permute-done.2 = f32[512,512]{0,1:T(8,128)} collective-permute-done((f32[512,512]{0,1:T(8,128)}, f32[512,512]{0,1:T(8,128)}, u32[]{:S(2)}, u32[]{:S(2)}) %collective-permute-start.2) | collective-permute-done | bytes 1048608 | tf_op jit(solution)/shard_map/ppermute | solution.py:235
  352.2 1.7 dynamic-slice_add_fusion.1
  353.9 2.2 dynamic-slice_add_fusion
  357.0 1.5 pad_maximum_fusion
  358.5 3.0 copy.168
  361.5 1.8 copy.170
  (119 shorter events, 13.0 us)
Async XLA Ops:
  7.2 3.3 copy-start
  7.2 118.4 %copy-start.31 = (s32[1,8]{1,0:T(1,128)S(1)}, s32[1,8]{1,0:T(1,128)}, u32[]{:S(2)}) copy-start(s32[1,8]{1,0:T(1,128)} %param.10) | copy-start | bytes 100
  7.2 116.5 %all-gather.5.cloned.1.call-start = ((), (), s32[]{:S(2)}) async-start(), calls=%async_computation.3 | async-start | bytes 7077888 | tf_op jit(solution)/shard_map/all_gather | solution.py:203
  10.4 187.1 %all-gather.7.cloned.1.call-start = ((), (), s32[]{:S(2)}) async-start(), calls=%async_computation.4 | async-start | bytes 4718592 | tf_op jit(solution)/shard_map/all_gather | solution.py:265
  141.0 0.6 copy-start.29
  142.4 15.6 %collective-permute-start = (bf16[384,256]{0,1:T(8,128)(2,1)}, bf16[384,256]{0,1:T(8,128)(2,1)}, u32[]{:S(2)}, u32[]{:S(2)}) collective-permute-start(bf16[384,256]{0,1:T(8,128)(2,1)} %pad_maximum_fusion.12), channel_id=1, source_target_pairs={{0,4},{4,0},{1,5},{5,1},{2,6},{6,2},{3,7},{7,3},{8,12},{12,8},{9,1... | collective-permute-start | bytes 589832 | tf_op jit(solution)/shard_map/ppermute | solution.py:248
  151.4 41.7 %all-to-all-start.1 = ((bf16[4,384,1024]{2,1,0:T(8,128)(2,1)}), bf16[4,384,1024]{2,1,0:T(8,128)(2,1)}, u32[]{:S(2)}, u32[]{:S(2)}) async-start(bf16[4,384,1024]{2,1,0:T(8,128)(2,1)} %broadcast_in_dim.76), calls=%async_computation.1 | async-start | bytes 6291456 | tf_op jit(solution)/shard_map/all_to_all | solution.py:217
  156.1 127.6 %all-gather.11.cloned.1.call-start = ((), (), s32[]{:S(2)}) async-start(), calls=%async_computation.6 | async-start | bytes 2949120 | tf_op jit(solution)/shard_map/all_gather | solution.py:226
  158.0 1.6 copy-start.17
  158.0 2.8 copy-start.19
  159.5 2.5 copy-start.11
  160.8 3.6 copy-start.2
  168.2 6.0 %copy-start.12 = (bf16[768,256]{0,1:T(8,128)(2,1)S(1)}, bf16[768,256]{0,1:T(8,128)(2,1)}, u32[]{:S(2)}) copy-start(bf16[768,256]{0,1:T(8,128)(2,1)} %copy-done.11) | copy-start | bytes 1179652
  168.2 7.1 %copy-start.6 = (f32[384,64]{1,0:T(8,128)S(1)}, f32[384,64]{1,0:T(8,128)}, u32[]{:S(2)}) copy-start(f32[384,64]{1,0:T(8,128)} %get-tuple-element.62) | copy-start | bytes 294916
  168.2 7.1 %copy-start.8 = (f32[384,64]{1,0:T(8,128)S(1)}, f32[384,64]{1,0:T(8,128)}, u32[]{:S(2)}) copy-start(f32[384,64]{1,0:T(8,128)} %get-tuple-element.63) | copy-start | bytes 294916
  172.8 1.5 copy-start.4
  202.0 1.9 copy-start.13
  203.9 2.6 copy-start.15
  203.9 2.6 copy-start.23
  205.3 3.5 copy-start.3
  208.9 2.4 copy-start.27
  211.3 6.9 %slice-start = ((s8[4718592]{0:T(1024)(128)(4,1)}), s8[4194304]{0:T(1024)(128)(4,1)S(1)}, s32[]{:S(2)}) async-start(s8[4718592]{0:T(1024)(128)(4,1)} %bitcast.156), calls=%async_computation.7 | async-start | bytes 8388608
  211.6 4.5 %copy-start.16 = (bf16[384,4,64]{2,0,1:T(8,128)(2,1)S(1)}, bf16[384,4,64]{2,0,1:T(8,128)(2,1)}, u32[]{:S(2)}) copy-start(bf16[384,4,64]{2,0,1:T(8,128)(2,1)} %copy-done.15) | copy-start | bytes 589828
  211.6 5.5 %copy-start.14 = (bf16[768,256]{0,1:T(8,128)(2,1)S(1)}, bf16[768,256]{0,1:T(8,128)(2,1)}, u32[]{:S(2)}) copy-start(bf16[768,256]{0,1:T(8,128)(2,1)} %copy-done.11) | copy-start | bytes 1179652
  211.6 6.6 %slice-start.1 = ((s8[4718592]{0:T(1024)(128)(4,1)}), s8[524288]{0:T(1024)(128)(4,1)S(1)}, s32[]{:S(2)}) async-start(s8[4718592]{0:T(1024)(128)(4,1)} %bitcast.156), calls=%async_computation.8 | async-start | bytes 1048576
  216.1 2.1 copy-start.24
  216.1 2.1 copy-start.32
  218.2 1.7 copy-start.5
  218.2 1.7 copy-start.18
  218.2 1.8 copy-start.20
  220.0 2.6 copy-start.28
  220.0 2.2 copy-start.7
  220.0 2.2 copy-start.9
  221.0 1.6 copy-start.21
  221.1 13.6 %copy-start.26 = (bf16[384,4,128]{0,2,1:T(8,128)(2,1)S(1)}, bf16[384,4,128]{0,2,1:T(8,128)(2,1)}, u32[]{:S(2)}) copy-start(bf16[384,4,128]{0,2,1:T(8,128)(2,1)} %copy.147) | copy-start | bytes 1179652
  221.1 10.3 %collective-permute-start.1 = (f32[384,256]{0,1:T(8,128)S(1)}, f32[384,256]{0,1:T(8,128)S(1)}, u32[]{:S(2)}, u32[]{:S(2)}) collective-permute-start(f32[384,256]{0,1:T(8,128)S(1)} %fusion.19), channel_id=1, source_target_pairs={{0,4},{4,0},{1,5},{5,1},{2,6},{6,2},{3,7},{7,3},{8,12},{12,8},{9,1... | collective-permute-start | bytes 1179656 | tf_op jit(solution)/shard_map/ppermute | solution.py:283
  234.1 86.7 %all-gather.9.cloned.1.call-start = ((), (), s32[]{:S(2)}) async-start(), calls=%async_computation.5 | async-start | bytes 1966080 | tf_op jit(solution)/shard_map/all_gather | solution.py:226
  234.7 5.0 %copy-start.10 = (bf16[4096,512]{1,0:T(8,128)(2,1)S(1)}, bf16[4096,512]{1,0:T(8,128)(2,1)}, u32[]{:S(2)}) copy-start(bf16[4096,512]{1,0:T(8,128)(2,1)} %all-gather.7.cloned.1.call-done) | copy-start | bytes 12582916
  243.7 89.5 %all-to-all-start.2 = ((bf16[384,4,1024]{2,0,1:T(8,128)(2,1)}), bf16[384,4,1024]{2,0,1:T(8,128)(2,1)S(1)}, u32[]{:S(2)}, u32[]{:S(2)}) async-start(bf16[384,4,1024]{2,0,1:T(8,128)(2,1)} %bitcast.159), calls=%async_computation.2 | async-start | bytes 6291456 | tf_op jit(solution)/shard_map/all_to_all | solution.py:302
  288.8 1.7 copy-start.22
  291.8 37.1 %copy-start.30 = (bf16[128,4,384]{2,0,1:T(8,128)(2,1)S(1)}, bf16[128,4,384]{2,0,1:T(8,128)(2,1)}, u32[]{:S(2)}) copy-start(bf16[128,4,384]{2,0,1:T(8,128)(2,1)} %get-tuple-element.67) | copy-start | bytes 1179652
  291.8 62.1 %collective-permute-start.3 = (f32[512,768]{0,1:T(8,128)}, f32[512,768]{0,1:T(8,128)}, u32[]{:S(2)}, u32[]{:S(2)}) collective-permute-start(f32[512,768]{0,1:T(8,128)} %constant_dynamic-slice_fusion), channel_id=1, source_target_pairs={{0,4},{4,0},{1,5},{5,1},{2,6},{6,2},{3,7},{7,3},{8,12},{12,8},{9,1... | collective-permute-start | bytes 4718600 | tf_op jit(solution)/shard_map/ppermute | solution.py:235
  325.0 1.3 copy-start.25
  327.4 24.7 %collective-permute-start.2 = (f32[512,512]{0,1:T(8,128)}, f32[512,512]{0,1:T(8,128)}, u32[]{:S(2)}, u32[]{:S(2)}) collective-permute-start(f32[512,512]{0,1:T(8,128)} %constant_dynamic-slice_fusion.1), channel_id=1, source_target_pairs={{0,4},{4,0},{1,5},{5,1},{2,6},{6,2},{3,7},{7,3},{8,12},{12,8},{9,1... | collective-permute-start | bytes 3145736 | tf_op jit(solution)/shard_map/ppermute | solution.py:235
  356.9 7.2 %copy-start.1 = (bf16[384,4096]{1,0:T(8,128)(2,1)S(1)}, bf16[384,4096]{1,0:T(8,128)(2,1)}, u32[]{:S(2)}) copy-start(bf16[384,4096]{1,0:T(8,128)(2,1)} %param.6) | copy-start | bytes 9437188
Sparse Core Ops, SparseCore 0:
  10.8 112.8 all-gather.4
  125.8 71.6 all-gather.6
  234.3 49.3 all-gather.10
  285.1 35.7 all-gather.8

commit v13 on v12

--- a/solution.py
+++ b/solution.py
@@ -222,8 +222,9 @@
         )
     weight_rows = w_query.shape[0]
 
-    def weight_grad(d_rows):
-        gathered = lax.all_gather(d_rows, "dp", axis=0, tiled=True)
+    def weight_grad(d_rows, gathered=None):
+        if gathered is None:
+            gathered = lax.all_gather(d_rows, "dp", axis=0, tiled=True)
         partial = lax.dot_general(
             hidden_cols, gathered, (((0,), (0,)), ((), ())), preferred_element_type=jnp.float32
         )
@@ -264,7 +265,7 @@
         w_rest = w_query[:, first_cols:]
         full_b = lax.all_gather(w_rest, rows_axes, axis=0, tiled=True)
         d_query_a, full_b, hidden_cols = lax.optimization_barrier((d_query_a, full_b, hidden_cols))
-        early_sum = weight_grad(d_query_a)
+        early_all = lax.all_gather(d_query_a, "dp", axis=0, tiled=True)
         proj_b = jnp.dot(hidden_in, full_b, preferred_element_type=jnp.float32)
         query_b = rotate(
             proj_b.reshape(num_rows, head_count - first_heads, 128), cosine, sine_table
@@ -272,6 +273,8 @@
         out_b, grad_qb, part_kb, part_vb = attend(
             query_b, *shared, dout_rows[:, first_heads:], *masks
         )
+        early_all, grad_qb = lax.optimization_barrier((early_all, grad_qb))
+        early_sum = weight_grad(d_query_a, early_all)
         d_query_b = unrotate(grad_qb, cosine, sine_table).astype(jnp.bfloat16).reshape(num_rows, -1)
         part_k, part_v = part_k + part_kb, part_v + part_vb
         out_parts.append(out_b)
@@ -298,6 +301,7 @@
     else:
         late_proj = jnp.concatenate([d_key, d_value], 1)
         early_sum = weight_grad(d_query_a)
+    early_sum, input_part = lax.optimization_barrier((early_sum, input_part))
     input_cols = input_part.shape[1] // head_groups
     input_split = lax.all_to_all(
         input_part.astype(jnp.bfloat16).reshape(num_rows, head_groups, input_cols),

time: 376 us -> 347 us (0.923)
  waiting for transfers between devices: 175 us -> 157 us
  local copies, waits for them, and re-layouts: 46.7 us -> 38.7 us
    all_gather x2 -> x1, waiting for transfers between devices: 63.9 us -> 13.6 us  [weight_grad(): gathered = lax.all_gather(d_rows, 'dp', axis=0, tiled=True)]
    ppermute x2, waiting for transfers between devices: 17.3 us -> 35.8 us  [weight_grad(): return own_part + lax.ppermute(away_part, 'ctx', [(0, 1), (1, 0)])]
    all_to_all x1, waiting for transfers between devices: 0.01 us -> 10.3 us  [local(): lax.all_to_all(input_part.astype(jnp.bfloat16).reshape(num_rows, head_gro...]
    unnamed x84 -> x77, local copies, waits for them, and re-layouts: 27.6 us -> 20.7 us
    all_gather x0 -> x1, waiting for transfers between devices: none -> 3.97 us  [local(): early_all = lax.all_gather(d_query_a, 'dp', axis=0, tiled=True)]
  transfers between devices with their start and end apart: 10 -> 10, of which waited for: 7 -> 9; matrix products, arithmetic and copies ran while one was open for 21% -> 29% of each run, Pallas kernels for 0% -> 0%
where the time goes in v13:
time: 347 us; the launch traced here: 342 us
  waiting for transfers between devices  157 us (45%)
  matrix products  50.4 us (15%)
  blocking collectives  42.6 us (12%)
  local copies, waits for them, and re-layouts  38.7 us (11%)
  other arithmetic  24.8 us (7%)
  between operations  14.8 us (4%)
  starting transfers between devices  13.8 us (4%)
    all_gather x1, waiting for transfers between devices, local(): full_a = lax.all_gather(local_a, rows_axes, axis=0, tiled=True)  70.5 us
    all_to_all x1, blocking collectives, local(): cols_part = lax.all_to_all(own_rows, 'dp', 1, 0, tiled=True)  42.6 us
    ppermute x2, waiting for transfers between devices, weight_grad(): return own_part + lax.ppermute(away_part, 'ctx', [(0, 1), (1, 0)])  35.8 us
    unnamed x77, local copies, waits for them, and re-layouts  20.7 us
    all_to_all x1, waiting for transfers between devices, local(): cols_all = lax.all_to_all(spread, 'head', 0, 0, tiled=False)  13.9 us
    all_gather x1, waiting for transfers between devices, weight_grad(): gathered = lax.all_gather(d_rows, 'dp', axis=0, tiled=True)  13.6 us
    all_to_all x1, waiting for transfers between devices, local(): lax.all_to_all(input_part.astype(jnp.bfloat16).reshape(num_rows, head_gro...  10.3 us
    dot_general x2, matrix products, weight_grad(): lax.dot_general(hidden_cols, gathered, (((0,), (0,)), ((), ())), preferre...  9.56 us
  transfers between devices with their start and end apart: 10, of which 9 were waited for; matrix products, arithmetic and copies ran while one was open for 29% of the time, Pallas kernels for 0%

profile of v13, /device:TPU:0, one launch (start us, length us, event | category | flops | bytes accessed | tf_op | source)
XLA Modules:
  0.0 341.8 jit_solution(14615419929764710002)
XLA Ops:
  7.2 1.2 slice.83
  8.5 1.9 pad_maximum_fusion.1
  10.6 42.6 %all_to_all.29 = bf16[96,4,1024]{2,0,1:T(8,128)(2,1)} all-to-all(bf16[96,4,1024]{2,0,1:T(8,128)(2,1)S(1)} %bitcast.174), channel_id=1, replica_groups=mesh['dp'=4,'ctx'=2,'head'=4] {'dp'}, dimensions={1} | all-to-all | bytes 1572864 | tf_op jit(solution)/shard_map/all_to_all | solution.py:210
  53.2 70.5 %all-gather.5.cloned.1.call-done = bf16[4096,768]{1,0:T(8,128)(2,1)} async-done(((bf16[512,768]{1,0:T(8,128)(2,1)}), bf16[4096,768]{1,0:T(8,128)(2,1)}) %all-gather.5.cloned.1.call-update) | async-done | bytes 6291472 | tf_op jit(solution)/shard_map/all_gather | solution.py:203
  123.7 1.9 slice.96
  125.8 2.3 copy.138
  128.1 1.9 fusion.55
  130.0 1.9 copy.206
  132.0 0.9 copy.203
  133.4 1.5 multiply_cosine_fusion
  134.9 5.6 %convolution_bitcast_fusion = f32[384,768]{0,1:T(8,128)S(1)} fusion(bf16[4096,768]{1,0:T(8,128)(2,1)} %all-gather.5.cloned.1.call-done, bf16[384,4096]{1,0:T(8,128)(2,1)S(1)} %copy-done), kind=kOutput, calls=%fused_computation.26 | convolution fusion | flops 2415919104 | bytes 10616832 | tf_op jit(solution)/shard_map/dot_general | solution.py:239
  142.9 0.9 fusion.57
  143.8 2.2 copy.202
  146.0 2.1 copy.201
  148.1 3.2 broadcast_in_dim.76
  151.4 4.7 %all-to-all-start.1 = ((bf16[4,384,1024]{2,1,0:T(8,128)(2,1)}), bf16[4,384,1024]{2,1,0:T(8,128)(2,1)}, u32[]{:S(2)}, u32[]{:S(2)}) async-start(bf16[4,384,1024]{2,1,0:T(8,128)(2,1)} %broadcast_in_dim.76), calls=%async_computation.1 | async-start | bytes 6291456 | tf_op jit(solution)/shard_map/all_to_all | solution.py:217
  156.6 1.9 subtract_convert_fusion.3
  158.5 1.5 maximum_select_fusion
  160.1 1.2 fusion.10
  161.3 1.2 select_reduce_fusion.1
  162.5 2.4 bitcast_convert_fusion.1
  164.9 2.3 copy.174
  167.2 1.5 multiply_reduce_fusion.1
  168.8 4.5 %fusion.6 = bf16[4,384,768]{1,2,0:T(8,128)(2,1)S(1)} fusion(f32[768,384,4]{1,0,2:T(8,128)} %copy-done.2, f32[4,384]{1,0:T(4,128)S(1)} %multiply_reduce_fusion.1, f32[4,384]{1,0:T(4,128)S(1)} %log_add_fusion.1, pred[384,768]{0,1:T(8,128)(4,1)S(1)} %fusion.16, bf16[768,256]{0,1:T(8,128)(2,1)} %copy-done.12, bf16[384,8,128]{0,2,1:T(8,128)(2,1)} %bitcast.167), kind=kOutput, calls=%fused_computation.11 | convolution fusion | flops 311427072 | bytes 7974912 | tf_op jit(solution)/shard_map/rhd,kd->hrk/dot_general | solution.py:90
  173.3 1.4 copy-done.4
  174.8 1.1 convolution_bitcast_fusion.2
  176.2 1.0 pad_maximum_fusion.9
  177.2 1.9 copy.143
  179.1 13.9 %all-to-all-done.1 = bf16[4,384,1024]{2,1,0:T(8,128)(2,1)} async-done(((bf16[4,384,1024]{2,1,0:T(8,128)(2,1)}), bf16[4,384,1024]{2,1,0:T(8,128)(2,1)}, u32[]{:S(2)}, u32[]{:S(2)}) %all-to-all-start.1) | async-done | bytes 3145760 | tf_op jit(solution)/shard_map/all_to_all | solution.py:217
  193.0 4.0 %copy.144 = bf16[4,4,96,1024]{3,2,1,0:T(8,128)(2,1)} copy(bf16[4,4,96,1024]{3,2,0,1:T(8,128)(2,1)} %bitcast.25) | data formatting | bytes 6291456 | tf_op jit(solution)/shard_map/transpose | solution.py:220
  197.7 4.6 %fusion.58 = f32[512,384]{1,0:T(8,128)S(1)} fusion(bf16[4096,512]{1,0:T(8,128)(2,1)} %all-gather.7.cloned.1.call-done, bf16[384,4096]{1,0:T(8,128)(2,1)S(1)} %copy-done), kind=kOutput, calls=%fused_computation.127 | convolution fusion | flops 1610612736 | bytes 8126464 | tf_op jit(solution)/shard_map/dot_general | solution.py:269
  202.9 1.3 subtract_convert_fusion.1
  204.2 1.2 fusion.11
  205.4 1.2 select_reduce_fusion
  206.6 2.1 bitcast_convert_fusion
  209.4 4.5 %fusion.1 = bf16[4,384,768]{1,2,0:T(8,128)(2,1)S(1)} fusion(f32[768,384,4]{1,0,2:T(8,128)} %copy-done.3, f32[4,384]{1,0:T(4,128)S(1)} %multiply_reduce_fusion, f32[4,384]{1,0:T(4,128)S(1)} %log_add_fusion, pred[384,768]{0,1:T(8,128)(4,1)S(1)} %fusion.16, bf16[768,256]{0,1:T(8,128)(2,1)S(1)} %copy-done.14, bf16[384,8,128]{0,2,1:T(8,128)(2,1)} %bitcast.168), kind=kOutput, calls=%fused_computation.3 | convolution fusion | flops 311427072 | bytes 7974912 | tf_op jit(solution)/shard_map/rhd,kd->hrk/dot_general | solution.py:90
  214.0 1.0 convolution_bitcast_fusion.5
  215.0 1.0 fusion.14
  216.0 1.7 convolution_bitcast_fusion.3
  217.7 1.9 fusion.15
  219.7 1.1 collective-permute-start.2
  220.7 1.1 convolution_bitcast_fusion.1
  221.8 8.1 %collective-permute-done.2 = f32[384,256]{0,1:T(8,128)S(1)} collective-permute-done((f32[384,256]{0,1:T(8,128)S(1)}, f32[384,256]{0,1:T(8,128)S(1)}, u32[]{:S(2)}, u32[]{:S(2)}) %collective-permute-start.2) | collective-permute-done | bytes 393248 | tf_op jit(solution)/shard_map/ppermute | solution.py:286
  230.5 4.0 %all-gather.9.cloned.1.call-done = bf16[1536,512]{0,1:T(8,128)(2,1)} async-done(((bf16[384,512]{0,1:T(8,128)(2,1)}), bf16[1536,512]{0,1:T(8,128)(2,1)}) %all-gather.9.cloned.1.call-update) | async-done | bytes 1572880 | tf_op jit(solution)/shard_map/all_gather | solution.py:268
  236.2 4.2 %fusion.59 = f32[1024,512]{1,0:T(8,128)S(1)} fusion(bf16[1536,1024]{1,0:T(8,128)(2,1)} %bitcast.164, bf16[1536,512]{0,1:T(8,128)(2,1)} %all-gather.9.cloned.1.call-done), kind=kOutput, calls=%fused_computation.128 | convolution fusion | flops 1610612736 | bytes 6815744 | tf_op jit(solution)/shard_map/dot_general | solution.py:228
  240.5 1.3 collective-permute-start.1
  241.8 5.2 %fusion.17 = f32[384,4096]{1,0:T(8,128)S(1)} fusion(bf16[4096,768]{1,0:T(8,128)(2,1)} %all-gather.5.cloned.1.call-done, bf16[384,128]{0,1:T(8,128)(2,1)S(1)} %slice.169, bf16[384,128]{0,1:T(8,128)(2,1)S(1)} %maximum_bitcast_fusion.1, bf16[384,512]{0,1:T(8,128)(2,1)S(1)} %bitcast.177), kind=kOutput, calls=%fused_computation.61 | convolution fusion | flops 2417688576 | bytes 13172736 | tf_op jit(solution)/shard_map/dot_general | solution.py:293
  247.0 1.9 convolution_add_fusion
  248.8 16.1 %collective-permute-done.1 = f32[512,512]{1,0:T(8,128)S(1)} collective-permute-done((f32[512,512]{1,0:T(8,128)S(1)}, f32[512,512]{1,0:T(8,128)S(1)}, u32[]{:S(2)}, u32[]{:S(2)}) %collective-permute-start.1) | collective-permute-done | bytes 1048608 | tf_op jit(solution)/shard_map/ppermute | solution.py:236
  265.0 1.2 dynamic-slice_add_fusion.1
  266.2 2.1 copy.211
  268.2 4.0 %all-to-all-start.2 = ((bf16[384,4,1024]{2,0,1:T(8,128)(2,1)}), bf16[384,4,1024]{2,0,1:T(8,128)(2,1)S(1)}, u32[]{:S(2)}, u32[]{:S(2)}) async-start(bf16[384,4,1024]{2,0,1:T(8,128)(2,1)} %bitcast.161), calls=%async_computation.2 | async-start | bytes 6291456 | tf_op jit(solution)/shard_map/all_to_all | solution.py:306
  272.2 13.6 %all-gather.11.cloned.1.call-done = bf16[1536,768]{0,1:T(8,128)(2,1)} async-done(((bf16[384,768]{0,1:T(8,128)(2,1)}), bf16[1536,768]{0,1:T(8,128)(2,1)}) %all-gather.11.cloned.1.call-update) | async-done | bytes 2359312 | tf_op jit(solution)/shard_map/all_gather | solution.py:227
  285.7 5.3 %fusion.60 = f32[1024,768]{1,0:T(8,128)S(1)} fusion(bf16[1536,1024]{1,0:T(8,128)(2,1)} %bitcast.165, bf16[1536,768]{0,1:T(8,128)(2,1)} %all-gather.11.cloned.1.call-done), kind=kOutput, calls=%fused_computation.129 | convolution fusion | flops 2415919104 | bytes 8650752 | tf_op jit(solution)/shard_map/dot_general | solution.py:228
  291.1 1.7 copy-done.21
  292.7 1.2 constant_dynamic-slice_fusion
  294.0 1.5 collective-permute-start.3
  295.5 1.0 pad_maximum_fusion.2
  296.4 2.3 copy.165
  298.7 10.3 %all-to-all-done.2 = bf16[384,4,1024]{2,0,1:T(8,128)(2,1)S(1)} async-done(((bf16[384,4,1024]{2,0,1:T(8,128)(2,1)}), bf16[384,4,1024]{2,0,1:T(8,128)(2,1)S(1)}, u32[]{:S(2)}, u32[]{:S(2)}) %all-to-all-start.2) | async-done | bytes 3145760 | tf_op jit(solution)/shard_map/all_to_all | solution.py:306
  309.1 1.7 reduce_sum.42
  310.8 19.6 %collective-permute-done.3 = f32[512,768]{1,0:T(8,128)} collective-permute-done((f32[512,768]{1,0:T(8,128)}, f32[512,768]{1,0:T(8,128)}, u32[]{:S(2)}, u32[]{:S(2)}) %collective-permute-start.3) | collective-permute-done | bytes 1572896 | tf_op jit(solution)/shard_map/ppermute | solution.py:236
  330.4 2.2 dynamic-slice_add_fusion
  333.6 1.5 pad_maximum_fusion
  (113 shorter events, 9.5 us)
Async XLA Ops:
  7.2 3.3 copy-start
  7.2 118.4 %copy-start.28 = (s32[1,8]{1,0:T(1,128)S(1)}, s32[1,8]{1,0:T(1,128)}, u32[]{:S(2)}) copy-start(s32[1,8]{1,0:T(1,128)} %param.10) | copy-start | bytes 100
  7.2 116.5 %all-gather.5.cloned.1.call-start = ((), (), s32[]{:S(2)}) async-start(), calls=%async_computation.3 | async-start | bytes 7077888 | tf_op jit(solution)/shard_map/all_gather | solution.py:203
  10.4 187.1 %all-gather.7.cloned.1.call-start = ((), (), s32[]{:S(2)}) async-start(), calls=%async_computation.4 | async-start | bytes 4718592 | tf_op jit(solution)/shard_map/all_gather | solution.py:266
  141.1 0.6 copy-start.25
  142.4 16.2 %collective-permute-start = (bf16[384,256]{0,1:T(8,128)(2,1)}, bf16[384,256]{0,1:T(8,128)(2,1)}, u32[]{:S(2)}, u32[]{:S(2)}) collective-permute-start(bf16[384,256]{0,1:T(8,128)(2,1)} %pad_maximum_fusion.12), channel_id=1, source_target_pairs={{0,4},{4,0},{1,5},{5,1},{2,6},{6,2},{3,7},{7,3},{8,12},{12,8},{9,1... | collective-permute-start | bytes 589832 | tf_op jit(solution)/shard_map/ppermute | solution.py:249
  151.4 41.7 %all-to-all-start.1 = ((bf16[4,384,1024]{2,1,0:T(8,128)(2,1)}), bf16[4,384,1024]{2,1,0:T(8,128)(2,1)}, u32[]{:S(2)}, u32[]{:S(2)}) async-start(bf16[4,384,1024]{2,1,0:T(8,128)(2,1)} %broadcast_in_dim.76), calls=%async_computation.1 | async-start | bytes 6291456 | tf_op jit(solution)/shard_map/all_to_all | solution.py:217
  156.0 78.4 %all-gather.9.cloned.1.call-start = ((), (), s32[]{:S(2)}) async-start(), calls=%async_computation.5 | async-start | bytes 1966080 | tf_op jit(solution)/shard_map/all_gather | solution.py:268
  158.5 1.5 copy-start.17
  158.5 2.8 copy-start.19
  160.0 2.5 copy-start.12
  161.3 3.6 %copy-start.2 = (f32[768,384,4]{1,0,2:T(8,128)}, f32[768,384,4]{1,0,2:T(8,128)S(1)}, u32[]{:S(2)}) copy-start(f32[768,384,4]{1,0,2:T(8,128)S(1)} %get-tuple-element.73) | copy-start | bytes 14155780
  168.7 6.0 %copy-start.13 = (bf16[768,256]{0,1:T(8,128)(2,1)S(1)}, bf16[768,256]{0,1:T(8,128)(2,1)}, u32[]{:S(2)}) copy-start(bf16[768,256]{0,1:T(8,128)(2,1)} %copy-done.12) | copy-start | bytes 1179652
  168.8 7.1 %copy-start.6 = (f32[384,64]{1,0:T(8,128)S(1)}, f32[384,64]{1,0:T(8,128)}, u32[]{:S(2)}) copy-start(f32[384,64]{1,0:T(8,128)} %get-tuple-element.70) | copy-start | bytes 294916
  168.8 7.1 %copy-start.8 = (f32[384,64]{1,0:T(8,128)S(1)}, f32[384,64]{1,0:T(8,128)}, u32[]{:S(2)}) copy-start(f32[384,64]{1,0:T(8,128)} %get-tuple-element.71) | copy-start | bytes 294916
  173.3 1.5 copy-start.4
  197.5 88.2 %all-gather.11.cloned.1.call-start = ((), (), s32[]{:S(2)}) async-start(), calls=%async_computation.6 | async-start | bytes 2949120 | tf_op jit(solution)/shard_map/all_gather | solution.py:227
  202.3 1.9 copy-start.14
  204.2 2.4 copy-start.15
  205.4 3.4 copy-start.3
  206.6 2.4 copy-start.24
  209.0 6.9 %slice-start.2 = ((s8[4718592]{0:T(1024)(128)(4,1)}), s8[4194304]{0:T(1024)(128)(4,1)S(1)}, s32[]{:S(2)}) async-start(s8[4718592]{0:T(1024)(128)(4,1)} %bitcast.158), calls=%async_computation.9 | async-start | bytes 8388608
  209.3 4.6 %copy-start.16 = (bf16[384,4,64]{2,0,1:T(8,128)(2,1)S(1)}, bf16[384,4,64]{2,0,1:T(8,128)(2,1)}, u32[]{:S(2)}) copy-start(bf16[384,4,64]{2,0,1:T(8,128)(2,1)} %copy-done.15) | copy-start | bytes 589828
  209.4 5.6 %copy-start.5 = (bf16[4,384,768]{1,2,0:T(8,128)(2,1)S(1)}, bf16[4,384,768]{1,2,0:T(8,128)(2,1)}, u32[]{:S(2)}) copy-start(bf16[4,384,768]{1,2,0:T(8,128)(2,1)} %copy-done.4) | copy-start | bytes 7077892
  209.4 5.6 %copy-start.18 = (bf16[384,4,64]{2,0,1:T(8,128)(2,1)S(1)}, bf16[384,4,64]{2,0,1:T(8,128)(2,1)}, u32[]{:S(2)}) copy-start(bf16[384,4,64]{2,0,1:T(8,128)(2,1)} %copy-done.17) | copy-start | bytes 589828
  209.4 5.6 %copy-start.20 = (bf16[384,4,64]{2,0,1:T(8,128)(2,1)S(1)}, bf16[384,4,64]{2,0,1:T(8,128)(2,1)}, u32[]{:S(2)}) copy-start(bf16[384,4,64]{2,0,1:T(8,128)(2,1)} %copy-done.19) | copy-start | bytes 589828
  209.4 6.6 %slice-start.3 = ((s8[4718592]{0:T(1024)(128)(4,1)}), s8[524288]{0:T(1024)(128)(4,1)S(1)}, s32[]{:S(2)}) async-start(s8[4718592]{0:T(1024)(128)(4,1)} %bitcast.158), calls=%async_computation.10 | async-start | bytes 1048576
  213.9 2.0 copy-start.22
  215.0 2.7 slice-start
  216.0 1.7 slice-start.1
  219.6 14.8 %copy-start.7 = (f32[384,64]{1,0:T(8,128)S(1)}, f32[384,64]{1,0:T(8,128)}, u32[]{:S(2)}) copy-start(f32[384,64]{1,0:T(8,128)} %get-tuple-element.70) | copy-start | bytes 294916
  219.6 14.8 %copy-start.9 = (f32[384,64]{1,0:T(8,128)S(1)}, f32[384,64]{1,0:T(8,128)}, u32[]{:S(2)}) copy-start(f32[384,64]{1,0:T(8,128)} %get-tuple-element.71) | copy-start | bytes 294916
  219.7 10.2 %collective-permute-start.2 = (f32[384,256]{0,1:T(8,128)S(1)}, f32[384,256]{0,1:T(8,128)S(1)}, u32[]{:S(2)}, u32[]{:S(2)}) collective-permute-start(f32[384,256]{0,1:T(8,128)S(1)} %fusion.19), channel_id=1, source_target_pairs={{0,4},{4,0},{1,5},{5,1},{2,6},{6,2},{3,7},{7,3},{8,12},{12,8},{9,1... | collective-permute-start | bytes 1179656 | tf_op jit(solution)/shard_map/ppermute | solution.py:286
  236.1 5.6 %copy-start.23 = (bf16[384,4,128]{0,2,1:T(8,128)(2,1)S(1)}, bf16[384,4,128]{0,2,1:T(8,128)(2,1)}, u32[]{:S(2)}) copy-start(bf16[384,4,128]{0,2,1:T(8,128)(2,1)} %copy.143) | copy-start | bytes 1179652
  240.5 6.5 %copy-start.11 = (bf16[4096,512]{1,0:T(8,128)(2,1)S(1)}, bf16[4096,512]{1,0:T(8,128)(2,1)}, u32[]{:S(2)}) copy-start(bf16[4096,512]{1,0:T(8,128)(2,1)} %all-gather.7.cloned.1.call-done) | copy-start | bytes 12582916
  240.5 24.5 %collective-permute-start.1 = (f32[512,512]{1,0:T(8,128)S(1)}, f32[512,512]{1,0:T(8,128)S(1)}, u32[]{:S(2)}, u32[]{:S(2)}) collective-permute-start(f32[512,512]{1,0:T(8,128)S(1)} %constant_dynamic-slice_fusion.1), channel_id=1, source_target_pairs={{0,4},{4,0},{1,5},{5,1},{2,6},{6,2},{3,7},{7,3},{8,12},{12,8},{9,1... | collective-permute-start | bytes 3145736 | tf_op jit(solution)/shard_map/ppermute | solution.py:236
  268.2 40.8 %all-to-all-start.2 = ((bf16[384,4,1024]{2,0,1:T(8,128)(2,1)}), bf16[384,4,1024]{2,0,1:T(8,128)(2,1)S(1)}, u32[]{:S(2)}, u32[]{:S(2)}) async-start(bf16[384,4,1024]{2,0,1:T(8,128)(2,1)} %bitcast.161), calls=%async_computation.2 | async-start | bytes 6291456 | tf_op jit(solution)/shard_map/all_to_all | solution.py:306
  272.2 23.3 %copy-start.26 = (bf16[128,4,384]{2,0,1:T(8,128)(2,1)S(1)}, bf16[128,4,384]{2,0,1:T(8,128)(2,1)}, u32[]{:S(2)}) copy-start(bf16[128,4,384]{2,0,1:T(8,128)(2,1)} %get-tuple-element.75) | copy-start | bytes 1179652
  285.7 9.7 %copy-start.27 = (bf16[128,4,384]{2,0,1:T(8,128)(2,1)S(1)}, bf16[128,4,384]{2,0,1:T(8,128)(2,1)}, u32[]{:S(2)}) copy-start(bf16[128,4,384]{2,0,1:T(8,128)(2,1)} %get-tuple-element.79) | copy-start | bytes 1179652
  291.1 1.7 copy-start.21
  294.0 36.4 %collective-permute-start.3 = (f32[512,768]{1,0:T(8,128)}, f32[512,768]{1,0:T(8,128)}, u32[]{:S(2)}, u32[]{:S(2)}) collective-permute-start(f32[512,768]{1,0:T(8,128)} %constant_dynamic-slice_fusion), channel_id=1, source_target_pairs={{0,4},{4,0},{1,5},{5,1},{2,6},{6,2},{3,7},{7,3},{8,12},{12,8},{9,1... | collective-permute-start | bytes 4718600 | tf_op jit(solution)/shard_map/ppermute | solution.py:236
  310.8 22.8 %copy-start.10 = (f32[512,512]{1,0:T(8,128)S(1)}, f32[512,512]{1,0:T(8,128)}, u32[]{:S(2)}) copy-start(f32[512,512]{1,0:T(8,128)} %dynamic-slice_add_fusion.1) | copy-start | bytes 3145732
  330.4 4.6 %copy-start.1 = (bf16[384,4096]{1,0:T(8,128)(2,1)S(1)}, bf16[384,4096]{1,0:T(8,128)(2,1)}, u32[]{:S(2)}) copy-start(bf16[384,4096]{1,0:T(8,128)(2,1)} %param.6) | copy-start | bytes 9437188
Sparse Core Ops, SparseCore 0:
  10.8 112.8 all-gather.4
  125.8 71.6 all-gather.6
  199.1 35.3 all-gather.8
  236.4 49.2 all-gather.10

commit v14 on v13

--- a/solution.py
+++ b/solution.py
@@ -276,6 +276,7 @@
         early_all, grad_qb = lax.optimization_barrier((early_all, grad_qb))
         early_sum = weight_grad(d_query_a, early_all)
         d_query_b = unrotate(grad_qb, cosine, sine_table).astype(jnp.bfloat16).reshape(num_rows, -1)
+        mid_all = lax.all_gather(d_query_b, "dp", axis=0, tiled=True)
         part_k, part_v = part_k + part_kb, part_v + part_vb
         out_parts.append(out_b)
     attended = jnp.concatenate(out_parts, 1).reshape(num_rows, query_cols)
@@ -297,7 +298,9 @@
         input_part = input_part + lax.dot_general(
             d_query_b, full_b, (((1,), (1,)), ((), ())), preferred_element_type=jnp.float32
         )
-        late_proj = jnp.concatenate([d_query_b, d_key, d_value], 1)
+        late_proj = jnp.concatenate([d_key, d_value], 1)
+        mid_sum = weight_grad(d_query_b, mid_all)
+        early_sum = jnp.concatenate([early_sum, mid_sum], 1)
     else:
         late_proj = jnp.concatenate([d_key, d_value], 1)
         early_sum = weight_grad(d_query_a)
@@ -309,8 +312,8 @@
     )
     grad_input = jnp.sum(input_split.astype(jnp.float32), axis=1).astype(jnp.bfloat16)
     late_sum = weight_grad(late_proj)
-    query_w = jnp.concatenate([early_sum, late_sum[:, : query_cols - first_cols]], 1)
-    rest = late_sum[:, query_cols - first_cols :]
+    query_w = early_sum
+    rest = late_sum
     return (attended, grad_input, query_w, rest[:, :128], rest[:, 128:])
 
 

time: 347 us -> 381 us (1.098)
  blocking collectives: 42.6 us -> 61.9 us
  local copies, waits for them, and re-layouts: 38.7 us -> 45 us
  matrix products: 50.4 us -> 54.4 us
    all_gather x0 -> x1, blocking collectives: none -> 19.2 us  [weight_grad(): gathered = lax.all_gather(d_rows, 'dp', axis=0, tiled=True)]
    all_gather x1, waiting for transfers between devices: 3.97 us -> 19.8 us  [local(): early_all = lax.all_gather(d_query_a, 'dp', axis=0, tiled=True)]
    all_to_all x1, waiting for transfers between devices: 10.3 us -> 0.01 us  [local(): lax.all_to_all(input_part.astype(jnp.bfloat16).reshape(num_rows, head_gro...]
    ppermute x2 -> x3, waiting for transfers between devices: 35.8 us -> 29.9 us  [weight_grad(): return own_part + lax.ppermute(away_part, 'ctx', [(0, 1), (1, 0)])]
    unnamed x77 -> x98, local copies, waits for them, and re-layouts: 20.7 us -> 24.7 us
    dot_general x2 -> x3, matrix products: 9.56 us -> 8.87 us  [weight_grad(): lax.dot_general(hidden_cols, gathered, (((0,), (0,)), ((), ())), preferre...]
  transfers between devices with their start and end apart: 10 -> 11, of which waited for: 9 -> 9; matrix products, arithmetic and copies ran while one was open for 29% -> 25% of each run, Pallas kernels for 0% -> 0%
where the time goes in v14:
time: 381 us; the launch traced here: 376 us
  waiting for transfers between devices  155 us (41%)
  blocking collectives  61.9 us (16%)
  matrix products  54.4 us (14%)
  local copies, waits for them, and re-layouts  45 us (12%)
  other arithmetic  27.8 us (7%)
  starting transfers between devices  16.7 us (4%)
  between operations  15.1 us (4%)
    all_gather x1, waiting for transfers between devices, local(): full_a = lax.all_gather(local_a, rows_axes, axis=0, tiled=True)  70.5 us
    all_to_all x1, blocking collectives, local(): cols_part = lax.all_to_all(own_rows, 'dp', 1, 0, tiled=True)  42.6 us
    ppermute x3, waiting for transfers between devices, weight_grad(): return own_part + lax.ppermute(away_part, 'ctx', [(0, 1), (1, 0)])  29.9 us
    unnamed x98, local copies, waits for them, and re-layouts  24.7 us
    all_gather x1, waiting for transfers between devices, local(): early_all = lax.all_gather(d_query_a, 'dp', axis=0, tiled=True)  19.8 us
    all_gather x1, blocking collectives, weight_grad(): gathered = lax.all_gather(d_rows, 'dp', axis=0, tiled=True)  19.2 us
    all_to_all x1, waiting for transfers between devices, local(): cols_all = lax.all_to_all(spread, 'head', 0, 0, tiled=False)  14.4 us
    all_gather x1, waiting for transfers between devices, local(): mid_all = lax.all_gather(d_query_b, 'dp', axis=0, tiled=True)  10.9 us
  transfers between devices with their start and end apart: 11, of which 9 were waited for; matrix products, arithmetic and copies ran while one was open for 25% of the time, Pallas kernels for 0%

profile of v14, /device:TPU:0, one launch (start us, length us, event | category | flops | bytes accessed | tf_op | source)
XLA Modules:
  0.0 375.7 jit_solution(14046336625221215437)
XLA Ops:
  7.2 1.2 slice.77
  8.5 1.9 pad_maximum_fusion.1
  10.6 42.6 %all_to_all.29 = bf16[96,4,1024]{2,0,1:T(8,128)(2,1)} all-to-all(bf16[96,4,1024]{2,0,1:T(8,128)(2,1)S(1)} %bitcast.177), channel_id=1, replica_groups=mesh['dp'=4,'ctx'=2,'head'=4] {'dp'}, dimensions={1} | all-to-all | bytes 1572864 | tf_op jit(solution)/shard_map/all_to_all | solution.py:210
  53.2 70.5 %all-gather.5.cloned.1.call-done = bf16[4096,768]{1,0:T(8,128)(2,1)} async-done(((bf16[512,768]{1,0:T(8,128)(2,1)}), bf16[4096,768]{1,0:T(8,128)(2,1)}) %all-gather.5.cloned.1.call-update) | async-done | bytes 6291472 | tf_op jit(solution)/shard_map/all_gather | solution.py:203
  123.7 1.9 slice.90
  125.8 2.3 copy.132
  128.1 1.9 fusion.58
  130.0 2.0 copy.195
  133.4 1.5 multiply_cosine_fusion
  134.9 5.6 %convolution_bitcast_fusion = f32[384,768]{0,1:T(8,128)S(1)} fusion(bf16[4096,768]{1,0:T(8,128)(2,1)} %all-gather.5.cloned.1.call-done, bf16[384,4096]{1,0:T(8,128)(2,1)S(1)} %copy-done), kind=kOutput, calls=%fused_computation.25 | convolution fusion | flops 2415919104 | bytes 10616832 | tf_op jit(solution)/shard_map/dot_general | solution.py:239
  143.9 2.2 copy.193
  146.0 2.1 copy.194
  148.2 3.2 broadcast_in_dim.76
  151.4 4.7 %all-to-all-start.1 = ((bf16[4,384,1024]{2,1,0:T(8,128)(2,1)}), bf16[4,384,1024]{2,1,0:T(8,128)(2,1)}, u32[]{:S(2)}, u32[]{:S(2)}) async-start(bf16[4,384,1024]{2,1,0:T(8,128)(2,1)} %broadcast_in_dim.76), calls=%async_computation.1 | async-start | bytes 6291456 | tf_op jit(solution)/shard_map/all_to_all | solution.py:217
  156.3 1.7 subtract_convert_fusion.3
  158.0 1.5 maximum_select_fusion
  159.5 1.2 fusion.10
  160.8 1.2 select_reduce_fusion.1
  162.0 2.4 bitcast_convert_fusion.1
  164.4 2.3 copy.167
  166.7 1.5 multiply_reduce_fusion.1
  168.2 4.5 %fusion.6 = bf16[4,384,768]{1,2,0:T(8,128)(2,1)S(1)} fusion(f32[768,384,4]{1,0,2:T(8,128)} %copy-done.2, f32[4,384]{1,0:T(4,128)S(1)} %multiply_reduce_fusion.1, f32[4,384]{1,0:T(4,128)S(1)} %log_add_fusion.1, pred[384,768]{0,1:T(8,128)(4,1)S(1)} %fusion.16, bf16[768,256]{0,1:T(8,128)(2,1)} %copy-done.11, bf16[384,8,128]{0,2,1:T(8,128)(2,1)} %bitcast.170), kind=kOutput, calls=%fused_computation.11 | convolution fusion | flops 311427072 | bytes 7974912 | tf_op jit(solution)/shard_map/rhd,kd->hrk/dot_general | solution.py:90
  172.8 1.5 copy-done.4
  174.2 1.1 convolution_bitcast_fusion.2
  176.7 1.9 copy.137
  178.6 14.4 %all-to-all-done.1 = bf16[4,384,1024]{2,1,0:T(8,128)(2,1)} async-done(((bf16[4,384,1024]{2,1,0:T(8,128)(2,1)}), bf16[4,384,1024]{2,1,0:T(8,128)(2,1)}, u32[]{:S(2)}, u32[]{:S(2)}) %all-to-all-start.1) | async-done | bytes 3145760 | tf_op jit(solution)/shard_map/all_to_all | solution.py:217
  193.1 4.0 %copy.138 = bf16[4,4,96,1024]{3,2,1,0:T(8,128)(2,1)} copy(bf16[4,4,96,1024]{3,2,0,1:T(8,128)(2,1)} %bitcast.25) | data formatting | bytes 6291456 | tf_op jit(solution)/shard_map/transpose | solution.py:220
  197.5 4.5 %fusion.62 = f32[512,384]{1,0:T(8,128)S(1)} fusion(bf16[4096,512]{1,0:T(8,128)(2,1)} %all-gather.7.cloned.1.call-done, bf16[384,4096]{1,0:T(8,128)(2,1)S(1)} %copy-done), kind=kOutput, calls=%fused_computation.130 | convolution fusion | flops 1610612736 | bytes 8126464 | tf_op jit(solution)/shard_map/dot_general | solution.py:269
  202.7 1.2 subtract_convert_fusion.1
  203.9 1.4 fusion.11
  205.4 2.1 copy-done.3
  207.5 1.2 select_reduce_fusion
  208.8 4.5 %bitcast_convert_fusion = (f32[4,384,128]{1,2,0:T(8,128)S(1)}, bf16[128,4,384]{2,0,1:T(8,128)(2,1)}) fusion(f32[768,384,4]{1,0,2:T(8,128)} %copy-done.3, f32[4,384]{1,0:T(4,128)S(1)} %log_add_fusion, pred[384,768]{0,1:T(8,128)(4,1)S(1)} %fusion.16, bf16[768,256]{0,1:T(8,128)(2,1)S(1)} %copy-done.13), kind=kOutput, calls=%fused_computation.72 | convolution fusion | flops 308281344 | bytes 6395904 | tf_op jit(solution)/shard_map/hrk,kd->rhd/dot_general | solution.py:86
  213.9 4.8 %fusion.1 = bf16[4,384,768]{1,2,0:T(8,128)(2,1)S(1)} fusion(f32[768,384,4]{1,0,2:T(8,128)} %copy-done.3, f32[4,384]{1,0:T(4,128)S(1)} %multiply_reduce_fusion, f32[4,384]{1,0:T(4,128)S(1)} %log_add_fusion, pred[384,768]{0,1:T(8,128)(4,1)S(1)} %fusion.16, bf16[768,256]{0,1:T(8,128)(2,1)S(1)} %copy-done.13, bf16[384,8,128]{0,2,1:T(8,128)(2,1)} %bitcast.171), kind=kOutput, calls=%fused_computation.3 | convolution fusion | flops 311427072 | bytes 7974912 | tf_op jit(solution)/shard_map/rhd,kd->hrk/dot_general | solution.py:90
  219.8 1.6 convolution_bitcast_fusion.3
  221.9 2.4 fusion.15
  224.4 19.8 %all-gather.9.cloned.1.call-done = bf16[1536,512]{0,1:T(8,128)(2,1)} async-done(((bf16[384,512]{0,1:T(8,128)(2,1)}), bf16[1536,512]{0,1:T(8,128)(2,1)}) %all-gather.9.cloned.1.call-update) | async-done | bytes 1572880 | tf_op jit(solution)/shard_map/all_gather | solution.py:268
  244.2 1.3 add_convert_fusion
  246.5 1.9 copy.147
  248.5 2.7 convolution_bitcast_fusion.5
  252.3 1.5 collective-permute-start.3
  253.8 8.9 %collective-permute-done.3 = f32[384,256]{0,1:T(8,128)S(1)} collective-permute-done((f32[384,256]{0,1:T(8,128)S(1)}, f32[384,256]{0,1:T(8,128)S(1)}, u32[]{:S(2)}, u32[]{:S(2)}) %collective-permute-start.3) | collective-permute-done | bytes 393248 | tf_op jit(solution)/shard_map/ppermute | solution.py:287
  265.5 4.3 %fusion.64 = f32[1024,512]{0,1:T(8,128)S(1)} fusion(bf16[1536,512]{0,1:T(8,128)(2,1)} %all-gather.9.cloned.1.call-done, bf16[1536,1024]{1,0:T(8,128)(2,1)} %bitcast.166), kind=kOutput, calls=%fused_computation.132 | convolution fusion | flops 1610612736 | bytes 6815744 | tf_op jit(solution)/shard_map/dot_general | solution.py:228
  269.8 1.3 copy-done.25
  271.1 1.1 constant_dynamic-slice_fusion.2
  272.3 1.5 collective-permute-start.1
  273.8 10.9 %all-gather.11.cloned.1.call-done = bf16[1536,512]{0,1:T(8,128)(2,1)} async-done(((bf16[384,512]{0,1:T(8,128)(2,1)}), bf16[1536,512]{0,1:T(8,128)(2,1)}) %all-gather.11.cloned.1.call-update) | async-done | bytes 1572880 | tf_op jit(solution)/shard_map/all_gather | solution.py:279
  284.6 3.5 fusion.65
  288.3 1.5 collective-permute-start.2
  289.8 4.8 %fusion.17 = f32[384,4096]{1,0:T(8,128)S(1)} fusion(bf16[4096,768]{1,0:T(8,128)(2,1)} %all-gather.5.cloned.1.call-done, bf16[384,128]{0,1:T(8,128)(2,1)S(1)} %copy-done.32, bf16[384,128]{0,1:T(8,128)(2,1)S(1)} %copy-done.34, bf16[384,512]{0,1:T(8,128)(2,1)S(1)} %bitcast.180), kind=kOutput, calls=%fused_computation.57 | convolution fusion | flops 2417688576 | bytes 13172736 | tf_op jit(solution)/shard_map/dot_general | solution.py:294
  294.7 1.9 convolution_add_fusion
  296.5 2.2 collective-permute-done.1
  298.7 1.4 dynamic-slice_add_fusion.1
  300.1 18.4 %collective-permute-done.2 = f32[512,512]{0,1:T(8,128)S(1)} collective-permute-done((f32[512,512]{0,1:T(8,128)S(1)}, f32[512,512]{0,1:T(8,128)S(1)}, u32[]{:S(2)}, u32[]{:S(2)}) %collective-permute-start.2) | collective-permute-done | bytes 1048608 | tf_op jit(solution)/shard_map/ppermute | solution.py:236
  318.8 1.6 pad_maximum_fusion
  320.3 2.1 copy.203
  322.4 4.9 %all-to-all-start.2 = ((bf16[384,4,1024]{2,0,1:T(8,128)(2,1)}), bf16[384,4,1024]{2,0,1:T(8,128)(2,1)}, u32[]{:S(2)}, u32[]{:S(2)}) async-start(bf16[384,4,1024]{2,0,1:T(8,128)(2,1)} %bitcast.163), calls=%async_computation.2 | async-start | bytes 6291456 | tf_op jit(solution)/shard_map/all_to_all | solution.py:309
  327.4 19.2 %all_gather.19 = bf16[1536,256]{0,1:T(8,128)(2,1)S(1)} all-gather(bf16[384,256]{0,1:T(8,128)(2,1)S(1)} %pad_maximum_fusion.8), channel_id=1, replica_groups=mesh['dp'=4,'ctx'=2,'head'=4] {'dp'}, dimensions={0}, use_global_device_ids=true | all-gather | bytes 983040 | tf_op jit(solution)/shard_map/all_gather | solution.py:227
  347.8 1.7 collective-permute-start.4
  349.6 1.2 copy.157
  350.7 9.3 %collective-permute-done.4 = f32[512,256]{1,0:T(8,128)} collective-permute-done((f32[512,256]{1,0:T(8,128)S(1)}, f32[512,256]{1,0:T(8,128)}, u32[]{:S(2)}, u32[]{:S(2)}) %collective-permute-start.4) | collective-permute-done | bytes 524320 | tf_op jit(solution)/shard_map/ppermute | solution.py:236
  360.0 1.4 dynamic-slice_add_fusion.2
  362.3 2.9 copy.158
  365.1 3.6 reduce_sum.42
  (139 shorter events, 17.1 us)
Async XLA Ops:
  7.2 3.3 copy-start
  7.2 118.4 %copy-start.38 = (s32[1,8]{1,0:T(1,128)S(1)}, s32[1,8]{1,0:T(1,128)}, u32[]{:S(2)}) copy-start(s32[1,8]{1,0:T(1,128)} %param.10) | copy-start | bytes 100
  7.2 116.5 %all-gather.5.cloned.1.call-start = ((), (), s32[]{:S(2)}) async-start(), calls=%async_computation.3 | async-start | bytes 7077888 | tf_op jit(solution)/shard_map/all_gather | solution.py:203
  10.4 187.1 %all-gather.7.cloned.1.call-start = ((), (), s32[]{:S(2)}) async-start(), calls=%async_computation.4 | async-start | bytes 4718592 | tf_op jit(solution)/shard_map/all_gather | solution.py:266
  141.1 0.6 copy-start.31
  142.4 15.6 %collective-permute-start = (bf16[384,256]{0,1:T(8,128)(2,1)}, bf16[384,256]{0,1:T(8,128)(2,1)}, u32[]{:S(2)}, u32[]{:S(2)}) collective-permute-start(bf16[384,256]{0,1:T(8,128)(2,1)} %pad_maximum_fusion.7), channel_id=1, source_target_pairs={{0,4},{4,0},{1,5},{5,1},{2,6},{6,2},{3,7},{7,3},{8,12},{12,8},{9,1... | collective-permute-start | bytes 589832 | tf_op jit(solution)/shard_map/ppermute | solution.py:249
  151.4 41.7 %all-to-all-start.1 = ((bf16[4,384,1024]{2,1,0:T(8,128)(2,1)}), bf16[4,384,1024]{2,1,0:T(8,128)(2,1)}, u32[]{:S(2)}, u32[]{:S(2)}) async-start(bf16[4,384,1024]{2,1,0:T(8,128)(2,1)} %broadcast_in_dim.76), calls=%async_computation.1 | async-start | bytes 6291456 | tf_op jit(solution)/shard_map/all_to_all | solution.py:217
  156.1 88.1 %all-gather.9.cloned.1.call-start = ((), (), s32[]{:S(2)}) async-start(), calls=%async_computation.5 | async-start | bytes 1966080 | tf_op jit(solution)/shard_map/all_gather | solution.py:268
  158.0 1.6 copy-start.18
  158.0 2.8 copy-start.20
  159.5 2.5 copy-start.11
  160.8 3.6 copy-start.2
  168.2 6.0 %copy-start.12 = (bf16[768,256]{0,1:T(8,128)(2,1)S(1)}, bf16[768,256]{0,1:T(8,128)(2,1)}, u32[]{:S(2)}) copy-start(bf16[768,256]{0,1:T(8,128)(2,1)} %copy-done.11) | copy-start | bytes 1179652
  168.2 7.1 %copy-start.7 = (f32[384,64]{1,0:T(8,128)S(1)}, f32[384,64]{1,0:T(8,128)}, u32[]{:S(2)}) copy-start(f32[384,64]{1,0:T(8,128)} %get-tuple-element.70) | copy-start | bytes 294916
  168.2 7.1 %copy-start.8 = (f32[384,64]{1,0:T(8,128)S(1)}, f32[384,64]{1,0:T(8,128)}, u32[]{:S(2)}) copy-start(f32[384,64]{1,0:T(8,128)} %get-tuple-element.71) | copy-start | bytes 294916
  172.8 1.5 copy-start.4
  202.1 1.9 copy-start.13
  203.9 4.7 %copy-start.15 = (bf16[384,4,64]{2,0,1:T(8,128)(2,1)}, bf16[384,4,64]{2,0,1:T(8,128)(2,1)S(1)}, u32[]{:S(2)}) copy-start(bf16[384,4,64]{2,0,1:T(8,128)(2,1)S(1)} %get-tuple-element.50) | copy-start | bytes 589828
  203.9 4.7 %copy-start.17 = (bf16[384,4,64]{2,0,1:T(8,128)(2,1)}, bf16[384,4,64]{2,0,1:T(8,128)(2,1)S(1)}, u32[]{:S(2)}) copy-start(bf16[384,4,64]{2,0,1:T(8,128)(2,1)S(1)} %get-tuple-element.51) | copy-start | bytes 589828
  205.4 2.1 copy-start.3
  208.7 4.8 %copy-start.28 = (bf16[384,4,128]{2,0,1:T(8,128)(2,1)S(1)}, bf16[384,4,128]{2,0,1:T(8,128)(2,1)}, u32[]{:S(2)}) copy-start(bf16[384,4,128]{2,0,1:T(8,128)(2,1)} %copy.198) | copy-start | bytes 1179652
  208.7 75.9 %all-gather.11.cloned.1.call-start = ((), (), s32[]{:S(2)}) async-start(), calls=%async_computation.6 | async-start | bytes 1966080 | tf_op jit(solution)/shard_map/all_gather | solution.py:279
  213.6 6.2 %slice-start.2 = ((s8[4718592]{0:T(1024)(128)(4,1)}), s8[4194304]{0:T(1024)(128)(4,1)S(1)}, s32[]{:S(2)}) async-start(s8[4718592]{0:T(1024)(128)(4,1)} %bitcast.160), calls=%async_computation.9 | async-start | bytes 8388608
  213.8 4.8 %copy-start.14 = (bf16[768,256]{0,1:T(8,128)(2,1)S(1)}, bf16[768,256]{0,1:T(8,128)(2,1)}, u32[]{:S(2)}) copy-start(bf16[768,256]{0,1:T(8,128)(2,1)} %copy-done.11) | copy-start | bytes 1179652
  213.9 5.9 %slice-start.3 = ((s8[4718592]{0:T(1024)(128)(4,1)}), s8[524288]{0:T(1024)(128)(4,1)S(1)}, s32[]{:S(2)}) async-start(s8[4718592]{0:T(1024)(128)(4,1)} %bitcast.160), calls=%async_computation.10 | async-start | bytes 1048576
  213.9 5.9 %copy-start.24 = (bf16[384,1024]{0,1:T(8,128)(2,1)S(1)}, bf16[384,1024]{0,1:T(8,128)(2,1)}, u32[]{:S(2)}) copy-start(bf16[384,1024]{0,1:T(8,128)(2,1)} %copy.132) | copy-start | bytes 2359300
  218.7 2.8 copy-start.6
  218.7 3.1 slice-start
  219.8 2.1 slice-start.1
  224.4 24.1 %copy-start.16 = (bf16[384,4,64]{2,0,1:T(8,128)(2,1)S(1)}, bf16[384,4,64]{2,0,1:T(8,128)(2,1)}, u32[]{:S(2)}) copy-start(bf16[384,4,64]{2,0,1:T(8,128)(2,1)} %copy-done.15) | copy-start | bytes 589828
  224.4 26.9 %copy-start.5 = (bf16[4,384,768]{1,2,0:T(8,128)(2,1)S(1)}, bf16[4,384,768]{1,2,0:T(8,128)(2,1)}, u32[]{:S(2)}) copy-start(bf16[4,384,768]{1,2,0:T(8,128)(2,1)} %copy-done.4) | copy-start | bytes 7077892
  245.5 5.7 %copy-start.19 = (bf16[384,4,64]{2,0,1:T(8,128)(2,1)S(1)}, bf16[384,4,64]{2,0,1:T(8,128)(2,1)}, u32[]{:S(2)}) copy-start(bf16[384,4,64]{2,0,1:T(8,128)(2,1)} %copy-done.18) | copy-start | bytes 589828
  245.5 5.7 %copy-start.21 = (bf16[384,4,64]{2,0,1:T(8,128)(2,1)S(1)}, bf16[384,4,64]{2,0,1:T(8,128)(2,1)}, u32[]{:S(2)}) copy-start(bf16[384,4,64]{2,0,1:T(8,128)(2,1)} %copy-done.20) | copy-start | bytes 589828
  248.5 3.8 copy-start.29
  252.3 10.4 %collective-permute-start.3 = (f32[384,256]{0,1:T(8,128)S(1)}, f32[384,256]{0,1:T(8,128)S(1)}, u32[]{:S(2)}, u32[]{:S(2)}) collective-permute-start(f32[384,256]{0,1:T(8,128)S(1)} %fusion.23), channel_id=1, source_target_pairs={{0,4},{4,0},{1,5},{5,1},{2,6},{6,2},{3,7},{7,3},{8,12},{12,8},{9,1... | collective-permute-start | bytes 1179656 | tf_op jit(solution)/shard_map/ppermute | solution.py:287
  265.5 19.2 %copy-start.22 = (bf16[4,4,96,1024]{3,2,1,0:T(8,128)(2,1)S(1)}, bf16[4,4,96,1024]{3,2,1,0:T(8,128)(2,1)}, u32[]{:S(2)}) copy-start(bf16[4,4,96,1024]{3,2,1,0:T(8,128)(2,1)} %copy.138) | copy-start | bytes 9437188
  269.8 1.3 copy-start.25
  272.3 17.5 %copy-start.27 = (bf16[384,4,128]{0,2,1:T(8,128)(2,1)S(1)}, bf16[384,4,128]{0,2,1:T(8,128)(2,1)}, u32[]{:S(2)}) copy-start(bf16[384,4,128]{0,2,1:T(8,128)(2,1)} %copy.137) | copy-start | bytes 1179652
  272.3 26.4 %collective-permute-start.1 = (f32[512,512]{0,1:T(8,128)}, f32[512,512]{0,1:T(8,128)}, u32[]{:S(2)}, u32[]{:S(2)}) collective-permute-start(f32[512,512]{0,1:T(8,128)} %constant_dynamic-slice_fusion.2), channel_id=1, source_target_pairs={{0,4},{4,0},{1,5},{5,1},{2,6},{6,2},{3,7},{7,3},{8,12},{12,8},{9,1... | collective-permute-start | bytes 3145736 | tf_op jit(solution)/shard_map/ppermute | solution.py:236
  284.6 5.2 %copy-start.32 = (bf16[384,128]{0,1:T(8,128)(2,1)S(1)}, bf16[384,128]{0,1:T(8,128)(2,1)}, u32[]{:S(2)}) copy-start(bf16[384,128]{0,1:T(8,128)(2,1)} %slice.161) | copy-start | bytes 294916
  284.6 5.2 %copy-start.34 = (bf16[384,128]{0,1:T(8,128)(2,1)S(1)}, bf16[384,128]{0,1:T(8,128)(2,1)}, u32[]{:S(2)}) copy-start(bf16[384,128]{0,1:T(8,128)(2,1)} %maximum_bitcast_fusion.1) | copy-start | bytes 294916
  288.2 6.4 %copy-start.9 = (bf16[384,4,128]{0,2,1:T(8,128)(2,1)S(1)}, bf16[384,4,128]{0,2,1:T(8,128)(2,1)}, u32[]{:S(2)}) copy-start(bf16[384,4,128]{0,2,1:T(8,128)(2,1)} %copy.147) | copy-start | bytes 1179652
  288.2 6.4 %copy-start.10 = (bf16[4096,512]{1,0:T(8,128)(2,1)S(1)}, bf16[4096,512]{1,0:T(8,128)(2,1)}, u32[]{:S(2)}) copy-start(bf16[4096,512]{1,0:T(8,128)(2,1)} %all-gather.7.cloned.1.call-done) | copy-start | bytes 12582916
  288.3 30.3 %collective-permute-start.2 = (f32[512,512]{0,1:T(8,128)S(1)}, f32[512,512]{0,1:T(8,128)S(1)}, u32[]{:S(2)}, u32[]{:S(2)}) collective-permute-start(f32[512,512]{0,1:T(8,128)S(1)} %constant_dynamic-slice_fusion.1), channel_id=1, source_target_pairs={{0,4},{4,0},{1,5},{5,1},{2,6},{6,2},{3,7},{7,3},{8,12},{12,8},{9,1... | collective-permute-start | bytes 3145736 | tf_op jit(solution)/shard_map/ppermute | solution.py:236
  294.7 4.0 %copy-start.26 = (f32[1024,512]{0,1:T(8,128)S(1)}, f32[1024,512]{0,1:T(8,128)}, u32[]{:S(2)}) copy-start(f32[1024,512]{0,1:T(8,128)} %copy-done.25) | copy-start | bytes 6291460
  322.4 4.9 %copy-start.33 = (bf16[384,128]{0,1:T(8,128)(2,1)S(1)}, bf16[384,128]{0,1:T(8,128)(2,1)}, u32[]{:S(2)}) copy-start(bf16[384,128]{0,1:T(8,128)(2,1)} %slice.161) | copy-start | bytes 294916
  322.4 4.9 %copy-start.35 = (bf16[384,128]{0,1:T(8,128)(2,1)S(1)}, bf16[384,128]{0,1:T(8,128)(2,1)}, u32[]{:S(2)}) copy-start(bf16[384,128]{0,1:T(8,128)(2,1)} %maximum_bitcast_fusion.1) | copy-start | bytes 294916
  322.4 24.2 %copy-start.23 = (bf16[4,4,96,1024]{3,2,1,0:T(8,128)(2,1)S(1)}, bf16[4,4,96,1024]{3,2,1,0:T(8,128)(2,1)}, u32[]{:S(2)}) copy-start(bf16[4,4,96,1024]{3,2,1,0:T(8,128)(2,1)} %copy.138) | copy-start | bytes 9437188
  322.4 42.7 %all-to-all-start.2 = ((bf16[384,4,1024]{2,0,1:T(8,128)(2,1)}), bf16[384,4,1024]{2,0,1:T(8,128)(2,1)}, u32[]{:S(2)}, u32[]{:S(2)}) async-start(bf16[384,4,1024]{2,0,1:T(8,128)(2,1)} %bitcast.163), calls=%async_computation.2 | async-start | bytes 6291456 | tf_op jit(solution)/shard_map/all_to_all | solution.py:309
  327.4 22.1 %copy-start.36 = (bf16[128,4,384]{2,0,1:T(8,128)(2,1)S(1)}, bf16[128,4,384]{2,0,1:T(8,128)(2,1)}, u32[]{:S(2)}) copy-start(bf16[128,4,384]{2,0,1:T(8,128)(2,1)} %get-tuple-element.75) | copy-start | bytes 1179652
  327.4 22.1 %copy-start.37 = (bf16[128,4,384]{2,0,1:T(8,128)(2,1)S(1)}, bf16[128,4,384]{2,0,1:T(8,128)(2,1)}, u32[]{:S(2)}) copy-start(bf16[128,4,384]{2,0,1:T(8,128)(2,1)} %get-tuple-element.79) | copy-start | bytes 1179652
  347.7 1.8 copy-start.30
  347.8 12.3 %collective-permute-start.4 = (f32[512,256]{1,0:T(8,128)S(1)}, f32[512,256]{1,0:T(8,128)}, u32[]{:S(2)}, u32[]{:S(2)}) collective-permute-start(f32[512,256]{1,0:T(8,128)S(1)} %constant_dynamic-slice_fusion), channel_id=1, source_target_pairs={{0,4},{4,0},{1,5},{5,1},{2,6},{6,2},{3,7},{7,3},{8,12},{12,8},{9,1... | collective-permute-start | bytes 1572872 | tf_op jit(solution)/shard_map/ppermute | solution.py:236
  360.0 8.8 %copy-start.1 = (bf16[384,4096]{1,0:T(8,128)(2,1)S(1)}, bf16[384,4096]{1,0:T(8,128)(2,1)}, u32[]{:S(2)}) copy-start(bf16[384,4096]{1,0:T(8,128)(2,1)} %param.6) | copy-start | bytes 9437188
Sparse Core Ops, SparseCore 0:
  10.8 112.8 all-gather.4
  125.8 71.6 all-gather.6
  208.8 35.3 all-gather.8
  248.6 36.0 all-gather.10

commit v15 on v13

--- a/solution.py
+++ b/solution.py
@@ -233,7 +233,8 @@
             away_part = lax.dynamic_slice_in_dim(
                 partial, (1 - ctx_index) * weight_rows, weight_rows, 0
             )
-            return own_part + lax.ppermute(away_part, "ctx", [(0, 1), (1, 0)])
+            sent = lax.ppermute(away_part.astype(jnp.bfloat16), "ctx", [(0, 1), (1, 0)])
+            return own_part + sent.astype(jnp.float32)
         return lax.psum_scatter(partial, "ctx", scatter_dimension=0, tiled=True)
 
     proj_a = jnp.dot(hidden_in, full_a, preferred_element_type=jnp.float32)

time: 347 us -> 327 us (0.942)
  waiting for transfers between devices: 157 us -> 140 us
    ppermute x2, waiting for transfers between devices: 35.8 us -> 14.8 us  [weight_grad(): sent = lax.ppermute(away_part.astype(jnp.bfloat16), 'ctx', [(0, 1), (1, 0)])]
    all_gather x1, waiting for transfers between devices: 13.6 us -> 20.8 us  [weight_grad(): gathered = lax.all_gather(d_rows, 'dp', axis=0, tiled=True)]
    unnamed x77 -> x85, local copies, waits for them, and re-layouts: 20.7 us -> 17.9 us
  transfers between devices with their start and end apart: 10 -> 10, of which waited for: 9 -> 9; matrix products, arithmetic and copies ran while one was open for 29% -> 30% of each run, Pallas kernels for 0% -> 0%
where the time goes in v15:
time: 327 us; the launch traced here: 322 us
  waiting for transfers between devices  140 us (43%)
  matrix products  47 us (14%)
  blocking collectives  42.6 us (13%)
  local copies, waits for them, and re-layouts  35.8 us (11%)
  other arithmetic  25.5 us (8%)
  starting transfers between devices  15.5 us (5%)
  between operations  14.9 us (5%)
    all_gather x1, waiting for transfers between devices, local(): full_a = lax.all_gather(local_a, rows_axes, axis=0, tiled=True)  70.5 us
    all_to_all x1, blocking collectives, local(): cols_part = lax.all_to_all(own_rows, 'dp', 1, 0, tiled=True)  42.6 us
    all_gather x1, waiting for transfers between devices, weight_grad(): gathered = lax.all_gather(d_rows, 'dp', axis=0, tiled=True)  20.8 us
    unnamed x85, local copies, waits for them, and re-layouts  17.9 us
    ppermute x2, waiting for transfers between devices, weight_grad(): sent = lax.ppermute(away_part.astype(jnp.bfloat16), 'ctx', [(0, 1), (1, 0)])  14.8 us
    all_to_all x1, waiting for transfers between devices, local(): cols_all = lax.all_to_all(spread, 'head', 0, 0, tiled=False)  13.9 us
    dot_general x2, matrix products, attend_whole(): jnp.einsum('rhd,kd->hrk', dout_rows, value_all, preferred_element_type=jn...  9.05 us
    ppermute x1, waiting for transfers between devices, local(): grad_kv = own_part + lax.ppermute(away_part, 'ctx', [(0, 1), (1, 0)])  8.12 us
  transfers between devices with their start and end apart: 10, of which 9 were waited for; matrix products, arithmetic and copies ran while one was open for 30% of the time, Pallas kernels for 0%

profile of v15, /device:TPU:0, one launch (start us, length us, event | category | flops | bytes accessed | tf_op | source)
XLA Modules:
  0.0 321.8 jit_solution(12890885880452591385)
XLA Ops:
  7.2 1.2 slice.83
  8.5 1.9 pad_maximum_fusion.1
  10.6 42.6 %all_to_all.29 = bf16[96,4,1024]{2,0,1:T(8,128)(2,1)} all-to-all(bf16[96,4,1024]{2,0,1:T(8,128)(2,1)S(1)} %bitcast.174), channel_id=1, replica_groups=mesh['dp'=4,'ctx'=2,'head'=4] {'dp'}, dimensions={1} | all-to-all | bytes 1572864 | tf_op jit(solution)/shard_map/all_to_all | solution.py:210
  53.2 70.5 %all-gather.5.cloned.1.call-done = bf16[4096,768]{1,0:T(8,128)(2,1)} async-done(((bf16[512,768]{1,0:T(8,128)(2,1)}), bf16[4096,768]{1,0:T(8,128)(2,1)}) %all-gather.5.cloned.1.call-update) | async-done | bytes 6291472 | tf_op jit(solution)/shard_map/all_gather | solution.py:203
  123.7 1.9 slice.96
  125.8 2.3 copy.138
  128.1 1.9 fusion.55
  130.0 1.9 copy.206
  132.0 0.9 copy.203
  133.4 1.5 multiply_cosine_fusion
  134.9 5.6 %convolution_bitcast_fusion = f32[384,768]{0,1:T(8,128)S(1)} fusion(bf16[4096,768]{1,0:T(8,128)(2,1)} %all-gather.5.cloned.1.call-done, bf16[384,4096]{1,0:T(8,128)(2,1)S(1)} %copy-done), kind=kOutput, calls=%fused_computation.27 | convolution fusion | flops 2415919104 | bytes 10616832 | tf_op jit(solution)/shard_map/dot_general | solution.py:240
  142.9 0.9 fusion.57
  143.9 2.2 copy.202
  146.0 2.1 copy.201
  148.2 3.2 %broadcast_in_dim.76 = bf16[4,384,1024]{2,1,0:T(8,128)(2,1)} broadcast(bf16[384,1024]{1,0:T(8,128)(2,1)} %bitcast.175), dimensions={1,2} | broadcast | bytes 3932160 | tf_op jit(solution)/shard_map/broadcast_in_dim | solution.py:216
  151.4 4.7 %all-to-all-start.1 = ((bf16[4,384,1024]{2,1,0:T(8,128)(2,1)}), bf16[4,384,1024]{2,1,0:T(8,128)(2,1)}, u32[]{:S(2)}, u32[]{:S(2)}) async-start(bf16[4,384,1024]{2,1,0:T(8,128)(2,1)} %broadcast_in_dim.76), calls=%async_computation.1 | async-start | bytes 6291456 | tf_op jit(solution)/shard_map/all_to_all | solution.py:217
  156.6 1.9 subtract_convert_fusion.3
  158.6 1.5 maximum_select_fusion
  160.1 1.2 fusion.10
  161.3 1.2 select_reduce_fusion.1
  162.5 2.4 bitcast_convert_fusion.1
  165.0 2.3 copy.174
  167.2 1.5 multiply_reduce_fusion.1
  168.8 4.5 %fusion.6 = bf16[4,384,768]{1,2,0:T(8,128)(2,1)S(1)} fusion(f32[768,384,4]{1,0,2:T(8,128)} %copy-done.2, f32[4,384]{1,0:T(4,128)S(1)} %multiply_reduce_fusion.1, f32[4,384]{1,0:T(4,128)S(1)} %log_add_fusion.1, pred[384,768]{0,1:T(8,128)(4,1)S(1)} %fusion.16, bf16[768,256]{0,1:T(8,128)(2,1)} %copy-done.12, bf16[384,8,128]{0,2,1:T(8,128)(2,1)} %bitcast.167), kind=kOutput, calls=%fused_computation.11 | convolution fusion | flops 311427072 | bytes 7974912 | tf_op jit(solution)/shard_map/rhd,kd->hrk/dot_general | solution.py:90
  173.3 1.4 copy-done.4
  174.8 1.1 convolution_bitcast_fusion.2
  176.2 1.0 pad_maximum_fusion.9
  177.2 1.9 copy.143
  179.2 13.9 %all-to-all-done.1 = bf16[4,384,1024]{2,1,0:T(8,128)(2,1)} async-done(((bf16[4,384,1024]{2,1,0:T(8,128)(2,1)}), bf16[4,384,1024]{2,1,0:T(8,128)(2,1)}, u32[]{:S(2)}, u32[]{:S(2)}) %all-to-all-start.1) | async-done | bytes 3145760 | tf_op jit(solution)/shard_map/all_to_all | solution.py:217
  193.0 4.0 %copy.144 = bf16[4,4,96,1024]{3,2,1,0:T(8,128)(2,1)} copy(bf16[4,4,96,1024]{3,2,0,1:T(8,128)(2,1)} %bitcast.25) | data formatting | bytes 6291456 | tf_op jit(solution)/shard_map/transpose | solution.py:220
  197.7 4.6 %fusion.58 = f32[512,384]{1,0:T(8,128)S(1)} fusion(bf16[4096,512]{1,0:T(8,128)(2,1)} %all-gather.7.cloned.1.call-done, bf16[384,4096]{1,0:T(8,128)(2,1)S(1)} %copy-done), kind=kOutput, calls=%fused_computation.127 | convolution fusion | flops 1610612736 | bytes 8126464 | tf_op jit(solution)/shard_map/dot_general | solution.py:270
  202.9 1.3 subtract_convert_fusion.1
  204.2 1.2 fusion.11
  205.4 1.2 select_reduce_fusion
  206.6 2.1 bitcast_convert_fusion
  209.4 4.5 %fusion.1 = bf16[4,384,768]{1,2,0:T(8,128)(2,1)S(1)} fusion(f32[768,384,4]{1,0,2:T(8,128)} %copy-done.3, f32[4,384]{1,0:T(4,128)S(1)} %multiply_reduce_fusion, f32[4,384]{1,0:T(4,128)S(1)} %log_add_fusion, pred[384,768]{0,1:T(8,128)(4,1)S(1)} %fusion.16, bf16[768,256]{0,1:T(8,128)(2,1)S(1)} %copy-done.14, bf16[384,8,128]{0,2,1:T(8,128)(2,1)} %bitcast.168), kind=kOutput, calls=%fused_computation.3 | convolution fusion | flops 311427072 | bytes 7974912 | tf_op jit(solution)/shard_map/rhd,kd->hrk/dot_general | solution.py:90
  214.0 1.0 convolution_bitcast_fusion.5
  215.0 1.0 fusion.14
  216.0 1.6 convolution_bitcast_fusion.3
  217.7 1.9 fusion.15
  219.7 1.1 collective-permute-start.2
  220.7 1.1 convolution_bitcast_fusion.1
  221.8 8.1 %collective-permute-done.2 = f32[384,256]{0,1:T(8,128)S(1)} collective-permute-done((f32[384,256]{0,1:T(8,128)S(1)}, f32[384,256]{0,1:T(8,128)S(1)}, u32[]{:S(2)}, u32[]{:S(2)}) %collective-permute-start.2) | collective-permute-done | bytes 393248 | tf_op jit(solution)/shard_map/ppermute | solution.py:287
  230.5 4.0 %all-gather.9.cloned.1.call-done = bf16[1536,512]{0,1:T(8,128)(2,1)} async-done(((bf16[384,512]{0,1:T(8,128)(2,1)}), bf16[1536,512]{0,1:T(8,128)(2,1)}) %all-gather.9.cloned.1.call-update) | async-done | bytes 1572880 | tf_op jit(solution)/shard_map/all_gather | solution.py:269
  235.2 0.9 pad_maximum_fusion.3
  236.2 5.1 %fusion.17 = f32[384,4096]{1,0:T(8,128)S(1)} fusion(bf16[4096,768]{1,0:T(8,128)(2,1)} %all-gather.5.cloned.1.call-done, bf16[384,128]{0,1:T(8,128)(2,1)} %copy-done.27, bf16[384,128]{0,1:T(8,128)(2,1)} %copy-done.28, bf16[384,512]{0,1:T(8,128)(2,1)} %bitcast.177), kind=kOutput, calls=%fused_computation.63 | convolution fusion | flops 2417688576 | bytes 13172736 | tf_op jit(solution)/shard_map/dot_general | solution.py:294
  241.3 1.9 fusion.59
  243.3 1.7 collective-permute-start.1
  245.0 1.9 convolution_add_fusion
  246.9 9.7 %collective-permute-done.1 = bf16[512,512]{1,0:T(8,128)(2,1)S(1)} collective-permute-done((bf16[512,512]{1,0:T(8,128)(2,1)S(1)}, bf16[512,512]{1,0:T(8,128)(2,1)S(1)}, u32[]{:S(2)}, u32[]{:S(2)}) %collective-permute-start.1) | collective-permute-done | bytes 524320 | tf_op jit(solution)/shard_map/ppermute | solution.py:236
  256.5 1.1 convert_add_fusion.1
  257.6 2.1 copy.211
  259.7 5.2 %all-to-all-start.2 = ((bf16[384,4,1024]{2,0,1:T(8,128)(2,1)}), bf16[384,4,1024]{2,0,1:T(8,128)(2,1)}, u32[]{:S(2)}, u32[]{:S(2)}) async-start(bf16[384,4,1024]{2,0,1:T(8,128)(2,1)} %bitcast.161), calls=%async_computation.2 | async-start | bytes 6291456 | tf_op jit(solution)/shard_map/all_to_all | solution.py:307
  264.9 20.8 %all-gather.11.cloned.1.call-done = bf16[1536,768]{0,1:T(8,128)(2,1)} async-done(((bf16[384,768]{0,1:T(8,128)(2,1)}), bf16[1536,768]{0,1:T(8,128)(2,1)}) %all-gather.11.cloned.1.call-update) | async-done | bytes 2359312 | tf_op jit(solution)/shard_map/all_gather | solution.py:227
  285.7 4.4 %fusion.60 = f32[1024,768]{1,0:T(8,128)S(1)} fusion(bf16[1536,1024]{1,0:T(8,128)(2,1)S(1)} %bitcast.165, bf16[1536,768]{0,1:T(8,128)(2,1)} %all-gather.11.cloned.1.call-done), kind=kOutput, calls=%fused_computation.129 | convolution fusion | flops 2415919104 | bytes 8650752 | tf_op jit(solution)/shard_map/dot_general | solution.py:228
  290.1 1.1 dynamic-slice_convert_fusion
  291.2 1.5 collective-permute-start.3
  292.8 1.2 copy.165
  294.0 7.9 %all-to-all-done.2 = bf16[384,4,1024]{2,0,1:T(8,128)(2,1)} async-done(((bf16[384,4,1024]{2,0,1:T(8,128)(2,1)}), bf16[384,4,1024]{2,0,1:T(8,128)(2,1)}, u32[]{:S(2)}, u32[]{:S(2)}) %all-to-all-start.2) | async-done | bytes 3145760 | tf_op jit(solution)/shard_map/all_to_all | solution.py:307
  301.9 3.8 %reduce_sum.42 = bf16[384,1024]{1,0:T(8,128)(2,1)} reduce(bf16[384,4,1024]{2,0,1:T(8,128)(2,1)} %all-to-all-done.2, bf16[]{:T(256)} %constant.40.clone.1), dimensions={1}, to_apply=%region_6.7 | reduce | flops 1179648 | bytes 3932162 | tf_op jit(solution)/shard_map/reduce_sum | solution.py:311
  305.7 5.1 %collective-permute-done.3 = bf16[512,768]{1,0:T(8,128)(2,1)} collective-permute-done((bf16[512,768]{1,0:T(8,128)(2,1)}, bf16[512,768]{1,0:T(8,128)(2,1)}, u32[]{:S(2)}, u32[]{:S(2)}) %collective-permute-start.3) | collective-permute-done | bytes 786464 | tf_op jit(solution)/shard_map/ppermute | solution.py:236
  310.8 1.8 convert_add_fusion
  312.6 0.8 fusion.54
  313.5 1.5 pad_maximum_fusion
  (121 shorter events, 7.9 us)
Async XLA Ops:
  7.2 3.3 %copy-start = (bf16[384,4096]{1,0:T(8,128)(2,1)S(1)}, bf16[384,4096]{1,0:T(8,128)(2,1)}, u32[]{:S(2)}) copy-start(bf16[384,4096]{1,0:T(8,128)(2,1)} %param.6) | copy-start | bytes 9437188
  7.2 118.4 %copy-start.32 = (s32[1,8]{1,0:T(1,128)S(1)}, s32[1,8]{1,0:T(1,128)}, u32[]{:S(2)}) copy-start(s32[1,8]{1,0:T(1,128)} %param.10) | copy-start | bytes 100
  7.2 116.5 %all-gather.5.cloned.1.call-start = ((), (), s32[]{:S(2)}) async-start(), calls=%async_computation.3 | async-start | bytes 7077888 | tf_op jit(solution)/shard_map/all_gather | solution.py:203
  10.4 187.1 %all-gather.7.cloned.1.call-start = ((), (), s32[]{:S(2)}) async-start(), calls=%async_computation.4 | async-start | bytes 4718592 | tf_op jit(solution)/shard_map/all_gather | solution.py:267
  141.1 0.6 copy-start.26
  142.4 16.2 %collective-permute-start = (bf16[384,256]{0,1:T(8,128)(2,1)}, bf16[384,256]{0,1:T(8,128)(2,1)}, u32[]{:S(2)}, u32[]{:S(2)}) collective-permute-start(bf16[384,256]{0,1:T(8,128)(2,1)} %pad_maximum_fusion.12), channel_id=1, source_target_pairs={{0,4},{4,0},{1,5},{5,1},{2,6},{6,2},{3,7},{7,3},{8,12},{12,8},{9,1... | collective-permute-start | bytes 589832 | tf_op jit(solution)/shard_map/ppermute | solution.py:250
  151.4 41.7 %all-to-all-start.1 = ((bf16[4,384,1024]{2,1,0:T(8,128)(2,1)}), bf16[4,384,1024]{2,1,0:T(8,128)(2,1)}, u32[]{:S(2)}, u32[]{:S(2)}) async-start(bf16[4,384,1024]{2,1,0:T(8,128)(2,1)} %broadcast_in_dim.76), calls=%async_computation.1 | async-start | bytes 6291456 | tf_op jit(solution)/shard_map/all_to_all | solution.py:217
  156.0 78.4 %all-gather.9.cloned.1.call-start = ((), (), s32[]{:S(2)}) async-start(), calls=%async_computation.5 | async-start | bytes 1966080 | tf_op jit(solution)/shard_map/all_gather | solution.py:269
  158.5 1.5 copy-start.17
  158.5 2.8 copy-start.19
  160.1 2.5 copy-start.12
  161.3 3.6 %copy-start.2 = (f32[768,384,4]{1,0,2:T(8,128)}, f32[768,384,4]{1,0,2:T(8,128)S(1)}, u32[]{:S(2)}) copy-start(f32[768,384,4]{1,0,2:T(8,128)S(1)} %get-tuple-element.73) | copy-start | bytes 14155780
  168.8 6.0 %copy-start.13 = (bf16[768,256]{0,1:T(8,128)(2,1)S(1)}, bf16[768,256]{0,1:T(8,128)(2,1)}, u32[]{:S(2)}) copy-start(bf16[768,256]{0,1:T(8,128)(2,1)} %copy-done.12) | copy-start | bytes 1179652
  168.8 7.1 %copy-start.6 = (f32[384,64]{1,0:T(8,128)S(1)}, f32[384,64]{1,0:T(8,128)}, u32[]{:S(2)}) copy-start(f32[384,64]{1,0:T(8,128)} %get-tuple-element.70) | copy-start | bytes 294916
  168.8 7.1 %copy-start.8 = (f32[384,64]{1,0:T(8,128)S(1)}, f32[384,64]{1,0:T(8,128)}, u32[]{:S(2)}) copy-start(f32[384,64]{1,0:T(8,128)} %get-tuple-element.71) | copy-start | bytes 294916
  173.3 1.5 copy-start.4
  197.5 88.2 %all-gather.11.cloned.1.call-start = ((), (), s32[]{:S(2)}) async-start(), calls=%async_computation.6 | async-start | bytes 2949120 | tf_op jit(solution)/shard_map/all_gather | solution.py:227
  202.3 1.9 copy-start.14
  204.2 2.4 copy-start.15
  205.4 3.4 %copy-start.3 = (f32[768,384,4]{1,0,2:T(8,128)}, f32[768,384,4]{1,0,2:T(8,128)S(1)}, u32[]{:S(2)}) copy-start(f32[768,384,4]{1,0,2:T(8,128)S(1)} %get-tuple-element.77) | copy-start | bytes 14155780
  206.6 2.4 copy-start.25
  209.1 6.9 %slice-start.2 = ((s8[4718592]{0:T(1024)(128)(4,1)}), s8[4194304]{0:T(1024)(128)(4,1)S(1)}, s32[]{:S(2)}) async-start(s8[4718592]{0:T(1024)(128)(4,1)} %bitcast.158), calls=%async_computation.9 | async-start | bytes 8388608
  209.3 4.6 %copy-start.16 = (bf16[384,4,64]{2,0,1:T(8,128)(2,1)S(1)}, bf16[384,4,64]{2,0,1:T(8,128)(2,1)}, u32[]{:S(2)}) copy-start(bf16[384,4,64]{2,0,1:T(8,128)(2,1)} %copy-done.15) | copy-start | bytes 589828
  209.4 5.6 %copy-start.5 = (bf16[4,384,768]{1,2,0:T(8,128)(2,1)S(1)}, bf16[4,384,768]{1,2,0:T(8,128)(2,1)}, u32[]{:S(2)}) copy-start(bf16[4,384,768]{1,2,0:T(8,128)(2,1)} %copy-done.4) | copy-start | bytes 7077892
  209.4 5.6 %copy-start.18 = (bf16[384,4,64]{2,0,1:T(8,128)(2,1)S(1)}, bf16[384,4,64]{2,0,1:T(8,128)(2,1)}, u32[]{:S(2)}) copy-start(bf16[384,4,64]{2,0,1:T(8,128)(2,1)} %copy-done.17) | copy-start | bytes 589828
  209.4 5.6 %copy-start.20 = (bf16[384,4,64]{2,0,1:T(8,128)(2,1)S(1)}, bf16[384,4,64]{2,0,1:T(8,128)(2,1)}, u32[]{:S(2)}) copy-start(bf16[384,4,64]{2,0,1:T(8,128)(2,1)} %copy-done.19) | copy-start | bytes 589828
  209.4 6.6 %slice-start.3 = ((s8[4718592]{0:T(1024)(128)(4,1)}), s8[524288]{0:T(1024)(128)(4,1)S(1)}, s32[]{:S(2)}) async-start(s8[4718592]{0:T(1024)(128)(4,1)} %bitcast.158), calls=%async_computation.10 | async-start | bytes 1048576
  214.0 2.0 copy-start.23
  215.0 2.7 slice-start
  216.0 1.7 slice-start.1
  219.6 14.8 %copy-start.7 = (f32[384,64]{1,0:T(8,128)S(1)}, f32[384,64]{1,0:T(8,128)}, u32[]{:S(2)}) copy-start(f32[384,64]{1,0:T(8,128)} %get-tuple-element.70) | copy-start | bytes 294916
  219.6 14.8 %copy-start.9 = (f32[384,64]{1,0:T(8,128)S(1)}, f32[384,64]{1,0:T(8,128)}, u32[]{:S(2)}) copy-start(f32[384,64]{1,0:T(8,128)} %get-tuple-element.71) | copy-start | bytes 294916
  219.7 10.2 %collective-permute-start.2 = (f32[384,256]{0,1:T(8,128)S(1)}, f32[384,256]{0,1:T(8,128)S(1)}, u32[]{:S(2)}, u32[]{:S(2)}) collective-permute-start(f32[384,256]{0,1:T(8,128)S(1)} %fusion.19), channel_id=1, source_target_pairs={{0,4},{4,0},{1,5},{5,1},{2,6},{6,2},{3,7},{7,3},{8,12},{12,8},{9,1... | collective-permute-start | bytes 1179656 | tf_op jit(solution)/shard_map/ppermute | solution.py:287
  230.0 6.2 %copy-start.27 = (bf16[384,128]{0,1:T(8,128)(2,1)}, bf16[384,128]{0,1:T(8,128)(2,1)S(1)}, u32[]{:S(2)}) copy-start(bf16[384,128]{0,1:T(8,128)(2,1)S(1)} %slice.169) | copy-start | bytes 294916
  230.5 5.7 %copy-start.28 = (bf16[384,128]{0,1:T(8,128)(2,1)}, bf16[384,128]{0,1:T(8,128)(2,1)S(1)}, u32[]{:S(2)}) copy-start(bf16[384,128]{0,1:T(8,128)(2,1)S(1)} %maximum_bitcast_fusion.1) | copy-start | bytes 294916
  236.2 5.1 %copy-start.21 = (bf16[4,4,96,1024]{3,2,1,0:T(8,128)(2,1)S(1)}, bf16[4,4,96,1024]{3,2,1,0:T(8,128)(2,1)}, u32[]{:S(2)}) copy-start(bf16[4,4,96,1024]{3,2,1,0:T(8,128)(2,1)} %copy.144) | copy-start | bytes 9437188
  236.2 5.1 %copy-start.31 = (bf16[1536,512]{0,1:T(8,128)(2,1)S(1)}, bf16[1536,512]{0,1:T(8,128)(2,1)}, u32[]{:S(2)}) copy-start(bf16[1536,512]{0,1:T(8,128)(2,1)} %all-gather.9.cloned.1.call-done) | copy-start | bytes 4718596
  241.3 3.7 %copy-start.11 = (bf16[4096,512]{1,0:T(8,128)(2,1)S(1)}, bf16[4096,512]{1,0:T(8,128)(2,1)}, u32[]{:S(2)}) copy-start(bf16[4096,512]{1,0:T(8,128)(2,1)} %all-gather.7.cloned.1.call-done) | copy-start | bytes 12582916
  243.3 13.2 %collective-permute-start.1 = (bf16[512,512]{1,0:T(8,128)(2,1)S(1)}, bf16[512,512]{1,0:T(8,128)(2,1)S(1)}, u32[]{:S(2)}, u32[]{:S(2)}) collective-permute-start(bf16[512,512]{1,0:T(8,128)(2,1)S(1)} %dynamic-slice_convert_fusion.1), channel_id=1, source_target_pairs={{0,4},{4,0},{1,5},{5,1},{2,6},{6,2},{3,7},{7,3},{8,12},{12,8},{9,1... | collective-permute-start | bytes 1572872 | tf_op jit(solution)/shard_map/ppermute | solution.py:236
  259.7 26.0 %copy-start.22 = (bf16[4,4,96,1024]{3,2,1,0:T(8,128)(2,1)S(1)}, bf16[4,4,96,1024]{3,2,1,0:T(8,128)(2,1)}, u32[]{:S(2)}) copy-start(bf16[4,4,96,1024]{3,2,1,0:T(8,128)(2,1)} %copy.144) | copy-start | bytes 9437188
  259.7 42.2 %all-to-all-start.2 = ((bf16[384,4,1024]{2,0,1:T(8,128)(2,1)}), bf16[384,4,1024]{2,0,1:T(8,128)(2,1)}, u32[]{:S(2)}, u32[]{:S(2)}) async-start(bf16[384,4,1024]{2,0,1:T(8,128)(2,1)} %bitcast.161), calls=%async_computation.2 | async-start | bytes 6291456 | tf_op jit(solution)/shard_map/all_to_all | solution.py:307
  264.9 27.8 %copy-start.29 = (bf16[128,4,384]{2,0,1:T(8,128)(2,1)S(1)}, bf16[128,4,384]{2,0,1:T(8,128)(2,1)}, u32[]{:S(2)}) copy-start(bf16[128,4,384]{2,0,1:T(8,128)(2,1)} %get-tuple-element.75) | copy-start | bytes 1179652
  285.7 7.0 %copy-start.30 = (bf16[128,4,384]{2,0,1:T(8,128)(2,1)S(1)}, bf16[128,4,384]{2,0,1:T(8,128)(2,1)}, u32[]{:S(2)}) copy-start(bf16[128,4,384]{2,0,1:T(8,128)(2,1)} %get-tuple-element.79) | copy-start | bytes 1179652
  290.1 2.6 copy-start.24
  291.2 19.6 %collective-permute-start.3 = (bf16[512,768]{1,0:T(8,128)(2,1)}, bf16[512,768]{1,0:T(8,128)(2,1)}, u32[]{:S(2)}, u32[]{:S(2)}) collective-permute-start(bf16[512,768]{1,0:T(8,128)(2,1)} %dynamic-slice_convert_fusion), channel_id=1, source_target_pairs={{0,4},{4,0},{1,5},{5,1},{2,6},{6,2},{3,7},{7,3},{8,12},{12,8},{9,1... | collective-permute-start | bytes 2359304 | tf_op jit(solution)/shard_map/ppermute | solution.py:236
  301.9 13.1 %copy-start.1 = (bf16[384,4096]{1,0:T(8,128)(2,1)S(1)}, bf16[384,4096]{1,0:T(8,128)(2,1)}, u32[]{:S(2)}) copy-start(bf16[384,4096]{1,0:T(8,128)(2,1)} %param.6) | copy-start | bytes 9437188
  305.7 7.9 %copy-start.10 = (f32[512,512]{1,0:T(8,128)S(1)}, f32[512,512]{1,0:T(8,128)}, u32[]{:S(2)}) copy-start(f32[512,512]{1,0:T(8,128)} %convert_add_fusion.1) | copy-start | bytes 3145732
Sparse Core Ops, SparseCore 0:
  10.8 112.8 all-gather.4
  125.8 71.6 all-gather.6
  199.1 35.3 all-gather.8
  236.5 49.2 all-gather.10

commit v16 on v15

--- a/solution.py
+++ b/solution.py
@@ -265,7 +265,7 @@
     if first_heads < head_count:
         w_rest = w_query[:, first_cols:]
         full_b = lax.all_gather(w_rest, rows_axes, axis=0, tiled=True)
-        d_query_a, full_b, hidden_cols = lax.optimization_barrier((d_query_a, full_b, hidden_cols))
+        d_query_a, full_b = lax.optimization_barrier((d_query_a, full_b))
         early_all = lax.all_gather(d_query_a, "dp", axis=0, tiled=True)
         proj_b = jnp.dot(hidden_in, full_b, preferred_element_type=jnp.float32)
         query_b = rotate(

time: 327 us -> 327 us (level)
    all_gather x1, waiting for transfers between devices: 0.46 us -> 18.4 us  [local(): full_b = lax.all_gather(w_rest, rows_axes, axis=0, tiled=True)]
    all_to_all x1, waiting for transfers between devices: 13.9 us -> 0.01 us  [local(): cols_all = lax.all_to_all(spread, 'head', 0, 0, tiled=False)]
    all_to_all x1, waiting for transfers between devices: 7.93 us -> 11.3 us  [local(): lax.all_to_all(input_part.astype(jnp.bfloat16).reshape(num_rows, head_gro...]
    all_gather x1, waiting for transfers between devices: 20.8 us -> 17.5 us  [weight_grad(): gathered = lax.all_gather(d_rows, 'dp', axis=0, tiled=True)]
    unnamed x85 -> x89, local copies, waits for them, and re-layouts: 17.9 us -> 17.9 us
  transfers between devices with their start and end apart: 10 -> 10, of which waited for: 9 -> 8; matrix products, arithmetic and copies ran while one was open for 30% -> 30% of each run, Pallas kernels for 0% -> 0%
where the time goes in v16:
time: 327 us; the launch traced here: 322 us
  waiting for transfers between devices  142 us (43%)
  matrix products  47.9 us (15%)
  blocking collectives  42.6 us (13%)
  local copies, waits for them, and re-layouts  34.1 us (10%)
  other arithmetic  25.6 us (8%)
  between operations  14.9 us (5%)
  starting transfers between devices  14.8 us (5%)
    all_gather x1, waiting for transfers between devices, local(): full_a = lax.all_gather(local_a, rows_axes, axis=0, tiled=True)  70.5 us
    all_to_all x1, blocking collectives, local(): cols_part = lax.all_to_all(own_rows, 'dp', 1, 0, tiled=True)  42.6 us
    all_gather x1, waiting for transfers between devices, local(): full_b = lax.all_gather(w_rest, rows_axes, axis=0, tiled=True)  18.4 us
    unnamed x89, local copies, waits for them, and re-layouts  17.9 us
    all_gather x1, waiting for transfers between devices, weight_grad(): gathered = lax.all_gather(d_rows, 'dp', axis=0, tiled=True)  17.5 us
    ppermute x2, waiting for transfers between devices, weight_grad(): sent = lax.ppermute(away_part.astype(jnp.bfloat16), 'ctx', [(0, 1), (1, 0)])  11.6 us
    all_to_all x1, waiting for transfers between devices, local(): lax.all_to_all(input_part.astype(jnp.bfloat16).reshape(num_rows, head_gro...  11.3 us
    dot_general x2, matrix products, attend_whole(): jnp.einsum('rhd,kd->hrk', dout_rows, value_all, preferred_element_type=jn...  9.06 us
  transfers between devices with their start and end apart: 10, of which 8 were waited for; matrix products, arithmetic and copies ran while one was open for 30% of the time, Pallas kernels for 0%

profile of v16, /device:TPU:0, one launch (start us, length us, event | category | flops | bytes accessed | tf_op | source)
XLA Modules:
  0.0 321.8 jit_solution(12983917045259641590)
XLA Ops:
  7.2 1.2 slice.83
  8.5 1.9 pad_maximum_fusion.1
  10.6 42.6 %all_to_all.29 = bf16[96,4,1024]{2,0,1:T(8,128)(2,1)} all-to-all(bf16[96,4,1024]{2,0,1:T(8,128)(2,1)S(1)} %bitcast.174), channel_id=1, replica_groups=mesh['dp'=4,'ctx'=2,'head'=4] {'dp'}, dimensions={1} | all-to-all | bytes 1572864 | tf_op jit(solution)/shard_map/all_to_all | solution.py:210
  53.2 70.5 %all-gather.5.cloned.1.call-done = bf16[4096,768]{1,0:T(8,128)(2,1)} async-done(((bf16[512,768]{1,0:T(8,128)(2,1)}), bf16[4096,768]{1,0:T(8,128)(2,1)}) %all-gather.5.cloned.1.call-update) | async-done | bytes 6291472 | tf_op jit(solution)/shard_map/all_gather | solution.py:203
  123.7 1.9 slice.96
  125.8 2.3 copy.138
  128.1 1.9 fusion.55
  130.0 1.9 copy.206
  132.0 0.9 copy.203
  133.4 1.5 multiply_cosine_fusion
  134.9 5.6 %convolution_bitcast_fusion = f32[384,768]{0,1:T(8,128)S(1)} fusion(bf16[4096,768]{1,0:T(8,128)(2,1)} %all-gather.5.cloned.1.call-done, bf16[384,4096]{1,0:T(8,128)(2,1)S(1)} %copy-done), kind=kOutput, calls=%fused_computation.27 | convolution fusion | flops 2415919104 | bytes 10616832 | tf_op jit(solution)/shard_map/dot_general | solution.py:240
  141.7 0.7 pad_maximum_fusion.12
  142.9 0.9 fusion.57
  143.9 2.2 copy.202
  146.0 2.1 copy.201
  148.2 3.2 %broadcast_in_dim.76 = bf16[4,384,1024]{2,1,0:T(8,128)(2,1)} broadcast(bf16[384,1024]{1,0:T(8,128)(2,1)} %bitcast.175), dimensions={1,2} | broadcast | bytes 3932160 | tf_op jit(solution)/shard_map/broadcast_in_dim | solution.py:216
  151.4 4.6 %all-to-all-start.1 = ((bf16[4,384,1024]{2,1,0:T(8,128)(2,1)}), bf16[4,384,1024]{2,1,0:T(8,128)(2,1)}, u32[]{:S(2)}, u32[]{:S(2)}) async-start(bf16[4,384,1024]{2,1,0:T(8,128)(2,1)} %broadcast_in_dim.76), calls=%async_computation.1 | async-start | bytes 6291456 | tf_op jit(solution)/shard_map/all_to_all | solution.py:217
  156.6 1.9 subtract_convert_fusion.3
  158.6 1.5 maximum_select_fusion
  160.1 1.2 fusion.10
  161.4 1.2 select_reduce_fusion.1
  162.5 2.4 bitcast_convert_fusion.1
  165.0 2.3 copy.174
  167.2 1.5 multiply_reduce_fusion.1
  168.8 4.5 %fusion.6 = bf16[4,384,768]{1,2,0:T(8,128)(2,1)S(1)} fusion(f32[768,384,4]{1,0,2:T(8,128)} %copy-done.2, f32[4,384]{1,0:T(4,128)S(1)} %multiply_reduce_fusion.1, f32[4,384]{1,0:T(4,128)S(1)} %log_add_fusion.1, pred[384,768]{0,1:T(8,128)(4,1)S(1)} %fusion.16, bf16[768,256]{0,1:T(8,128)(2,1)} %copy-done.12, bf16[384,8,128]{0,2,1:T(8,128)(2,1)} %bitcast.167), kind=kOutput, calls=%fused_computation.11 | convolution fusion | flops 311427072 | bytes 7974912 | tf_op jit(solution)/shard_map/rhd,kd->hrk/dot_general | solution.py:90
  173.3 1.4 copy-done.4
  174.7 1.1 convolution_bitcast_fusion.2
  176.2 1.0 pad_maximum_fusion.9
  177.2 1.9 copy.143
  179.1 18.4 %all-gather.7.cloned.1.call-done = bf16[4096,512]{1,0:T(8,128)(2,1)} async-done(((bf16[512,512]{1,0:T(8,128)(2,1)}), bf16[4096,512]{1,0:T(8,128)(2,1)}) %all-gather.7.cloned.1.call-update) | async-done | bytes 4194320 | tf_op jit(solution)/shard_map/all_gather | solution.py:267
  197.7 4.6 %fusion.58 = f32[512,384]{1,0:T(8,128)S(1)} fusion(bf16[4096,512]{1,0:T(8,128)(2,1)} %all-gather.7.cloned.1.call-done, bf16[384,4096]{1,0:T(8,128)(2,1)S(1)} %copy-done), kind=kOutput, calls=%fused_computation.127 | convolution fusion | flops 1610612736 | bytes 8126464 | tf_op jit(solution)/shard_map/dot_general | solution.py:270
  202.9 1.3 subtract_convert_fusion.1
  204.2 1.2 fusion.11
  205.4 1.2 select_reduce_fusion
  206.6 2.1 bitcast_convert_fusion
  209.4 4.5 %fusion.1 = bf16[4,384,768]{1,2,0:T(8,128)(2,1)S(1)} fusion(f32[768,384,4]{1,0,2:T(8,128)} %copy-done.3, f32[4,384]{1,0:T(4,128)S(1)} %multiply_reduce_fusion, f32[4,384]{1,0:T(4,128)S(1)} %log_add_fusion, pred[384,768]{0,1:T(8,128)(4,1)S(1)} %fusion.16, bf16[768,256]{0,1:T(8,128)(2,1)S(1)} %copy-done.14, bf16[384,8,128]{0,2,1:T(8,128)(2,1)} %bitcast.168), kind=kOutput, calls=%fused_computation.3 | convolution fusion | flops 311427072 | bytes 7974912 | tf_op jit(solution)/shard_map/rhd,kd->hrk/dot_general | solution.py:90
  214.0 1.0 convolution_bitcast_fusion.5
  215.0 1.0 fusion.14
  216.0 1.7 convolution_bitcast_fusion.3
  217.7 1.9 fusion.15
  220.2 1.1 convolution_bitcast_fusion.1
  221.3 8.1 %collective-permute-done.2 = f32[384,256]{0,1:T(8,128)S(1)} collective-permute-done((f32[384,256]{0,1:T(8,128)S(1)}, f32[384,256]{0,1:T(8,128)S(1)}, u32[]{:S(2)}, u32[]{:S(2)}) %collective-permute-start.2) | collective-permute-done | bytes 393248 | tf_op jit(solution)/shard_map/ppermute | solution.py:287
  229.9 4.5 %all-gather.9.cloned.1.call-done = bf16[1536,512]{0,1:T(8,128)(2,1)} async-done(((bf16[384,512]{0,1:T(8,128)(2,1)}), bf16[1536,512]{0,1:T(8,128)(2,1)}) %all-gather.9.cloned.1.call-update) | async-done | bytes 1572880 | tf_op jit(solution)/shard_map/all_gather | solution.py:269
  235.2 0.9 pad_maximum_fusion.3
  236.2 2.3 copy.148
  238.6 6.1 %fusion.17 = f32[384,4096]{1,0:T(8,128)S(1)} fusion(bf16[4096,768]{1,0:T(8,128)(2,1)} %all-gather.5.cloned.1.call-done, bf16[384,128]{0,1:T(8,128)(2,1)S(1)} %copy-done.28, bf16[384,128]{0,1:T(8,128)(2,1)S(1)} %copy-done.30, bf16[384,512]{0,1:T(8,128)(2,1)} %bitcast.177), kind=kOutput, calls=%fused_computation.63 | convolution fusion | flops 2417688576 | bytes 13172736 | tf_op jit(solution)/shard_map/dot_general | solution.py:294
  244.7 1.8 fusion.59
  246.6 1.6 collective-permute-start.1
  248.2 1.9 convolution_add_fusion
  250.0 9.8 %collective-permute-done.1 = bf16[512,512]{1,0:T(8,128)(2,1)S(1)} collective-permute-done((bf16[512,512]{1,0:T(8,128)(2,1)S(1)}, bf16[512,512]{1,0:T(8,128)(2,1)S(1)}, u32[]{:S(2)}, u32[]{:S(2)}) %collective-permute-start.1) | collective-permute-done | bytes 524320 | tf_op jit(solution)/shard_map/ppermute | solution.py:236
  259.8 1.1 convert_add_fusion.1
  261.0 2.1 copy.211
  263.1 5.2 %all-to-all-start.2 = ((bf16[384,4,1024]{2,0,1:T(8,128)(2,1)}), bf16[384,4,1024]{2,0,1:T(8,128)(2,1)}, u32[]{:S(2)}, u32[]{:S(2)}) async-start(bf16[384,4,1024]{2,0,1:T(8,128)(2,1)} %bitcast.161), calls=%async_computation.2 | async-start | bytes 6291456 | tf_op jit(solution)/shard_map/all_to_all | solution.py:307
  268.2 17.5 %all-gather.11.cloned.1.call-done = bf16[1536,768]{0,1:T(8,128)(2,1)} async-done(((bf16[384,768]{0,1:T(8,128)(2,1)}), bf16[1536,768]{0,1:T(8,128)(2,1)}) %all-gather.11.cloned.1.call-update) | async-done | bytes 2359312 | tf_op jit(solution)/shard_map/all_gather | solution.py:227
  285.7 4.4 %fusion.60 = f32[1024,768]{1,0:T(8,128)S(1)} fusion(bf16[1536,1024]{1,0:T(8,128)(2,1)S(1)} %bitcast.165, bf16[1536,768]{0,1:T(8,128)(2,1)} %all-gather.11.cloned.1.call-done), kind=kOutput, calls=%fused_computation.129 | convolution fusion | flops 2415919104 | bytes 8650752 | tf_op jit(solution)/shard_map/dot_general | solution.py:228
  290.1 1.1 dynamic-slice_convert_fusion
  291.2 1.5 collective-permute-start.3
  292.8 1.2 copy.165
  293.9 11.3 %all-to-all-done.2 = bf16[384,4,1024]{2,0,1:T(8,128)(2,1)} async-done(((bf16[384,4,1024]{2,0,1:T(8,128)(2,1)}), bf16[384,4,1024]{2,0,1:T(8,128)(2,1)}, u32[]{:S(2)}, u32[]{:S(2)}) %all-to-all-start.2) | async-done | bytes 3145760 | tf_op jit(solution)/shard_map/all_to_all | solution.py:307
  305.2 3.8 %reduce_sum.42 = bf16[384,1024]{1,0:T(8,128)(2,1)} reduce(bf16[384,4,1024]{2,0,1:T(8,128)(2,1)} %all-to-all-done.2, bf16[]{:T(256)} %constant.40.clone.1), dimensions={1}, to_apply=%region_6.7 | reduce | flops 1179648 | bytes 3932162 | tf_op jit(solution)/shard_map/reduce_sum | solution.py:311
  309.0 1.7 collective-permute-done.3
  310.7 1.8 convert_add_fusion
  312.5 0.8 fusion.54
  313.5 1.5 pad_maximum_fusion
  (125 shorter events, 7.3 us)
Async XLA Ops:
  7.2 3.3 %copy-start = (bf16[384,4096]{1,0:T(8,128)(2,1)S(1)}, bf16[384,4096]{1,0:T(8,128)(2,1)}, u32[]{:S(2)}) copy-start(bf16[384,4096]{1,0:T(8,128)(2,1)} %param.6) | copy-start | bytes 9437188
  7.2 118.4 %copy-start.34 = (s32[1,8]{1,0:T(1,128)S(1)}, s32[1,8]{1,0:T(1,128)}, u32[]{:S(2)}) copy-start(s32[1,8]{1,0:T(1,128)} %param.10) | copy-start | bytes 100
  7.2 116.5 %all-gather.5.cloned.1.call-start = ((), (), s32[]{:S(2)}) async-start(), calls=%async_computation.3 | async-start | bytes 7077888 | tf_op jit(solution)/shard_map/all_gather | solution.py:203
  10.4 187.1 %all-gather.7.cloned.1.call-start = ((), (), s32[]{:S(2)}) async-start(), calls=%async_computation.4 | async-start | bytes 4718592 | tf_op jit(solution)/shard_map/all_gather | solution.py:267
  141.1 0.7 copy-start.26
  142.4 16.2 %collective-permute-start = (bf16[384,256]{0,1:T(8,128)(2,1)}, bf16[384,256]{0,1:T(8,128)(2,1)}, u32[]{:S(2)}, u32[]{:S(2)}) collective-permute-start(bf16[384,256]{0,1:T(8,128)(2,1)} %pad_maximum_fusion.12), channel_id=1, source_target_pairs={{0,4},{4,0},{1,5},{5,1},{2,6},{6,2},{3,7},{7,3},{8,12},{12,8},{9,1... | collective-permute-start | bytes 589832 | tf_op jit(solution)/shard_map/ppermute | solution.py:250
  151.4 84.7 %all-to-all-start.1 = ((bf16[4,384,1024]{2,1,0:T(8,128)(2,1)}), bf16[4,384,1024]{2,1,0:T(8,128)(2,1)}, u32[]{:S(2)}, u32[]{:S(2)}) async-start(bf16[4,384,1024]{2,1,0:T(8,128)(2,1)} %broadcast_in_dim.76), calls=%async_computation.1 | async-start | bytes 6291456 | tf_op jit(solution)/shard_map/all_to_all | solution.py:217
  156.1 78.3 %all-gather.9.cloned.1.call-start = ((), (), s32[]{:S(2)}) async-start(), calls=%async_computation.5 | async-start | bytes 1966080 | tf_op jit(solution)/shard_map/all_gather | solution.py:269
  158.5 1.5 copy-start.17
  158.6 2.8 copy-start.19
  160.1 2.5 copy-start.12
  161.3 3.6 %copy-start.2 = (f32[768,384,4]{1,0,2:T(8,128)}, f32[768,384,4]{1,0,2:T(8,128)S(1)}, u32[]{:S(2)}) copy-start(f32[768,384,4]{1,0,2:T(8,128)S(1)} %get-tuple-element.71) | copy-start | bytes 14155780
  168.8 6.0 %copy-start.13 = (bf16[768,256]{0,1:T(8,128)(2,1)S(1)}, bf16[768,256]{0,1:T(8,128)(2,1)}, u32[]{:S(2)}) copy-start(bf16[768,256]{0,1:T(8,128)(2,1)} %copy-done.12) | copy-start | bytes 1179652
  168.8 7.0 %copy-start.6 = (f32[384,64]{1,0:T(8,128)S(1)}, f32[384,64]{1,0:T(8,128)}, u32[]{:S(2)}) copy-start(f32[384,64]{1,0:T(8,128)} %get-tuple-element.68) | copy-start | bytes 294916
  168.8 7.0 %copy-start.8 = (f32[384,64]{1,0:T(8,128)S(1)}, f32[384,64]{1,0:T(8,128)}, u32[]{:S(2)}) copy-start(f32[384,64]{1,0:T(8,128)} %get-tuple-element.69) | copy-start | bytes 294916
  173.3 1.4 copy-start.4
  197.5 88.2 %all-gather.11.cloned.1.call-start = ((), (), s32[]{:S(2)}) async-start(), calls=%async_computation.6 | async-start | bytes 2949120 | tf_op jit(solution)/shard_map/all_gather | solution.py:227
  202.3 1.9 copy-start.14
  204.2 2.4 copy-start.15
  205.4 3.4 %copy-start.3 = (f32[768,384,4]{1,0,2:T(8,128)}, f32[768,384,4]{1,0,2:T(8,128)S(1)}, u32[]{:S(2)}) copy-start(f32[768,384,4]{1,0,2:T(8,128)S(1)} %get-tuple-element.75) | copy-start | bytes 14155780
  206.6 2.4 copy-start.25
  209.0 6.9 %slice-start.2 = ((s8[4718592]{0:T(1024)(128)(4,1)}), s8[4194304]{0:T(1024)(128)(4,1)S(1)}, s32[]{:S(2)}) async-start(s8[4718592]{0:T(1024)(128)(4,1)} %bitcast.158), calls=%async_computation.9 | async-start | bytes 8388608
  209.3 4.6 %copy-start.16 = (bf16[384,4,64]{2,0,1:T(8,128)(2,1)S(1)}, bf16[384,4,64]{2,0,1:T(8,128)(2,1)}, u32[]{:S(2)}) copy-start(bf16[384,4,64]{2,0,1:T(8,128)(2,1)} %copy-done.15) | copy-start | bytes 589828
  209.4 5.6 %copy-start.5 = (bf16[4,384,768]{1,2,0:T(8,128)(2,1)S(1)}, bf16[4,384,768]{1,2,0:T(8,128)(2,1)}, u32[]{:S(2)}) copy-start(bf16[4,384,768]{1,2,0:T(8,128)(2,1)} %copy-done.4) | copy-start | bytes 7077892
  209.4 5.6 %copy-start.18 = (bf16[384,4,64]{2,0,1:T(8,128)(2,1)S(1)}, bf16[384,4,64]{2,0,1:T(8,128)(2,1)}, u32[]{:S(2)}) copy-start(bf16[384,4,64]{2,0,1:T(8,128)(2,1)} %copy-done.17) | copy-start | bytes 589828
  209.4 5.6 %copy-start.20 = (bf16[384,4,64]{2,0,1:T(8,128)(2,1)S(1)}, bf16[384,4,64]{2,0,1:T(8,128)(2,1)}, u32[]{:S(2)}) copy-start(bf16[384,4,64]{2,0,1:T(8,128)(2,1)} %copy-done.19) | copy-start | bytes 589828
  209.4 6.6 %slice-start.3 = ((s8[4718592]{0:T(1024)(128)(4,1)}), s8[524288]{0:T(1024)(128)(4,1)S(1)}, s32[]{:S(2)}) async-start(s8[4718592]{0:T(1024)(128)(4,1)} %bitcast.158), calls=%async_computation.10 | async-start | bytes 1048576
  213.9 2.0 copy-start.23
  215.0 2.7 slice-start
  216.0 1.7 slice-start.1
  219.6 14.8 %copy-start.7 = (f32[384,64]{1,0:T(8,128)S(1)}, f32[384,64]{1,0:T(8,128)}, u32[]{:S(2)}) copy-start(f32[384,64]{1,0:T(8,128)} %get-tuple-element.68) | copy-start | bytes 294916
  219.6 14.8 %copy-start.9 = (f32[384,64]{1,0:T(8,128)S(1)}, f32[384,64]{1,0:T(8,128)}, u32[]{:S(2)}) copy-start(f32[384,64]{1,0:T(8,128)} %get-tuple-element.69) | copy-start | bytes 294916
  219.7 9.7 %collective-permute-start.2 = (f32[384,256]{0,1:T(8,128)S(1)}, f32[384,256]{0,1:T(8,128)S(1)}, u32[]{:S(2)}, u32[]{:S(2)}) collective-permute-start(f32[384,256]{0,1:T(8,128)S(1)} %fusion.19), channel_id=1, source_target_pairs={{0,4},{4,0},{1,5},{5,1},{2,6},{6,2},{3,7},{7,3},{8,12},{12,8},{9,1... | collective-permute-start | bytes 1179656 | tf_op jit(solution)/shard_map/ppermute | solution.py:287
  229.4 6.7 %copy-start.27 = (bf16[384,128]{0,1:T(8,128)(2,1)}, bf16[384,128]{0,1:T(8,128)(2,1)S(1)}, u32[]{:S(2)}) copy-start(bf16[384,128]{0,1:T(8,128)(2,1)S(1)} %slice.169) | copy-start | bytes 294916
  229.9 6.2 %copy-start.29 = (bf16[384,128]{0,1:T(8,128)(2,1)}, bf16[384,128]{0,1:T(8,128)(2,1)S(1)}, u32[]{:S(2)}) copy-start(bf16[384,128]{0,1:T(8,128)(2,1)S(1)} %maximum_bitcast_fusion.1) | copy-start | bytes 294916
  236.2 2.4 copy-start.28
  236.2 2.4 copy-start.30
  238.5 6.1 %copy-start.21 = (bf16[4,4,96,1024]{3,2,1,0:T(8,128)(2,1)}, bf16[4,4,96,1024]{3,2,1,0:T(8,128)(2,1)S(1)}, u32[]{:S(2)}) copy-start(bf16[4,4,96,1024]{3,2,1,0:T(8,128)(2,1)S(1)} %copy.148) | copy-start | bytes 9437188
  238.6 6.1 %copy-start.33 = (bf16[1536,512]{0,1:T(8,128)(2,1)S(1)}, bf16[1536,512]{0,1:T(8,128)(2,1)}, u32[]{:S(2)}) copy-start(bf16[1536,512]{0,1:T(8,128)(2,1)} %all-gather.9.cloned.1.call-done) | copy-start | bytes 4718596
  244.7 3.5 %copy-start.11 = (bf16[4096,512]{1,0:T(8,128)(2,1)S(1)}, bf16[4096,512]{1,0:T(8,128)(2,1)}, u32[]{:S(2)}) copy-start(bf16[4096,512]{1,0:T(8,128)(2,1)} %all-gather.7.cloned.1.call-done) | copy-start | bytes 12582916
  246.6 13.2 %collective-permute-start.1 = (bf16[512,512]{1,0:T(8,128)(2,1)S(1)}, bf16[512,512]{1,0:T(8,128)(2,1)S(1)}, u32[]{:S(2)}, u32[]{:S(2)}) collective-permute-start(bf16[512,512]{1,0:T(8,128)(2,1)S(1)} %dynamic-slice_convert_fusion.1), channel_id=1, source_target_pairs={{0,4},{4,0},{1,5},{5,1},{2,6},{6,2},{3,7},{7,3},{8,12},{12,8},{9,1... | collective-permute-start | bytes 1572872 | tf_op jit(solution)/shard_map/ppermute | solution.py:236
  263.1 22.7 %copy-start.22 = (bf16[4,4,96,1024]{3,2,1,0:T(8,128)(2,1)S(1)}, bf16[4,4,96,1024]{3,2,1,0:T(8,128)(2,1)}, u32[]{:S(2)}) copy-start(bf16[4,4,96,1024]{3,2,1,0:T(8,128)(2,1)} %copy-done.21) | copy-start | bytes 9437188
  263.1 42.2 %all-to-all-start.2 = ((bf16[384,4,1024]{2,0,1:T(8,128)(2,1)}), bf16[384,4,1024]{2,0,1:T(8,128)(2,1)}, u32[]{:S(2)}, u32[]{:S(2)}) async-start(bf16[384,4,1024]{2,0,1:T(8,128)(2,1)} %bitcast.161), calls=%async_computation.2 | async-start | bytes 6291456 | tf_op jit(solution)/shard_map/all_to_all | solution.py:307
  268.2 24.4 %copy-start.31 = (bf16[128,4,384]{2,0,1:T(8,128)(2,1)S(1)}, bf16[128,4,384]{2,0,1:T(8,128)(2,1)}, u32[]{:S(2)}) copy-start(bf16[128,4,384]{2,0,1:T(8,128)(2,1)} %get-tuple-element.73) | copy-start | bytes 1179652
  285.7 6.9 %copy-start.32 = (bf16[128,4,384]{2,0,1:T(8,128)(2,1)S(1)}, bf16[128,4,384]{2,0,1:T(8,128)(2,1)}, u32[]{:S(2)}) copy-start(bf16[128,4,384]{2,0,1:T(8,128)(2,1)} %get-tuple-element.77) | copy-start | bytes 1179652
  290.1 2.6 copy-start.24
  291.2 19.6 %collective-permute-start.3 = (bf16[512,768]{1,0:T(8,128)(2,1)}, bf16[512,768]{1,0:T(8,128)(2,1)}, u32[]{:S(2)}, u32[]{:S(2)}) collective-permute-start(bf16[512,768]{1,0:T(8,128)(2,1)} %dynamic-slice_convert_fusion), channel_id=1, source_target_pairs={{0,4},{4,0},{1,5},{5,1},{2,6},{6,2},{3,7},{7,3},{8,12},{12,8},{9,1... | collective-permute-start | bytes 2359304 | tf_op jit(solution)/shard_map/ppermute | solution.py:236
  305.2 9.8 %copy-start.1 = (bf16[384,4096]{1,0:T(8,128)(2,1)S(1)}, bf16[384,4096]{1,0:T(8,128)(2,1)}, u32[]{:S(2)}) copy-start(bf16[384,4096]{1,0:T(8,128)(2,1)} %param.6) | copy-start | bytes 9437188
  309.0 4.5 %copy-start.10 = (f32[512,512]{1,0:T(8,128)S(1)}, f32[512,512]{1,0:T(8,128)}, u32[]{:S(2)}) copy-start(f32[512,512]{1,0:T(8,128)} %convert_add_fusion.1) | copy-start | bytes 3145732
Sparse Core Ops, SparseCore 0:
  10.8 112.8 all-gather.4
  125.8 71.6 all-gather.6
  199.1 35.2 all-gather.8
  236.4 49.2 all-gather.10

commit v17 on v16

--- a/solution.py
+++ b/solution.py
@@ -207,10 +207,11 @@
     if split_rows:
         quarter = num_rows // head_groups
         own_rows = lax.dynamic_slice_in_dim(hidden_in, lax.axis_index("head") * quarter, quarter, 0)
+        own_rows, full_a = lax.optimization_barrier((own_rows, full_a))
         cols_part = lax.all_to_all(own_rows, "dp", 1, 0, tiled=True)
     else:
         cols_part = lax.all_to_all(hidden_in, "dp", 1, 0, tiled=True)
-    full_a, w_query, cols_part = lax.optimization_barrier((full_a, w_query, cols_part))
+    full_a, w_query = lax.optimization_barrier((full_a, w_query))
     hidden_cols = cols_part
     if split_rows:
         spread = jnp.broadcast_to(cols_part[None], (head_groups,) + cols_part.shape)

time: 327 us -> 323 us (0.988)
  blocking collectives: 42.6 us -> 0 us
  waiting for transfers between devices: 142 us -> 171 us
  starting transfers between devices: 14.8 us -> 20.2 us
  local copies, waits for them, and re-layouts: 34.1 us -> 38.9 us
    all_to_all x1 -> x0, blocking collectives: 42.6 us -> none  [local(): cols_part = lax.all_to_all(own_rows, 'dp', 1, 0, tiled=True)]
    all_gather x1, waiting for transfers between devices: 70.5 us -> 101 us  [local(): full_a = lax.all_gather(local_a, rows_axes, axis=0, tiled=True)]
    all_to_all x0 -> x1, starting transfers between devices: none -> 4.72 us  [local(): cols_part = lax.all_to_all(own_rows, 'dp', 1, 0, tiled=True)]
    unnamed x89 -> x93, local copies, waits for them, and re-layouts: 17.9 us -> 17.9 us
  transfers between devices with their start and end apart: 10 -> 11, of which waited for: 8 -> 9; matrix products, arithmetic and copies ran while one was open for 30% -> 32% of each run, Pallas kernels for 0% -> 0%
where the time goes in v17:
time: 323 us; the launch traced here: 318 us
  waiting for transfers between devices  171 us (53%)
  matrix products  48 us (15%)
  local copies, waits for them, and re-layouts  38.9 us (12%)
  other arithmetic  25.3 us (8%)
  starting transfers between devices  20.2 us (6%)
  between operations  14.9 us (5%)
    all_gather x1, waiting for transfers between devices, local(): full_a = lax.all_gather(local_a, rows_axes, axis=0, tiled=True)  101 us
    unnamed x93, local copies, waits for them, and re-layouts  17.9 us
    all_gather x1, waiting for transfers between devices, weight_grad(): gathered = lax.all_gather(d_rows, 'dp', axis=0, tiled=True)  17.8 us
    all_gather x1, waiting for transfers between devices, local(): full_b = lax.all_gather(w_rest, rows_axes, axis=0, tiled=True)  15.7 us
    ppermute x2, waiting for transfers between devices, weight_grad(): sent = lax.ppermute(away_part.astype(jnp.bfloat16), 'ctx', [(0, 1), (1, 0)])  12 us
    all_to_all x1, waiting for transfers between devices, local(): lax.all_to_all(input_part.astype(jnp.bfloat16).reshape(num_rows, head_gro...  10.9 us
    dot_general x2, matrix products, attend_whole(): jnp.einsum('rhd,kd->hrk', dout_rows, value_all, preferred_element_type=jn...  9.03 us
    ppermute x1, waiting for transfers between devices, local(): grad_kv = own_part + lax.ppermute(away_part, 'ctx', [(0, 1), (1, 0)])  8.47 us
  transfers between devices with their start and end apart: 11, of which 9 were waited for; matrix products, arithmetic and copies ran while one was open for 32% of the time, Pallas kernels for 0%

profile of v17, /device:TPU:0, one launch (start us, length us, event | category | flops | bytes accessed | tf_op | source)
XLA Modules:
  0.0 318.2 jit_solution(12985828952311407095)
XLA Ops:
  7.2 1.2 slice.83
  8.5 1.9 pad_maximum_fusion.1
  11.4 101.1 %all-gather.5.cloned.1.call-done = bf16[4096,768]{1,0:T(8,128)(2,1)} async-done(((bf16[512,768]{1,0:T(8,128)(2,1)}), bf16[4096,768]{1,0:T(8,128)(2,1)}) %all-gather.5.cloned.1.call-update) | async-done | bytes 6291472 | tf_op jit(solution)/shard_map/all_gather | solution.py:203
  112.5 1.9 slice.96
  114.6 2.3 copy.137
  116.9 1.9 fusion.55
  118.9 1.9 copy.206
  122.3 1.5 multiply_cosine_fusion
  123.8 5.6 %convolution_bitcast_fusion = f32[384,768]{0,1:T(8,128)S(1)} fusion(bf16[4096,768]{1,0:T(8,128)(2,1)} %all-gather.5.cloned.1.call-done, bf16[384,4096]{1,0:T(8,128)(2,1)S(1)} %copy-done), kind=kOutput, calls=%fused_computation.27 | convolution fusion | flops 2415919104 | bytes 10616832 | tf_op jit(solution)/shard_map/dot_general | solution.py:241
  129.4 1.0 slice.115
  131.4 4.7 %all-to-all-start = ((bf16[96,4,1024]{2,0,1:T(8,128)(2,1)}), bf16[96,4,1024]{2,0,1:T(8,128)(2,1)}, u32[]{:S(2)}, u32[]{:S(2)}) async-start(bf16[96,4,1024]{2,0,1:T(8,128)(2,1)} %bitcast.171), calls=%async_computation | async-start | bytes 1572864 | tf_op jit(solution)/shard_map/all_to_all | solution.py:211
  136.1 0.9 slice_bitcast_fusion.3
  139.4 2.0 fusion.57
  141.5 2.1 copy.202
  143.6 2.1 copy.201
  145.8 1.7 subtract_convert_fusion.3
  147.5 1.5 maximum_select_fusion
  149.0 1.2 fusion.10
  150.3 1.2 select_reduce_fusion.1
  151.4 2.4 bitcast_convert_fusion.1
  153.9 2.3 copy.174
  156.2 1.5 multiply_reduce_fusion.1
  157.7 4.5 %fusion.6 = bf16[4,384,768]{1,2,0:T(8,128)(2,1)S(1)} fusion(f32[768,384,4]{1,0,2:T(8,128)} %copy-done.2, f32[4,384]{1,0:T(4,128)S(1)} %multiply_reduce_fusion.1, f32[4,384]{1,0:T(4,128)S(1)} %log_add_fusion.1, pred[384,768]{0,1:T(8,128)(4,1)S(1)} %fusion.16, bf16[768,256]{0,1:T(8,128)(2,1)} %copy-done.12, bf16[384,8,128]{0,2,1:T(8,128)(2,1)} %bitcast.167), kind=kOutput, calls=%fused_computation.11 | convolution fusion | flops 311427072 | bytes 7974912 | tf_op jit(solution)/shard_map/rhd,kd->hrk/dot_general | solution.py:90
  162.3 1.4 copy-done.4
  163.7 1.1 convolution_bitcast_fusion.2
  165.1 1.0 pad_maximum_fusion.9
  166.1 1.9 copy.142
  168.0 1.4 all-to-all-done
  169.4 3.2 %broadcast_in_dim.79 = bf16[4,384,1024]{2,1,0:T(8,128)(2,1)} broadcast(bf16[384,1024]{1,0:T(8,128)(2,1)} %bitcast.29), dimensions={1,2} | broadcast | bytes 3932160 | tf_op jit(solution)/shard_map/broadcast_in_dim | solution.py:217
  172.7 4.6 %all-to-all-start.1 = ((bf16[4,384,1024]{2,1,0:T(8,128)(2,1)}), bf16[4,384,1024]{2,1,0:T(8,128)(2,1)}, u32[]{:S(2)}, u32[]{:S(2)}) async-start(bf16[4,384,1024]{2,1,0:T(8,128)(2,1)} %broadcast_in_dim.79), calls=%async_computation.1 | async-start | bytes 6291456 | tf_op jit(solution)/shard_map/all_to_all | solution.py:218
  177.4 15.7 %all-gather.7.cloned.1.call-done = bf16[4096,512]{1,0:T(8,128)(2,1)} async-done(((bf16[512,512]{1,0:T(8,128)(2,1)}), bf16[4096,512]{1,0:T(8,128)(2,1)}) %all-gather.7.cloned.1.call-update) | async-done | bytes 4194320 | tf_op jit(solution)/shard_map/all_gather | solution.py:268
  193.3 4.6 %fusion.58 = f32[512,384]{1,0:T(8,128)S(1)} fusion(bf16[4096,512]{1,0:T(8,128)(2,1)} %all-gather.7.cloned.1.call-done, bf16[384,4096]{1,0:T(8,128)(2,1)S(1)} %copy-done), kind=kOutput, calls=%fused_computation.127 | convolution fusion | flops 1610612736 | bytes 8126464 | tf_op jit(solution)/shard_map/dot_general | solution.py:271
  198.4 1.2 subtract_convert_fusion.1
  199.7 1.2 fusion.11
  200.9 1.2 select_reduce_fusion
  202.1 2.1 bitcast_convert_fusion
  204.9 4.5 %fusion.1 = bf16[4,384,768]{1,2,0:T(8,128)(2,1)S(1)} fusion(f32[768,384,4]{1,0,2:T(8,128)} %copy-done.3, f32[4,384]{1,0:T(4,128)S(1)} %multiply_reduce_fusion, f32[4,384]{1,0:T(4,128)S(1)} %log_add_fusion, pred[384,768]{0,1:T(8,128)(4,1)S(1)} %fusion.16, bf16[768,256]{0,1:T(8,128)(2,1)S(1)} %copy-done.14, bf16[384,8,128]{0,2,1:T(8,128)(2,1)} %bitcast.168), kind=kOutput, calls=%fused_computation.3 | convolution fusion | flops 311427072 | bytes 7974912 | tf_op jit(solution)/shard_map/rhd,kd->hrk/dot_general | solution.py:90
  209.5 1.0 convolution_bitcast_fusion.5
  210.5 1.0 fusion.14
  211.5 1.7 convolution_bitcast_fusion.3
  213.2 1.9 fusion.15
  215.1 1.6 collective-permute-start.2
  216.8 1.1 convolution_bitcast_fusion.1
  217.8 8.5 %collective-permute-done.2 = f32[384,256]{0,1:T(8,128)S(1)} collective-permute-done((f32[384,256]{0,1:T(8,128)S(1)}, f32[384,256]{0,1:T(8,128)S(1)}, u32[]{:S(2)}, u32[]{:S(2)}) %collective-permute-start.2) | collective-permute-done | bytes 393248 | tf_op jit(solution)/shard_map/ppermute | solution.py:288
  226.9 3.3 %all-gather.9.cloned.1.call-done = bf16[1536,512]{0,1:T(8,128)(2,1)} async-done(((bf16[384,512]{0,1:T(8,128)(2,1)}), bf16[1536,512]{0,1:T(8,128)(2,1)}) %all-gather.9.cloned.1.call-update) | async-done | bytes 1572880 | tf_op jit(solution)/shard_map/all_gather | solution.py:270
  232.0 2.3 copy.148
  234.4 6.1 %fusion.17 = f32[384,4096]{1,0:T(8,128)S(1)} fusion(bf16[4096,768]{1,0:T(8,128)(2,1)} %all-gather.5.cloned.1.call-done, bf16[384,128]{0,1:T(8,128)(2,1)S(1)} %copy-done.30, bf16[384,128]{0,1:T(8,128)(2,1)S(1)} %copy-done.32, bf16[384,512]{0,1:T(8,128)(2,1)} %bitcast.176), kind=kOutput, calls=%fused_computation.63 | convolution fusion | flops 2417688576 | bytes 13172736 | tf_op jit(solution)/shard_map/dot_general | solution.py:295
  240.5 1.8 fusion.59
  242.4 1.7 collective-permute-start.1
  244.1 1.9 convolution_add_fusion
  246.0 9.9 %collective-permute-done.1 = bf16[512,512]{1,0:T(8,128)(2,1)S(1)} collective-permute-done((bf16[512,512]{1,0:T(8,128)(2,1)S(1)}, bf16[512,512]{1,0:T(8,128)(2,1)S(1)}, u32[]{:S(2)}, u32[]{:S(2)}) %collective-permute-start.1) | collective-permute-done | bytes 524320 | tf_op jit(solution)/shard_map/ppermute | solution.py:237
  255.9 1.1 convert_add_fusion.1
  257.1 2.1 copy.211
  259.1 5.2 %all-to-all-start.2 = ((bf16[384,4,1024]{2,0,1:T(8,128)(2,1)}), bf16[384,4,1024]{2,0,1:T(8,128)(2,1)}, u32[]{:S(2)}, u32[]{:S(2)}) async-start(bf16[384,4,1024]{2,0,1:T(8,128)(2,1)} %bitcast.161), calls=%async_computation.2 | async-start | bytes 6291456 | tf_op jit(solution)/shard_map/all_to_all | solution.py:308
  264.3 17.8 %all-gather.11.cloned.1.call-done = bf16[1536,768]{0,1:T(8,128)(2,1)} async-done(((bf16[384,768]{0,1:T(8,128)(2,1)}), bf16[1536,768]{0,1:T(8,128)(2,1)}) %all-gather.11.cloned.1.call-update) | async-done | bytes 2359312 | tf_op jit(solution)/shard_map/all_gather | solution.py:228
  282.2 4.4 %fusion.60 = f32[1024,768]{1,0:T(8,128)S(1)} fusion(bf16[1536,1024]{1,0:T(8,128)(2,1)S(1)} %bitcast.165, bf16[1536,768]{0,1:T(8,128)(2,1)} %all-gather.11.cloned.1.call-done), kind=kOutput, calls=%fused_computation.129 | convolution fusion | flops 2415919104 | bytes 8650752 | tf_op jit(solution)/shard_map/dot_general | solution.py:229
  286.5 1.1 dynamic-slice_convert_fusion
  287.6 1.5 collective-permute-start.3
  289.2 1.2 copy.165
  290.4 10.9 %all-to-all-done.2 = bf16[384,4,1024]{2,0,1:T(8,128)(2,1)} async-done(((bf16[384,4,1024]{2,0,1:T(8,128)(2,1)}), bf16[384,4,1024]{2,0,1:T(8,128)(2,1)}, u32[]{:S(2)}, u32[]{:S(2)}) %all-to-all-start.2) | async-done | bytes 3145760 | tf_op jit(solution)/shard_map/all_to_all | solution.py:308
  301.3 3.8 %reduce_sum.42 = bf16[384,1024]{1,0:T(8,128)(2,1)} reduce(bf16[384,4,1024]{2,0,1:T(8,128)(2,1)} %all-to-all-done.2, bf16[]{:T(256)} %constant.40.clone.1), dimensions={1}, to_apply=%region_6.7 | reduce | flops 1179648 | bytes 3932162 | tf_op jit(solution)/shard_map/reduce_sum | solution.py:312
  305.1 2.1 collective-permute-done.3
  307.2 1.8 convert_add_fusion
  309.9 1.5 pad_maximum_fusion
  (130 shorter events, 11.3 us)
Async XLA Ops:
  7.2 3.3 %copy-start = (bf16[384,4096]{1,0:T(8,128)(2,1)S(1)}, bf16[384,4096]{1,0:T(8,128)(2,1)}, u32[]{:S(2)}) copy-start(bf16[384,4096]{1,0:T(8,128)(2,1)} %param.6) | copy-start | bytes 9437188
  7.2 107.3 %copy-start.36 = (s32[1,8]{1,0:T(1,128)S(1)}, s32[1,8]{1,0:T(1,128)}, u32[]{:S(2)}) copy-start(s32[1,8]{1,0:T(1,128)} %param.10) | copy-start | bytes 100
  7.2 105.3 %all-gather.5.cloned.1.call-start = ((), (), s32[]{:S(2)}) async-start(), calls=%async_computation.3 | async-start | bytes 7077888 | tf_op jit(solution)/shard_map/all_gather | solution.py:203
  10.4 182.6 %all-gather.7.cloned.1.call-start = ((), (), s32[]{:S(2)}) async-start(), calls=%async_computation.4 | async-start | bytes 4718592 | tf_op jit(solution)/shard_map/all_gather | solution.py:268
  123.8 6.7 %copy-start.24 = (bf16[96,4096]{1,0:T(8,128)(2,1)S(1)}, bf16[96,4096]{1,0:T(8,128)(2,1)}, u32[]{:S(2)}) copy-start(bf16[96,4096]{1,0:T(8,128)(2,1)} %constant_dynamic-slice_fusion) | copy-start | bytes 2359300
  129.4 2.0 copy-start.27
  131.4 38.0 %all-to-all-start = ((bf16[96,4,1024]{2,0,1:T(8,128)(2,1)}), bf16[96,4,1024]{2,0,1:T(8,128)(2,1)}, u32[]{:S(2)}, u32[]{:S(2)}) async-start(bf16[96,4,1024]{2,0,1:T(8,128)(2,1)} %bitcast.171), calls=%async_computation | async-start | bytes 1572864 | tf_op jit(solution)/shard_map/all_to_all | solution.py:211
  137.5 0.7 copy-start.28
  138.9 8.6 %collective-permute-start = (bf16[384,256]{0,1:T(8,128)(2,1)}, bf16[384,256]{0,1:T(8,128)(2,1)}, u32[]{:S(2)}, u32[]{:S(2)}) collective-permute-start(bf16[384,256]{0,1:T(8,128)(2,1)} %pad_maximum_fusion.12), channel_id=1, source_target_pairs={{0,4},{4,0},{1,5},{5,1},{2,6},{6,2},{3,7},{7,3},{8,12},{12,8},{9,1... | collective-permute-start | bytes 589832 | tf_op jit(solution)/shard_map/ppermute | solution.py:251
  147.5 1.5 copy-start.17
  147.5 2.8 copy-start.19
  149.0 2.5 copy-start.12
  150.2 3.6 %copy-start.2 = (f32[768,384,4]{1,0,2:T(8,128)}, f32[768,384,4]{1,0,2:T(8,128)S(1)}, u32[]{:S(2)}) copy-start(f32[768,384,4]{1,0,2:T(8,128)S(1)} %get-tuple-element.73) | copy-start | bytes 14155780
  157.7 6.0 %copy-start.13 = (bf16[768,256]{0,1:T(8,128)(2,1)S(1)}, bf16[768,256]{0,1:T(8,128)(2,1)}, u32[]{:S(2)}) copy-start(bf16[768,256]{0,1:T(8,128)(2,1)} %copy-done.12) | copy-start | bytes 1179652
  157.7 7.0 %copy-start.6 = (f32[384,64]{1,0:T(8,128)S(1)}, f32[384,64]{1,0:T(8,128)}, u32[]{:S(2)}) copy-start(f32[384,64]{1,0:T(8,128)} %get-tuple-element.70) | copy-start | bytes 294916
  157.7 7.0 %copy-start.8 = (f32[384,64]{1,0:T(8,128)S(1)}, f32[384,64]{1,0:T(8,128)}, u32[]{:S(2)}) copy-start(f32[384,64]{1,0:T(8,128)} %get-tuple-element.71) | copy-start | bytes 294916
  162.2 1.4 copy-start.4
  172.7 59.3 %all-to-all-start.1 = ((bf16[4,384,1024]{2,1,0:T(8,128)(2,1)}), bf16[4,384,1024]{2,1,0:T(8,128)(2,1)}, u32[]{:S(2)}, u32[]{:S(2)}) async-start(bf16[4,384,1024]{2,1,0:T(8,128)(2,1)} %broadcast_in_dim.79), calls=%async_computation.1 | async-start | bytes 6291456 | tf_op jit(solution)/shard_map/all_to_all | solution.py:218
  177.3 52.9 %all-gather.9.cloned.1.call-start = ((), (), s32[]{:S(2)}) async-start(), calls=%async_computation.5 | async-start | bytes 1966080 | tf_op jit(solution)/shard_map/all_gather | solution.py:270
  193.0 89.1 %all-gather.11.cloned.1.call-start = ((), (), s32[]{:S(2)}) async-start(), calls=%async_computation.6 | async-start | bytes 2949120 | tf_op jit(solution)/shard_map/all_gather | solution.py:228
  197.8 1.9 copy-start.14
  199.7 2.4 copy-start.15
  200.9 3.4 %copy-start.3 = (f32[768,384,4]{1,0,2:T(8,128)}, f32[768,384,4]{1,0,2:T(8,128)S(1)}, u32[]{:S(2)}) copy-start(f32[768,384,4]{1,0,2:T(8,128)S(1)} %get-tuple-element.77) | copy-start | bytes 14155780
  202.1 2.4 copy-start.26
  204.6 6.9 %slice-start.2 = ((s8[4718592]{0:T(1024)(128)(4,1)}), s8[4194304]{0:T(1024)(128)(4,1)S(1)}, s32[]{:S(2)}) async-start(s8[4718592]{0:T(1024)(128)(4,1)} %bitcast.158), calls=%async_computation.9 | async-start | bytes 8388608
  204.9 4.6 %copy-start.16 = (bf16[384,4,64]{2,0,1:T(8,128)(2,1)S(1)}, bf16[384,4,64]{2,0,1:T(8,128)(2,1)}, u32[]{:S(2)}) copy-start(bf16[384,4,64]{2,0,1:T(8,128)(2,1)} %copy-done.15) | copy-start | bytes 589828
  204.9 5.6 %copy-start.5 = (bf16[4,384,768]{1,2,0:T(8,128)(2,1)S(1)}, bf16[4,384,768]{1,2,0:T(8,128)(2,1)}, u32[]{:S(2)}) copy-start(bf16[4,384,768]{1,2,0:T(8,128)(2,1)} %copy-done.4) | copy-start | bytes 7077892
  204.9 5.6 %copy-start.18 = (bf16[384,4,64]{2,0,1:T(8,128)(2,1)S(1)}, bf16[384,4,64]{2,0,1:T(8,128)(2,1)}, u32[]{:S(2)}) copy-start(bf16[384,4,64]{2,0,1:T(8,128)(2,1)} %copy-done.17) | copy-start | bytes 589828
  204.9 5.6 %copy-start.20 = (bf16[384,4,64]{2,0,1:T(8,128)(2,1)S(1)}, bf16[384,4,64]{2,0,1:T(8,128)(2,1)}, u32[]{:S(2)}) copy-start(bf16[384,4,64]{2,0,1:T(8,128)(2,1)} %copy-done.19) | copy-start | bytes 589828
  204.9 6.6 %slice-start.3 = ((s8[4718592]{0:T(1024)(128)(4,1)}), s8[524288]{0:T(1024)(128)(4,1)S(1)}, s32[]{:S(2)}) async-start(s8[4718592]{0:T(1024)(128)(4,1)} %bitcast.158), calls=%async_computation.10 | async-start | bytes 1048576
  209.4 2.0 copy-start.23
  210.5 2.7 slice-start
  211.5 1.7 slice-start.1
  215.1 15.1 %copy-start.7 = (f32[384,64]{1,0:T(8,128)S(1)}, f32[384,64]{1,0:T(8,128)}, u32[]{:S(2)}) copy-start(f32[384,64]{1,0:T(8,128)} %get-tuple-element.70) | copy-start | bytes 294916
  215.1 15.1 %copy-start.9 = (f32[384,64]{1,0:T(8,128)S(1)}, f32[384,64]{1,0:T(8,128)}, u32[]{:S(2)}) copy-start(f32[384,64]{1,0:T(8,128)} %get-tuple-element.71) | copy-start | bytes 294916
  215.1 11.2 %collective-permute-start.2 = (f32[384,256]{0,1:T(8,128)S(1)}, f32[384,256]{0,1:T(8,128)S(1)}, u32[]{:S(2)}, u32[]{:S(2)}) collective-permute-start(f32[384,256]{0,1:T(8,128)S(1)} %fusion.19), channel_id=1, source_target_pairs={{0,4},{4,0},{1,5},{5,1},{2,6},{6,2},{3,7},{7,3},{8,12},{12,8},{9,1... | collective-permute-start | bytes 1179656 | tf_op jit(solution)/shard_map/ppermute | solution.py:288
  226.4 5.6 %copy-start.29 = (bf16[384,128]{0,1:T(8,128)(2,1)}, bf16[384,128]{0,1:T(8,128)(2,1)S(1)}, u32[]{:S(2)}) copy-start(bf16[384,128]{0,1:T(8,128)(2,1)S(1)} %slice.169) | copy-start | bytes 294916
  226.9 5.1 %copy-start.31 = (bf16[384,128]{0,1:T(8,128)(2,1)}, bf16[384,128]{0,1:T(8,128)(2,1)S(1)}, u32[]{:S(2)}) copy-start(bf16[384,128]{0,1:T(8,128)(2,1)S(1)} %maximum_bitcast_fusion.1) | copy-start | bytes 294916
  232.0 2.4 copy-start.30
  232.0 2.4 copy-start.32
  234.4 6.1 %copy-start.21 = (bf16[4,4,96,1024]{3,2,1,0:T(8,128)(2,1)}, bf16[4,4,96,1024]{3,2,1,0:T(8,128)(2,1)S(1)}, u32[]{:S(2)}) copy-start(bf16[4,4,96,1024]{3,2,1,0:T(8,128)(2,1)S(1)} %copy.148) | copy-start | bytes 9437188
  234.4 6.1 %copy-start.35 = (bf16[1536,512]{0,1:T(8,128)(2,1)S(1)}, bf16[1536,512]{0,1:T(8,128)(2,1)}, u32[]{:S(2)}) copy-start(bf16[1536,512]{0,1:T(8,128)(2,1)} %all-gather.9.cloned.1.call-done) | copy-start | bytes 4718596
  240.5 3.7 %copy-start.11 = (bf16[4096,512]{1,0:T(8,128)(2,1)S(1)}, bf16[4096,512]{1,0:T(8,128)(2,1)}, u32[]{:S(2)}) copy-start(bf16[4096,512]{1,0:T(8,128)(2,1)} %all-gather.7.cloned.1.call-done) | copy-start | bytes 12582916
  242.4 13.5 %collective-permute-start.1 = (bf16[512,512]{1,0:T(8,128)(2,1)S(1)}, bf16[512,512]{1,0:T(8,128)(2,1)S(1)}, u32[]{:S(2)}, u32[]{:S(2)}) collective-permute-start(bf16[512,512]{1,0:T(8,128)(2,1)S(1)} %dynamic-slice_convert_fusion.1), channel_id=1, source_target_pairs={{0,4},{4,0},{1,5},{5,1},{2,6},{6,2},{3,7},{7,3},{8,12},{12,8},{9,1... | collective-permute-start | bytes 1572872 | tf_op jit(solution)/shard_map/ppermute | solution.py:237
  259.1 23.0 %copy-start.22 = (bf16[4,4,96,1024]{3,2,1,0:T(8,128)(2,1)S(1)}, bf16[4,4,96,1024]{3,2,1,0:T(8,128)(2,1)}, u32[]{:S(2)}) copy-start(bf16[4,4,96,1024]{3,2,1,0:T(8,128)(2,1)} %copy-done.21) | copy-start | bytes 9437188
  259.1 42.2 %all-to-all-start.2 = ((bf16[384,4,1024]{2,0,1:T(8,128)(2,1)}), bf16[384,4,1024]{2,0,1:T(8,128)(2,1)}, u32[]{:S(2)}, u32[]{:S(2)}) async-start(bf16[384,4,1024]{2,0,1:T(8,128)(2,1)} %bitcast.161), calls=%async_computation.2 | async-start | bytes 6291456 | tf_op jit(solution)/shard_map/all_to_all | solution.py:308
  264.3 24.8 %copy-start.33 = (bf16[128,4,384]{2,0,1:T(8,128)(2,1)S(1)}, bf16[128,4,384]{2,0,1:T(8,128)(2,1)}, u32[]{:S(2)}) copy-start(bf16[128,4,384]{2,0,1:T(8,128)(2,1)} %get-tuple-element.75) | copy-start | bytes 1179652
  282.2 6.9 %copy-start.34 = (bf16[128,4,384]{2,0,1:T(8,128)(2,1)S(1)}, bf16[128,4,384]{2,0,1:T(8,128)(2,1)}, u32[]{:S(2)}) copy-start(bf16[128,4,384]{2,0,1:T(8,128)(2,1)} %get-tuple-element.79) | copy-start | bytes 1179652
  286.5 2.6 copy-start.25
  287.6 19.5 %collective-permute-start.3 = (bf16[512,768]{1,0:T(8,128)(2,1)}, bf16[512,768]{1,0:T(8,128)(2,1)}, u32[]{:S(2)}, u32[]{:S(2)}) collective-permute-start(bf16[512,768]{1,0:T(8,128)(2,1)} %dynamic-slice_convert_fusion), channel_id=1, source_target_pairs={{0,4},{4,0},{1,5},{5,1},{2,6},{6,2},{3,7},{7,3},{8,12},{12,8},{9,1... | collective-permute-start | bytes 2359304 | tf_op jit(solution)/shard_map/ppermute | solution.py:237
  301.3 10.1 %copy-start.1 = (bf16[384,4096]{1,0:T(8,128)(2,1)S(1)}, bf16[384,4096]{1,0:T(8,128)(2,1)}, u32[]{:S(2)}) copy-start(bf16[384,4096]{1,0:T(8,128)(2,1)} %param.6) | copy-start | bytes 9437188
  305.1 4.8 %copy-start.10 = (f32[512,512]{1,0:T(8,128)S(1)}, f32[512,512]{1,0:T(8,128)}, u32[]{:S(2)}) copy-start(f32[512,512]{1,0:T(8,128)} %convert_add_fusion.1) | copy-start | bytes 3145732
Sparse Core Ops, SparseCore 0:
  10.8 101.7 all-gather.4
  114.7 78.3 all-gather.6
  194.6 35.5 all-gather.8
  232.2 49.8 all-gather.10

commit v18 on v17

--- a/solution.py
+++ b/solution.py
@@ -303,14 +303,15 @@
     else:
         late_proj = jnp.concatenate([d_key, d_value], 1)
         early_sum = weight_grad(d_query_a)
-    early_sum, input_part = lax.optimization_barrier((early_sum, input_part))
     input_cols = input_part.shape[1] // head_groups
     input_split = lax.all_to_all(
         input_part.astype(jnp.bfloat16).reshape(num_rows, head_groups, input_cols),
         "head", 1, 1, tiled=False,
     )
     grad_input = jnp.sum(input_split.astype(jnp.float32), axis=1).astype(jnp.bfloat16)
-    late_sum = weight_grad(late_proj)
+    late_all = lax.all_gather(late_proj, "dp", axis=0, tiled=True)
+    early_sum, late_all = lax.optimization_barrier((early_sum, late_all))
+    late_sum = weight_grad(late_proj, late_all)
     query_w = jnp.concatenate([early_sum, late_sum[:, : query_cols - first_cols]], 1)
     rest = late_sum[:, query_cols - first_cols :]
     return (attended, grad_input, query_w, rest[:, :128], rest[:, 128:])

time: 323 us -> 351 us (1.087)
  waiting for transfers between devices: 171 us -> 184 us
  matrix products: 48 us -> 55.4 us
  other arithmetic: 25.3 us -> 32.4 us
    all_gather x1, waiting for transfers between devices: 15.7 us -> 31.1 us  [local(): full_b = lax.all_gather(w_rest, rows_axes, axis=0, tiled=True)]
    all_to_all x1, waiting for transfers between devices: 0.01 us -> 12.5 us  [local(): cols_all = lax.all_to_all(spread, 'head', 0, 0, tiled=False)]
    ppermute x1, waiting for transfers between devices: 8.47 us -> 0.01 us  [local(): grad_kv = own_part + lax.ppermute(away_part, 'ctx', [(0, 1), (1, 0)])]
    all_gather x1, waiting for transfers between devices: 3.32 us -> 11.7 us  [local(): early_all = lax.all_gather(d_query_a, 'dp', axis=0, tiled=True)]
    all_gather x1, waiting for transfers between devices: 17.8 us -> 9.99 us  [local(): late_all = lax.all_gather(late_proj, 'dp', axis=0, tiled=True)]
    ppermute x2, waiting for transfers between devices: 12 us -> 4.96 us  [weight_grad(): sent = lax.ppermute(away_part.astype(jnp.bfloat16), 'ctx', [(0, 1), (1, 0)])]
    dot_general x2, matrix products: 3.52 us -> 8.19 us  [attend_whole(): jnp.einsum('hrk,rhd->kd', prob_b, dout_rows, preferred_element_type=jnp.f...]
    unnamed x93 -> x89, local copies, waits for them, and re-layouts: 17.9 us -> 20.6 us
  transfers between devices with their start and end apart: 11 -> 11, of which waited for: 9 -> 8; matrix products, arithmetic and copies ran while one was open for 32% -> 33% of each run, Pallas kernels for 0% -> 0%
where the time goes in v18:
time: 351 us; the launch traced here: 346 us
  waiting for transfers between devices  184 us (52%)
  matrix products  55.4 us (16%)
  local copies, waits for them, and re-layouts  41.5 us (12%)
  other arithmetic  32.4 us (9%)
  starting transfers between devices  18.1 us (5%)
  between operations  14.8 us (4%)
    all_gather x1, waiting for transfers between devices, local(): full_a = lax.all_gather(local_a, rows_axes, axis=0, tiled=True)  101 us
    all_gather x1, waiting for transfers between devices, local(): full_b = lax.all_gather(w_rest, rows_axes, axis=0, tiled=True)  31.1 us
    unnamed x89, local copies, waits for them, and re-layouts  20.6 us
    all_to_all x1, waiting for transfers between devices, local(): cols_all = lax.all_to_all(spread, 'head', 0, 0, tiled=False)  12.5 us
    all_to_all x1, waiting for transfers between devices, local(): lax.all_to_all(input_part.astype(jnp.bfloat16).reshape(num_rows, head_gro...  12.1 us
    all_gather x1, waiting for transfers between devices, local(): early_all = lax.all_gather(d_query_a, 'dp', axis=0, tiled=True)  11.7 us
    all_gather x1, waiting for transfers between devices, local(): late_all = lax.all_gather(late_proj, 'dp', axis=0, tiled=True)  9.99 us
    dot_general x2, matrix products, attend_whole(): jnp.einsum('rhd,kd->hrk', dout_rows, value_all, preferred_element_type=jn...  9.03 us
  transfers between devices with their start and end apart: 11, of which 8 were waited for; matrix products, arithmetic and copies ran while one was open for 33% of the time, Pallas kernels for 0%

profile of v18, /device:TPU:0, one launch (start us, length us, event | category | flops | bytes accessed | tf_op | source)
XLA Modules:
  0.0 345.8 jit_solution(14764811507958073658)
XLA Ops:
  7.2 1.2 slice.83
  8.5 1.9 pad_maximum_fusion.1
  11.4 101.1 %all-gather.5.cloned.1.call-done = bf16[4096,768]{1,0:T(8,128)(2,1)} async-done(((bf16[512,768]{1,0:T(8,128)(2,1)}), bf16[4096,768]{1,0:T(8,128)(2,1)}) %all-gather.5.cloned.1.call-update) | async-done | bytes 6291472 | tf_op jit(solution)/shard_map/all_gather | solution.py:203
  112.5 1.9 slice.96
  114.7 2.4 copy.137
  117.0 1.9 fusion.55
  119.0 2.0 copy.203
  122.4 1.5 multiply_cosine_fusion
  123.9 5.6 %convolution_bitcast_fusion = f32[384,768]{0,1:T(8,128)S(1)} fusion(bf16[4096,768]{1,0:T(8,128)(2,1)} %all-gather.5.cloned.1.call-done, bf16[384,4096]{1,0:T(8,128)(2,1)S(1)} %copy-done), kind=kOutput, calls=%fused_computation.27 | convolution fusion | flops 2415919104 | bytes 10616832 | tf_op jit(solution)/shard_map/dot_general | solution.py:241
  129.6 1.1 fusion.57
  130.7 2.1 copy.202
  132.9 2.2 copy.201
  138.3 2.1 copy.212
  140.4 4.2 %all-to-all-start.1 = ((bf16[96,4,1024]{2,0,1:T(8,128)(2,1)}), bf16[96,4,1024]{2,0,1:T(8,128)(2,1)}, u32[]{:S(2)}, u32[]{:S(2)}) async-start(bf16[96,4,1024]{2,0,1:T(8,128)(2,1)} %bitcast.168), calls=%async_computation.1 | async-start | bytes 1572864 | tf_op jit(solution)/shard_map/all_to_all | solution.py:211
  145.2 1.7 subtract_convert_fusion.3
  146.9 1.5 maximum_select_fusion
  148.5 1.2 fusion.10
  149.7 1.2 select_reduce_fusion.1
  150.9 2.4 bitcast_convert_fusion.1
  153.3 2.3 copy.174
  155.6 1.5 multiply_reduce_fusion.1
  157.2 4.5 %fusion.6 = bf16[4,384,768]{1,2,0:T(8,128)(2,1)S(1)} fusion(f32[768,384,4]{1,0,2:T(8,128)} %copy-done.2, f32[4,384]{1,0:T(4,128)S(1)} %multiply_reduce_fusion.1, f32[4,384]{1,0:T(4,128)S(1)} %log_add_fusion.1, pred[384,768]{0,1:T(8,128)(4,1)S(1)} %fusion.16, bf16[768,256]{0,1:T(8,128)(2,1)} %copy-done.13, bf16[384,8,128]{0,2,1:T(8,128)(2,1)} %bitcast.164), kind=kOutput, calls=%fused_computation.11 | convolution fusion | flops 311427072 | bytes 7974912 | tf_op jit(solution)/shard_map/rhd,kd->hrk/dot_general | solution.py:90
  161.7 1.4 copy-done.4
  163.1 1.1 convolution_bitcast_fusion.2
  164.6 1.0 pad_maximum_fusion.9
  165.6 1.9 copy.142
  167.5 31.1 %all-gather.7.cloned.1.call-done = bf16[4096,512]{1,0:T(8,128)(2,1)} async-done(((bf16[512,512]{1,0:T(8,128)(2,1)}), bf16[4096,512]{1,0:T(8,128)(2,1)}) %all-gather.7.cloned.1.call-update) | async-done | bytes 4194320 | tf_op jit(solution)/shard_map/all_gather | solution.py:268
  198.6 4.5 %fusion.58 = f32[512,384]{1,0:T(8,128)S(1)} fusion(bf16[4096,512]{1,0:T(8,128)(2,1)} %all-gather.7.cloned.1.call-done, bf16[384,4096]{1,0:T(8,128)(2,1)S(1)} %copy-done), kind=kOutput, calls=%fused_computation.127 | convolution fusion | flops 1610612736 | bytes 8126464 | tf_op jit(solution)/shard_map/dot_general | solution.py:271
  203.8 1.2 subtract_convert_fusion.1
  205.0 1.4 fusion.11
  206.5 1.2 select_reduce_fusion
  207.7 2.2 bitcast_convert_fusion
  210.4 4.5 %fusion.1 = bf16[4,384,768]{1,2,0:T(8,128)(2,1)S(1)} fusion(f32[768,384,4]{1,0,2:T(8,128)} %copy-done.3, f32[4,384]{1,0:T(4,128)S(1)} %multiply_reduce_fusion, f32[4,384]{1,0:T(4,128)S(1)} %log_add_fusion, pred[384,768]{0,1:T(8,128)(4,1)S(1)} %fusion.16, bf16[768,256]{0,1:T(8,128)(2,1)S(1)} %copy-done.15, bf16[384,8,128]{0,2,1:T(8,128)(2,1)} %bitcast.165), kind=kOutput, calls=%fused_computation.3 | convolution fusion | flops 311427072 | bytes 7974912 | tf_op jit(solution)/shard_map/rhd,kd->hrk/dot_general | solution.py:90
  215.0 1.4 copy-done.6
  216.3 1.0 convolution_bitcast_fusion.5
  217.4 1.0 fusion.14
  218.4 4.1 %convolution_bitcast_fusion.3 = f32[768,128]{0,1:T(8,128)S(1)} fusion(bf16[384,8,128]{0,2,1:T(8,128)(2,1)} %bitcast.166, f32[768,384,4]{1,0,2:T(8,128)} %copy-done.3, f32[4,384]{1,0:T(4,128)S(1)} %log_add_fusion, pred[384,768]{0,1:T(8,128)(4,1)S(1)} %fusion.16), kind=kOutput, calls=%fused_computation.32 | convolution fusion | flops 307888128 | bytes 5806080 | tf_op jit(solution)/shard_map/hrk,rhd->kd/dot_general | solution.py:94
  222.5 4.1 %fusion.15 = f32[768,128]{0,1:T(8,128)S(1)} fusion(f32[768,128]{0,1:T(8,128)S(1)} %convolution_bitcast_fusion.3, bf16[384,8,128]{0,2,1:T(8,128)(2,1)S(1)} %bitcast.167, f32[768,384,4]{1,0,2:T(8,128)} %copy-done.2, f32[4,384]{1,0:T(4,128)S(1)} %log_add_fusion.1, pred[384,768]{0,1:T(8,128)(4,1)S(1)} %fusion.16), kind=kOutput, calls=%fused_computation.37 | convolution fusion | flops 307986432 | bytes 6199296 | tf_op jit(solution)/shard_map/hrk,rhd->kd/dot_general | solution.py:94
  227.5 1.4 collective-permute-start.1
  228.8 3.2 broadcast_in_dim.80
  232.1 3.8 %all-to-all-start.2 = ((bf16[4,384,1024]{2,1,0:T(8,128)(2,1)}), bf16[4,384,1024]{2,1,0:T(8,128)(2,1)S(1)}, u32[]{:S(2)}, u32[]{:S(2)}) async-start(bf16[4,384,1024]{2,1,0:T(8,128)(2,1)} %broadcast_in_dim.80), calls=%async_computation.2 | async-start | bytes 6291456 | tf_op jit(solution)/shard_map/all_to_all | solution.py:218
  236.2 3.7 %convolution_bitcast_fusion.1 = f32[384,4,128]{2,0,1:T(8,128)} fusion(bf16[4,384,768]{1,2,0:T(8,128)(2,1)} %copy-done.6, bf16[768,256]{0,1:T(8,128)(2,1)} %copy-done.13), kind=kOutput, calls=%fused_computation.28 | convolution fusion | flops 301989888 | bytes 3342336 | tf_op jit(solution)/shard_map/hrk,kd->rhd/dot_general | solution.py:92
  239.9 1.2 fusion.21
  242.9 11.7 %all-gather.9.cloned.1.call-done = bf16[1536,512]{0,1:T(8,128)(2,1)} async-done(((bf16[384,512]{0,1:T(8,128)(2,1)}), bf16[1536,512]{0,1:T(8,128)(2,1)}) %all-gather.9.cloned.1.call-update) | async-done | bytes 1572880 | tf_op jit(solution)/shard_map/all_gather | solution.py:270
  254.6 1.7 add_convert_fusion.1
  257.3 1.2 copy.159
  258.5 1.8 pad_maximum_fusion.3
  260.4 12.5 %all-to-all-done.2 = bf16[4,384,1024]{2,1,0:T(8,128)(2,1)S(1)} async-done(((bf16[4,384,1024]{2,1,0:T(8,128)(2,1)}), bf16[4,384,1024]{2,1,0:T(8,128)(2,1)S(1)}, u32[]{:S(2)}, u32[]{:S(2)}) %all-to-all-start.2) | async-done | bytes 3145760 | tf_op jit(solution)/shard_map/all_to_all | solution.py:218
  273.9 6.0 %fusion.17 = f32[384,4096]{1,0:T(8,128)S(1)} fusion(bf16[4096,768]{1,0:T(8,128)(2,1)} %all-gather.5.cloned.1.call-done, bf16[384,128]{0,1:T(8,128)(2,1)S(1)} %copy-done.33, bf16[384,128]{0,1:T(8,128)(2,1)S(1)} %copy-done.34, bf16[384,512]{0,1:T(8,128)(2,1)S(1)} %bitcast.173), kind=kOutput, calls=%fused_computation.63 | convolution fusion | flops 2417688576 | bytes 13172736 | tf_op jit(solution)/shard_map/dot_general | solution.py:295
  280.0 1.8 fusion.59
  284.0 1.8 add_convert_fusion
  285.8 2.1 copy.211
  287.9 5.2 %all-to-all-start = ((bf16[384,4,1024]{2,0,1:T(8,128)(2,1)}), bf16[384,4,1024]{2,0,1:T(8,128)(2,1)}, u32[]{:S(2)}, u32[]{:S(2)}) async-start(bf16[384,4,1024]{2,0,1:T(8,128)(2,1)} %bitcast.158), calls=%async_computation | async-start | bytes 6291456 | tf_op jit(solution)/shard_map/all_to_all | solution.py:307
  293.1 4.1 %collective-permute-done.2 = bf16[512,512]{1,0:T(8,128)(2,1)} collective-permute-done((bf16[512,512]{1,0:T(8,128)(2,1)}, bf16[512,512]{1,0:T(8,128)(2,1)}, u32[]{:S(2)}, u32[]{:S(2)}) %collective-permute-start.2) | collective-permute-done | bytes 524320 | tf_op jit(solution)/shard_map/ppermute | solution.py:237
  297.2 2.6 convert_add_fusion.1
  299.8 10.0 %all-gather.11.cloned.1.call-done = bf16[1536,768]{0,1:T(8,128)(2,1)} async-done(((bf16[384,768]{0,1:T(8,128)(2,1)}), bf16[1536,768]{0,1:T(8,128)(2,1)}) %all-gather.11.cloned.1.call-update) | async-done | bytes 2359312 | tf_op jit(solution)/shard_map/all_gather | solution.py:312
  309.8 4.4 %fusion.60 = f32[1024,768]{1,0:T(8,128)S(1)} fusion(bf16[1536,1024]{1,0:T(8,128)(2,1)S(1)} %bitcast.162, bf16[1536,768]{0,1:T(8,128)(2,1)} %all-gather.11.cloned.1.call-done), kind=kOutput, calls=%fused_computation.129 | convolution fusion | flops 2415919104 | bytes 8650752 | tf_op jit(solution)/shard_map/dot_general | solution.py:229
  314.1 1.0 dynamic-slice_convert_fusion
  315.2 1.5 collective-permute-start.3
  316.8 1.2 copy.165
  317.9 12.1 %all-to-all-done = bf16[384,4,1024]{2,0,1:T(8,128)(2,1)} async-done(((bf16[384,4,1024]{2,0,1:T(8,128)(2,1)}), bf16[384,4,1024]{2,0,1:T(8,128)(2,1)}, u32[]{:S(2)}, u32[]{:S(2)}) %all-to-all-start) | async-done | bytes 3145760 | tf_op jit(solution)/shard_map/all_to_all | solution.py:307
  330.1 3.8 %reduce_sum.42 = bf16[384,1024]{1,0:T(8,128)(2,1)} reduce(bf16[384,4,1024]{2,0,1:T(8,128)(2,1)} %all-to-all-done, bf16[]{:T(256)} %constant.38.clone.1), dimensions={1}, to_apply=%region_6.7 | reduce | flops 1179648 | bytes 3932162 | tf_op jit(solution)/shard_map/reduce_sum | solution.py:311
  334.7 1.8 convert_add_fusion
  337.5 1.5 pad_maximum_fusion
  (124 shorter events, 17.3 us)
Async XLA Ops:
  7.2 3.3 copy-start
  7.2 107.3 %copy-start.38 = (s32[1,8]{1,0:T(1,128)S(1)}, s32[1,8]{1,0:T(1,128)}, u32[]{:S(2)}) copy-start(s32[1,8]{1,0:T(1,128)} %param.10) | copy-start | bytes 100
  7.2 105.3 %all-gather.5.cloned.1.call-start = ((), (), s32[]{:S(2)}) async-start(), calls=%async_computation.3 | async-start | bytes 7077888 | tf_op jit(solution)/shard_map/all_gather | solution.py:203
  10.4 188.2 %all-gather.7.cloned.1.call-start = ((), (), s32[]{:S(2)}) async-start(), calls=%async_computation.4 | async-start | bytes 4718592 | tf_op jit(solution)/shard_map/all_gather | solution.py:268
  129.5 1.3 copy-start.31
  136.5 0.7 copy-start.32
  137.8 9.1 %collective-permute-start = (bf16[384,256]{0,1:T(8,128)(2,1)}, bf16[384,256]{0,1:T(8,128)(2,1)}, u32[]{:S(2)}, u32[]{:S(2)}) collective-permute-start(bf16[384,256]{0,1:T(8,128)(2,1)} %pad_maximum_fusion.12), channel_id=1, source_target_pairs={{0,4},{4,0},{1,5},{5,1},{2,6},{6,2},{3,7},{7,3},{8,12},{12,8},{9,1... | collective-permute-start | bytes 589832 | tf_op jit(solution)/shard_map/ppermute | solution.py:251
  140.4 88.4 %all-to-all-start.1 = ((bf16[96,4,1024]{2,0,1:T(8,128)(2,1)}), bf16[96,4,1024]{2,0,1:T(8,128)(2,1)}, u32[]{:S(2)}, u32[]{:S(2)}) async-start(bf16[96,4,1024]{2,0,1:T(8,128)(2,1)} %bitcast.168), calls=%async_computation.1 | async-start | bytes 1572864 | tf_op jit(solution)/shard_map/all_to_all | solution.py:211
  144.6 110.0 %all-gather.9.cloned.1.call-start = ((), (), s32[]{:S(2)}) async-start(), calls=%async_computation.5 | async-start | bytes 1966080 | tf_op jit(solution)/shard_map/all_gather | solution.py:270
  146.9 1.6 copy-start.18
  146.9 2.8 copy-start.20
  148.4 2.5 copy-start.13
  149.7 3.6 %copy-start.2 = (f32[768,384,4]{1,0,2:T(8,128)}, f32[768,384,4]{1,0,2:T(8,128)S(1)}, u32[]{:S(2)}) copy-start(f32[768,384,4]{1,0,2:T(8,128)S(1)} %get-tuple-element.73) | copy-start | bytes 14155780
  157.1 6.0 %copy-start.14 = (bf16[768,256]{0,1:T(8,128)(2,1)S(1)}, bf16[768,256]{0,1:T(8,128)(2,1)}, u32[]{:S(2)}) copy-start(bf16[768,256]{0,1:T(8,128)(2,1)} %copy-done.13) | copy-start | bytes 1179652
  157.1 7.1 %copy-start.7 = (f32[384,64]{1,0:T(8,128)S(1)}, f32[384,64]{1,0:T(8,128)}, u32[]{:S(2)}) copy-start(f32[384,64]{1,0:T(8,128)} %get-tuple-element.70) | copy-start | bytes 294916
  157.2 7.1 %copy-start.9 = (f32[384,64]{1,0:T(8,128)S(1)}, f32[384,64]{1,0:T(8,128)}, u32[]{:S(2)}) copy-start(f32[384,64]{1,0:T(8,128)} %get-tuple-element.71) | copy-start | bytes 294916
  161.7 1.4 copy-start.4
  203.2 1.9 copy-start.15
  205.0 2.6 copy-start.16
  206.4 3.4 copy-start.3
  207.6 2.5 copy-start.28
  210.4 6.0 %copy-start.17 = (bf16[384,4,64]{2,0,1:T(8,128)(2,1)S(1)}, bf16[384,4,64]{2,0,1:T(8,128)(2,1)}, u32[]{:S(2)}) copy-start(bf16[384,4,64]{2,0,1:T(8,128)(2,1)} %copy-done.16) | copy-start | bytes 589828
  210.4 6.9 %copy-start.5 = (bf16[4,384,768]{1,2,0:T(8,128)(2,1)S(1)}, bf16[4,384,768]{1,2,0:T(8,128)(2,1)}, u32[]{:S(2)}) copy-start(bf16[4,384,768]{1,2,0:T(8,128)(2,1)} %copy-done.4) | copy-start | bytes 7077892
  210.4 6.9 %copy-start.19 = (bf16[384,4,64]{2,0,1:T(8,128)(2,1)S(1)}, bf16[384,4,64]{2,0,1:T(8,128)(2,1)}, u32[]{:S(2)}) copy-start(bf16[384,4,64]{2,0,1:T(8,128)(2,1)} %copy-done.18) | copy-start | bytes 589828
  210.4 6.9 %copy-start.21 = (bf16[384,4,64]{2,0,1:T(8,128)(2,1)S(1)}, bf16[384,4,64]{2,0,1:T(8,128)(2,1)}, u32[]{:S(2)}) copy-start(bf16[384,4,64]{2,0,1:T(8,128)(2,1)} %copy-done.20) | copy-start | bytes 589828
  214.9 1.4 copy-start.6
  218.4 8.3 %copy-start.22 = (f32[768,128]{0,1:T(8,128)}, f32[768,128]{0,1:T(8,128)S(1)}, u32[]{:S(2)}) copy-start(f32[768,128]{0,1:T(8,128)S(1)} %fusion.14) | copy-start | bytes 1179652
  218.4 4.1 %copy-start.25 = (bf16[384,1024]{0,1:T(8,128)(2,1)S(1)}, bf16[384,1024]{0,1:T(8,128)(2,1)}, u32[]{:S(2)}) copy-start(bf16[384,1024]{0,1:T(8,128)(2,1)} %copy.137) | copy-start | bytes 2359300
  226.6 5.5 %copy-start.29 = (f32[768,128]{0,1:T(8,128)}, f32[768,128]{0,1:T(8,128)S(1)}, u32[]{:S(2)}) copy-start(f32[768,128]{0,1:T(8,128)S(1)} %fusion.15) | copy-start | bytes 1179652
  227.5 12.4 %collective-permute-start.1 = (f32[384,256]{0,1:T(8,128)}, f32[384,256]{0,1:T(8,128)}, u32[]{:S(2)}, u32[]{:S(2)}) collective-permute-start(f32[384,256]{0,1:T(8,128)} %fusion.19), channel_id=1, source_target_pairs={{0,4},{4,0},{1,5},{5,1},{2,6},{6,2},{3,7},{7,3},{8,12},{12,8},{9,1... | collective-permute-start | bytes 1179656 | tf_op jit(solution)/shard_map/ppermute | solution.py:288
  232.1 22.5 %copy-start.8 = (f32[384,64]{1,0:T(8,128)S(1)}, f32[384,64]{1,0:T(8,128)}, u32[]{:S(2)}) copy-start(f32[384,64]{1,0:T(8,128)} %get-tuple-element.70) | copy-start | bytes 294916
  232.1 22.5 %copy-start.10 = (f32[384,64]{1,0:T(8,128)S(1)}, f32[384,64]{1,0:T(8,128)}, u32[]{:S(2)}) copy-start(f32[384,64]{1,0:T(8,128)} %get-tuple-element.71) | copy-start | bytes 294916
  232.1 40.7 %all-to-all-start.2 = ((bf16[4,384,1024]{2,1,0:T(8,128)(2,1)}), bf16[4,384,1024]{2,1,0:T(8,128)(2,1)S(1)}, u32[]{:S(2)}, u32[]{:S(2)}) async-start(bf16[4,384,1024]{2,1,0:T(8,128)(2,1)} %broadcast_in_dim.80), calls=%async_computation.2 | async-start | bytes 6291456 | tf_op jit(solution)/shard_map/all_to_all | solution.py:218
  235.9 73.8 %all-gather.11.cloned.1.call-start = ((), (), s32[]{:S(2)}) async-start(), calls=%async_computation.6 | async-start | bytes 2949120 | tf_op jit(solution)/shard_map/all_gather | solution.py:312
  272.8 1.0 copy-start.27
  272.8 1.0 copy-start.33
  272.8 1.1 copy-start.34
  273.9 6.0 %copy-start.23 = (bf16[4,4,96,1024]{3,2,1,0:T(8,128)(2,1)}, bf16[4,4,96,1024]{3,2,1,0:T(8,128)(2,1)S(1)}, u32[]{:S(2)}) copy-start(bf16[4,4,96,1024]{3,2,1,0:T(8,128)(2,1)S(1)} %copy.162) | copy-start | bytes 9437188
  273.9 6.0 %copy-start.37 = (bf16[1536,512]{0,1:T(8,128)(2,1)S(1)}, bf16[1536,512]{0,1:T(8,128)(2,1)}, u32[]{:S(2)}) copy-start(bf16[1536,512]{0,1:T(8,128)(2,1)} %all-gather.9.cloned.1.call-done) | copy-start | bytes 4718596
  279.9 4.0 %copy-start.12 = (bf16[4096,512]{1,0:T(8,128)(2,1)S(1)}, bf16[4096,512]{1,0:T(8,128)(2,1)}, u32[]{:S(2)}) copy-start(bf16[4096,512]{1,0:T(8,128)(2,1)} %all-gather.7.cloned.1.call-done) | copy-start | bytes 12582916
  281.8 1.5 copy-start.30
  283.3 13.9 %collective-permute-start.2 = (bf16[512,512]{1,0:T(8,128)(2,1)}, bf16[512,512]{1,0:T(8,128)(2,1)}, u32[]{:S(2)}, u32[]{:S(2)}) collective-permute-start(bf16[512,512]{1,0:T(8,128)(2,1)} %dynamic-slice_convert_fusion.1), channel_id=1, source_target_pairs={{0,4},{4,0},{1,5},{5,1},{2,6},{6,2},{3,7},{7,3},{8,12},{12,8},{9,1... | collective-permute-start | bytes 1572872 | tf_op jit(solution)/shard_map/ppermute | solution.py:237
  287.9 21.8 %copy-start.24 = (bf16[4,4,96,1024]{3,2,1,0:T(8,128)(2,1)S(1)}, bf16[4,4,96,1024]{3,2,1,0:T(8,128)(2,1)}, u32[]{:S(2)}) copy-start(bf16[4,4,96,1024]{3,2,1,0:T(8,128)(2,1)} %copy-done.23) | copy-start | bytes 9437188
  287.9 42.2 %all-to-all-start = ((bf16[384,4,1024]{2,0,1:T(8,128)(2,1)}), bf16[384,4,1024]{2,0,1:T(8,128)(2,1)}, u32[]{:S(2)}, u32[]{:S(2)}) async-start(bf16[384,4,1024]{2,0,1:T(8,128)(2,1)} %bitcast.158), calls=%async_computation | async-start | bytes 6291456 | tf_op jit(solution)/shard_map/all_to_all | solution.py:307
  299.8 16.9 %copy-start.35 = (bf16[128,4,384]{2,0,1:T(8,128)(2,1)S(1)}, bf16[128,4,384]{2,0,1:T(8,128)(2,1)}, u32[]{:S(2)}) copy-start(bf16[128,4,384]{2,0,1:T(8,128)(2,1)} %get-tuple-element.75) | copy-start | bytes 1179652
  309.8 6.9 %copy-start.36 = (bf16[128,4,384]{2,0,1:T(8,128)(2,1)S(1)}, bf16[128,4,384]{2,0,1:T(8,128)(2,1)}, u32[]{:S(2)}) copy-start(bf16[128,4,384]{2,0,1:T(8,128)(2,1)} %get-tuple-element.79) | copy-start | bytes 1179652
  314.1 2.5 copy-start.26
  315.2 19.6 %collective-permute-start.3 = (bf16[512,768]{1,0:T(8,128)(2,1)}, bf16[512,768]{1,0:T(8,128)(2,1)}, u32[]{:S(2)}, u32[]{:S(2)}) collective-permute-start(bf16[512,768]{1,0:T(8,128)(2,1)} %dynamic-slice_convert_fusion), channel_id=1, source_target_pairs={{0,4},{4,0},{1,5},{5,1},{2,6},{6,2},{3,7},{7,3},{8,12},{12,8},{9,1... | collective-permute-start | bytes 2359304 | tf_op jit(solution)/shard_map/ppermute | solution.py:237
  330.1 8.9 %copy-start.1 = (bf16[384,4096]{1,0:T(8,128)(2,1)S(1)}, bf16[384,4096]{1,0:T(8,128)(2,1)}, u32[]{:S(2)}) copy-start(bf16[384,4096]{1,0:T(8,128)(2,1)} %param.6) | copy-start | bytes 9437188
  333.9 3.6 %copy-start.11 = (f32[512,512]{1,0:T(8,128)S(1)}, f32[512,512]{1,0:T(8,128)}, u32[]{:S(2)}) copy-start(f32[512,512]{1,0:T(8,128)} %convert_add_fusion.1) | copy-start | bytes 3145732
Sparse Core Ops, SparseCore 0:
  10.8 101.7 all-gather.4
  114.7 83.9 all-gather.6
  218.5 36.0 all-gather.8
  260.5 49.2 all-gather.10

commit v19 on v17

--- a/solution.py
+++ b/solution.py
@@ -186,7 +186,7 @@
 def local(hidden_in, w_query, w_key, w_value, lengths, attn_grad):
     num_rows = hidden_in.shape[0]
     head_count = w_query.shape[1] // 128
-    first_heads = head_count // 2 if head_count % 2 == 0 else head_count
+    first_heads = (head_count * 5) // 8 if head_count >= 2 else head_count
     first_cols = first_heads * 128
     query_cols = head_count * 128
     start_row = lax.axis_index("ctx") * num_rows

time: 323 us -> 335 us (1.037)
  matrix products: 48 us -> 59.8 us
  local copies, waits for them, and re-layouts: 38.9 us -> 43.4 us
    all_gather x1, waiting for transfers between devices: 3.32 us -> 14.5 us  [local(): early_all = lax.all_gather(d_query_a, 'dp', axis=0, tiled=True)]
    ppermute x1, waiting for transfers between devices: 8.47 us -> 0.01 us  [local(): grad_kv = own_part + lax.ppermute(away_part, 'ctx', [(0, 1), (1, 0)])]
    ppermute x2, waiting for transfers between devices: 12 us -> 7.04 us  [weight_grad(): sent = lax.ppermute(away_part.astype(jnp.bfloat16), 'ctx', [(0, 1), (1, 0)])]
    all_to_all x1, waiting for transfers between devices: 0.01 us -> 4.96 us  [local(): cols_all = lax.all_to_all(spread, 'head', 0, 0, tiled=False)]
    dot_general x2, matrix products: 6.21 us -> 10.6 us  [weight_grad(): lax.dot_general(hidden_cols, gathered, (((0,), (0,)), ((), ())), preferre...]
    dot_general x2, matrix products: 3.52 us -> 7.48 us  [attend_whole(): jnp.einsum('hrk,rhd->kd', prob_b, dout_rows, preferred_element_type=jnp.f...]
    all_gather x1, waiting for transfers between devices: 17.8 us -> 14.3 us  [weight_grad(): gathered = lax.all_gather(d_rows, 'dp', axis=0, tiled=True)]
    dot_general x2, matrix products: 1.96 us -> 5.36 us  [attend_whole(): jnp.einsum('hrk,rhd->kd', d_score, query_rows, preferred_element_type=jnp...]
  transfers between devices with their start and end apart: 11 -> 11, of which waited for: 9 -> 7; matrix products, arithmetic and copies ran while one was open for 32% -> 33% of each run, Pallas kernels for 0% -> 0%
where the time goes in v19:
time: 335 us; the launch traced here: 330 us
  waiting for transfers between devices  169 us (50%)
  matrix products  59.8 us (18%)
  local copies, waits for them, and re-layouts  43.4 us (13%)
  other arithmetic  26.3 us (8%)
  starting transfers between devices  17 us (5%)
  between operations  14.6 us (4%)
    all_gather x1, waiting for transfers between devices, local(): full_a = lax.all_gather(local_a, rows_axes, axis=0, tiled=True)  104 us
    unnamed x76, local copies, waits for them, and re-layouts  20.7 us
    all_gather x1, waiting for transfers between devices, local(): early_all = lax.all_gather(d_query_a, 'dp', axis=0, tiled=True)  14.5 us
    all_gather x1, waiting for transfers between devices, weight_grad(): gathered = lax.all_gather(d_rows, 'dp', axis=0, tiled=True)  14.3 us
    all_gather x1, waiting for transfers between devices, local(): full_b = lax.all_gather(w_rest, rows_axes, axis=0, tiled=True)  13.8 us
    dot_general x2, matrix products, weight_grad(): lax.dot_general(hidden_cols, gathered, (((0,), (0,)), ((), ())), preferre...  10.6 us
    all_to_all x1, waiting for transfers between devices, local(): lax.all_to_all(input_part.astype(jnp.bfloat16).reshape(num_rows, head_gro...  10.2 us
    dot_general x2, matrix products, attend_whole(): jnp.einsum('rhd,kd->hrk', dout_rows, value_all, preferred_element_type=jn...  9.06 us
  transfers between devices with their start and end apart: 11, of which 7 were waited for; matrix products, arithmetic and copies ran while one was open for 33% of the time, Pallas kernels for 0%

profile of v19, /device:TPU:0, one launch (start us, length us, event | category | flops | bytes accessed | tf_op | source)
XLA Modules:
  0.0 330.0 jit_solution(5549284026582354650)
XLA Ops:
  7.2 1.3 slice.83
  8.5 2.0 pad_maximum_fusion.1
  10.6 2.3 copy.139
  12.8 1.0 slice.123
  13.8 1.9 slice.118
  16.8 2.1 copy.205
  19.3 1.5 multiply_cosine_fusion
  20.9 0.9 constant_dynamic-slice_fusion
  21.8 103.8 %all-gather.5.cloned.1.call-done = bf16[4096,896]{1,0:T(8,128)(2,1)} async-done(((bf16[512,896]{1,0:T(8,128)(2,1)}), bf16[4096,896]{1,0:T(8,128)(2,1)}) %all-gather.5.cloned.1.call-update) | async-done | bytes 7340048 | tf_op jit(solution)/shard_map/all_gather | solution.py:203
  125.6 6.4 %convolution_bitcast_fusion = f32[384,896]{0,1:T(8,128)S(1)} fusion(bf16[4096,896]{1,0:T(8,128)(2,1)} %all-gather.5.cloned.1.call-done, bf16[384,4096]{1,0:T(8,128)(2,1)S(1)} %copy-done), kind=kOutput, calls=%fused_computation.25 | convolution fusion | flops 2818572288 | bytes 11862016 | tf_op jit(solution)/shard_map/dot_general | solution.py:241
  132.0 1.1 slice.115
  133.1 0.9 copy.214
  134.1 4.2 %all-to-all-start = ((bf16[96,4,1024]{2,0,1:T(8,128)(2,1)}), bf16[96,4,1024]{2,0,1:T(8,128)(2,1)}, u32[]{:S(2)}, u32[]{:S(2)}) async-start(bf16[96,4,1024]{2,0,1:T(8,128)(2,1)} %bitcast.167), calls=%async_computation | async-start | bytes 1572864 | tf_op jit(solution)/shard_map/all_to_all | solution.py:211
  138.5 1.8 slice.96
  140.3 0.9 slice_bitcast_fusion.3
  143.6 2.2 fusion.59
  145.9 2.3 copy.204
  148.2 2.3 copy.203
  150.5 1.8 subtract_convert_fusion.1
  152.4 1.6 maximum_select_fusion
  154.0 1.6 fusion.5
  155.6 1.4 select_reduce_fusion
  157.0 3.0 bitcast_convert_fusion
  160.0 2.5 copy.176
  162.5 1.7 multiply_reduce_fusion
  164.2 5.3 %fusion.1 = bf16[5,384,768]{1,2,0:T(8,128)(2,1)S(1)} fusion(f32[768,384,5]{1,0,2:T(8,128)} %copy-done.2, f32[5,384]{1,0:T(8,128)S(1)} %multiply_reduce_fusion, f32[5,384]{1,0:T(8,128)S(1)} %log_add_fusion, pred[384,768]{0,1:T(8,128)(4,1)S(1)} %fusion.16, bf16[768,256]{0,1:T(8,128)(2,1)} %copy-done.13, bf16[384,8,128]{0,2,1:T(8,128)(2,1)} %bitcast.163), kind=kOutput, calls=%fused_computation.3 | convolution fusion | flops 389283840 | bytes 9845760 | tf_op jit(solution)/shard_map/rhd,kd->hrk/dot_general | solution.py:90
  169.6 1.3 convolution_bitcast_fusion.1
  171.5 1.1 pad_maximum_fusion.4
  172.5 2.1 copy.144
  174.6 4.6 %convolution_bitcast_fusion.6 = f32[768,128]{0,1:T(8,128)} fusion(bf16[5,384,768]{1,2,0:T(8,128)(2,1)} %copy-done.5, bf16[384,5,64]{2,0,1:T(8,128)(2,1)} %copy-done.12, bf16[384,5,64]{2,0,1:T(8,128)(2,1)} %copy-done.11), kind=kOutput, calls=%fused_computation.37 | convolution fusion | flops 378470400 | bytes 3833856 | tf_op jit(solution)/shard_map/hrk,rhd->kd/dot_general | solution.py:93
  179.2 5.2 %convolution_bitcast_fusion.5 = f32[768,128]{0,1:T(8,128)} fusion(bf16[384,8,128]{0,2,1:T(8,128)(2,1)S(1)} %bitcast.166, f32[768,384,5]{1,0,2:T(8,128)} %copy-done.2, f32[5,384]{1,0:T(8,128)S(1)} %log_add_fusion, pred[384,768]{0,1:T(8,128)(4,1)S(1)} %fusion.16), kind=kOutput, calls=%fused_computation.36 | convolution fusion | flops 384860160 | bytes 7090176 | tf_op jit(solution)/shard_map/hrk,rhd->kd/dot_general | solution.py:94
  184.3 3.2 broadcast_in_dim.92
  187.5 4.7 %all-to-all-start.1 = ((bf16[4,384,1024]{2,1,0:T(8,128)(2,1)}), bf16[4,384,1024]{2,1,0:T(8,128)(2,1)}, u32[]{:S(2)}, u32[]{:S(2)}) async-start(bf16[4,384,1024]{2,1,0:T(8,128)(2,1)} %broadcast_in_dim.92), calls=%async_computation.1 | async-start | bytes 6291456 | tf_op jit(solution)/shard_map/all_to_all | solution.py:218
  192.2 13.8 %all-gather.7.cloned.1.call-done = bf16[4096,384]{1,0:T(8,128)(2,1)} async-done(((bf16[512,384]{1,0:T(8,128)(2,1)}), bf16[4096,384]{1,0:T(8,128)(2,1)}) %all-gather.7.cloned.1.call-update) | async-done | bytes 3145744 | tf_op jit(solution)/shard_map/all_gather | solution.py:268
  206.1 3.7 %fusion.61 = f32[384,384]{1,0:T(8,128)S(1)} fusion(bf16[4096,384]{1,0:T(8,128)(2,1)} %all-gather.7.cloned.1.call-done, bf16[384,4096]{1,0:T(8,128)(2,1)S(1)} %copy-done), kind=kOutput, calls=%fused_computation.127 | convolution fusion | flops 1207959552 | bytes 6881280 | tf_op jit(solution)/shard_map/dot_general | solution.py:271
  210.3 1.2 subtract_convert_fusion.3
  211.5 1.0 fusion.12
  212.5 0.9 select_reduce_fusion.1
  213.5 1.9 bitcast_convert_fusion.1
  215.8 3.7 %fusion.8 = bf16[3,384,768]{1,2,0:T(8,128)(2,1)S(1)} fusion(f32[768,384,3]{1,0,2:T(8,128)} %copy-done.3, f32[3,384]{1,0:T(4,128)S(1)} %multiply_reduce_fusion.1, f32[3,384]{1,0:T(4,128)S(1)} %log_add_fusion.1, pred[384,768]{0,1:T(8,128)(4,1)S(1)} %fusion.16, bf16[768,256]{0,1:T(8,128)(2,1)S(1)} %copy-done.15, bf16[384,8,128]{0,2,1:T(8,128)(2,1)} %bitcast.164), kind=kOutput, calls=%fused_computation.14 | convolution fusion | flops 233570304 | bytes 6107136 | tf_op jit(solution)/shard_map/rhd,kd->hrk/dot_general | solution.py:90
  220.4 2.3 fusion.15
  224.2 5.0 %all-to-all-done.1 = bf16[4,384,1024]{2,1,0:T(8,128)(2,1)} async-done(((bf16[4,384,1024]{2,1,0:T(8,128)(2,1)}), bf16[4,384,1024]{2,1,0:T(8,128)(2,1)}, u32[]{:S(2)}, u32[]{:S(2)}) %all-to-all-start.1) | async-done | bytes 3145760 | tf_op jit(solution)/shard_map/all_to_all | solution.py:218
  229.2 4.0 %copy.150 = bf16[4,4,96,1024]{3,2,1,0:T(8,128)(2,1)} copy(bf16[4,4,96,1024]{3,2,0,1:T(8,128)(2,1)} %bitcast.31) | data formatting | bytes 6291456 | tf_op jit(solution)/shard_map/transpose | solution.py:221
  234.0 1.0 fusion.25
  235.5 14.5 %all-gather.9.cloned.1.call-done = bf16[1536,640]{0,1:T(8,128)(2,1)} async-done(((bf16[384,640]{0,1:T(8,128)(2,1)}), bf16[1536,640]{0,1:T(8,128)(2,1)}) %all-gather.9.cloned.1.call-update) | async-done | bytes 1966096 | tf_op jit(solution)/shard_map/all_gather | solution.py:270
  251.6 5.4 %fusion.62 = f32[1024,640]{1,0:T(8,128)S(1)} fusion(bf16[1536,1024]{1,0:T(8,128)(2,1)} %bitcast.159, bf16[1536,640]{0,1:T(8,128)(2,1)} %all-gather.9.cloned.1.call-done), kind=kOutput, calls=%fused_computation.128 | convolution fusion | flops 2013265920 | bytes 7733248 | tf_op jit(solution)/shard_map/dot_general | solution.py:229
  257.1 1.5 collective-permute-start.1
  258.6 5.9 %fusion.17 = f32[384,4096]{1,0:T(8,128)S(1)} fusion(bf16[4096,896]{1,0:T(8,128)(2,1)} %all-gather.5.cloned.1.call-done, bf16[384,128]{0,1:T(8,128)(2,1)S(1)} %slice.169, bf16[384,128]{0,1:T(8,128)(2,1)S(1)} %maximum_bitcast_fusion.1, bf16[384,640]{0,1:T(8,128)(2,1)S(1)} %bitcast.173), kind=kOutput, calls=%fused_computation.54 | convolution fusion | flops 2820636672 | bytes 14319616 | tf_op jit(solution)/shard_map/dot_general | solution.py:295
  264.6 1.8 convolution_add_fusion
  266.4 7.0 %collective-permute-done.1 = bf16[512,640]{1,0:T(8,128)(2,1)S(1)} collective-permute-done((bf16[512,640]{1,0:T(8,128)(2,1)S(1)}, bf16[512,640]{1,0:T(8,128)(2,1)S(1)}, u32[]{:S(2)}, u32[]{:S(2)}) %collective-permute-start.1) | collective-permute-done | bytes 655392 | tf_op jit(solution)/shard_map/ppermute | solution.py:237
  273.5 1.2 convert_add_fusion.1
  274.6 2.0 copy.213
  276.7 3.7 %all-to-all-start.2 = ((bf16[384,4,1024]{2,0,1:T(8,128)(2,1)}), bf16[384,4,1024]{2,0,1:T(8,128)(2,1)S(1)}, u32[]{:S(2)}, u32[]{:S(2)}) async-start(bf16[384,4,1024]{2,0,1:T(8,128)(2,1)} %bitcast.156), calls=%async_computation.2 | async-start | bytes 6291456 | tf_op jit(solution)/shard_map/all_to_all | solution.py:308
  280.4 14.3 %all-gather.11.cloned.1.call-done = bf16[1536,640]{0,1:T(8,128)(2,1)} async-done(((bf16[384,640]{0,1:T(8,128)(2,1)}), bf16[1536,640]{0,1:T(8,128)(2,1)}) %all-gather.11.cloned.1.call-update) | async-done | bytes 1966096 | tf_op jit(solution)/shard_map/all_gather | solution.py:228
  294.7 5.2 %fusion.63 = f32[1024,640]{1,0:T(8,128)S(1)} fusion(bf16[1536,1024]{1,0:T(8,128)(2,1)} %bitcast.160, bf16[1536,640]{0,1:T(8,128)(2,1)} %all-gather.11.cloned.1.call-done), kind=kOutput, calls=%fused_computation.129 | convolution fusion | flops 2013265920 | bytes 7733248 | tf_op jit(solution)/shard_map/dot_general | solution.py:229
  299.9 1.5 copy-done.24
  301.4 0.9 dynamic-slice_convert_fusion
  302.3 1.5 collective-permute-start.3
  303.8 1.0 pad_maximum_fusion.2
  304.7 2.3 copy.167
  307.0 10.2 %all-to-all-done.2 = bf16[384,4,1024]{2,0,1:T(8,128)(2,1)S(1)} async-done(((bf16[384,4,1024]{2,0,1:T(8,128)(2,1)}), bf16[384,4,1024]{2,0,1:T(8,128)(2,1)S(1)}, u32[]{:S(2)}, u32[]{:S(2)}) %all-to-all-start.2) | async-done | bytes 3145760 | tf_op jit(solution)/shard_map/all_to_all | solution.py:308
  317.3 1.7 reduce_sum.42
  319.0 1.8 convert_add_fusion
  321.7 1.6 pad_maximum_fusion
  (111 shorter events, 12.0 us)
Async XLA Ops:
  7.2 13.7 %copy-start = (bf16[384,4096]{1,0:T(8,128)(2,1)S(1)}, bf16[384,4096]{1,0:T(8,128)(2,1)}, u32[]{:S(2)}) copy-start(bf16[384,4096]{1,0:T(8,128)(2,1)} %param.6) | copy-start | bytes 9437188
  7.2 8.5 %copy-start.30 = (s32[1,8]{1,0:T(1,128)S(1)}, s32[1,8]{1,0:T(1,128)}, u32[]{:S(2)}) copy-start(s32[1,8]{1,0:T(1,128)} %param.10) | copy-start | bytes 100
  7.2 118.4 %all-gather.5.cloned.1.call-start = ((), (), s32[]{:S(2)}) async-start(), calls=%async_computation.3 | async-start | bytes 8257536 | tf_op jit(solution)/shard_map/all_gather | solution.py:203
  125.6 7.5 %copy-start.19 = (bf16[96,4096]{1,0:T(8,128)(2,1)S(1)}, bf16[96,4096]{1,0:T(8,128)(2,1)}, u32[]{:S(2)}) copy-start(bf16[96,4096]{1,0:T(8,128)(2,1)} %constant_dynamic-slice_fusion) | copy-start | bytes 2359300
  132.0 2.1 copy-start.25
  134.1 50.2 %all-to-all-start = ((bf16[96,4,1024]{2,0,1:T(8,128)(2,1)}), bf16[96,4,1024]{2,0,1:T(8,128)(2,1)}, u32[]{:S(2)}, u32[]{:S(2)}) async-start(bf16[96,4,1024]{2,0,1:T(8,128)(2,1)} %bitcast.167), calls=%async_computation | async-start | bytes 1572864 | tf_op jit(solution)/shard_map/all_to_all | solution.py:211
  138.3 67.7 %all-gather.7.cloned.1.call-start = ((), (), s32[]{:S(2)}) async-start(), calls=%async_computation.4 | async-start | bytes 3538944 | tf_op jit(solution)/shard_map/all_gather | solution.py:268
  141.7 0.6 copy-start.27
  143.1 9.3 %collective-permute-start = (bf16[384,256]{0,1:T(8,128)(2,1)}, bf16[384,256]{0,1:T(8,128)(2,1)}, u32[]{:S(2)}, u32[]{:S(2)}) collective-permute-start(bf16[384,256]{0,1:T(8,128)(2,1)} %pad_maximum_fusion.8), channel_id=1, source_target_pairs={{0,4},{4,0},{1,5},{5,1},{2,6},{6,2},{3,7},{7,3},{8,12},{12,8},{9,1... | collective-permute-start | bytes 589832 | tf_op jit(solution)/shard_map/ppermute | solution.py:251
  152.4 3.2 copy-start.11
  152.4 3.2 copy-start.12
  154.0 3.1 copy-start.13
  155.6 4.5 %copy-start.2 = (f32[768,384,5]{1,0,2:T(8,128)}, f32[768,384,5]{1,0,2:T(8,128)S(1)}, u32[]{:S(2)}) copy-start(f32[768,384,5]{1,0,2:T(8,128)S(1)} %get-tuple-element.71) | copy-start | bytes 17694724
  164.2 5.3 %copy-start.14 = (bf16[768,256]{0,1:T(8,128)(2,1)S(1)}, bf16[768,256]{0,1:T(8,128)(2,1)}, u32[]{:S(2)}) copy-start(bf16[768,256]{0,1:T(8,128)(2,1)} %copy-done.13) | copy-start | bytes 1179652
  169.6 1.9 copy-start.5
  169.6 1.3 copy-start.7
  169.6 1.5 copy-start.9
  174.6 4.6 %copy-start.18 = (bf16[384,1024]{0,1:T(8,128)(2,1)S(1)}, bf16[384,1024]{0,1:T(8,128)(2,1)}, u32[]{:S(2)}) copy-start(bf16[384,1024]{0,1:T(8,128)(2,1)} %copy.139) | copy-start | bytes 2359300
  187.5 41.7 %all-to-all-start.1 = ((bf16[4,384,1024]{2,1,0:T(8,128)(2,1)}), bf16[4,384,1024]{2,1,0:T(8,128)(2,1)}, u32[]{:S(2)}, u32[]{:S(2)}) async-start(bf16[4,384,1024]{2,1,0:T(8,128)(2,1)} %broadcast_in_dim.92), calls=%async_computation.1 | async-start | bytes 6291456 | tf_op jit(solution)/shard_map/all_to_all | solution.py:218
  192.2 57.9 %all-gather.9.cloned.1.call-start = ((), (), s32[]{:S(2)}) async-start(), calls=%async_computation.5 | async-start | bytes 2457600 | tf_op jit(solution)/shard_map/all_gather | solution.py:270
  206.0 88.7 %all-gather.11.cloned.1.call-start = ((), (), s32[]{:S(2)}) async-start(), calls=%async_computation.6 | async-start | bytes 2457600 | tf_op jit(solution)/shard_map/all_gather | solution.py:228
  209.8 1.7 copy-start.15
  212.5 2.8 copy-start.3
  213.5 2.1 copy-start.26
  215.8 3.8 %copy-start.22 = (f32[768,128]{0,1:T(8,128)S(1)}, f32[768,128]{0,1:T(8,128)}, u32[]{:S(2)}) copy-start(f32[768,128]{0,1:T(8,128)} %convolution_bitcast_fusion.6) | copy-start | bytes 1179652
  215.8 4.6 %copy-start.4 = (f32[768,384,3]{1,0,2:T(8,128)S(1)}, f32[768,384,3]{1,0,2:T(8,128)}, u32[]{:S(2)}) copy-start(f32[768,384,3]{1,0,2:T(8,128)} %copy-done.3) | copy-start | bytes 10616836
  215.8 4.6 %copy-start.31 = (f32[768,128]{0,1:T(8,128)S(1)}, f32[768,128]{0,1:T(8,128)}, u32[]{:S(2)}) copy-start(f32[768,128]{0,1:T(8,128)} %convolution_bitcast_fusion.5) | copy-start | bytes 1179652
  220.4 2.3 copy-start.16
  222.8 6.4 %copy-start.23 = (f32[768,128]{0,1:T(8,128)}, f32[768,128]{0,1:T(8,128)S(1)}, u32[]{:S(2)}) copy-start(f32[768,128]{0,1:T(8,128)S(1)} %fusion.15) | copy-start | bytes 1179652
  223.7 10.4 %collective-permute-start.2 = (f32[384,256]{0,1:T(8,128)}, f32[384,256]{0,1:T(8,128)S(1)}, u32[]{:S(2)}, u32[]{:S(2)}) collective-permute-start(f32[384,256]{0,1:T(8,128)} %fusion.23), channel_id=1, source_target_pairs={{0,4},{4,0},{1,5},{5,1},{2,6},{6,2},{3,7},{7,3},{8,12},{12,8},{9,1... | collective-permute-start | bytes 1179656 | tf_op jit(solution)/shard_map/ppermute | solution.py:288
  229.2 4.9 %copy-start.17 = (f32[768,128]{0,1:T(8,128)S(1)}, f32[768,128]{0,1:T(8,128)}, u32[]{:S(2)}) copy-start(f32[768,128]{0,1:T(8,128)} %copy-done.16) | copy-start | bytes 1179652
  233.2 16.9 %copy-start.8 = (f32[384,64]{1,0:T(8,128)S(1)}, f32[384,64]{1,0:T(8,128)}, u32[]{:S(2)}) copy-start(f32[384,64]{1,0:T(8,128)} %get-tuple-element.68) | copy-start | bytes 294916
  233.2 16.9 %copy-start.10 = (f32[384,64]{1,0:T(8,128)S(1)}, f32[384,64]{1,0:T(8,128)}, u32[]{:S(2)}) copy-start(f32[384,64]{1,0:T(8,128)} %get-tuple-element.69) | copy-start | bytes 294916
  251.6 7.0 %copy-start.21 = (bf16[384,5,128]{0,2,1:T(8,128)(2,1)S(1)}, bf16[384,5,128]{0,2,1:T(8,128)(2,1)}, u32[]{:S(2)}) copy-start(bf16[384,5,128]{0,2,1:T(8,128)(2,1)} %copy.144) | copy-start | bytes 1474564
  257.1 7.5 %copy-start.20 = (bf16[4096,384]{1,0:T(8,128)(2,1)S(1)}, bf16[4096,384]{1,0:T(8,128)(2,1)}, u32[]{:S(2)}) copy-start(bf16[4096,384]{1,0:T(8,128)(2,1)} %all-gather.7.cloned.1.call-done) | copy-start | bytes 9437188
  257.1 16.4 %collective-permute-start.1 = (bf16[512,640]{1,0:T(8,128)(2,1)S(1)}, bf16[512,640]{1,0:T(8,128)(2,1)S(1)}, u32[]{:S(2)}, u32[]{:S(2)}) collective-permute-start(bf16[512,640]{1,0:T(8,128)(2,1)S(1)} %dynamic-slice_convert_fusion.1), channel_id=1, source_target_pairs={{0,4},{4,0},{1,5},{5,1},{2,6},{6,2},{3,7},{7,3},{8,12},{12,8},{9,1... | collective-permute-start | bytes 1966088 | tf_op jit(solution)/shard_map/ppermute | solution.py:237
  276.7 40.6 %all-to-all-start.2 = ((bf16[384,4,1024]{2,0,1:T(8,128)(2,1)}), bf16[384,4,1024]{2,0,1:T(8,128)(2,1)S(1)}, u32[]{:S(2)}, u32[]{:S(2)}) async-start(bf16[384,4,1024]{2,0,1:T(8,128)(2,1)} %bitcast.156), calls=%async_computation.2 | async-start | bytes 6291456 | tf_op jit(solution)/shard_map/all_to_all | solution.py:308
  280.4 23.4 %copy-start.29 = (bf16[128,3,384]{2,0,1:T(8,128)(2,1)S(1)}, bf16[128,3,384]{2,0,1:T(8,128)(2,1)}, u32[]{:S(2)}) copy-start(bf16[128,3,384]{2,0,1:T(8,128)(2,1)} %get-tuple-element.77) | copy-start | bytes 884740
  294.7 9.1 %copy-start.28 = (bf16[128,5,384]{2,0,1:T(8,128)(2,1)S(1)}, bf16[128,5,384]{2,0,1:T(8,128)(2,1)}, u32[]{:S(2)}) copy-start(bf16[128,5,384]{2,0,1:T(8,128)(2,1)} %get-tuple-element.73) | copy-start | bytes 1474564
  299.9 1.5 copy-start.24
  302.3 16.7 %collective-permute-start.3 = (bf16[512,640]{1,0:T(8,128)(2,1)}, bf16[512,640]{1,0:T(8,128)(2,1)}, u32[]{:S(2)}, u32[]{:S(2)}) collective-permute-start(bf16[512,640]{1,0:T(8,128)(2,1)} %dynamic-slice_convert_fusion), channel_id=1, source_target_pairs={{0,4},{4,0},{1,5},{5,1},{2,6},{6,2},{3,7},{7,3},{8,12},{12,8},{9,1... | collective-permute-start | bytes 1966088 | tf_op jit(solution)/shard_map/ppermute | solution.py:237
  319.0 2.7 copy-start.6
  319.0 4.3 %copy-start.1 = (bf16[384,4096]{1,0:T(8,128)(2,1)S(1)}, bf16[384,4096]{1,0:T(8,128)(2,1)}, u32[]{:S(2)}) copy-start(bf16[384,4096]{1,0:T(8,128)(2,1)} %param.6) | copy-start | bytes 9437188
Sparse Core Ops, SparseCore 0:
  10.8 114.7 all-gather.4
  141.3 64.6 all-gather.6
  207.6 42.4 all-gather.8
  252.1 42.5 all-gather.10

commit v20 on v19

--- a/solution.py
+++ b/solution.py
@@ -186,7 +186,7 @@
 def local(hidden_in, w_query, w_key, w_value, lengths, attn_grad):
     num_rows = hidden_in.shape[0]
     head_count = w_query.shape[1] // 128
-    first_heads = (head_count * 5) // 8 if head_count >= 2 else head_count
+    first_heads = (head_count * 3) // 8 if head_count >= 3 else head_count
     first_cols = first_heads * 128
     query_cols = head_count * 128
     start_row = lax.axis_index("ctx") * num_rows

time: 335 us -> 359 us (1.072)
  local copies, waits for them, and re-layouts: 43.4 us -> 54.9 us
  waiting for transfers between devices: 169 us -> 180 us
  other arithmetic: 26.3 us -> 30.1 us
    all_gather x1, waiting for transfers between devices: 13.8 us -> 41.4 us  [local(): full_b = lax.all_gather(w_rest, rows_axes, axis=0, tiled=True)]
    all_to_all x1, waiting for transfers between devices: 4.96 us -> 22.4 us  [local(): cols_all = lax.all_to_all(spread, 'head', 0, 0, tiled=False)]
    all_gather x1, waiting for transfers between devices: 104 us -> 88.4 us  [local(): full_a = lax.all_gather(local_a, rows_axes, axis=0, tiled=True)]
    all_gather x1, waiting for transfers between devices: 14.5 us -> 0.01 us  [local(): early_all = lax.all_gather(d_query_a, 'dp', axis=0, tiled=True)]
    unnamed x76 -> x111, local copies, waits for them, and re-layouts: 20.7 us -> 31.4 us
    all_gather x1, waiting for transfers between devices: 14.3 us -> 6.33 us  [weight_grad(): gathered = lax.all_gather(d_rows, 'dp', axis=0, tiled=True)]
    all_to_all x1, waiting for transfers between devices: 10.2 us -> 14.8 us  [local(): lax.all_to_all(input_part.astype(jnp.bfloat16).reshape(num_rows, head_gro...]
    transpose x1, local copies, waits for them, and re-layouts: 4.02 us -> 0.31 us  [local(): hidden_cols = cols_all.reshape(head_groups, dp_count, quarter, -1).transp...]
  transfers between devices with their start and end apart: 11 -> 11, of which waited for: 7 -> 6; matrix products, arithmetic and copies ran while one was open for 33% -> 34% of each run, Pallas kernels for 0% -> 0%
where the time goes in v20:
time: 359 us; the launch traced here: 353 us
  waiting for transfers between devices  180 us (50%)
  matrix products  56.8 us (16%)
  local copies, waits for them, and re-layouts  54.9 us (15%)
  other arithmetic  30.1 us (8%)
  starting transfers between devices  16.8 us (5%)
  between operations  14.6 us (4%)
    all_gather x1, waiting for transfers between devices, local(): full_a = lax.all_gather(local_a, rows_axes, axis=0, tiled=True)  88.4 us
    all_gather x1, waiting for transfers between devices, local(): full_b = lax.all_gather(w_rest, rows_axes, axis=0, tiled=True)  41.4 us
    unnamed x111, local copies, waits for them, and re-layouts  31.4 us
    all_to_all x1, waiting for transfers between devices, local(): cols_all = lax.all_to_all(spread, 'head', 0, 0, tiled=False)  22.4 us
    all_to_all x1, waiting for transfers between devices, local(): lax.all_to_all(input_part.astype(jnp.bfloat16).reshape(num_rows, head_gro...  14.8 us
    dot_general x2, matrix products, attend_whole(): jnp.einsum('rhd,kd->hrk', dout_rows, value_all, preferred_element_type=jn...  9.23 us
    dot_general x2, matrix products, weight_grad(): lax.dot_general(hidden_cols, gathered, (((0,), (0,)), ((), ())), preferre...  7.6 us
  transfers between devices with their start and end apart: 11, of which 6 were waited for; matrix products, arithmetic and copies ran while one was open for 34% of the time, Pallas kernels for 0%

profile of v20, /device:TPU:0, one launch (start us, length us, event | category | flops | bytes accessed | tf_op | source)
XLA Modules:
  0.0 353.2 jit_solution(7037142882489076226)
XLA Ops:
  7.2 1.2 slice.83
  8.4 1.9 pad_maximum_fusion.3
  11.3 88.4 %all-gather.5.cloned.1.call-done = bf16[4096,640]{1,0:T(8,128)(2,1)} async-done(((bf16[512,640]{1,0:T(8,128)(2,1)}), bf16[4096,640]{1,0:T(8,128)(2,1)}) %all-gather.5.cloned.1.call-update) | async-done | bytes 5242896 | tf_op jit(solution)/shard_map/all_gather | solution.py:203
  99.8 2.0 slice.96
  101.8 2.3 copy.147
  104.1 1.0 slice.118
  105.1 1.9 slice.123
  108.0 2.1 copy.217
  110.6 1.5 multiply_cosine_fusion
  112.1 5.5 %convolution_bitcast_fusion.1 = f32[384,640]{0,1:T(8,128)S(1)} fusion(bf16[4096,640]{1,0:T(8,128)(2,1)} %all-gather.5.cloned.1.call-done, bf16[384,4096]{1,0:T(8,128)(2,1)S(1)} %copy-done), kind=kOutput, calls=%fused_computation.28 | convolution fusion | flops 2013265920 | bytes 9371648 | tf_op jit(solution)/shard_map/dot_general | solution.py:241
  119.5 4.2 %all-to-all-start = ((bf16[96,4,1024]{2,0,1:T(8,128)(2,1)}), bf16[96,4,1024]{2,0,1:T(8,128)(2,1)}, u32[]{:S(2)}, u32[]{:S(2)}) async-start(bf16[96,4,1024]{2,0,1:T(8,128)(2,1)} %bitcast.167), calls=%async_computation | async-start | bytes 1572864 | tf_op jit(solution)/shard_map/all_to_all | solution.py:211
  127.2 1.9 fusion.60
  129.1 2.0 copy.213
  131.2 2.0 copy.212
  133.2 1.5 subtract_convert_fusion.3
  134.7 1.4 maximum_select_fusion
  136.1 1.0 fusion.12
  138.1 2.1 bitcast_convert_fusion.1
  140.2 2.1 copy.186
  142.3 1.4 multiply_reduce_fusion.1
  143.7 3.8 %fusion.8 = bf16[3,384,768]{1,2,0:T(8,128)(2,1)S(1)} fusion(f32[768,384,3]{1,0,2:T(8,128)} %copy-done.3, f32[3,384]{1,0:T(4,128)S(1)} %multiply_reduce_fusion.1, f32[3,384]{1,0:T(4,128)S(1)} %log_add_fusion.1, pred[384,768]{0,1:T(8,128)(4,1)S(1)} %fusion.16, bf16[768,256]{0,1:T(8,128)(2,1)} %copy-done.18, bf16[384,8,128]{0,2,1:T(8,128)(2,1)} %bitcast.163), kind=kOutput, calls=%fused_computation.14 | convolution fusion | flops 233570304 | bytes 6104064 | tf_op jit(solution)/shard_map/rhd,kd->hrk/dot_general | solution.py:90
  147.5 1.2 copy-done.6
  150.8 1.8 copy.152
  152.6 41.4 %all-gather.7.cloned.1.call-done = bf16[4096,640]{1,0:T(8,128)(2,1)} async-done(((bf16[512,640]{1,0:T(8,128)(2,1)}), bf16[4096,640]{1,0:T(8,128)(2,1)}) %all-gather.7.cloned.1.call-update) | async-done | bytes 5242896 | tf_op jit(solution)/shard_map/all_gather | solution.py:268
  194.0 5.4 %fusion.61 = f32[640,384]{1,0:T(8,128)S(1)} fusion(bf16[4096,640]{1,0:T(8,128)(2,1)} %all-gather.7.cloned.1.call-done, bf16[384,4096]{1,0:T(8,128)(2,1)S(1)} %copy-done), kind=kOutput, calls=%fused_computation.127 | convolution fusion | flops 2013265920 | bytes 9371648 | tf_op jit(solution)/shard_map/dot_general | solution.py:271
  199.8 1.3 copy.215
  201.2 1.5 subtract_convert_fusion.1
  202.7 1.8 fusion.5
  204.5 1.4 select_reduce_fusion
  206.2 2.6 convolution_bitcast_fusion.5
  208.7 3.0 bitcast_convert_fusion
  211.8 1.5 copy.197
  213.7 5.4 %fusion.1 = bf16[5,384,768]{1,2,0:T(8,128)(2,1)S(1)} fusion(f32[768,384,5]{1,0,2:T(8,128)} %copy-done.2, f32[5,384]{1,0:T(8,128)S(1)} %multiply_reduce_fusion, f32[5,384]{1,0:T(8,128)S(1)} %log_add_fusion, pred[384,768]{0,1:T(8,128)(4,1)S(1)} %fusion.16, bf16[768,256]{0,1:T(8,128)(2,1)} %copy-done.18, bf16[384,8,128]{0,2,1:T(8,128)(2,1)} %bitcast.164), kind=kOutput, calls=%fused_computation.2 | convolution fusion | flops 389283840 | bytes 9845760 | tf_op jit(solution)/shard_map/rhd,kd->hrk/dot_general | solution.py:90
  219.2 1.1 convolution_bitcast_fusion.6
  222.5 2.3 fusion.15
  226.5 3.2 broadcast_in_dim.92
  229.7 3.7 %all-to-all-start.1 = ((bf16[4,384,1024]{2,1,0:T(8,128)(2,1)}), bf16[4,384,1024]{2,1,0:T(8,128)(2,1)S(1)}, u32[]{:S(2)}, u32[]{:S(2)}) async-start(bf16[4,384,1024]{2,1,0:T(8,128)(2,1)} %broadcast_in_dim.92), calls=%async_computation.1 | async-start | bytes 6291456 | tf_op jit(solution)/shard_map/all_to_all | solution.py:218
  233.8 4.2 %convolution_bitcast_fusion = f32[384,5,128]{2,0,1:T(8,128)} fusion(bf16[5,384,768]{1,2,0:T(8,128)(2,1)} %copy-done.5, bf16[768,256]{0,1:T(8,128)(2,1)} %copy-done.18), kind=kOutput, calls=%fused_computation.27 | convolution fusion | flops 377487360 | bytes 4128768 | tf_op jit(solution)/shard_map/hrk,kd->rhd/dot_general | solution.py:92
  238.0 1.1 fusion.25
  240.9 1.9 add_convert_fusion
  242.8 1.1 pad_maximum_fusion.5
  243.8 2.0 copy.171
  245.8 2.0 pad_maximum_fusion.2
  247.9 22.4 %all-to-all-done.1 = bf16[4,384,1024]{2,1,0:T(8,128)(2,1)S(1)} async-done(((bf16[4,384,1024]{2,1,0:T(8,128)(2,1)}), bf16[4,384,1024]{2,1,0:T(8,128)(2,1)S(1)}, u32[]{:S(2)}, u32[]{:S(2)}) %all-to-all-start.1) | async-done | bytes 3145760 | tf_op jit(solution)/shard_map/all_to_all | solution.py:218
  271.3 6.6 %fusion.17 = f32[384,4096]{1,0:T(8,128)S(1)} fusion(bf16[4096,640]{1,0:T(8,128)(2,1)} %all-gather.5.cloned.1.call-done, bf16[384,128]{0,1:T(8,128)(2,1)S(1)} %copy-done.37, bf16[384,128]{0,1:T(8,128)(2,1)S(1)} %copy-done.38, bf16[384,384]{0,1:T(8,128)(2,1)S(1)} %bitcast.171), kind=kOutput, calls=%fused_computation.61 | convolution fusion | flops 2014740480 | bytes 12025856 | tf_op jit(solution)/shard_map/dot_general | solution.py:295
  277.9 1.8 fusion.62
  279.8 1.3 collective-permute-start.1
  281.1 2.9 convolution_add_fusion
  284.0 6.6 %collective-permute-done.1 = bf16[512,384]{1,0:T(8,128)(2,1)S(1)} collective-permute-done((bf16[512,384]{1,0:T(8,128)(2,1)S(1)}, bf16[512,384]{1,0:T(8,128)(2,1)S(1)}, u32[]{:S(2)}, u32[]{:S(2)}) %collective-permute-start.1) | collective-permute-done | bytes 393248 | tf_op jit(solution)/shard_map/ppermute | solution.py:237
  291.6 2.0 copy.222
  293.6 4.2 %all-to-all-start.2 = ((bf16[384,4,1024]{2,0,1:T(8,128)(2,1)}), bf16[384,4,1024]{2,0,1:T(8,128)(2,1)S(1)}, u32[]{:S(2)}, u32[]{:S(2)}) async-start(bf16[384,4,1024]{2,0,1:T(8,128)(2,1)} %bitcast.157), calls=%async_computation.2 | async-start | bytes 6291456 | tf_op jit(solution)/shard_map/all_to_all | solution.py:308
  297.8 6.3 %all-gather.11.cloned.1.call-done = bf16[1536,896]{0,1:T(8,128)(2,1)} async-done(((bf16[384,896]{0,1:T(8,128)(2,1)}), bf16[1536,896]{0,1:T(8,128)(2,1)}) %all-gather.11.cloned.1.call-update) | async-done | bytes 2752528 | tf_op jit(solution)/shard_map/all_gather | solution.py:228
  304.1 5.8 %fusion.63 = f32[1024,896]{0,1:T(8,128)S(1)} fusion(bf16[1536,896]{0,1:T(8,128)(2,1)} %all-gather.11.cloned.1.call-done, bf16[1536,1024]{1,0:T(8,128)(2,1)} %bitcast.159), kind=kOutput, calls=%fused_computation.129 | convolution fusion | flops 2818572288 | bytes 9568256 | tf_op jit(solution)/shard_map/dot_general | solution.py:229
  309.9 1.8 copy-done.32
  311.7 1.1 dynamic-slice_convert_fusion
  312.8 1.5 collective-permute-start.3
  315.2 2.3 copy.174
  317.5 2.4 copy.173
  319.9 14.8 %all-to-all-done.2 = bf16[384,4,1024]{2,0,1:T(8,128)(2,1)S(1)} async-done(((bf16[384,4,1024]{2,0,1:T(8,128)(2,1)}), bf16[384,4,1024]{2,0,1:T(8,128)(2,1)S(1)}, u32[]{:S(2)}, u32[]{:S(2)}) %all-to-all-start.2) | async-done | bytes 3145760 | tf_op jit(solution)/shard_map/all_to_all | solution.py:308
  334.7 1.7 reduce_sum.42
  336.4 2.1 convert_add_fusion
  339.4 1.5 pad_maximum_fusion
  340.9 3.0 copy.175
  343.9 1.8 copy.177
  (148 shorter events, 22.6 us)
Async XLA Ops:
  7.2 3.2 copy-start
  7.2 92.6 %all-gather.5.cloned.1.call-start = ((), (), s32[]{:S(2)}) async-start(), calls=%async_computation.3 | async-start | bytes 5898240 | tf_op jit(solution)/shard_map/all_gather | solution.py:203
  10.3 96.6 %copy-start.44 = (s32[1,8]{1,0:T(1,128)S(1)}, s32[1,8]{1,0:T(1,128)}, u32[]{:S(2)}) copy-start(s32[1,8]{1,0:T(1,128)} %param.10) | copy-start | bytes 100
  10.3 183.7 %all-gather.7.cloned.1.call-start = ((), (), s32[]{:S(2)}) async-start(), calls=%async_computation.4 | async-start | bytes 5898240 | tf_op jit(solution)/shard_map/all_gather | solution.py:268
  112.1 6.4 %copy-start.26 = (bf16[96,4096]{1,0:T(8,128)(2,1)S(1)}, bf16[96,4096]{1,0:T(8,128)(2,1)}, u32[]{:S(2)}) copy-start(bf16[96,4096]{1,0:T(8,128)(2,1)} %constant_dynamic-slice_fusion) | copy-start | bytes 2359300
  117.6 1.9 copy-start.40
  119.5 107.0 %all-to-all-start = ((bf16[96,4,1024]{2,0,1:T(8,128)(2,1)}), bf16[96,4,1024]{2,0,1:T(8,128)(2,1)}, u32[]{:S(2)}, u32[]{:S(2)}) async-start(bf16[96,4,1024]{2,0,1:T(8,128)(2,1)} %bitcast.167), calls=%async_computation | async-start | bytes 1572864 | tf_op jit(solution)/shard_map/all_to_all | solution.py:211
  123.7 117.2 %all-gather.9.cloned.1.call-start = ((), (), s32[]{:S(2)}) async-start(), calls=%async_computation.5 | async-start | bytes 1474560 | tf_op jit(solution)/shard_map/all_gather | solution.py:270
  125.3 0.6 copy-start.39
  126.7 8.0 %collective-permute-start = (bf16[384,256]{0,1:T(8,128)(2,1)}, bf16[384,256]{0,1:T(8,128)(2,1)}, u32[]{:S(2)}, u32[]{:S(2)}) collective-permute-start(bf16[384,256]{0,1:T(8,128)(2,1)} %pad_maximum_fusion.8), channel_id=1, source_target_pairs={{0,4},{4,0},{1,5},{5,1},{2,6},{6,2},{3,7},{7,3},{8,12},{12,8},{9,1... | collective-permute-start | bytes 589832 | tf_op jit(solution)/shard_map/ppermute | solution.py:251
  134.7 1.5 copy-start.27
  134.7 2.5 copy-start.29
  136.1 2.0 copy-start.18
  137.2 3.0 copy-start.3
  143.7 5.0 %copy-start.19 = (bf16[768,256]{0,1:T(8,128)(2,1)S(1)}, bf16[768,256]{0,1:T(8,128)(2,1)}, u32[]{:S(2)}) copy-start(bf16[768,256]{0,1:T(8,128)(2,1)} %copy-done.18) | copy-start | bytes 1179652
  143.7 5.9 %copy-start.8 = (f32[384,64]{1,0:T(8,128)S(1)}, f32[384,64]{1,0:T(8,128)}, u32[]{:S(2)}) copy-start(f32[384,64]{1,0:T(8,128)} %get-tuple-element.68) | copy-start | bytes 294916
  143.7 5.9 %copy-start.11 = (f32[384,64]{1,0:T(8,128)S(1)}, f32[384,64]{1,0:T(8,128)}, u32[]{:S(2)}) copy-start(f32[384,64]{1,0:T(8,128)} %get-tuple-element.69) | copy-start | bytes 294916
  147.5 1.2 copy-start.6
  199.4 1.8 copy-start.9
  199.4 1.7 copy-start.12
  199.5 3.1 copy-start.20
  202.6 1.8 copy-start.14
  202.6 1.8 copy-start.16
  204.4 4.3 %copy-start.2 = (f32[768,384,5]{1,0,2:T(8,128)}, f32[768,384,5]{1,0,2:T(8,128)S(1)}, u32[]{:S(2)}) copy-start(f32[768,384,5]{1,0,2:T(8,128)S(1)} %get-tuple-element.75) | copy-start | bytes 17694724
  204.5 1.7 copy-start.25
  208.7 4.6 %copy-start.33 = (bf16[384,5,128]{2,0,1:T(8,128)(2,1)S(1)}, bf16[384,5,128]{2,0,1:T(8,128)(2,1)}, u32[]{:S(2)}) copy-start(bf16[384,5,128]{2,0,1:T(8,128)(2,1)} %copy.217) | copy-start | bytes 1474564
  213.6 5.5 %copy-start.15 = (bf16[384,5,64]{2,0,1:T(8,128)(2,1)S(1)}, bf16[384,5,64]{2,0,1:T(8,128)(2,1)}, u32[]{:S(2)}) copy-start(bf16[384,5,64]{2,0,1:T(8,128)(2,1)} %copy-done.14) | copy-start | bytes 737284
  213.7 5.5 %copy-start.17 = (bf16[384,5,64]{2,0,1:T(8,128)(2,1)S(1)}, bf16[384,5,64]{2,0,1:T(8,128)(2,1)}, u32[]{:S(2)}) copy-start(bf16[384,5,64]{2,0,1:T(8,128)(2,1)} %copy-done.16) | copy-start | bytes 737284
  213.7 6.6 %copy-start.7 = (bf16[3,384,768]{1,2,0:T(8,128)(2,1)S(1)}, bf16[3,384,768]{1,2,0:T(8,128)(2,1)}, u32[]{:S(2)}) copy-start(bf16[3,384,768]{1,2,0:T(8,128)(2,1)} %copy-done.6) | copy-start | bytes 5308420
  219.1 2.3 copy-start.5
  219.1 1.2 copy-start.28
  219.2 1.5 copy-start.30
  219.2 3.2 copy-start.4
  219.2 3.3 copy-start.45
  222.5 2.3 copy-start.21
  224.8 0.9 copy-start.35
  225.7 12.3 %collective-permute-start.2 = (f32[384,256]{0,1:T(8,128)}, f32[384,256]{0,1:T(8,128)}, u32[]{:S(2)}, u32[]{:S(2)}) collective-permute-start(f32[384,256]{0,1:T(8,128)} %fusion.23), channel_id=1, source_target_pairs={{0,4},{4,0},{1,5},{5,1},{2,6},{6,2},{3,7},{7,3},{8,12},{12,8},{9,1... | collective-permute-start | bytes 1179656 | tf_op jit(solution)/shard_map/ppermute | solution.py:288
  229.7 40.6 %all-to-all-start.1 = ((bf16[4,384,1024]{2,1,0:T(8,128)(2,1)}), bf16[4,384,1024]{2,1,0:T(8,128)(2,1)S(1)}, u32[]{:S(2)}, u32[]{:S(2)}) async-start(bf16[4,384,1024]{2,1,0:T(8,128)(2,1)} %broadcast_in_dim.92), calls=%async_computation.1 | async-start | bytes 6291456 | tf_op jit(solution)/shard_map/all_to_all | solution.py:218
  233.5 7.4 %copy-start.10 = (f32[384,64]{1,0:T(8,128)S(1)}, f32[384,64]{1,0:T(8,128)}, u32[]{:S(2)}) copy-start(f32[384,64]{1,0:T(8,128)} %get-tuple-element.68) | copy-start | bytes 294916
  233.5 7.4 %copy-start.13 = (f32[384,64]{1,0:T(8,128)S(1)}, f32[384,64]{1,0:T(8,128)}, u32[]{:S(2)}) copy-start(f32[384,64]{1,0:T(8,128)} %get-tuple-element.69) | copy-start | bytes 294916
  233.5 70.6 %all-gather.11.cloned.1.call-start = ((), (), s32[]{:S(2)}) async-start(), calls=%async_computation.6 | async-start | bytes 3440640 | tf_op jit(solution)/shard_map/all_gather | solution.py:228
  233.8 4.2 %copy-start.22 = (f32[768,128]{0,1:T(8,128)S(1)}, f32[768,128]{0,1:T(8,128)}, u32[]{:S(2)}) copy-start(f32[768,128]{0,1:T(8,128)} %copy-done.21) | copy-start | bytes 1179652
  233.8 4.2 %copy-start.36 = (f32[768,128]{0,1:T(8,128)S(1)}, f32[768,128]{0,1:T(8,128)}, u32[]{:S(2)}) copy-start(f32[768,128]{0,1:T(8,128)} %copy-done.35) | copy-start | bytes 1179652
  247.9 22.8 %copy-start.31 = (bf16[384,3,128]{0,2,1:T(8,128)(2,1)S(1)}, bf16[384,3,128]{0,2,1:T(8,128)(2,1)}, u32[]{:S(2)}) copy-start(bf16[384,3,128]{0,2,1:T(8,128)(2,1)} %copy.152) | copy-start | bytes 884740
  247.9 22.8 %copy-start.37 = (bf16[384,128]{0,1:T(8,128)(2,1)S(1)}, bf16[384,128]{0,1:T(8,128)(2,1)}, u32[]{:S(2)}) copy-start(bf16[384,128]{0,1:T(8,128)(2,1)} %slice.169) | copy-start | bytes 294916
  270.4 0.9 copy-start.38
  270.4 10.7 %slice-start = ((s8[5242880]{0:T(1024)(128)(4,1)}), s8[4194304]{0:T(1024)(128)(4,1)S(1)}, s32[]{:S(2)}) async-start(s8[5242880]{0:T(1024)(128)(4,1)} %bitcast.179), calls=%async_computation.7 | async-start | bytes 8388608
  271.3 6.6 %copy-start.24 = (bf16[4,4,96,1024]{3,2,1,0:T(8,128)(2,1)}, bf16[4,4,96,1024]{3,2,1,0:T(8,128)(2,1)S(1)}, u32[]{:S(2)}) copy-start(bf16[4,4,96,1024]{3,2,1,0:T(8,128)(2,1)S(1)} %copy.158) | copy-start | bytes 9437188
  271.3 6.6 %copy-start.43 = (bf16[1536,384]{0,1:T(8,128)(2,1)S(1)}, bf16[1536,384]{0,1:T(8,128)(2,1)}, u32[]{:S(2)}) copy-start(bf16[1536,384]{0,1:T(8,128)(2,1)} %all-gather.9.cloned.1.call-done) | copy-start | bytes 3538948
  271.3 9.8 %slice-start.1 = ((s8[5242880]{0:T(1024)(128)(4,1)}), s8[1048576]{0:T(1024)(128)(4,1)S(1)}, s32[]{:S(2)}) async-start(s8[5242880]{0:T(1024)(128)(4,1)} %bitcast.179), calls=%async_computation.8 | async-start | bytes 2097152
  277.9 3.2 copy-start.34
  279.8 10.8 %collective-permute-start.1 = (bf16[512,384]{1,0:T(8,128)(2,1)S(1)}, bf16[512,384]{1,0:T(8,128)(2,1)S(1)}, u32[]{:S(2)}, u32[]{:S(2)}) collective-permute-start(bf16[512,384]{1,0:T(8,128)(2,1)S(1)} %dynamic-slice_convert_fusion.1), channel_id=1, source_target_pairs={{0,4},{4,0},{1,5},{5,1},{2,6},{6,2},{3,7},{7,3},{8,12},{12,8},{9,1... | collective-permute-start | bytes 1179656 | tf_op jit(solution)/shard_map/ppermute | solution.py:237
  293.6 41.1 %all-to-all-start.2 = ((bf16[384,4,1024]{2,0,1:T(8,128)(2,1)}), bf16[384,4,1024]{2,0,1:T(8,128)(2,1)S(1)}, u32[]{:S(2)}, u32[]{:S(2)}) async-start(bf16[384,4,1024]{2,0,1:T(8,128)(2,1)} %bitcast.157), calls=%async_computation.2 | async-start | bytes 6291456 | tf_op jit(solution)/shard_map/all_to_all | solution.py:308
  297.8 16.5 %copy-start.42 = (bf16[128,3,384]{2,0,1:T(8,128)(2,1)S(1)}, bf16[128,3,384]{2,0,1:T(8,128)(2,1)}, u32[]{:S(2)}) copy-start(bf16[128,3,384]{2,0,1:T(8,128)(2,1)} %get-tuple-element.73) | copy-start | bytes 884740
  304.1 10.1 %copy-start.41 = (bf16[128,5,384]{2,0,1:T(8,128)(2,1)S(1)}, bf16[128,5,384]{2,0,1:T(8,128)(2,1)}, u32[]{:S(2)}) copy-start(bf16[128,5,384]{2,0,1:T(8,128)(2,1)} %get-tuple-element.77) | copy-start | bytes 1474564
  309.9 1.8 copy-start.32
  312.8 23.6 %collective-permute-start.3 = (bf16[512,896]{0,1:T(8,128)(2,1)}, bf16[512,896]{0,1:T(8,128)(2,1)}, u32[]{:S(2)}, u32[]{:S(2)}) collective-permute-start(bf16[512,896]{0,1:T(8,128)(2,1)} %dynamic-slice_convert_fusion), channel_id=1, source_target_pairs={{0,4},{4,0},{1,5},{5,1},{2,6},{6,2},{3,7},{7,3},{8,12},{12,8},{9,1... | collective-permute-start | bytes 2752520 | tf_op jit(solution)/shard_map/ppermute | solution.py:237
  336.4 3.0 copy-start.23
  339.3 7.2 %copy-start.1 = (bf16[384,4096]{1,0:T(8,128)(2,1)S(1)}, bf16[384,4096]{1,0:T(8,128)(2,1)}, u32[]{:S(2)}) copy-start(bf16[384,4096]{1,0:T(8,128)(2,1)} %param.6) | copy-start | bytes 9437188
Sparse Core Ops, SparseCore 0:
  10.8 88.9 all-gather.4
  102.0 92.0 all-gather.6
  211.9 28.2 all-gather.8
  248.0 56.0 all-gather.10

commit v21 on v17

--- a/solution.py
+++ b/solution.py
@@ -285,7 +285,8 @@
     if ctx_count == 2:
         own_part = lax.dynamic_slice_in_dim(parts_kv, ctx_index * num_rows, num_rows, 0)
         away_part = lax.dynamic_slice_in_dim(parts_kv, (1 - ctx_index) * num_rows, num_rows, 0)
-        grad_kv = own_part + lax.ppermute(away_part, "ctx", [(0, 1), (1, 0)])
+        got_part = lax.ppermute(away_part.astype(jnp.bfloat16), "ctx", [(0, 1), (1, 0)])
+        grad_kv = own_part + got_part.astype(jnp.float32)
     else:
         grad_kv = lax.psum_scatter(parts_kv, "ctx", scatter_dimension=0, tiled=True)
     grad_k, grad_v = grad_kv[:, :128], grad_kv[:, 128:]

time: 323 us -> 323 us (level)
    ppermute x1, waiting for transfers between devices: 8.47 us -> 4.29 us  [local(): lax.ppermute(away_part.astype(jnp.bfloat16), 'ctx', [(0, 1), (1, 0)])]
    unnamed x93 -> x91, local copies, waits for them, and re-layouts: 17.9 us -> 19 us
where the time goes in v21:
time: 323 us; the launch traced here: 318 us
  waiting for transfers between devices  170 us (53%)
  matrix products  48.1 us (15%)
  local copies, waits for them, and re-layouts  40.1 us (12%)
  other arithmetic  25.3 us (8%)
  starting transfers between devices  20.2 us (6%)
  between operations  14.9 us (5%)
    all_gather x1, waiting for transfers between devices, local(): full_a = lax.all_gather(local_a, rows_axes, axis=0, tiled=True)  101 us
    unnamed x91, local copies, waits for them, and re-layouts  19 us
    all_gather x1, waiting for transfers between devices, weight_grad(): gathered = lax.all_gather(d_rows, 'dp', axis=0, tiled=True)  17.8 us
    all_gather x1, waiting for transfers between devices, local(): full_b = lax.all_gather(w_rest, rows_axes, axis=0, tiled=True)  15.7 us
    ppermute x2, waiting for transfers between devices, weight_grad(): sent = lax.ppermute(away_part.astype(jnp.bfloat16), 'ctx', [(0, 1), (1, 0)])  12 us
    all_to_all x1, waiting for transfers between devices, local(): lax.all_to_all(input_part.astype(jnp.bfloat16).reshape(num_rows, head_gro...  10.9 us
    dot_general x2, matrix products, attend_whole(): jnp.einsum('rhd,kd->hrk', dout_rows, value_all, preferred_element_type=jn...  8.92 us
  transfers between devices with their start and end apart: 11, of which 9 were waited for; matrix products, arithmetic and copies ran while one was open for 32% of the time, Pallas kernels for 0%

profile of v21, /device:TPU:0, one launch (start us, length us, event | category | flops | bytes accessed | tf_op | source)
XLA Modules:
  0.0 318.2 jit_solution(3018745162552676950)
XLA Ops:
  7.2 1.2 slice.83
  8.5 1.9 pad_maximum_fusion.1
  11.4 101.1 %all-gather.5.cloned.1.call-done = bf16[4096,768]{1,0:T(8,128)(2,1)} async-done(((bf16[512,768]{1,0:T(8,128)(2,1)}), bf16[4096,768]{1,0:T(8,128)(2,1)}) %all-gather.5.cloned.1.call-update) | async-done | bytes 6291472 | tf_op jit(solution)/shard_map/all_gather | solution.py:203
  112.5 1.9 slice.96
  114.6 2.3 copy.137
  117.0 1.9 fusion.56
  118.9 1.9 copy.206
  122.3 1.5 multiply_cosine_fusion
  123.8 5.6 %convolution_bitcast_fusion = f32[384,768]{0,1:T(8,128)S(1)} fusion(bf16[4096,768]{1,0:T(8,128)(2,1)} %all-gather.5.cloned.1.call-done, bf16[384,4096]{1,0:T(8,128)(2,1)S(1)} %copy-done), kind=kOutput, calls=%fused_computation.27 | convolution fusion | flops 2415919104 | bytes 10616832 | tf_op jit(solution)/shard_map/dot_general | solution.py:241
  129.5 1.0 slice.115
  131.4 4.7 %all-to-all-start = ((bf16[96,4,1024]{2,0,1:T(8,128)(2,1)}), bf16[96,4,1024]{2,0,1:T(8,128)(2,1)}, u32[]{:S(2)}, u32[]{:S(2)}) async-start(bf16[96,4,1024]{2,0,1:T(8,128)(2,1)} %bitcast.171), calls=%async_computation | async-start | bytes 1572864 | tf_op jit(solution)/shard_map/all_to_all | solution.py:211
  139.5 2.0 fusion.58
  141.5 2.1 copy.202
  143.7 2.1 copy.201
  145.8 1.7 subtract_convert_fusion.3
  147.5 1.5 maximum_select_fusion
  149.0 1.2 fusion.10
  150.3 1.2 select_reduce_fusion.1
  151.5 2.4 bitcast_convert_fusion.1
  153.9 2.3 copy.174
  156.2 1.5 multiply_reduce_fusion.1
  157.7 4.5 %fusion.6 = bf16[4,384,768]{1,2,0:T(8,128)(2,1)S(1)} fusion(f32[768,384,4]{1,0,2:T(8,128)} %copy-done.2, f32[4,384]{1,0:T(4,128)S(1)} %multiply_reduce_fusion.1, f32[4,384]{1,0:T(4,128)S(1)} %log_add_fusion.1, pred[384,768]{0,1:T(8,128)(4,1)S(1)} %fusion.16, bf16[768,256]{0,1:T(8,128)(2,1)} %copy-done.12, bf16[384,8,128]{0,2,1:T(8,128)(2,1)} %bitcast.167), kind=kOutput, calls=%fused_computation.11 | convolution fusion | flops 311427072 | bytes 7974912 | tf_op jit(solution)/shard_map/rhd,kd->hrk/dot_general | solution.py:90
  162.3 1.4 copy-done.4
  163.7 1.1 convolution_bitcast_fusion.2
  165.1 1.0 pad_maximum_fusion.9
  166.1 1.9 copy.142
  168.1 1.4 all-to-all-done
  169.5 3.2 %broadcast_in_dim.79 = bf16[4,384,1024]{2,1,0:T(8,128)(2,1)} broadcast(bf16[384,1024]{1,0:T(8,128)(2,1)} %bitcast.29), dimensions={1,2} | broadcast | bytes 3932160 | tf_op jit(solution)/shard_map/broadcast_in_dim | solution.py:217
  172.7 4.6 %all-to-all-start.1 = ((bf16[4,384,1024]{2,1,0:T(8,128)(2,1)}), bf16[4,384,1024]{2,1,0:T(8,128)(2,1)}, u32[]{:S(2)}, u32[]{:S(2)}) async-start(bf16[4,384,1024]{2,1,0:T(8,128)(2,1)} %broadcast_in_dim.79), calls=%async_computation.1 | async-start | bytes 6291456 | tf_op jit(solution)/shard_map/all_to_all | solution.py:218
  177.4 15.7 %all-gather.7.cloned.1.call-done = bf16[4096,512]{1,0:T(8,128)(2,1)} async-done(((bf16[512,512]{1,0:T(8,128)(2,1)}), bf16[4096,512]{1,0:T(8,128)(2,1)}) %all-gather.7.cloned.1.call-update) | async-done | bytes 4194320 | tf_op jit(solution)/shard_map/all_gather | solution.py:268
  193.3 4.6 %fusion.59 = f32[512,384]{1,0:T(8,128)S(1)} fusion(bf16[4096,512]{1,0:T(8,128)(2,1)} %all-gather.7.cloned.1.call-done, bf16[384,4096]{1,0:T(8,128)(2,1)S(1)} %copy-done), kind=kOutput, calls=%fused_computation.128 | convolution fusion | flops 1610612736 | bytes 8126464 | tf_op jit(solution)/shard_map/dot_general | solution.py:271
  198.5 1.2 subtract_convert_fusion.1
  199.7 1.2 fusion.11
  201.0 1.2 select_reduce_fusion
  202.2 2.4 bitcast_convert_fusion
  204.6 1.4 copy.185
  206.3 4.4 %fusion.1 = bf16[4,384,768]{1,2,0:T(8,128)(2,1)S(1)} fusion(f32[768,384,4]{1,0,2:T(8,128)} %copy-done.3, f32[4,384]{1,0:T(4,128)S(1)} %multiply_reduce_fusion, f32[4,384]{1,0:T(4,128)S(1)} %log_add_fusion, pred[384,768]{0,1:T(8,128)(4,1)S(1)} %fusion.16, bf16[768,256]{0,1:T(8,128)(2,1)S(1)} %copy-done.14, bf16[384,8,128]{0,2,1:T(8,128)(2,1)S(1)} %bitcast.168), kind=kOutput, calls=%fused_computation.3 | convolution fusion | flops 311427072 | bytes 7974912 | tf_op jit(solution)/shard_map/rhd,kd->hrk/dot_general | solution.py:90
  210.8 1.6 convolution_bitcast_fusion.3
  212.4 1.0 convolution_bitcast_fusion.5
  213.5 1.9 fusion.15
  215.4 1.0 fusion.14
  216.4 1.6 collective-permute-start.2
  218.0 1.1 convolution_bitcast_fusion.1
  219.0 4.3 %collective-permute-done.2 = bf16[384,256]{0,1:T(8,128)(2,1)S(1)} collective-permute-done((bf16[384,256]{0,1:T(8,128)(2,1)S(1)}, bf16[384,256]{0,1:T(8,128)(2,1)S(1)}, u32[]{:S(2)}, u32[]{:S(2)}) %collective-permute-start.2) | collective-permute-done | bytes 196640 | tf_op jit(solution)/shard_map/ppermute | solution.py:288
  223.9 6.3 %all-gather.9.cloned.1.call-done = bf16[1536,512]{0,1:T(8,128)(2,1)} async-done(((bf16[384,512]{0,1:T(8,128)(2,1)}), bf16[1536,512]{0,1:T(8,128)(2,1)}) %all-gather.9.cloned.1.call-update) | async-done | bytes 1572880 | tf_op jit(solution)/shard_map/all_gather | solution.py:270
  232.0 2.3 copy.148
  234.3 6.1 %fusion.17 = f32[384,4096]{1,0:T(8,128)S(1)} fusion(bf16[4096,768]{1,0:T(8,128)(2,1)} %all-gather.5.cloned.1.call-done, bf16[384,128]{0,1:T(8,128)(2,1)S(1)} %copy-done.29, bf16[384,128]{0,1:T(8,128)(2,1)S(1)} %copy-done.31, bf16[384,512]{0,1:T(8,128)(2,1)} %bitcast.176), kind=kOutput, calls=%fused_computation.63 | convolution fusion | flops 2417688576 | bytes 13172736 | tf_op jit(solution)/shard_map/dot_general | solution.py:296
  240.4 1.8 fusion.60
  242.4 1.8 collective-permute-start.1
  244.1 1.9 convolution_add_fusion
  246.0 9.9 %collective-permute-done.1 = bf16[512,512]{1,0:T(8,128)(2,1)S(1)} collective-permute-done((bf16[512,512]{1,0:T(8,128)(2,1)S(1)}, bf16[512,512]{1,0:T(8,128)(2,1)S(1)}, u32[]{:S(2)}, u32[]{:S(2)}) %collective-permute-start.1) | collective-permute-done | bytes 524320 | tf_op jit(solution)/shard_map/ppermute | solution.py:237
  255.9 1.1 convert_add_fusion.1
  257.0 2.1 copy.211
  259.1 5.2 %all-to-all-start.2 = ((bf16[384,4,1024]{2,0,1:T(8,128)(2,1)}), bf16[384,4,1024]{2,0,1:T(8,128)(2,1)}, u32[]{:S(2)}, u32[]{:S(2)}) async-start(bf16[384,4,1024]{2,0,1:T(8,128)(2,1)} %bitcast.161), calls=%async_computation.2 | async-start | bytes 6291456 | tf_op jit(solution)/shard_map/all_to_all | solution.py:309
  264.3 17.8 %all-gather.11.cloned.1.call-done = bf16[1536,768]{0,1:T(8,128)(2,1)} async-done(((bf16[384,768]{0,1:T(8,128)(2,1)}), bf16[1536,768]{0,1:T(8,128)(2,1)}) %all-gather.11.cloned.1.call-update) | async-done | bytes 2359312 | tf_op jit(solution)/shard_map/all_gather | solution.py:228
  282.1 4.4 %fusion.61 = f32[1024,768]{1,0:T(8,128)S(1)} fusion(bf16[1536,1024]{1,0:T(8,128)(2,1)S(1)} %bitcast.165, bf16[1536,768]{0,1:T(8,128)(2,1)} %all-gather.11.cloned.1.call-done), kind=kOutput, calls=%fused_computation.130 | convolution fusion | flops 2415919104 | bytes 8650752 | tf_op jit(solution)/shard_map/dot_general | solution.py:229
  286.5 1.1 dynamic-slice_convert_fusion
  287.6 1.5 collective-permute-start.3
  289.2 1.2 copy.165
  290.3 10.9 %all-to-all-done.2 = bf16[384,4,1024]{2,0,1:T(8,128)(2,1)} async-done(((bf16[384,4,1024]{2,0,1:T(8,128)(2,1)}), bf16[384,4,1024]{2,0,1:T(8,128)(2,1)}, u32[]{:S(2)}, u32[]{:S(2)}) %all-to-all-start.2) | async-done | bytes 3145760 | tf_op jit(solution)/shard_map/all_to_all | solution.py:309
  301.3 3.8 %reduce_sum.42 = bf16[384,1024]{1,0:T(8,128)(2,1)} reduce(bf16[384,4,1024]{2,0,1:T(8,128)(2,1)} %all-to-all-done.2, bf16[]{:T(256)} %constant.40.clone.1), dimensions={1}, to_apply=%region_6.7 | reduce | flops 1179648 | bytes 3932162 | tf_op jit(solution)/shard_map/reduce_sum | solution.py:313
  305.0 2.1 collective-permute-done.3
  307.1 1.8 convert_add_fusion
  309.9 1.5 pad_maximum_fusion
  (128 shorter events, 11.9 us)
Async XLA Ops:
  7.2 3.3 %copy-start = (bf16[384,4096]{1,0:T(8,128)(2,1)S(1)}, bf16[384,4096]{1,0:T(8,128)(2,1)}, u32[]{:S(2)}) copy-start(bf16[384,4096]{1,0:T(8,128)(2,1)} %param.6) | copy-start | bytes 9437188
  7.2 107.3 %copy-start.35 = (s32[1,8]{1,0:T(1,128)S(1)}, s32[1,8]{1,0:T(1,128)}, u32[]{:S(2)}) copy-start(s32[1,8]{1,0:T(1,128)} %param.10) | copy-start | bytes 100
  7.2 105.3 %all-gather.5.cloned.1.call-start = ((), (), s32[]{:S(2)}) async-start(), calls=%async_computation.3 | async-start | bytes 7077888 | tf_op jit(solution)/shard_map/all_gather | solution.py:203
  10.4 182.6 %all-gather.7.cloned.1.call-start = ((), (), s32[]{:S(2)}) async-start(), calls=%async_computation.4 | async-start | bytes 4718592 | tf_op jit(solution)/shard_map/all_gather | solution.py:268
  123.8 6.7 %copy-start.23 = (bf16[96,4096]{1,0:T(8,128)(2,1)S(1)}, bf16[96,4096]{1,0:T(8,128)(2,1)}, u32[]{:S(2)}) copy-start(bf16[96,4096]{1,0:T(8,128)(2,1)} %constant_dynamic-slice_fusion) | copy-start | bytes 2359300
  129.4 2.0 copy-start.26
  131.4 38.0 %all-to-all-start = ((bf16[96,4,1024]{2,0,1:T(8,128)(2,1)}), bf16[96,4,1024]{2,0,1:T(8,128)(2,1)}, u32[]{:S(2)}, u32[]{:S(2)}) async-start(bf16[96,4,1024]{2,0,1:T(8,128)(2,1)} %bitcast.171), calls=%async_computation | async-start | bytes 1572864 | tf_op jit(solution)/shard_map/all_to_all | solution.py:211
  137.6 0.6 copy-start.27
  138.9 8.6 %collective-permute-start = (bf16[384,256]{0,1:T(8,128)(2,1)}, bf16[384,256]{0,1:T(8,128)(2,1)}, u32[]{:S(2)}, u32[]{:S(2)}) collective-permute-start(bf16[384,256]{0,1:T(8,128)(2,1)} %pad_maximum_fusion.12), channel_id=1, source_target_pairs={{0,4},{4,0},{1,5},{5,1},{2,6},{6,2},{3,7},{7,3},{8,12},{12,8},{9,1... | collective-permute-start | bytes 589832 | tf_op jit(solution)/shard_map/ppermute | solution.py:251
  147.5 1.5 copy-start.15
  147.5 2.8 copy-start.17
  149.0 2.5 copy-start.12
  150.3 3.6 %copy-start.2 = (f32[768,384,4]{1,0,2:T(8,128)}, f32[768,384,4]{1,0,2:T(8,128)S(1)}, u32[]{:S(2)}) copy-start(f32[768,384,4]{1,0,2:T(8,128)S(1)} %get-tuple-element.73) | copy-start | bytes 14155780
  157.7 6.0 %copy-start.13 = (bf16[768,256]{0,1:T(8,128)(2,1)S(1)}, bf16[768,256]{0,1:T(8,128)(2,1)}, u32[]{:S(2)}) copy-start(bf16[768,256]{0,1:T(8,128)(2,1)} %copy-done.12) | copy-start | bytes 1179652
  157.7 7.0 %copy-start.6 = (f32[384,64]{1,0:T(8,128)S(1)}, f32[384,64]{1,0:T(8,128)}, u32[]{:S(2)}) copy-start(f32[384,64]{1,0:T(8,128)} %get-tuple-element.70) | copy-start | bytes 294916
  157.7 7.0 %copy-start.8 = (f32[384,64]{1,0:T(8,128)S(1)}, f32[384,64]{1,0:T(8,128)}, u32[]{:S(2)}) copy-start(f32[384,64]{1,0:T(8,128)} %get-tuple-element.71) | copy-start | bytes 294916
  162.3 1.4 copy-start.4
  172.7 59.2 %all-to-all-start.1 = ((bf16[4,384,1024]{2,1,0:T(8,128)(2,1)}), bf16[4,384,1024]{2,1,0:T(8,128)(2,1)}, u32[]{:S(2)}, u32[]{:S(2)}) async-start(bf16[4,384,1024]{2,1,0:T(8,128)(2,1)} %broadcast_in_dim.79), calls=%async_computation.1 | async-start | bytes 6291456 | tf_op jit(solution)/shard_map/all_to_all | solution.py:218
  177.3 52.8 %all-gather.9.cloned.1.call-start = ((), (), s32[]{:S(2)}) async-start(), calls=%async_computation.5 | async-start | bytes 1966080 | tf_op jit(solution)/shard_map/all_gather | solution.py:270
  193.1 89.0 %all-gather.11.cloned.1.call-start = ((), (), s32[]{:S(2)}) async-start(), calls=%async_computation.6 | async-start | bytes 2949120 | tf_op jit(solution)/shard_map/all_gather | solution.py:228
  197.9 1.9 copy-start.14
  201.0 3.6 %copy-start.3 = (f32[768,384,4]{1,0,2:T(8,128)}, f32[768,384,4]{1,0,2:T(8,128)S(1)}, u32[]{:S(2)}) copy-start(f32[768,384,4]{1,0,2:T(8,128)S(1)} %get-tuple-element.77) | copy-start | bytes 14155780
  202.1 3.8 %copy-start.25 = (bf16[384,4,128]{2,0,1:T(8,128)(2,1)S(1)}, bf16[384,4,128]{2,0,1:T(8,128)(2,1)}, u32[]{:S(2)}) copy-start(bf16[384,4,128]{2,0,1:T(8,128)(2,1)} %copy.206) | copy-start | bytes 1179652
  202.2 4.1 %copy-start.21 = (bf16[384,1024]{0,1:T(8,128)(2,1)S(1)}, bf16[384,1024]{0,1:T(8,128)(2,1)}, u32[]{:S(2)}) copy-start(bf16[384,1024]{0,1:T(8,128)(2,1)} %copy.137) | copy-start | bytes 2359300
  206.0 4.7 %slice-start.2 = ((s8[4718592]{0:T(1024)(128)(4,1)}), s8[4194304]{0:T(1024)(128)(4,1)S(1)}, s32[]{:S(2)}) async-start(s8[4718592]{0:T(1024)(128)(4,1)} %bitcast.158), calls=%async_computation.9 | async-start | bytes 8388608
  206.3 4.4 %slice-start.3 = ((s8[4718592]{0:T(1024)(128)(4,1)}), s8[524288]{0:T(1024)(128)(4,1)S(1)}, s32[]{:S(2)}) async-start(s8[4718592]{0:T(1024)(128)(4,1)} %bitcast.158), calls=%async_computation.10 | async-start | bytes 1048576
  206.3 7.1 %slice-start = ((s8[4718592]{0:T(1024)(128)(4,1)}), s8[524288]{0:T(1024)(128)(4,1)S(1)}, s32[]{:S(2)}) async-start(s8[4718592]{0:T(1024)(128)(4,1)} %bitcast.156), calls=%async_computation.7 | async-start | bytes 1048576
  210.7 2.7 slice-start.1
  210.8 2.7 copy-start.22
  213.4 1.9 copy-start.5
  213.4 1.9 copy-start.16
  213.5 1.9 copy-start.18
  215.4 14.8 %copy-start.7 = (f32[384,64]{1,0:T(8,128)S(1)}, f32[384,64]{1,0:T(8,128)}, u32[]{:S(2)}) copy-start(f32[384,64]{1,0:T(8,128)} %get-tuple-element.70) | copy-start | bytes 294916
  215.4 14.8 %copy-start.9 = (f32[384,64]{1,0:T(8,128)S(1)}, f32[384,64]{1,0:T(8,128)}, u32[]{:S(2)}) copy-start(f32[384,64]{1,0:T(8,128)} %get-tuple-element.71) | copy-start | bytes 294916
  216.4 6.9 %collective-permute-start.2 = (bf16[384,256]{0,1:T(8,128)(2,1)S(1)}, bf16[384,256]{0,1:T(8,128)(2,1)S(1)}, u32[]{:S(2)}, u32[]{:S(2)}) collective-permute-start(bf16[384,256]{0,1:T(8,128)(2,1)S(1)} %fusion.20), channel_id=1, source_target_pairs={{0,4},{4,0},{1,5},{5,1},{2,6},{6,2},{3,7},{7,3},{8,12},{12,8},{9,1... | collective-permute-start | bytes 589832 | tf_op jit(solution)/shard_map/ppermute | solution.py:288
  223.4 8.5 %copy-start.28 = (bf16[384,128]{0,1:T(8,128)(2,1)}, bf16[384,128]{0,1:T(8,128)(2,1)S(1)}, u32[]{:S(2)}) copy-start(bf16[384,128]{0,1:T(8,128)(2,1)S(1)} %slice.169) | copy-start | bytes 294916
  223.9 8.0 %copy-start.30 = (bf16[384,128]{0,1:T(8,128)(2,1)}, bf16[384,128]{0,1:T(8,128)(2,1)S(1)}, u32[]{:S(2)}) copy-start(bf16[384,128]{0,1:T(8,128)(2,1)S(1)} %maximum_bitcast_fusion.1) | copy-start | bytes 294916
  231.9 2.4 copy-start.29
  231.9 2.4 copy-start.31
  234.3 6.1 %copy-start.19 = (bf16[4,4,96,1024]{3,2,1,0:T(8,128)(2,1)}, bf16[4,4,96,1024]{3,2,1,0:T(8,128)(2,1)S(1)}, u32[]{:S(2)}) copy-start(bf16[4,4,96,1024]{3,2,1,0:T(8,128)(2,1)S(1)} %copy.148) | copy-start | bytes 9437188
  234.3 6.1 %copy-start.34 = (bf16[1536,512]{0,1:T(8,128)(2,1)S(1)}, bf16[1536,512]{0,1:T(8,128)(2,1)}, u32[]{:S(2)}) copy-start(bf16[1536,512]{0,1:T(8,128)(2,1)} %all-gather.9.cloned.1.call-done) | copy-start | bytes 4718596
  240.4 3.7 %copy-start.11 = (bf16[4096,512]{1,0:T(8,128)(2,1)S(1)}, bf16[4096,512]{1,0:T(8,128)(2,1)}, u32[]{:S(2)}) copy-start(bf16[4096,512]{1,0:T(8,128)(2,1)} %all-gather.7.cloned.1.call-done) | copy-start | bytes 12582916
  242.4 13.5 %collective-permute-start.1 = (bf16[512,512]{1,0:T(8,128)(2,1)S(1)}, bf16[512,512]{1,0:T(8,128)(2,1)S(1)}, u32[]{:S(2)}, u32[]{:S(2)}) collective-permute-start(bf16[512,512]{1,0:T(8,128)(2,1)S(1)} %dynamic-slice_convert_fusion.1), channel_id=1, source_target_pairs={{0,4},{4,0},{1,5},{5,1},{2,6},{6,2},{3,7},{7,3},{8,12},{12,8},{9,1... | collective-permute-start | bytes 1572872 | tf_op jit(solution)/shard_map/ppermute | solution.py:237
  259.1 23.0 %copy-start.20 = (bf16[4,4,96,1024]{3,2,1,0:T(8,128)(2,1)S(1)}, bf16[4,4,96,1024]{3,2,1,0:T(8,128)(2,1)}, u32[]{:S(2)}) copy-start(bf16[4,4,96,1024]{3,2,1,0:T(8,128)(2,1)} %copy-done.19) | copy-start | bytes 9437188
  259.1 42.2 %all-to-all-start.2 = ((bf16[384,4,1024]{2,0,1:T(8,128)(2,1)}), bf16[384,4,1024]{2,0,1:T(8,128)(2,1)}, u32[]{:S(2)}, u32[]{:S(2)}) async-start(bf16[384,4,1024]{2,0,1:T(8,128)(2,1)} %bitcast.161), calls=%async_computation.2 | async-start | bytes 6291456 | tf_op jit(solution)/shard_map/all_to_all | solution.py:309
  264.3 24.8 %copy-start.32 = (bf16[128,4,384]{2,0,1:T(8,128)(2,1)S(1)}, bf16[128,4,384]{2,0,1:T(8,128)(2,1)}, u32[]{:S(2)}) copy-start(bf16[128,4,384]{2,0,1:T(8,128)(2,1)} %get-tuple-element.75) | copy-start | bytes 1179652
  282.1 6.9 %copy-start.33 = (bf16[128,4,384]{2,0,1:T(8,128)(2,1)S(1)}, bf16[128,4,384]{2,0,1:T(8,128)(2,1)}, u32[]{:S(2)}) copy-start(bf16[128,4,384]{2,0,1:T(8,128)(2,1)} %get-tuple-element.79) | copy-start | bytes 1179652
  286.5 2.6 copy-start.24
  287.6 19.6 %collective-permute-start.3 = (bf16[512,768]{1,0:T(8,128)(2,1)}, bf16[512,768]{1,0:T(8,128)(2,1)}, u32[]{:S(2)}, u32[]{:S(2)}) collective-permute-start(bf16[512,768]{1,0:T(8,128)(2,1)} %dynamic-slice_convert_fusion), channel_id=1, source_target_pairs={{0,4},{4,0},{1,5},{5,1},{2,6},{6,2},{3,7},{7,3},{8,12},{12,8},{9,1... | collective-permute-start | bytes 2359304 | tf_op jit(solution)/shard_map/ppermute | solution.py:237
  301.3 10.1 %copy-start.1 = (bf16[384,4096]{1,0:T(8,128)(2,1)S(1)}, bf16[384,4096]{1,0:T(8,128)(2,1)}, u32[]{:S(2)}) copy-start(bf16[384,4096]{1,0:T(8,128)(2,1)} %param.6) | copy-start | bytes 9437188
  305.0 4.9 %copy-start.10 = (f32[512,512]{1,0:T(8,128)S(1)}, f32[512,512]{1,0:T(8,128)}, u32[]{:S(2)}) copy-start(f32[512,512]{1,0:T(8,128)} %convert_add_fusion.1) | copy-start | bytes 3145732
Sparse Core Ops, SparseCore 0:
  10.8 101.7 all-gather.4
  114.7 78.3 all-gather.6
  194.6 35.4 all-gather.8
  232.2 49.8 all-gather.10
